TPU v7x, 32 devices: a whole 2x2x4 slice. The times are simulated.
32 devices in a mesh: gx: 4 (over z), gy: 4 (over x, core), sa: 2 (over y).
Axes of the slice: x: 2, y: 2, z: 4, core: 2. Of those that a mesh axis runs over, the one named last changes fastest.
Arguments:
- source: float32 [16, 256, 1024], P('sa', 'gx', 'gy'), parts along dimension 0, may hold values from -6 to 6
- sample_seeds: int32 [16], P('sa'), parts along dimension 0, may hold values from 0 to 7, each once
- perm_levels: float32 [16, 8], P('sa'), parts along dimension 0, may hold values from 0.1 to 10
- perm_classes: int32 [256, 1024], P('gx', 'gy'), may hold values from 0 to 7
Outputs:
- solution: float32 [16, 256, 1024], P('sa', 'gx', 'gy'), parts along dimension 0
- correction: float32 [16, 128, 512], P('sa', 'gx', 'gy'), parts along dimension 0
There are 2 independent parts, one for each index of `sa`. A program takes and returns all parts, laid end to end along the dimension named above; an argument that names none is the same for every part. Nothing has to cross between parts.
Inputs may be any that keep to these rules, and one draw needn't show every extreme that they name: `sample_seeds`: each of 0 to 7 appears once.
All inputs are finite; a program needn't handle non-finite values.
Results may differ from a plain program's by a relative error of at most 0.0003.
Values sent between devices are 32-bit elements; how exact they have to be, the bound alone decides.
No kernel may reach another device: no remote copies, remote signals or barrier semaphores. Data moves between devices by JAX's collectives and lax.ppermute only.
A program may use at most 128 MiB of HBM per device.

v0:
```python
import jax
import jax.numpy as jnp
from jax import lax
from jax.sharding import PartitionSpec as P

SWEEPS = 4


DAMPING = 0.8


def with_halo(block, sides, width):
    for axis, dim in sides:
        count = lax.axis_size(axis)
        forward = [(i, i + 1) for i in range(count - 1)]
        backward = [(target, source) for source, target in forward]
        low = lax.ppermute(
            lax.slice_in_dim(block, block.shape[dim] - width, None, axis=dim), axis, forward
        )
        high = lax.ppermute(lax.slice_in_dim(block, 0, width, axis=dim), axis, backward)
        block = jnp.concatenate([low, block, high], axis=dim)
    return block


def neighbours(padded):
    return (
        padded[..., 2:, 1:-1],
        padded[..., :-2, 1:-1],
        padded[..., 1:-1, 2:],
        padded[..., 1:-1, :-2],
    )


def couplings(perm_padded):
    middle = perm_padded[..., 1:-1, 1:-1]
    linkage = tuple(
        (
            jnp.where(beside > 0.0, 2.0 * middle * beside / (middle + beside), 2.0 * middle)
            for beside in neighbours(perm_padded)
        )
    )
    diagonal = linkage[0] + linkage[1] + linkage[2] + linkage[3]
    return (linkage, diagonal)


def operator(linkage, diagonal, current, padded):
    beside_all = neighbours(padded)
    return diagonal * current - (
        linkage[0] * beside_all[0]
        + linkage[1] * beside_all[1]
        + linkage[2] * beside_all[2]
        + linkage[3] * beside_all[3]
    )


def permeability(sample_seeds, perm_levels, perm_classes):
    choose = (
        sample_seeds[:, None] == jnp.arange(perm_levels.shape[0], dtype=jnp.int32)[None, :]
    ).astype(jnp.float32)
    sample_levels = jnp.sum(choose[:, :, None] * perm_levels[None, :, :], axis=1)
    result = jnp.zeros((sample_seeds.shape[0],) + perm_classes.shape, jnp.float32)
    for category in range(perm_levels.shape[1]):
        result = result + jnp.where(
            perm_classes[None] == category, sample_levels[:, category, None, None], 0.0
        )
    return result


def restrict(values):
    return values.reshape(values.shape[0], values.shape[1] // 2, 2, values.shape[2] // 2, 2).sum(
        axis=(2, 4)
    )


def shards(source, sample_seeds, perm_levels, perm_classes):
    depth = 2
    perm_field = permeability(sample_seeds, perm_levels, perm_classes)
    perm_wide = with_halo(perm_field, (("gx", 1), ("gy", 2)), depth)
    linkage, diagonal = couplings(perm_wide[:, 1:-1, 1:-1])
    current = DAMPING * source / diagonal
    for sweep_index in range(SWEEPS):
        padded = with_halo(current, (("gx", 1), ("gy", 2)), 1)
        residual = source - operator(linkage, diagonal, current, padded)
        if sweep_index + 1 < SWEEPS:
            current = current + DAMPING * residual / diagonal
    coarse_rhs = restrict(residual)
    coarse_wide = 0.25 * restrict(perm_wide)
    coarse_links, coarse_diagonal = couplings(coarse_wide)
    first = DAMPING * coarse_rhs / coarse_diagonal
    padded_first = with_halo(first, (("gx", 1), ("gy", 2)), 1)
    correction = (
        first
        + DAMPING
        * (coarse_rhs - operator(coarse_links, coarse_diagonal, first, padded_first))
        / coarse_diagonal
    )
    updated = current + jnp.repeat(jnp.repeat(correction, 2, axis=1), 2, axis=2)
    return (updated, correction)


def solution(mesh):
    placed = (P("sa", "gx", "gy"), P("sa"), P("sa", None), P("gx", "gy"))
    return jax.shard_map(
        shards,
        mesh=mesh,
        in_specs=placed,
        out_specs=(P("sa", "gx", "gy"), P("sa", "gx", "gy")),
        check_vma=False,
    )
```

profile of v0, /device:TPU:18, one launch (start us, length us, event | category | flops | bytes accessed | tf_op | source)
XLA Modules:
  0.0 244.7 jit_solution(13801891095398662126)
XLA Ops:
  6.3 2.4 collective-permute-start
  9.1 3.5 %collective-permute-start.1 = (f32[8,2,256]{2,0,1:T(8,128)S(1)}, f32[8,2,256]{2,0,1:T(8,128)S(1)}, u32[]{:S(2)}, u32[]{:S(2)}) collective-permute-start(f32[8,2,256]{2,0,1:T(8,128)S(1)} %copy.343), channel_id=1, source_target_pairs={{0,8},{8,16},{16,24},{1,9},{9,17},{17,25},{2,10},{10,18},{18,26},{... | collective-permute-start | bytes 49160 | tf_op jit(solution)/shard_map/ppermute | solution.py:17
  13.0 1.7 collective-permute-done.1
  16.1 1.9 collective-permute-start.3
  18.1 3.6 %collective-permute-start.2 = (f32[8,68,2]{1,0,2:T(8,128)S(1)}, f32[8,68,2]{1,0,2:T(8,128)S(1)}, u32[]{:S(2)}, u32[]{:S(2)}) collective-permute-start(f32[8,68,2]{1,0,2:T(8,128)S(1)} %get-tuple-element.40), channel_id=1, source_target_pairs={{2,0},{4,2},{6,4},{3,1},{5,3},{7,5},{10,8},{12,10},{14,12},{11,9},... | collective-permute-start | bytes 13064 | tf_op jit(solution)/shard_map/ppermute | solution.py:20
  21.7 1.5 copy.332
  23.2 6.8 %fusion.48 = (f32[8,64,256]{1,0,2:T(8,128)S(1)}, f32[8,64,256]{1,0,2:T(8,128)}, f32[8,64,256]{1,0,2:T(8,128)}, f32[8,64,256]{1,0,2:T(8,128)}, f32[8,64,256]{1,0,2:T(8,128)}) fusion(f32[8,64,256]{1,0,2:T(8,128)S(1)} %copy.332, f32[8,64,256]{1,0,2:T(8,128)S(1)} %select_add_fusion, f32[8,2,256]{1,0,2:T(8,128)} %copy-done.17, f32[8,2,256]{1,0,2:T(8,128)} %copy-done.16, ...), kind=kLoop, calls=%fused_computation.98 | loop fusion | flops 4456448 | bytes 3711488 | tf_op jit(solution)/shard_map/div | solution.py:80
  30.0 1.7 fusion.67
  31.7 1.5 copy.349
  33.2 3.5 %collective-permute-start.5 = (f32[8,1,256]{2,0,1:T(8,128)S(1)}, f32[8,1,256]{2,0,1:T(8,128)S(1)}, u32[]{:S(2)}, u32[]{:S(2)}) collective-permute-start(f32[8,1,256]{2,0,1:T(8,128)S(1)} %copy.349), channel_id=1, source_target_pairs={{0,8},{8,16},{16,24},{1,9},{9,17},{17,25},{2,10},{10,18},{18,26},{... | collective-permute-start | bytes 24584 | tf_op jit(solution)/shard_map/ppermute | solution.py:17
  36.7 1.5 copy.347
  38.3 2.4 collective-permute-start.4
  40.7 1.4 copy.350
  42.0 1.8 collective-permute-done.4
  43.8 1.4 copy.348
  46.2 2.1 collective-permute-start.6
  48.3 2.3 collective-permute-start.7
  50.7 2.6 %collective-permute-done.7 = f32[8,66,1]{1,0,2:T(8,128)S(1)} collective-permute-done((f32[8,66,1]{1,0,2:T(8,128)S(1)}, f32[8,66,1]{1,0,2:T(8,128)S(1)}, u32[]{:S(2)}, u32[]{:S(2)}) %collective-permute-start.7) | collective-permute-done | bytes 2144 | tf_op jit(solution)/shard_map/ppermute | solution.py:17
  53.3 5.6 %fusion.39 = f32[8,64,256]{1,0,2:T(8,128)S(1)} fusion(f32[8,64,256]{1,0,2:T(8,128)S(1)} %get-tuple-element.26, f32[8,64,256]{1,0,2:T(8,128)S(1)} %copy.332, f32[8,64,256]{1,0,2:T(8,128)} %get-tuple-element.30, f32[8,66,1]{1,0,2:T(8,128)S(1)} %collective-permute-done.7, f32[8,1,256]{1,0,2:T(8,128)} %copy.348, f32[8,1,256]{1,0,2:T(8,128)} %copy.350, ...), kind=kLoop, calls=%fused_computation.65 | loop fusion | flops 3145728 | bytes 3690624 | tf_op jit(solution)/shard_map/add | solution.py:85
  58.8 1.3 fusion.66
  60.2 1.5 copy.356
  61.7 2.6 %collective-permute-start.9 = (f32[8,1,256]{2,0,1:T(8,128)S(1)}, f32[8,1,256]{2,0,1:T(8,128)S(1)}, u32[]{:S(2)}, u32[]{:S(2)}) collective-permute-start(f32[8,1,256]{2,0,1:T(8,128)S(1)} %copy.356), channel_id=1, source_target_pairs={{0,8},{8,16},{16,24},{1,9},{9,17},{17,25},{2,10},{10,18},{18,26},{... | collective-permute-start | bytes 24584 | tf_op jit(solution)/shard_map/ppermute | solution.py:17
  64.7 3.4 %collective-permute-start.8 = (f32[8,1,256]{2,0,1:T(8,128)S(1)}, f32[8,1,256]{2,0,1:T(8,128)S(1)}, u32[]{:S(2)}, u32[]{:S(2)}) collective-permute-start(f32[8,1,256]{2,0,1:T(8,128)S(1)} %copy.354), channel_id=1, source_target_pairs={{8,0},{16,8},{24,16},{9,1},{17,9},{25,17},{10,2},{18,10},{26,18},{... | collective-permute-start | bytes 24584 | tf_op jit(solution)/shard_map/ppermute | solution.py:20
  68.1 1.4 copy.357
  70.3 1.4 copy.355
  72.6 2.0 collective-permute-start.10
  74.7 2.6 %collective-permute-start.11 = (f32[8,66,1]{1,0,2:T(8,128)S(1)}, f32[8,66,1]{1,0,2:T(8,128)S(1)}, u32[]{:S(2)}, u32[]{:S(2)}) collective-permute-start(f32[8,66,1]{1,0,2:T(8,128)S(1)} %get-tuple-element.36), channel_id=1, source_target_pairs={{0,2},{2,4},{4,6},{1,3},{3,5},{5,7},{8,10},{10,12},{12,14},{9,11},... | collective-permute-start | bytes 6344 | tf_op jit(solution)/shard_map/ppermute | solution.py:17
  77.3 2.3 collective-permute-done.11
  79.6 5.6 %fusion.27 = f32[8,64,256]{1,0,2:T(8,128)S(1)} fusion(f32[8,64,256]{1,0,2:T(8,128)S(1)} %copy-done.1, f32[8,64,256]{1,0,2:T(8,128)S(1)} %copy.332, f32[8,64,256]{1,0,2:T(8,128)} %get-tuple-element.30, f32[8,66,1]{1,0,2:T(8,128)S(1)} %collective-permute-done.11, f32[8,1,256]{1,0,2:T(8,128)} %copy.355, f32[8,1,256]{1,0,2:T(8,128)} %copy.357, ...), kind=kLoop, calls=%fused_computation.45 | loop fusion | flops 3145728 | bytes 3690624 | tf_op jit(solution)/shard_map/add | solution.py:85
  85.2 1.3 fusion.65
  86.5 1.5 copy.363
  88.1 1.9 collective-permute-start.13
  90.4 4.1 %collective-permute-start.12 = (f32[8,1,256]{2,0,1:T(8,128)S(1)}, f32[8,1,256]{2,0,1:T(8,128)S(1)}, u32[]{:S(2)}, u32[]{:S(2)}) collective-permute-start(f32[8,1,256]{2,0,1:T(8,128)S(1)} %copy.361), channel_id=1, source_target_pairs={{8,0},{16,8},{24,16},{9,1},{17,9},{25,17},{10,2},{18,10},{26,18},{... | collective-permute-start | bytes 24584 | tf_op jit(solution)/shard_map/ppermute | solution.py:20
  94.5 1.4 copy.364
  96.1 1.4 copy.362
  98.4 2.0 collective-permute-start.14
  100.4 2.4 collective-permute-start.15
  102.8 2.5 %collective-permute-done.15 = f32[8,66,1]{1,0,2:T(8,128)S(1)} collective-permute-done((f32[8,66,1]{1,0,2:T(8,128)S(1)}, f32[8,66,1]{1,0,2:T(8,128)S(1)}, u32[]{:S(2)}, u32[]{:S(2)}) %collective-permute-start.15) | collective-permute-done | bytes 2144 | tf_op jit(solution)/shard_map/ppermute | solution.py:17
  105.4 5.6 %fusion.15 = f32[8,64,256]{1,0,2:T(8,128)S(1)} fusion(f32[8,64,256]{1,0,2:T(8,128)S(1)} %copy-done.4, f32[8,64,256]{1,0,2:T(8,128)S(1)} %copy.332, f32[8,64,256]{1,0,2:T(8,128)} %get-tuple-element.30, f32[8,66,1]{1,0,2:T(8,128)S(1)} %collective-permute-done.15, f32[8,1,256]{1,0,2:T(8,128)} %copy.362, f32[8,1,256]{1,0,2:T(8,128)} %copy.364, ...), kind=kLoop, calls=%fused_computation.25 | loop fusion | flops 3145728 | bytes 3690624 | tf_op jit(solution)/shard_map/add | solution.py:85
  111.0 1.7 fusion.64
  112.7 1.5 copy.370
  114.2 1.6 copy.368
  115.8 3.9 %collective-permute-start.16 = (f32[8,1,256]{2,0,1:T(8,128)S(1)}, f32[8,1,256]{2,0,1:T(8,128)S(1)}, u32[]{:S(2)}, u32[]{:S(2)}) collective-permute-start(f32[8,1,256]{2,0,1:T(8,128)S(1)} %copy.368), channel_id=1, source_target_pairs={{8,0},{16,8},{24,16},{9,1},{17,9},{25,17},{10,2},{18,10},{26,18},{... | collective-permute-start | bytes 24584 | tf_op jit(solution)/shard_map/ppermute | solution.py:20
  119.7 2.1 collective-permute-start.17
  121.9 3.1 %pad_maximum_fusion = f32[8,68,260]{1,0,2:T(8,128)} fusion(f32[8,68,2]{1,0,2:T(8,128)S(1)} %collective-permute-done.2, f32[8,2,256]{1,0,2:T(8,128)} %copy-done.16, f32[8,64,256]{1,0,2:T(8,128)S(1)} %select_add_fusion, f32[8,2,256]{1,0,2:T(8,128)} %copy-done.17, f32[8,68,2]{1,0,2:T(8,128)S(1)} %collective-permute-done.3), kind=kLoop, calls=%fused_computation | loop fusion | flops 565760 | bytes 1131520 | tf_op jit(solution)/shard_map/concatenate | solution.py:21
  125.0 6.7 %copy.377 = f32[8,68,260]{0,2,1:T(8,128)} copy(f32[8,68,260]{1,0,2:T(8,128)} %pad_maximum_fusion) | data formatting | bytes 1131520 | tf_op jit(solution)/shard_map/concatenate | solution.py:21
  131.7 11.5 %reshape.64 = f32[8,34,2,130,2]{0,4,3,2,1:T(2,128)} reshape(f32[8,68,260]{0,2,1:T(8,128)} %copy.377) | data formatting | bytes 1131520 | tf_op jit(solution)/shard_map/reshape | solution.py:70
  143.2 40.2 %reduce_sum.29 = f32[8,34,130]{0,2,1:T(8,128)} reduce(f32[8,34,2,130,2]{0,4,3,2,1:T(2,128)} %reshape.64, f32[]{:T(128)} %constant.14.clone.1), dimensions={2,4}, to_apply=%region_2.3 | reduce | flops 106080 | bytes 707204 | tf_op jit(solution)/shard_map/reduce_sum | solution.py:70
  183.5 3.8 %copy.378 = f32[8,34,130]{2,1,0:T(8,128)} copy(f32[8,34,130]{0,2,1:T(8,128)} %reduce_sum.29) | data formatting | bytes 282880 | tf_op jit(solution)/shard_map/reduce_sum | solution.py:70
  187.2 1.3 copy.371
  188.6 1.4 copy.369
  190.9 2.0 collective-permute-start.18
  192.9 2.7 %collective-permute-start.19 = (f32[8,66,1]{1,0,2:T(8,128)S(1)}, f32[8,66,1]{1,0,2:T(8,128)S(1)}, u32[]{:S(2)}, u32[]{:S(2)}) collective-permute-start(f32[8,66,1]{1,0,2:T(8,128)S(1)} %get-tuple-element.32), channel_id=1, source_target_pairs={{0,2},{2,4},{4,6},{1,3},{3,5},{5,7},{8,10},{10,12},{12,14},{9,11},... | collective-permute-start | bytes 6344 | tf_op jit(solution)/shard_map/ppermute | solution.py:17
  196.6 1.2 collective-permute-done.19
  197.9 6.3 %fusion.3 = f32[8,64,256]{1,0,2:T(8,128)} fusion(f32[8,64,256]{1,0,2:T(8,128)S(1)} %copy.332, f32[8,64,256]{1,0,2:T(8,128)} %get-tuple-element.30, f32[8,66,1]{1,0,2:T(8,128)S(1)} %collective-permute-done.19, f32[8,1,256]{1,0,2:T(8,128)} %copy.369, f32[8,64,256]{1,0,2:T(8,128)S(1)} %fusion.15, f32[8,1,256]{1,0,2:T(8,128)} %copy.371, ...), kind=kLoop, calls=%fused_computation.5 | loop fusion | flops 2752512 | bytes 3690624 | tf_op jit(solution)/shard_map/sub | solution.py:83
  204.2 8.2 %copy.375 = f32[8,64,256]{0,2,1:T(8,128)} copy(f32[8,64,256]{1,0,2:T(8,128)} %fusion.3) | data formatting | bytes 1048576 | tf_op jit(solution)/shard_map/sub | solution.py:83
  212.4 9.5 %reduce_sum.28 = f32[8,32,128]{0,2,1:T(8,128)S(1)} reduce(f32[8,32,2,128,2]{0,4,3,2,1:T(2,128)} %bitcast.8, f32[]{:T(128)} %constant.14.clone.1), dimensions={2,4}, to_apply=%region_1.2 | reduce | flops 98304 | bytes 655364 | tf_op jit(solution)/shard_map/reduce_sum | solution.py:70
  222.0 1.2 copy.376
  224.4 4.1 %collective-permute-start.20 = (f32[8,1,128]{2,1,0:T(1,128)S(1)}, f32[8,1,128]{2,1,0:T(1,128)S(1)}, u32[]{:S(2)}, u32[]{:S(2)}) collective-permute-start(f32[8,1,128]{2,1,0:T(1,128)S(1)} %get-tuple-element.55), channel_id=1, source_target_pairs={{8,0},{16,8},{24,16},{9,1},{17,9},{25,17},{10,2},{18,10},{26,18},{... | collective-permute-start | bytes 12296 | tf_op jit(solution)/shard_map/ppermute | solution.py:20
  228.5 1.9 collective-permute-start.21
  230.5 3.5 %collective-permute-done.21 = f32[8,1,128]{2,1,0:T(1,128)S(1)} collective-permute-done((f32[8,1,128]{2,1,0:T(1,128)S(1)}, f32[8,1,128]{2,1,0:T(1,128)S(1)}, u32[]{:S(2)}, u32[]{:S(2)}) %collective-permute-start.21) | collective-permute-done | bytes 4128 | tf_op jit(solution)/shard_map/ppermute | solution.py:17
  234.1 1.9 collective-permute-start.22
  236.0 2.4 collective-permute-start.23
  238.6 3.8 %collective-permute-done.23 = f32[8,34,1]{2,0,1:T(8,128)S(1)} collective-permute-done((f32[8,34,1]{2,0,1:T(8,128)S(1)}, f32[8,34,1]{2,0,1:T(8,128)S(1)}, u32[]{:S(2)}, u32[]{:S(2)}) %collective-permute-start.23) | collective-permute-done | bytes 1120 | tf_op jit(solution)/shard_map/ppermute | solution.py:17
  (94 shorter events, 18.3 us)
Async XLA Ops:
  6.3 6.2 %collective-permute-start = (f32[8,2,256]{2,0,1:T(8,128)S(1)}, f32[8,2,256]{2,0,1:T(8,128)S(1)}, u32[]{:S(2)}, u32[]{:S(2)}) collective-permute-start(f32[8,2,256]{2,0,1:T(8,128)S(1)} %copy.341), channel_id=1, source_target_pairs={{8,0},{16,8},{24,16},{9,1},{17,9},{25,17},{10,2},{18,10},{26,18},{... | collective-permute-start | bytes 49160 | tf_op jit(solution)/shard_map/ppermute | solution.py:20
  9.1 5.6 %collective-permute-start.1 = (f32[8,2,256]{2,0,1:T(8,128)S(1)}, f32[8,2,256]{2,0,1:T(8,128)S(1)}, u32[]{:S(2)}, u32[]{:S(2)}) collective-permute-start(f32[8,2,256]{2,0,1:T(8,128)S(1)} %copy.343), channel_id=1, source_target_pairs={{0,8},{8,16},{16,24},{1,9},{9,17},{17,25},{2,10},{10,18},{18,26},{... | collective-permute-start | bytes 49160 | tf_op jit(solution)/shard_map/ppermute | solution.py:17
  13.0 2.2 copy-start.16
  15.2 1.0 copy-start.17
  16.1 7.0 %collective-permute-start.3 = (f32[8,68,2]{1,0,2:T(8,128)S(1)}, f32[8,68,2]{1,0,2:T(8,128)S(1)}, u32[]{:S(2)}, u32[]{:S(2)}) collective-permute-start(f32[8,68,2]{1,0,2:T(8,128)S(1)} %get-tuple-element.39), channel_id=1, source_target_pairs={{0,2},{2,4},{4,6},{1,3},{3,5},{5,7},{8,10},{10,12},{12,14},{9,11},... | collective-permute-start | bytes 13064 | tf_op jit(solution)/shard_map/ppermute | solution.py:17
  18.1 5.1 %collective-permute-start.2 = (f32[8,68,2]{1,0,2:T(8,128)S(1)}, f32[8,68,2]{1,0,2:T(8,128)S(1)}, u32[]{:S(2)}, u32[]{:S(2)}) collective-permute-start(f32[8,68,2]{1,0,2:T(8,128)S(1)} %get-tuple-element.40), channel_id=1, source_target_pairs={{2,0},{4,2},{6,4},{3,1},{5,3},{7,5},{10,8},{12,10},{14,12},{11,9},... | collective-permute-start | bytes 13064 | tf_op jit(solution)/shard_map/ppermute | solution.py:20
  33.2 7.4 %collective-permute-start.5 = (f32[8,1,256]{2,0,1:T(8,128)S(1)}, f32[8,1,256]{2,0,1:T(8,128)S(1)}, u32[]{:S(2)}, u32[]{:S(2)}) collective-permute-start(f32[8,1,256]{2,0,1:T(8,128)S(1)} %copy.349), channel_id=1, source_target_pairs={{0,8},{8,16},{16,24},{1,9},{9,17},{17,25},{2,10},{10,18},{18,26},{... | collective-permute-start | bytes 24584 | tf_op jit(solution)/shard_map/ppermute | solution.py:17
  38.3 5.6 %collective-permute-start.4 = (f32[8,1,256]{2,0,1:T(8,128)S(1)}, f32[8,1,256]{2,0,1:T(8,128)S(1)}, u32[]{:S(2)}, u32[]{:S(2)}) collective-permute-start(f32[8,1,256]{2,0,1:T(8,128)S(1)} %copy.347), channel_id=1, source_target_pairs={{8,0},{16,8},{24,16},{9,1},{17,9},{25,17},{10,2},{18,10},{26,18},{... | collective-permute-start | bytes 24584 | tf_op jit(solution)/shard_map/ppermute | solution.py:20
  45.3 8.0 %copy-start.5 = (f32[8,64,256]{1,0,2:T(8,128)S(1)}, f32[8,64,256]{1,0,2:T(8,128)}, u32[]{:S(2)}) copy-start(f32[8,64,256]{1,0,2:T(8,128)} %get-tuple-element.27) | copy-start | bytes 1572868
  45.3 8.0 %copy-start.9 = (f32[8,64,256]{1,0,2:T(8,128)S(1)}, f32[8,64,256]{1,0,2:T(8,128)}, u32[]{:S(2)}) copy-start(f32[8,64,256]{1,0,2:T(8,128)} %get-tuple-element.28) | copy-start | bytes 1572868
  45.3 8.0 %copy-start.13 = (f32[8,64,256]{1,0,2:T(8,128)S(1)}, f32[8,64,256]{1,0,2:T(8,128)}, u32[]{:S(2)}) copy-start(f32[8,64,256]{1,0,2:T(8,128)} %get-tuple-element.29) | copy-start | bytes 1572868
  46.2 4.5 %collective-permute-start.6 = (f32[8,66,1]{1,0,2:T(8,128)S(1)}, f32[8,66,1]{1,0,2:T(8,128)S(1)}, u32[]{:S(2)}, u32[]{:S(2)}) collective-permute-start(f32[8,66,1]{1,0,2:T(8,128)S(1)} %get-tuple-element.37), channel_id=1, source_target_pairs={{2,0},{4,2},{6,4},{3,1},{5,3},{7,5},{10,8},{12,10},{14,12},{11,9},... | collective-permute-start | bytes 6344 | tf_op jit(solution)/shard_map/ppermute | solution.py:20
  48.3 4.9 %collective-permute-start.7 = (f32[8,66,1]{1,0,2:T(8,128)S(1)}, f32[8,66,1]{1,0,2:T(8,128)S(1)}, u32[]{:S(2)}, u32[]{:S(2)}) collective-permute-start(f32[8,66,1]{1,0,2:T(8,128)S(1)} %get-tuple-element.38), channel_id=1, source_target_pairs={{0,2},{2,4},{4,6},{1,3},{3,5},{5,7},{8,10},{10,12},{12,14},{9,11},... | collective-permute-start | bytes 6344 | tf_op jit(solution)/shard_map/ppermute | solution.py:17
  58.8 1.3 copy-start
  61.7 6.4 %collective-permute-start.9 = (f32[8,1,256]{2,0,1:T(8,128)S(1)}, f32[8,1,256]{2,0,1:T(8,128)S(1)}, u32[]{:S(2)}, u32[]{:S(2)}) collective-permute-start(f32[8,1,256]{2,0,1:T(8,128)S(1)} %copy.356), channel_id=1, source_target_pairs={{0,8},{8,16},{16,24},{1,9},{9,17},{17,25},{2,10},{10,18},{18,26},{... | collective-permute-start | bytes 24584 | tf_op jit(solution)/shard_map/ppermute | solution.py:17
  64.7 7.0 %copy-start.1 = (f32[8,64,256]{1,0,2:T(8,128)S(1)}, f32[8,64,256]{1,0,2:T(8,128)}, u32[]{:S(2)}) copy-start(f32[8,64,256]{1,0,2:T(8,128)} %copy-done) | copy-start | bytes 1572868
  64.7 5.7 %collective-permute-start.8 = (f32[8,1,256]{2,0,1:T(8,128)S(1)}, f32[8,1,256]{2,0,1:T(8,128)S(1)}, u32[]{:S(2)}, u32[]{:S(2)}) collective-permute-start(f32[8,1,256]{2,0,1:T(8,128)S(1)} %copy.354), channel_id=1, source_target_pairs={{8,0},{16,8},{24,16},{9,1},{17,9},{25,17},{10,2},{18,10},{26,18},{... | collective-permute-start | bytes 24584 | tf_op jit(solution)/shard_map/ppermute | solution.py:20
  71.7 7.9 %copy-start.6 = (f32[8,64,256]{1,0,2:T(8,128)S(1)}, f32[8,64,256]{1,0,2:T(8,128)}, u32[]{:S(2)}) copy-start(f32[8,64,256]{1,0,2:T(8,128)} %get-tuple-element.27) | copy-start | bytes 1572868
  71.7 7.9 %copy-start.10 = (f32[8,64,256]{1,0,2:T(8,128)S(1)}, f32[8,64,256]{1,0,2:T(8,128)}, u32[]{:S(2)}) copy-start(f32[8,64,256]{1,0,2:T(8,128)} %get-tuple-element.28) | copy-start | bytes 1572868
  71.7 7.9 %copy-start.14 = (f32[8,64,256]{1,0,2:T(8,128)S(1)}, f32[8,64,256]{1,0,2:T(8,128)}, u32[]{:S(2)}) copy-start(f32[8,64,256]{1,0,2:T(8,128)} %get-tuple-element.29) | copy-start | bytes 1572868
  72.6 4.6 %collective-permute-start.10 = (f32[8,66,1]{1,0,2:T(8,128)S(1)}, f32[8,66,1]{1,0,2:T(8,128)S(1)}, u32[]{:S(2)}, u32[]{:S(2)}) collective-permute-start(f32[8,66,1]{1,0,2:T(8,128)S(1)} %get-tuple-element.35), channel_id=1, source_target_pairs={{2,0},{4,2},{6,4},{3,1},{5,3},{7,5},{10,8},{12,10},{14,12},{11,9},... | collective-permute-start | bytes 6344 | tf_op jit(solution)/shard_map/ppermute | solution.py:20
  74.7 4.9 %collective-permute-start.11 = (f32[8,66,1]{1,0,2:T(8,128)S(1)}, f32[8,66,1]{1,0,2:T(8,128)S(1)}, u32[]{:S(2)}, u32[]{:S(2)}) collective-permute-start(f32[8,66,1]{1,0,2:T(8,128)S(1)} %get-tuple-element.36), channel_id=1, source_target_pairs={{0,2},{2,4},{4,6},{1,3},{3,5},{5,7},{8,10},{10,12},{12,14},{9,11},... | collective-permute-start | bytes 6344 | tf_op jit(solution)/shard_map/ppermute | solution.py:17
  85.2 1.3 copy-start.2
  88.1 6.4 %collective-permute-start.13 = (f32[8,1,256]{2,0,1:T(8,128)S(1)}, f32[8,1,256]{2,0,1:T(8,128)S(1)}, u32[]{:S(2)}, u32[]{:S(2)}) collective-permute-start(f32[8,1,256]{2,0,1:T(8,128)S(1)} %copy.363), channel_id=1, source_target_pairs={{0,8},{8,16},{16,24},{1,9},{9,17},{17,25},{2,10},{10,18},{18,26},{... | collective-permute-start | bytes 24584 | tf_op jit(solution)/shard_map/ppermute | solution.py:17
  90.4 7.0 %copy-start.3 = (f32[8,64,256]{1,0,2:T(8,128)S(1)}, f32[8,64,256]{1,0,2:T(8,128)}, u32[]{:S(2)}) copy-start(f32[8,64,256]{1,0,2:T(8,128)} %copy-done.2) | copy-start | bytes 1572868
  90.4 5.7 %collective-permute-start.12 = (f32[8,1,256]{2,0,1:T(8,128)S(1)}, f32[8,1,256]{2,0,1:T(8,128)S(1)}, u32[]{:S(2)}, u32[]{:S(2)}) collective-permute-start(f32[8,1,256]{2,0,1:T(8,128)S(1)} %copy.361), channel_id=1, source_target_pairs={{8,0},{16,8},{24,16},{9,1},{17,9},{25,17},{10,2},{18,10},{26,18},{... | collective-permute-start | bytes 24584 | tf_op jit(solution)/shard_map/ppermute | solution.py:20
  97.4 7.9 %copy-start.4 = (f32[8,64,256]{1,0,2:T(8,128)S(1)}, f32[8,64,256]{1,0,2:T(8,128)}, u32[]{:S(2)}) copy-start(f32[8,64,256]{1,0,2:T(8,128)} %copy-done.2) | copy-start | bytes 1572868
  97.5 7.9 %copy-start.7 = (f32[8,64,256]{1,0,2:T(8,128)S(1)}, f32[8,64,256]{1,0,2:T(8,128)}, u32[]{:S(2)}) copy-start(f32[8,64,256]{1,0,2:T(8,128)} %get-tuple-element.27) | copy-start | bytes 1572868
  97.5 7.9 %copy-start.11 = (f32[8,64,256]{1,0,2:T(8,128)S(1)}, f32[8,64,256]{1,0,2:T(8,128)}, u32[]{:S(2)}) copy-start(f32[8,64,256]{1,0,2:T(8,128)} %get-tuple-element.28) | copy-start | bytes 1572868
  98.4 4.5 %collective-permute-start.14 = (f32[8,66,1]{1,0,2:T(8,128)S(1)}, f32[8,66,1]{1,0,2:T(8,128)S(1)}, u32[]{:S(2)}, u32[]{:S(2)}) collective-permute-start(f32[8,66,1]{1,0,2:T(8,128)S(1)} %get-tuple-element.33), channel_id=1, source_target_pairs={{2,0},{4,2},{6,4},{3,1},{5,3},{7,5},{10,8},{12,10},{14,12},{11,9},... | collective-permute-start | bytes 6344 | tf_op jit(solution)/shard_map/ppermute | solution.py:20
  100.4 4.9 %collective-permute-start.15 = (f32[8,66,1]{1,0,2:T(8,128)S(1)}, f32[8,66,1]{1,0,2:T(8,128)S(1)}, u32[]{:S(2)}, u32[]{:S(2)}) collective-permute-start(f32[8,66,1]{1,0,2:T(8,128)S(1)} %get-tuple-element.34), channel_id=1, source_target_pairs={{0,2},{2,4},{4,6},{1,3},{3,5},{5,7},{8,10},{10,12},{12,14},{9,11},... | collective-permute-start | bytes 6344 | tf_op jit(solution)/shard_map/ppermute | solution.py:17
  115.8 72.8 %collective-permute-start.16 = (f32[8,1,256]{2,0,1:T(8,128)S(1)}, f32[8,1,256]{2,0,1:T(8,128)S(1)}, u32[]{:S(2)}, u32[]{:S(2)}) collective-permute-start(f32[8,1,256]{2,0,1:T(8,128)S(1)} %copy.368), channel_id=1, source_target_pairs={{8,0},{16,8},{24,16},{9,1},{17,9},{25,17},{10,2},{18,10},{26,18},{... | collective-permute-start | bytes 24584 | tf_op jit(solution)/shard_map/ppermute | solution.py:20
  119.7 67.5 %collective-permute-start.17 = (f32[8,1,256]{2,0,1:T(8,128)S(1)}, f32[8,1,256]{2,0,1:T(8,128)S(1)}, u32[]{:S(2)}, u32[]{:S(2)}) collective-permute-start(f32[8,1,256]{2,0,1:T(8,128)S(1)} %copy.370), channel_id=1, source_target_pairs={{0,8},{8,16},{16,24},{1,9},{9,17},{17,25},{2,10},{10,18},{18,26},{... | collective-permute-start | bytes 24584 | tf_op jit(solution)/shard_map/ppermute | solution.py:17
  190.0 7.9 %copy-start.8 = (f32[8,64,256]{1,0,2:T(8,128)S(1)}, f32[8,64,256]{1,0,2:T(8,128)}, u32[]{:S(2)}) copy-start(f32[8,64,256]{1,0,2:T(8,128)} %get-tuple-element.27) | copy-start | bytes 1572868
  190.0 7.9 %copy-start.12 = (f32[8,64,256]{1,0,2:T(8,128)S(1)}, f32[8,64,256]{1,0,2:T(8,128)}, u32[]{:S(2)}) copy-start(f32[8,64,256]{1,0,2:T(8,128)} %get-tuple-element.28) | copy-start | bytes 1572868
  190.0 7.9 %copy-start.15 = (f32[8,64,256]{1,0,2:T(8,128)S(1)}, f32[8,64,256]{1,0,2:T(8,128)}, u32[]{:S(2)}) copy-start(f32[8,64,256]{1,0,2:T(8,128)} %get-tuple-element.29) | copy-start | bytes 1572868
  190.9 5.7 %collective-permute-start.18 = (f32[8,66,1]{1,0,2:T(8,128)S(1)}, f32[8,66,1]{1,0,2:T(8,128)S(1)}, u32[]{:S(2)}, u32[]{:S(2)}) collective-permute-start(f32[8,66,1]{1,0,2:T(8,128)S(1)} %get-tuple-element.31), channel_id=1, source_target_pairs={{2,0},{4,2},{6,4},{3,1},{5,3},{7,5},{10,8},{12,10},{14,12},{11,9},... | collective-permute-start | bytes 6344 | tf_op jit(solution)/shard_map/ppermute | solution.py:20
  192.9 4.9 %collective-permute-start.19 = (f32[8,66,1]{1,0,2:T(8,128)S(1)}, f32[8,66,1]{1,0,2:T(8,128)S(1)}, u32[]{:S(2)}, u32[]{:S(2)}) collective-permute-start(f32[8,66,1]{1,0,2:T(8,128)S(1)} %get-tuple-element.32), channel_id=1, source_target_pairs={{0,2},{2,4},{4,6},{1,3},{3,5},{5,7},{8,10},{10,12},{12,14},{9,11},... | collective-permute-start | bytes 6344 | tf_op jit(solution)/shard_map/ppermute | solution.py:17
  224.4 18.2 %copy-start.18 = (f32[8,32,128]{2,1,0:T(8,128)S(1)}, f32[8,32,128]{2,1,0:T(8,128)}, u32[]{:S(2)}) copy-start(f32[8,32,128]{2,1,0:T(8,128)} %copy.376) | copy-start | bytes 393220
  224.4 6.1 %collective-permute-start.20 = (f32[8,1,128]{2,1,0:T(1,128)S(1)}, f32[8,1,128]{2,1,0:T(1,128)S(1)}, u32[]{:S(2)}, u32[]{:S(2)}) collective-permute-start(f32[8,1,128]{2,1,0:T(1,128)S(1)} %get-tuple-element.55), channel_id=1, source_target_pairs={{8,0},{16,8},{24,16},{9,1},{17,9},{25,17},{10,2},{18,10},{26,18},{... | collective-permute-start | bytes 12296 | tf_op jit(solution)/shard_map/ppermute | solution.py:20
  228.5 5.5 %collective-permute-start.21 = (f32[8,1,128]{2,1,0:T(1,128)S(1)}, f32[8,1,128]{2,1,0:T(1,128)S(1)}, u32[]{:S(2)}, u32[]{:S(2)}) collective-permute-start(f32[8,1,128]{2,1,0:T(1,128)S(1)} %get-tuple-element.56), channel_id=1, source_target_pairs={{0,8},{8,16},{16,24},{1,9},{9,17},{17,25},{2,10},{10,18},{18,26},{... | collective-permute-start | bytes 12296 | tf_op jit(solution)/shard_map/ppermute | solution.py:17
  234.1 4.5 %collective-permute-start.22 = (f32[8,34,1]{2,0,1:T(8,128)S(1)}, f32[8,34,1]{2,0,1:T(8,128)S(1)}, u32[]{:S(2)}, u32[]{:S(2)}) collective-permute-start(f32[8,34,1]{2,0,1:T(8,128)S(1)} %get-tuple-element.53), channel_id=1, source_target_pairs={{2,0},{4,2},{6,4},{3,1},{5,3},{7,5},{10,8},{12,10},{14,12},{11,9},... | collective-permute-start | bytes 3272 | tf_op jit(solution)/shard_map/ppermute | solution.py:20
  236.0 6.4 %collective-permute-start.23 = (f32[8,34,1]{2,0,1:T(8,128)S(1)}, f32[8,34,1]{2,0,1:T(8,128)S(1)}, u32[]{:S(2)}, u32[]{:S(2)}) collective-permute-start(f32[8,34,1]{2,0,1:T(8,128)S(1)} %get-tuple-element.54), channel_id=1, source_target_pairs={{0,2},{2,4},{4,6},{1,3},{3,5},{5,7},{8,10},{10,12},{12,14},{9,11},... | collective-permute-start | bytes 3272 | tf_op jit(solution)/shard_map/ppermute | solution.py:17
  242.9 0.7 copy-start.19
where the time goes:
time: 247 us; the launch traced here: 245 us
  other arithmetic  92.9 us (38%)
  local copies, waits for them, and re-layouts  66 us (27%)
  starting transfers between devices  63.8 us (26%)
  waiting for transfers between devices  20.7 us (8%)
    reduce_sum x2, other arithmetic, restrict(): values.reshape(values.shape[0], values.shape[1] // 2, 2, values.shape[2]...  49.8 us
    ppermute x12, starting transfers between devices, with_halo(): lax.ppermute(lax.slice_in_dim(block, 0, width, axis=dim), axis, backward)  34 us
    ppermute x12, starting transfers between devices, with_halo(): lax.ppermute(lax.slice_in_dim(block, block.shape[dim] - width, None, axis...  29.8 us
    ppermute x12, waiting for transfers between devices, with_halo(): lax.ppermute(lax.slice_in_dim(block, block.shape[dim] - width, None, axis...  17.6 us
    add x3, other arithmetic, shards(): current = current + DAMPING * residual / diagonal  16.8 us
    slice x9, local copies, waits for them, and re-layouts, with_halo(): lax.slice_in_dim(block, block.shape[dim] - width, None, axis=dim)  12.6 us
    reshape x1, local copies, waits for them, and re-layouts, restrict(): values.reshape(values.shape[0], values.shape[1] // 2, 2, values.shape[2]...  11.5 us
    sub x1, local copies, waits for them, and re-layouts, shards(): residual = source - operator(linkage, diagonal, current, padded)  8.23 us
  transfers between devices with their start and end apart: 24, of which 11 were waited for; matrix products, arithmetic and copies ran while one was open for 31% of the time, Pallas kernels for 0%

commit v1 on v0

--- a/solution.py
+++ b/solution.py
@@ -4,9 +4,8 @@
 from jax.sharding import PartitionSpec as P
 
 SWEEPS = 4
-
-
 DAMPING = 0.8
+HALO = 8
 
 
 def with_halo(block, sides, width):
@@ -31,6 +30,10 @@
     )
 
 
+def pad_edges(values):
+    return jnp.pad(values, ((0, 0), (1, 1), (1, 1)))
+
+
 def couplings(perm_padded):
     middle = perm_padded[..., 1:-1, 1:-1]
     linkage = tuple(
@@ -53,48 +56,84 @@
     )
 
 
-def permeability(sample_seeds, perm_levels, perm_classes):
+def permeability(sample_seeds, perm_levels, classes):
     choose = (
         sample_seeds[:, None] == jnp.arange(perm_levels.shape[0], dtype=jnp.int32)[None, :]
     ).astype(jnp.float32)
     sample_levels = jnp.sum(choose[:, :, None] * perm_levels[None, :, :], axis=1)
-    result = jnp.zeros((sample_seeds.shape[0],) + perm_classes.shape, jnp.float32)
+    result = jnp.zeros((sample_seeds.shape[0],) + classes.shape, jnp.float32)
     for category in range(perm_levels.shape[1]):
         result = result + jnp.where(
-            perm_classes[None] == category, sample_levels[:, category, None, None], 0.0
+            classes[None] == category, sample_levels[:, category, None, None], 0.0
         )
     return result
 
 
+def inside_mask(rows, cols, width):
+    own_x = rows - 2 * width
+    own_y = cols - 2 * width
+    r = lax.broadcasted_iota(jnp.int32, (rows, cols), 0) - width + lax.axis_index("gx") * own_x
+    c = lax.broadcasted_iota(jnp.int32, (rows, cols), 1) - width + lax.axis_index("gy") * own_y
+    return (r >= 0) & (r < lax.axis_size("gx") * own_x) & (c >= 0) & (c < lax.axis_size("gy") * own_y)
+
+
+def pair_matrix(fine, coarse):
+    f = lax.broadcasted_iota(jnp.int32, (fine, coarse), 0)
+    c = lax.broadcasted_iota(jnp.int32, (fine, coarse), 1)
+    return (f // 2 == c).astype(jnp.float32)
+
+
 def restrict(values):
-    return values.reshape(values.shape[0], values.shape[1] // 2, 2, values.shape[2] // 2, 2).sum(
-        axis=(2, 4)
-    )
+    rows, cols = values.shape[1], values.shape[2]
+    ry = pair_matrix(cols, cols // 2)
+    rx = pair_matrix(rows, rows // 2)
+    hi = lax.Precision.HIGHEST
+    half = jnp.einsum("sxy,yj->sxj", values, ry, precision=hi)
+    return jnp.einsum("xi,sxj->sij", rx, half, precision=hi)
+
+
+def prolong(values):
+    rows, cols = values.shape[1], values.shape[2]
+    ey = pair_matrix(2 * cols, cols)
+    ex = pair_matrix(2 * rows, rows)
+    hi = lax.Precision.HIGHEST
+    wide = jnp.einsum("sij,yj->siy", values, ey, precision=hi)
+    return jnp.einsum("xi,siy->sxy", ex, wide, precision=hi)
 
 
 def shards(source, sample_seeds, perm_levels, perm_classes):
-    depth = 2
-    perm_field = permeability(sample_seeds, perm_levels, perm_classes)
-    perm_wide = with_halo(perm_field, (("gx", 1), ("gy", 2)), depth)
-    linkage, diagonal = couplings(perm_wide[:, 1:-1, 1:-1])
-    current = DAMPING * source / diagonal
+    h = HALO
+    count, rows, cols = source.shape
+    stacked = jnp.concatenate([source, perm_classes.astype(jnp.float32)[None]], axis=0)
+    wide = with_halo(stacked, (("gx", 1), ("gy", 2)), h)
+    source_wide = wide[:count]
+    classes_wide = wide[count].astype(jnp.int32)
+    inside = inside_mask(rows + 2 * h, cols + 2 * h, h)
+    perm_field = jnp.where(
+        inside[None], permeability(sample_seeds, perm_levels, classes_wide), 0.0
+    )
+    linkage, diagonal = couplings(pad_edges(perm_field))
+    safe_diagonal = jnp.where(inside[None], diagonal, 1.0)
+    current = DAMPING * source_wide / safe_diagonal
     for sweep_index in range(SWEEPS):
-        padded = with_halo(current, (("gx", 1), ("gy", 2)), 1)
-        residual = source - operator(linkage, diagonal, current, padded)
+        residual = source_wide - operator(linkage, diagonal, current, pad_edges(current))
         if sweep_index + 1 < SWEEPS:
-            current = current + DAMPING * residual / diagonal
+            current = current + DAMPING * residual / safe_diagonal
     coarse_rhs = restrict(residual)
-    coarse_wide = 0.25 * restrict(perm_wide)
-    coarse_links, coarse_diagonal = couplings(coarse_wide)
-    first = DAMPING * coarse_rhs / coarse_diagonal
-    padded_first = with_halo(first, (("gx", 1), ("gy", 2)), 1)
+    coarse_perm = 0.25 * restrict(perm_field)
+    coarse_inside = inside_mask((rows + 2 * h) // 2, (cols + 2 * h) // 2, h // 2)
+    coarse_links, coarse_diagonal = couplings(pad_edges(coarse_perm))
+    coarse_safe = jnp.where(coarse_inside[None], coarse_diagonal, 1.0)
+    first = DAMPING * coarse_rhs / coarse_safe
     correction = (
         first
         + DAMPING
-        * (coarse_rhs - operator(coarse_links, coarse_diagonal, first, padded_first))
-        / coarse_diagonal
+        * (coarse_rhs - operator(coarse_links, coarse_diagonal, first, pad_edges(first)))
+        / coarse_safe
     )
-    updated = current + jnp.repeat(jnp.repeat(correction, 2, axis=1), 2, axis=2)
+    c = h // 2
+    correction = correction[:, c : c + rows // 2, c : c + cols // 2]
+    updated = current[:, h : h + rows, h : h + cols] + prolong(correction)
     return (updated, correction)
 
 

time: 247 us -> 39.5 us (0.16)
  the two profiles are of different devices: /device:TPU:18 before, /device:TPU:1 now
where the time goes in v1:
time: 39.5 us; the launch traced here: 39.2 us
  starting transfers between devices  12.4 us (31%)
  other arithmetic  10.3 us (26%)
  waiting for transfers between devices  8.56 us (22%)
  matrix products  6.71 us (17%)
  between operations  0.88 us (2%)
  local copies, waits for them, and re-layouts  0.46 us (1%)
    ppermute x2, starting transfers between devices, with_halo(): lax.ppermute(lax.slice_in_dim(block, block.shape[dim] - width, None, axis...  9.14 us
    ppermute x2, waiting for transfers between devices, with_halo(): lax.ppermute(lax.slice_in_dim(block, 0, width, axis=dim), axis, backward)  6.06 us
    dot_general x2, matrix products, restrict(): half = jnp.einsum('sxy,yj->sxj', values, ry, precision=hi)  3.55 us
    ppermute x2, starting transfers between devices, with_halo(): lax.ppermute(lax.slice_in_dim(block, 0, width, axis=dim), axis, backward)  3.21 us
    add x3, other arithmetic, shards(): current = current + DAMPING * residual / safe_diagonal  2.89 us
    ppermute x2, waiting for transfers between devices, with_halo(): lax.ppermute(lax.slice_in_dim(block, block.shape[dim] - width, None, axis...  2.5 us
    dot_general x2, matrix products, restrict(): return jnp.einsum('xi,sxj->sij', rx, half, precision=hi)  1.53 us
    div x1, other arithmetic, shards(): current = DAMPING * source_wide / safe_diagonal  1.44 us
  transfers between devices with their start and end apart: 4, of which 3 were waited for; matrix products, arithmetic and copies ran while one was open for 5% of the time, Pallas kernels for 0%

profile of v1, /device:TPU:1, one launch (start us, length us, event | category | flops | bytes accessed | tf_op | source)
XLA Modules:
  0.0 39.2 jit_solution(1225603104958268407)
XLA Ops:
  0.6 0.0 copy-start
  0.6 0.9 %convert_bitcast_fusion = f32[1,64,256]{2,1,0:T(8,128)S(1)} fusion(s32[64,256]{1,0:T(8,128)} %param.7), kind=kLoop, calls=%fused_computation.150 | loop fusion | flops 16384 | bytes 131072 | tf_op jit(solution)/shard_map/broadcast_in_dim | solution.py:107
  1.5 0.9 %pad_maximum_fusion.3 = (f32[9,8,256]{2,1,0:T(8,128)S(1)}, f32[9,8,256]{2,1,0:T(8,128)S(1)}) fusion(f32[1,64,256]{2,1,0:T(8,128)S(1)} %convert_bitcast_fusion, f32[8,64,256]{2,1,0:T(8,128)} %param.4), kind=kLoop, calls=%fused_computation.147 | loop fusion | flops 36864 | bytes 737280 | tf_op jit(solution)/shard_map/slice | solution.py:17
  2.4 4.0 %collective-permute-start = (f32[9,8,256]{2,1,0:T(8,128)S(1)}, f32[9,8,256]{2,1,0:T(8,128)S(1)}, u32[]{:S(2)}, u32[]{:S(2)}) collective-permute-start(f32[9,8,256]{2,1,0:T(8,128)S(1)} %get-tuple-element.24), channel_id=1, source_target_pairs={{0,8},{8,16},{16,24},{1,9},{9,17},{17,25},{2,10},{10,18},{18,26},{... | collective-permute-start | bytes 221192 | tf_op jit(solution)/shard_map/ppermute | solution.py:16
  6.5 1.3 %collective-permute-start.1 = (f32[9,8,256]{2,1,0:T(8,128)S(1)}, f32[9,8,256]{2,1,0:T(8,128)S(1)}, u32[]{:S(2)}, u32[]{:S(2)}) collective-permute-start(f32[9,8,256]{2,1,0:T(8,128)S(1)} %get-tuple-element.25), channel_id=1, source_target_pairs={{8,0},{16,8},{24,16},{9,1},{17,9},{25,17},{10,2},{18,10},{26,18},{... | collective-permute-start | bytes 221192 | tf_op jit(solution)/shard_map/ppermute | solution.py:19
  7.9 0.7 %fusion.102 = f32[8,8]{1,0:T(8,128)S(1)} fusion(s32[8]{0:T(128)} %param.5), kind=kLoop, calls=%fused_computation.180 | loop fusion | flops 128 | bytes 288 | tf_op jit(solution)/shard_map/convert_element_type | solution.py:62
  8.6 0.8 %multiply_reduce_fusion = f32[8,8]{1,0:T(8,128)S(1)} fusion(f32[8,8]{1,0:T(8,128)} %param.6, f32[8,8]{1,0:T(8,128)S(1)} %fusion.102), kind=kLoop, calls=%fused_computation.153 | loop fusion | flops 960 | bytes 768 | tf_op jit(solution)/shard_map/reduce_sum | solution.py:63
  9.4 0.3 slice_reduce_fusion.7
  9.7 0.1 and_and_fusion
  9.8 0.1 and_and_fusion.1
  9.9 0.0 collective-permute-done
  9.9 1.7 %collective-permute-done.1 = f32[9,8,256]{2,1,0:T(8,128)S(1)} collective-permute-done((f32[9,8,256]{2,1,0:T(8,128)S(1)}, f32[9,8,256]{2,1,0:T(8,128)S(1)}, u32[]{:S(2)}, u32[]{:S(2)}) %collective-permute-start.1) | collective-permute-done | bytes 73760 | tf_op jit(solution)/shard_map/ppermute | solution.py:19
  11.6 0.0 copy-done
  11.6 0.1 pad_maximum_fusion.1
  11.6 0.2 fusion.111
  11.8 5.1 %collective-permute-start.2 = (f32[9,80,8]{2,1,0:T(8,128)S(1)}, f32[9,80,8]{2,1,0:T(8,128)S(1)}, u32[]{:S(2)}, u32[]{:S(2)}) collective-permute-start(f32[9,80,8]{2,1,0:T(8,128)S(1)} %get-tuple-element.22), channel_id=1, source_target_pairs={{0,2},{2,4},{4,6},{1,3},{3,5},{5,7},{8,10},{10,12},{12,14},{9,11},... | collective-permute-start | bytes 69128 | tf_op jit(solution)/shard_map/ppermute | solution.py:16
  16.9 1.9 %collective-permute-start.3 = (f32[9,80,8]{2,1,0:T(8,128)S(1)}, f32[9,80,8]{2,1,0:T(8,128)S(1)}, u32[]{:S(2)}, u32[]{:S(2)}) collective-permute-start(f32[9,80,8]{2,1,0:T(8,128)S(1)} %get-tuple-element.23), channel_id=1, source_target_pairs={{2,0},{4,2},{6,4},{3,1},{5,3},{7,5},{10,8},{12,10},{14,12},{11,9},... | collective-permute-start | bytes 69128 | tf_op jit(solution)/shard_map/ppermute | solution.py:19
  18.8 2.5 %collective-permute-done.2 = f32[9,80,8]{2,1,0:T(8,128)S(1)} collective-permute-done((f32[9,80,8]{2,1,0:T(8,128)S(1)}, f32[9,80,8]{2,1,0:T(8,128)S(1)}, u32[]{:S(2)}, u32[]{:S(2)}) %collective-permute-start.2) | collective-permute-done | bytes 23072 | tf_op jit(solution)/shard_map/ppermute | solution.py:16
  21.3 4.4 %collective-permute-done.3 = f32[9,80,8]{2,1,0:T(8,128)S(1)} collective-permute-done((f32[9,80,8]{2,1,0:T(8,128)S(1)}, f32[9,80,8]{2,1,0:T(8,128)S(1)}, u32[]{:S(2)}, u32[]{:S(2)}) %collective-permute-start.3) | collective-permute-done | bytes 23072 | tf_op jit(solution)/shard_map/ppermute | solution.py:19
  25.7 0.1 compare_bitcast_fusion.7
  25.9 0.1 compare_bitcast_fusion.6
  26.0 0.7 %add_select_fusion = f32[8,80,272]{2,1,0:T(8,128)S(1)} fusion(f32[8]{0:T(128)S(1)} %get-tuple-element.3, f32[8]{0:T(128)S(1)} %get-tuple-element.4, f32[8]{0:T(128)S(1)} %get-tuple-element.5, f32[8]{0:T(128)S(1)} %get-tuple-element.6, f32[8]{0:T(128)S(1)} %get-tuple-element.7, f32[8]{0:T(128)S(1)} %get-tuple-element.8, f32[8]{0:T(128)S(1)} %get-tuple-element.9, ...), kind=kLoop, calls=%fused_computation.84 | loop fusion | flops 2785280 | bytes 892416 | tf_op jit(solution)/shard_map/jit(_where)/select_n | solution.py:112
  26.7 0.5 %pad_maximum_fusion = f32[9,80,272]{2,1,0:T(8,128)S(1)} fusion(f32[9,80,8]{2,1,0:T(8,128)S(1)} %collective-permute-done.3, f32[9,8,256]{2,1,0:T(8,128)S(1)} %collective-permute-done.1, f32[1,64,256]{2,1,0:T(8,128)S(1)} %convert_bitcast_fusion, f32[8,64,256]{2,1,0:T(8,128)S(1)} %copy-done, f32[9,8,256]{2,1,0:T(8,128)S(1)} %collective-permute-done, ...), kind=kLoop, calls=%fused_computation.3 | loop fusion | flops 979200 | bytes 1566720 | tf_op jit(solution)/shard_map/concatenate | solution.py:20
  27.1 1.4 %fusion.56 = (f32[8,80,272]{2,1,0:T(8,128)S(1)}, f32[8,80,272]{2,1,0:T(8,128)S(1)}, f32[8,80,272]{2,1,0:T(8,128)S(1)}, f32[8,80,272]{2,1,0:T(8,128)S(1)}, f32[8,80,272]{2,1,0:T(8,128)S(1)}) fusion(f32[9,80,272]{2,1,0:T(8,128)S(1)} %pad_maximum_fusion, pred[80,272]{1,0:T(8,128)(4,1)S(1)} %and_and_fusion, f32[8,80,272]{2,1,0:T(8,128)S(1)} %add_select_fusion), kind=kLoop, calls=%fused_computation.83 | loop fusion | flops 4700160 | bytes 4896000 | tf_op jit(solution)/shard_map/div | solution.py:117
  28.6 1.0 %fusion.9 = f32[8,80,272]{2,1,0:T(8,128)S(1)} fusion(f32[8,80,272]{2,1,0:T(8,128)S(1)} %get-tuple-element.13, f32[8,80,272]{2,1,0:T(8,128)S(1)} %get-tuple-element.17, f32[8,80,272]{2,1,0:T(8,128)S(1)} %get-tuple-element.14, f32[8,80,272]{2,1,0:T(8,128)S(1)} %get-tuple-element.15, f32[8,80,272]{2,1,0:T(8,128)S(1)} %get-tuple-element.16, ...), kind=kLoop, calls=%fused_computation.32 | loop fusion | flops 2959360 | bytes 4896000 | tf_op jit(solution)/shard_map/add | solution.py:121
  29.6 1.0 %fusion.21 = f32[8,80,272]{2,1,0:T(8,128)S(1)} fusion(f32[8,80,272]{2,1,0:T(8,128)S(1)} %fusion.9, f32[8,80,272]{2,1,0:T(8,128)S(1)} %get-tuple-element.17, f32[8,80,272]{2,1,0:T(8,128)S(1)} %get-tuple-element.14, f32[8,80,272]{2,1,0:T(8,128)S(1)} %get-tuple-element.15, f32[8,80,272]{2,1,0:T(8,128)S(1)} %get-tuple-element.16, ...), kind=kLoop, calls=%fused_computation.44 | loop fusion | flops 2959360 | bytes 4896000 | tf_op jit(solution)/shard_map/add | solution.py:121
  30.5 1.0 %fusion.33 = f32[8,80,272]{2,1,0:T(8,128)S(1)} fusion(f32[8,80,272]{2,1,0:T(8,128)S(1)} %fusion.21, f32[8,80,272]{2,1,0:T(8,128)S(1)} %get-tuple-element.17, f32[8,80,272]{2,1,0:T(8,128)S(1)} %get-tuple-element.14, f32[8,80,272]{2,1,0:T(8,128)S(1)} %get-tuple-element.15, f32[8,80,272]{2,1,0:T(8,128)S(1)} %get-tuple-element.16, ...), kind=kLoop, calls=%fused_computation.56 | loop fusion | flops 2959360 | bytes 4896000 | tf_op jit(solution)/shard_map/add | solution.py:121
  31.5 1.8 %fusion.75 = f32[8,80,136]{1,2,0:T(8,128)S(1)} fusion(s32[272]{0:T(512)S(1)} %get-tuple-element.38, s32[272]{0:T(512)S(1)} %get-tuple-element.39, pred[272]{0:T(512)(128)(4,1)S(1)} %fusion.107, f32[8]{0:T(128)S(1)} %get-tuple-element.3, f32[8]{0:T(128)S(1)} %get-tuple-element.4, f32[8]{0:T(128)S(1)} %get-tuple-element.5, f32[8]{0:T(128)S(1)} %get-tuple-element.6, ...), kind=kOutput, calls=%fused_computation.139 | convolution fusion | flops 286957824 | bytes 546704 | tf_op jit(solution)/shard_map/sxy,yj->sxj/dot_general | solution.py:91
  33.3 1.7 %fusion.43 = f32[8,80,136]{1,2,0:T(8,128)S(1)} fusion(f32[8,80,272]{2,1,0:T(8,128)S(1)} %get-tuple-element.17, f32[8,80,272]{2,1,0:T(8,128)S(1)} %fusion.33, f32[8,80,272]{2,1,0:T(8,128)S(1)} %get-tuple-element.14, f32[8,80,272]{2,1,0:T(8,128)S(1)} %get-tuple-element.15, f32[8,80,272]{2,1,0:T(8,128)S(1)} %get-tuple-element.16, ...), kind=kOutput, calls=%fused_computation.66 | convolution fusion | flops 286435584 | bytes 6251008 | tf_op jit(solution)/shard_map/sxy,yj->sxj/dot_general | solution.py:91
  35.0 0.6 %fusion.90 = f32[8,136,40]{1,2,0:T(8,128)S(1)} fusion(f32[8,80,136]{1,2,0:T(8,128)S(1)} %fusion.75, s32[80]{0:T(128)S(1)} %get-tuple-element.40, s32[80]{0:T(128)S(1)} %get-tuple-element.41, pred[80]{0:T(512)(128)(4,1)S(1)} %compare_and_fusion.3), kind=kOutput, calls=%fused_computation.158 | convolution fusion | flops 41785600 | bytes 522960 | tf_op jit(solution)/shard_map/xi,sxj->sij/dot_general | solution.py:92
  35.7 0.9 %multiply_divide_fusion = (f32[8,40,136]{2,1,0:T(8,128)S(1)}, f32[8,40,136]{2,1,0:T(8,128)S(1)}, f32[8,40,136]{2,1,0:T(8,128)S(1)}, f32[8,40,136]{2,1,0:T(8,128)S(1)}) fusion(pred[40,136]{1,0:T(8,128)(4,1)S(1)} %and_and_fusion.1, f32[8,40,136]{2,1,0:T(8,128)S(1)} %multiply_bitcast_fusion, f32[8,136,40]{1,2,0:T(8,128)S(1)} %fusion.90, ...), kind=kOutput, calls=%fused_computation.115 | convolution fusion | flops 42960640 | bytes 1398800 | tf_op jit(solution)/shard_map/xi,sxj->sij/dot_general | solution.py:92
  36.6 0.6 %fusion.60 = (f32[8,40,136]{2,1,0:T(8,128)S(1)}, f32[8,40,136]{2,1,0:T(8,128)S(1)}) fusion(f32[8,40,136]{2,1,0:T(8,128)S(1)} %get-tuple-element.10, f32[8,40,136]{2,1,0:T(8,128)S(1)} %multiply_bitcast_fusion, f32[8,136,40]{1,2,0:T(8,128)S(1)} %fusion.90), kind=kLoop, calls=%fused_computation.97 | loop fusion | flops 1175040 | bytes 870400 | tf_op jit(solution)/shard_map/add | solution.py:52
  37.2 0.3 fusion.69
  37.6 0.0 copy-start.1
  37.6 0.4 %fusion.73 = f32[8,32,256]{2,1,0:T(8,128)S(1)} fusion(f32[8,32,128]{2,1,0:T(8,128)S(1)} %fusion.69, s32[256]{0:T(256)S(1)} %get-tuple-element.42, s32[256]{0:T(256)S(1)} %get-tuple-element.43, pred[256]{0:T(512)(128)(4,1)S(1)} %compare_and_fusion.1), kind=kOutput, calls=%fused_computation.128 | convolution fusion | flops 100728832 | bytes 395520 | tf_op jit(solution)/shard_map/sij,yj->siy/dot_general | solution.py:100
  38.0 1.2 %fusion = f32[8,64,256]{2,1,0:T(8,128)} fusion(f32[8,32,256]{2,1,0:T(8,128)S(1)} %fusion.73, f32[8,80,272]{2,1,0:T(8,128)S(1)} %fusion.33, s32[64]{0:T(128)S(1)} %get-tuple-element.44, s32[64]{0:T(128)S(1)} %get-tuple-element.45, pred[64]{0:T(512)(128)(4,1)S(1)} %compare_and_fusion), kind=kOutput, calls=%fused_computation.1 | convolution fusion | flops 50466816 | bytes 1311296 | tf_op jit(solution)/shard_map/xi,siy->sxy/dot_general | solution.py:101
  39.2 0.0 copy-done.1
  (13 shorter events, 0.1 us)
Async XLA Ops:
  0.6 10.9 %copy-start = (f32[8,64,256]{2,1,0:T(8,128)S(1)}, f32[8,64,256]{2,1,0:T(8,128)}, u32[]{:S(2)}) copy-start(f32[8,64,256]{2,1,0:T(8,128)} %param.4) | copy-start | bytes 1572868
  2.4 7.5 %collective-permute-start = (f32[9,8,256]{2,1,0:T(8,128)S(1)}, f32[9,8,256]{2,1,0:T(8,128)S(1)}, u32[]{:S(2)}, u32[]{:S(2)}) collective-permute-start(f32[9,8,256]{2,1,0:T(8,128)S(1)} %get-tuple-element.24), channel_id=1, source_target_pairs={{0,8},{8,16},{16,24},{1,9},{9,17},{17,25},{2,10},{10,18},{18,26},{... | collective-permute-start | bytes 221192 | tf_op jit(solution)/shard_map/ppermute | solution.py:16
  6.5 5.1 %collective-permute-start.1 = (f32[9,8,256]{2,1,0:T(8,128)S(1)}, f32[9,8,256]{2,1,0:T(8,128)S(1)}, u32[]{:S(2)}, u32[]{:S(2)}) collective-permute-start(f32[9,8,256]{2,1,0:T(8,128)S(1)} %get-tuple-element.25), channel_id=1, source_target_pairs={{8,0},{16,8},{24,16},{9,1},{17,9},{25,17},{10,2},{18,10},{26,18},{... | collective-permute-start | bytes 221192 | tf_op jit(solution)/shard_map/ppermute | solution.py:19
  11.8 9.6 %collective-permute-start.2 = (f32[9,80,8]{2,1,0:T(8,128)S(1)}, f32[9,80,8]{2,1,0:T(8,128)S(1)}, u32[]{:S(2)}, u32[]{:S(2)}) collective-permute-start(f32[9,80,8]{2,1,0:T(8,128)S(1)} %get-tuple-element.22), channel_id=1, source_target_pairs={{0,2},{2,4},{4,6},{1,3},{3,5},{5,7},{8,10},{10,12},{12,14},{9,11},... | collective-permute-start | bytes 69128 | tf_op jit(solution)/shard_map/ppermute | solution.py:16
  16.9 8.8 %collective-permute-start.3 = (f32[9,80,8]{2,1,0:T(8,128)S(1)}, f32[9,80,8]{2,1,0:T(8,128)S(1)}, u32[]{:S(2)}, u32[]{:S(2)}) collective-permute-start(f32[9,80,8]{2,1,0:T(8,128)S(1)} %get-tuple-element.23), channel_id=1, source_target_pairs={{2,0},{4,2},{6,4},{3,1},{5,3},{7,5},{10,8},{12,10},{14,12},{11,9},... | collective-permute-start | bytes 69128 | tf_op jit(solution)/shard_map/ppermute | solution.py:19
  37.6 1.7 %copy-start.1 = (f32[8,32,128]{2,1,0:T(8,128)}, f32[8,32,128]{2,1,0:T(8,128)S(1)}, u32[]{:S(2)}) copy-start(f32[8,32,128]{2,1,0:T(8,128)S(1)} %fusion.69) | copy-start | bytes 393220

commit v2 on v1

--- a/solution.py
+++ b/solution.py
@@ -8,17 +8,33 @@
 HALO = 8
 
 
-def with_halo(block, sides, width):
-    for axis, dim in sides:
-        count = lax.axis_size(axis)
-        forward = [(i, i + 1) for i in range(count - 1)]
-        backward = [(target, source) for source, target in forward]
-        low = lax.ppermute(
-            lax.slice_in_dim(block, block.shape[dim] - width, None, axis=dim), axis, forward
-        )
-        high = lax.ppermute(lax.slice_in_dim(block, 0, width, axis=dim), axis, backward)
-        block = jnp.concatenate([low, block, high], axis=dim)
-    return block
+def shifted(piece, dx, dy):
+    nx = lax.axis_size("gx")
+    ny = lax.axis_size("gy")
+    pairs = [
+        (i * ny + j, (i + dx) * ny + (j + dy))
+        for i in range(nx)
+        for j in range(ny)
+        if 0 <= i + dx < nx and 0 <= j + dy < ny
+    ]
+    return lax.ppermute(piece, ("gx", "gy"), pairs)
+
+
+def with_halo(block, width):
+    rows, cols = block.shape[1], block.shape[2]
+    low_x = slice(rows - width, rows)
+    high_x = slice(0, width)
+    low_y = slice(cols - width, cols)
+    high_y = slice(0, width)
+    every = slice(None)
+    grid = []
+    for dx, sx in ((1, low_x), (0, every), (-1, high_x)):
+        line = []
+        for dy, sy in ((1, low_y), (0, every), (-1, high_y)):
+            piece = block[:, sx, sy]
+            line.append(block if dx == 0 and dy == 0 else shifted(piece, dx, dy))
+        grid.append(jnp.concatenate(line, axis=2))
+    return jnp.concatenate(grid, axis=1)
 
 
 def neighbours(padded):
@@ -105,7 +121,7 @@
     h = HALO
     count, rows, cols = source.shape
     stacked = jnp.concatenate([source, perm_classes.astype(jnp.float32)[None]], axis=0)
-    wide = with_halo(stacked, (("gx", 1), ("gy", 2)), h)
+    wide = with_halo(stacked, h)
     source_wide = wide[:count]
     classes_wide = wide[count].astype(jnp.int32)
     inside = inside_mask(rows + 2 * h, cols + 2 * h, h)

time: 39.5 us -> 45.6 us (1.15)
  the two profiles are of different devices: /device:TPU:1 before, /device:TPU:18 now
where the time goes in v2:
time: 45.6 us; the launch traced here: 45.2 us
  starting transfers between devices  24.3 us (53%)
  other arithmetic  9.02 us (20%)
  matrix products  6.71 us (15%)
  waiting for transfers between devices  3.85 us (8%)
  between operations  0.99 us (2%)
    ppermute x8, starting transfers between devices, shifted(): return lax.ppermute(piece, ('gx', 'gy'), pairs)  24.3 us
    ppermute x8, waiting for transfers between devices, shifted(): return lax.ppermute(piece, ('gx', 'gy'), pairs)  3.85 us
    dot_general x2, matrix products, restrict(): half = jnp.einsum('sxy,yj->sxj', values, ry, precision=hi)  3.55 us
    add x3, other arithmetic, shards(): current = current + DAMPING * residual / safe_diagonal  2.89 us
    dot_general x2, matrix products, restrict(): return jnp.einsum('xi,sxj->sij', rx, half, precision=hi)  1.53 us
    div x1, other arithmetic, shards(): current = DAMPING * source_wide / safe_diagonal  1.44 us
    dot_general x1, matrix products, prolong(): return jnp.einsum('xi,siy->sxy', ex, wide, precision=hi)  1.22 us
  transfers between devices with their start and end apart: 8, of which 2 were waited for; matrix products, arithmetic and copies ran while one was open for 2% of the time, Pallas kernels for 0%

profile of v2, /device:TPU:18, one launch (start us, length us, event | category | flops | bytes accessed | tf_op | source)
XLA Modules:
  0.0 45.2 jit_solution(10600951071172497784)
XLA Ops:
  0.6 0.0 copy-start
  0.6 0.9 %convert_bitcast_fusion = f32[1,64,256]{2,1,0:T(8,128)S(1)} fusion(s32[64,256]{1,0:T(8,128)} %param.7), kind=kLoop, calls=%fused_computation.159 | loop fusion | flops 16384 | bytes 131072 | tf_op jit(solution)/shard_map/broadcast_in_dim | solution.py:123
  1.5 0.9 %pad_maximum_fusion.3 = (f32[9,8,8]{2,1,0:T(8,128)S(1)}, f32[9,8,8]{2,1,0:T(8,128)S(1)}, f32[9,8,8]{2,1,0:T(8,128)S(1)}, f32[9,8,8]{2,1,0:T(8,128)S(1)}) fusion(f32[1,64,256]{2,1,0:T(8,128)S(1)} %convert_bitcast_fusion, f32[8,64,256]{2,1,0:T(8,128)} %param.4), kind=kLoop, calls=%fused_computation.165 | loop fusion | flops 2304 | bytes 599040 | tf_op jit(solution)/shard_map/slice | solution.py:34
  2.4 0.0 copy-start.3
  2.4 0.0 copy-start.2
  2.5 2.9 %collective-permute-start = (f32[9,8,8]{2,1,0:T(8,128)S(1)}, f32[9,8,8]{2,1,0:T(8,128)S(1)}, u32[]{:S(2)}, u32[]{:S(2)}) collective-permute-start(f32[9,8,8]{2,1,0:T(8,128)S(1)} %get-tuple-element.22), channel_id=1, source_target_pairs={{0,10},{2,12},{4,14},{8,18},{10,20},{12,22},{16,26},{18,28},{20,30... | collective-permute-start | bytes 6920 | tf_op jit(solution)/shard_map/ppermute | solution.py:20
  5.4 1.9 %collective-permute-start.2 = (f32[9,8,8]{2,1,0:T(8,128)S(1)}, f32[9,8,8]{2,1,0:T(8,128)S(1)}, u32[]{:S(2)}, u32[]{:S(2)}) collective-permute-start(f32[9,8,8]{2,1,0:T(8,128)S(1)} %get-tuple-element.25), channel_id=1, source_target_pairs={{2,8},{4,10},{6,12},{10,16},{12,18},{14,20},{18,24},{20,26},{22,28... | collective-permute-start | bytes 6920 | tf_op jit(solution)/shard_map/ppermute | solution.py:20
  7.3 3.6 %collective-permute-start.5 = (f32[9,8,8]{2,1,0:T(8,128)S(1)}, f32[9,8,8]{2,1,0:T(8,128)S(1)}, u32[]{:S(2)}, u32[]{:S(2)}) collective-permute-start(f32[9,8,8]{2,1,0:T(8,128)S(1)} %get-tuple-element.23), channel_id=1, source_target_pairs={{8,2},{10,4},{12,6},{16,10},{18,12},{20,14},{24,18},{26,20},{28,22... | collective-permute-start | bytes 6920 | tf_op jit(solution)/shard_map/ppermute | solution.py:20
  11.0 4.4 %collective-permute-start.7 = (f32[9,8,8]{2,1,0:T(8,128)S(1)}, f32[9,8,8]{2,1,0:T(8,128)S(1)}, u32[]{:S(2)}, u32[]{:S(2)}) collective-permute-start(f32[9,8,8]{2,1,0:T(8,128)S(1)} %get-tuple-element.24), channel_id=1, source_target_pairs={{10,0},{12,2},{14,4},{18,8},{20,10},{22,12},{26,16},{28,18},{30,20... | collective-permute-start | bytes 6920 | tf_op jit(solution)/shard_map/ppermute | solution.py:20
  15.4 0.0 copy-done
  15.4 0.1 fusion.68
  15.6 1.9 %collective-permute-start.3 = (f32[9,64,8]{2,1,0:T(8,128)S(1)}, f32[9,64,8]{2,1,0:T(8,128)S(1)}, u32[]{:S(2)}, u32[]{:S(2)}) collective-permute-start(f32[9,64,8]{2,1,0:T(8,128)S(1)} %get-tuple-element.28), channel_id=1, source_target_pairs={{0,2},{2,4},{4,6},{8,10},{10,12},{12,14},{16,18},{18,20},{20,22},{... | collective-permute-start | bytes 55304 | tf_op jit(solution)/shard_map/ppermute | solution.py:20
  17.6 0.0 copy-done.3
  17.6 0.1 fusion.106
  17.7 0.0 copy-done.2
  17.7 0.1 multiply_reduce_fusion
  17.8 0.3 slice_reduce_fusion.7
  18.1 0.1 and_and_fusion
  18.2 0.1 and_and_fusion.1
  18.3 0.0 collective-permute-done
  18.3 3.6 %collective-permute-start.4 = (f32[9,64,8]{2,1,0:T(8,128)S(1)}, f32[9,64,8]{2,1,0:T(8,128)S(1)}, u32[]{:S(2)}, u32[]{:S(2)}) collective-permute-start(f32[9,64,8]{2,1,0:T(8,128)S(1)} %get-tuple-element.29), channel_id=1, source_target_pairs={{2,0},{4,2},{6,4},{10,8},{12,10},{14,12},{18,16},{20,18},{22,20},{... | collective-permute-start | bytes 55304 | tf_op jit(solution)/shard_map/ppermute | solution.py:20
  22.0 0.0 collective-permute-done.2
  22.0 3.5 %collective-permute-start.1 = (f32[9,8,256]{2,1,0:T(8,128)S(1)}, f32[9,8,256]{2,1,0:T(8,128)S(1)}, u32[]{:S(2)}, u32[]{:S(2)}) collective-permute-start(f32[9,8,256]{2,1,0:T(8,128)S(1)} %get-tuple-element.26), channel_id=1, source_target_pairs={{0,8},{2,10},{4,12},{6,14},{8,16},{10,18},{12,20},{14,22},{16,24},... | collective-permute-start | bytes 221192 | tf_op jit(solution)/shard_map/ppermute | solution.py:20
  25.5 0.0 collective-permute-done.5
  25.5 2.4 %collective-permute-start.6 = (f32[9,8,256]{2,1,0:T(8,128)S(1)}, f32[9,8,256]{2,1,0:T(8,128)S(1)}, u32[]{:S(2)}, u32[]{:S(2)}) collective-permute-start(f32[9,8,256]{2,1,0:T(8,128)S(1)} %get-tuple-element.27), channel_id=1, source_target_pairs={{8,0},{10,2},{12,4},{14,6},{16,8},{18,10},{20,12},{22,14},{24,16},... | collective-permute-start | bytes 221192 | tf_op jit(solution)/shard_map/ppermute | solution.py:20
  27.9 0.0 collective-permute-done.7
  27.9 0.0 collective-permute-done.3
  27.9 0.0 collective-permute-done.4
  27.9 0.3 collective-permute-done.1
  28.2 3.5 %collective-permute-done.6 = f32[9,8,256]{2,1,0:T(8,128)S(1)} collective-permute-done((f32[9,8,256]{2,1,0:T(8,128)S(1)}, f32[9,8,256]{2,1,0:T(8,128)S(1)}, u32[]{:S(2)}, u32[]{:S(2)}) %collective-permute-start.6) | collective-permute-done | bytes 73760 | tf_op jit(solution)/shard_map/ppermute | solution.py:20
  31.7 0.1 compare_bitcast_fusion.7
  31.8 0.1 compare_bitcast_fusion.6
  32.0 0.7 %add_select_fusion = f32[8,80,272]{2,1,0:T(8,128)S(1)} fusion(f32[8]{0:T(128)S(1)} %get-tuple-element.3, f32[8]{0:T(128)S(1)} %get-tuple-element.4, f32[8]{0:T(128)S(1)} %get-tuple-element.5, f32[8]{0:T(128)S(1)} %get-tuple-element.6, f32[8]{0:T(128)S(1)} %get-tuple-element.7, f32[8]{0:T(128)S(1)} %get-tuple-element.8, f32[8]{0:T(128)S(1)} %get-tuple-element.9, ...), kind=kLoop, calls=%fused_computation.88 | loop fusion | flops 2785280 | bytes 892416 | tf_op jit(solution)/shard_map/jit(_where)/select_n | solution.py:128
  32.7 0.5 %maximum_maximum_fusion = f32[9,80,272]{2,1,0:T(8,128)S(1)} fusion(f32[9,8,8]{2,1,0:T(8,128)S(1)} %collective-permute-done.7, f32[9,8,256]{2,1,0:T(8,128)S(1)} %collective-permute-done.6, f32[9,8,8]{2,1,0:T(8,128)S(1)} %collective-permute-done.5, f32[9,64,8]{2,1,0:T(8,128)S(1)} %collective-permute-done.4, f32[1,64,256]{2,1,0:T(8,128)S(1)} %convert_bitcast_fusion, ...), kind=kLoop, calls=%fused_computation.7 | loop fusion | flops 1762560 | bytes 1566720 | tf_op jit(solution)/shard_map/concatenate | solution.py:37
  33.1 1.4 %fusion.56 = (f32[8,80,272]{2,1,0:T(8,128)S(1)}, f32[8,80,272]{2,1,0:T(8,128)S(1)}, f32[8,80,272]{2,1,0:T(8,128)S(1)}, f32[8,80,272]{2,1,0:T(8,128)S(1)}, f32[8,80,272]{2,1,0:T(8,128)S(1)}) fusion(f32[9,80,272]{2,1,0:T(8,128)S(1)} %maximum_maximum_fusion, pred[80,272]{1,0:T(8,128)(4,1)S(1)} %and_and_fusion, f32[8,80,272]{2,1,0:T(8,128)S(1)} %add_select_fusion), kind=kLoop, calls=%fused_computation.87 | loop fusion | flops 4700160 | bytes 4896000 | tf_op jit(solution)/shard_map/div | solution.py:133
  34.6 1.0 %fusion.9 = f32[8,80,272]{2,1,0:T(8,128)S(1)} fusion(f32[8,80,272]{2,1,0:T(8,128)S(1)} %get-tuple-element.13, f32[8,80,272]{2,1,0:T(8,128)S(1)} %get-tuple-element.17, f32[8,80,272]{2,1,0:T(8,128)S(1)} %get-tuple-element.14, f32[8,80,272]{2,1,0:T(8,128)S(1)} %get-tuple-element.15, f32[8,80,272]{2,1,0:T(8,128)S(1)} %get-tuple-element.16, ...), kind=kLoop, calls=%fused_computation.36 | loop fusion | flops 2959360 | bytes 4896000 | tf_op jit(solution)/shard_map/add | solution.py:137
  35.5 1.0 %fusion.21 = f32[8,80,272]{2,1,0:T(8,128)S(1)} fusion(f32[8,80,272]{2,1,0:T(8,128)S(1)} %fusion.9, f32[8,80,272]{2,1,0:T(8,128)S(1)} %get-tuple-element.17, f32[8,80,272]{2,1,0:T(8,128)S(1)} %get-tuple-element.14, f32[8,80,272]{2,1,0:T(8,128)S(1)} %get-tuple-element.15, f32[8,80,272]{2,1,0:T(8,128)S(1)} %get-tuple-element.16, ...), kind=kLoop, calls=%fused_computation.48 | loop fusion | flops 2959360 | bytes 4896000 | tf_op jit(solution)/shard_map/add | solution.py:137
  36.5 1.0 %fusion.33 = f32[8,80,272]{2,1,0:T(8,128)S(1)} fusion(f32[8,80,272]{2,1,0:T(8,128)S(1)} %fusion.21, f32[8,80,272]{2,1,0:T(8,128)S(1)} %get-tuple-element.17, f32[8,80,272]{2,1,0:T(8,128)S(1)} %get-tuple-element.14, f32[8,80,272]{2,1,0:T(8,128)S(1)} %get-tuple-element.15, f32[8,80,272]{2,1,0:T(8,128)S(1)} %get-tuple-element.16, ...), kind=kLoop, calls=%fused_computation.60 | loop fusion | flops 2959360 | bytes 4896000 | tf_op jit(solution)/shard_map/add | solution.py:137
  37.5 1.8 %fusion.77 = f32[8,80,136]{1,2,0:T(8,128)S(1)} fusion(s32[272]{0:T(512)S(1)} %get-tuple-element.42, s32[272]{0:T(512)S(1)} %get-tuple-element.43, pred[272]{0:T(512)(128)(4,1)S(1)} %fusion.111, f32[8]{0:T(128)S(1)} %get-tuple-element.3, f32[8]{0:T(128)S(1)} %get-tuple-element.4, f32[8]{0:T(128)S(1)} %get-tuple-element.5, f32[8]{0:T(128)S(1)} %get-tuple-element.6, ...), kind=kOutput, calls=%fused_computation.148 | convolution fusion | flops 286957824 | bytes 546704 | tf_op jit(solution)/shard_map/sxy,yj->sxj/dot_general | solution.py:107
  39.3 1.7 %fusion.43 = f32[8,80,136]{1,2,0:T(8,128)S(1)} fusion(f32[8,80,272]{2,1,0:T(8,128)S(1)} %get-tuple-element.17, f32[8,80,272]{2,1,0:T(8,128)S(1)} %fusion.33, f32[8,80,272]{2,1,0:T(8,128)S(1)} %get-tuple-element.14, f32[8,80,272]{2,1,0:T(8,128)S(1)} %get-tuple-element.15, f32[8,80,272]{2,1,0:T(8,128)S(1)} %get-tuple-element.16, ...), kind=kOutput, calls=%fused_computation.70 | convolution fusion | flops 286435584 | bytes 6251008 | tf_op jit(solution)/shard_map/sxy,yj->sxj/dot_general | solution.py:107
  41.0 0.6 %fusion.94 = f32[8,136,40]{1,2,0:T(8,128)S(1)} fusion(f32[8,80,136]{1,2,0:T(8,128)S(1)} %fusion.77, s32[80]{0:T(128)S(1)} %get-tuple-element.44, s32[80]{0:T(128)S(1)} %get-tuple-element.45, pred[80]{0:T(512)(128)(4,1)S(1)} %compare_and_fusion.3), kind=kOutput, calls=%fused_computation.171 | convolution fusion | flops 41785600 | bytes 522960 | tf_op jit(solution)/shard_map/xi,sxj->sij/dot_general | solution.py:108
  41.7 0.9 %multiply_divide_fusion = (f32[8,40,136]{2,1,0:T(8,128)S(1)}, f32[8,40,136]{2,1,0:T(8,128)S(1)}, f32[8,40,136]{2,1,0:T(8,128)S(1)}, f32[8,40,136]{2,1,0:T(8,128)S(1)}) fusion(pred[40,136]{1,0:T(8,128)(4,1)S(1)} %and_and_fusion.1, f32[8,40,136]{2,1,0:T(8,128)S(1)} %multiply_bitcast_fusion, f32[8,136,40]{1,2,0:T(8,128)S(1)} %fusion.94, ...), kind=kOutput, calls=%fused_computation.122 | convolution fusion | flops 42960640 | bytes 1398800 | tf_op jit(solution)/shard_map/xi,sxj->sij/dot_general | solution.py:108
  42.6 0.6 %fusion.60 = (f32[8,40,136]{2,1,0:T(8,128)S(1)}, f32[8,40,136]{2,1,0:T(8,128)S(1)}) fusion(f32[8,40,136]{2,1,0:T(8,128)S(1)} %get-tuple-element.10, f32[8,40,136]{2,1,0:T(8,128)S(1)} %multiply_bitcast_fusion, f32[8,136,40]{1,2,0:T(8,128)S(1)} %fusion.94), kind=kLoop, calls=%fused_computation.104 | loop fusion | flops 1175040 | bytes 870400 | tf_op jit(solution)/shard_map/add | solution.py:68
  43.2 0.3 fusion.71
  43.5 0.0 copy-start.1
  43.6 0.4 fusion.75
  44.0 1.2 %fusion = f32[8,64,256]{2,1,0:T(8,128)} fusion(f32[8,32,256]{2,1,0:T(8,128)S(1)} %fusion.75, f32[8,80,272]{2,1,0:T(8,128)S(1)} %fusion.33, s32[64]{0:T(128)S(1)} %get-tuple-element.48, s32[64]{0:T(128)S(1)} %get-tuple-element.49, pred[64]{0:T(512)(128)(4,1)S(1)} %compare_and_fusion), kind=kOutput, calls=%fused_computation.5 | convolution fusion | flops 50466816 | bytes 1311296 | tf_op jit(solution)/shard_map/xi,siy->sxy/dot_general | solution.py:117
  45.2 0.0 copy-done.1
  (14 shorter events, 0.1 us)
Async XLA Ops:
  0.6 14.8 %copy-start = (f32[8,64,256]{2,1,0:T(8,128)S(1)}, f32[8,64,256]{2,1,0:T(8,128)}, u32[]{:S(2)}) copy-start(f32[8,64,256]{2,1,0:T(8,128)} %param.4) | copy-start | bytes 1572868
  2.4 15.2 %copy-start.3 = (s32[8]{0:T(128)S(1)}, s32[8]{0:T(128)}, u32[]{:S(2)}) copy-start(s32[8]{0:T(128)} %param.5) | copy-start | bytes 100
  2.4 15.3 %copy-start.2 = (f32[8,8]{1,0:T(8,128)S(1)}, f32[8,8]{1,0:T(8,128)}, u32[]{:S(2)}) copy-start(f32[8,8]{1,0:T(8,128)} %param.6) | copy-start | bytes 772
  2.5 15.8 %collective-permute-start = (f32[9,8,8]{2,1,0:T(8,128)S(1)}, f32[9,8,8]{2,1,0:T(8,128)S(1)}, u32[]{:S(2)}, u32[]{:S(2)}) collective-permute-start(f32[9,8,8]{2,1,0:T(8,128)S(1)} %get-tuple-element.22), channel_id=1, source_target_pairs={{0,10},{2,12},{4,14},{8,18},{10,20},{12,22},{16,26},{18,28},{20,30... | collective-permute-start | bytes 6920 | tf_op jit(solution)/shard_map/ppermute | solution.py:20
  5.4 16.6 %collective-permute-start.2 = (f32[9,8,8]{2,1,0:T(8,128)S(1)}, f32[9,8,8]{2,1,0:T(8,128)S(1)}, u32[]{:S(2)}, u32[]{:S(2)}) collective-permute-start(f32[9,8,8]{2,1,0:T(8,128)S(1)} %get-tuple-element.25), channel_id=1, source_target_pairs={{2,8},{4,10},{6,12},{10,16},{12,18},{14,20},{18,24},{20,26},{22,28... | collective-permute-start | bytes 6920 | tf_op jit(solution)/shard_map/ppermute | solution.py:20
  7.3 18.2 %collective-permute-start.5 = (f32[9,8,8]{2,1,0:T(8,128)S(1)}, f32[9,8,8]{2,1,0:T(8,128)S(1)}, u32[]{:S(2)}, u32[]{:S(2)}) collective-permute-start(f32[9,8,8]{2,1,0:T(8,128)S(1)} %get-tuple-element.23), channel_id=1, source_target_pairs={{8,2},{10,4},{12,6},{16,10},{18,12},{20,14},{24,18},{26,20},{28,22... | collective-permute-start | bytes 6920 | tf_op jit(solution)/shard_map/ppermute | solution.py:20
  11.0 16.9 %collective-permute-start.7 = (f32[9,8,8]{2,1,0:T(8,128)S(1)}, f32[9,8,8]{2,1,0:T(8,128)S(1)}, u32[]{:S(2)}, u32[]{:S(2)}) collective-permute-start(f32[9,8,8]{2,1,0:T(8,128)S(1)} %get-tuple-element.24), channel_id=1, source_target_pairs={{10,0},{12,2},{14,4},{18,8},{20,10},{22,12},{26,16},{28,18},{30,20... | collective-permute-start | bytes 6920 | tf_op jit(solution)/shard_map/ppermute | solution.py:20
  15.6 12.3 %collective-permute-start.3 = (f32[9,64,8]{2,1,0:T(8,128)S(1)}, f32[9,64,8]{2,1,0:T(8,128)S(1)}, u32[]{:S(2)}, u32[]{:S(2)}) collective-permute-start(f32[9,64,8]{2,1,0:T(8,128)S(1)} %get-tuple-element.28), channel_id=1, source_target_pairs={{0,2},{2,4},{4,6},{8,10},{10,12},{12,14},{16,18},{18,20},{20,22},{... | collective-permute-start | bytes 55304 | tf_op jit(solution)/shard_map/ppermute | solution.py:20
  18.3 9.6 %collective-permute-start.4 = (f32[9,64,8]{2,1,0:T(8,128)S(1)}, f32[9,64,8]{2,1,0:T(8,128)S(1)}, u32[]{:S(2)}, u32[]{:S(2)}) collective-permute-start(f32[9,64,8]{2,1,0:T(8,128)S(1)} %get-tuple-element.29), channel_id=1, source_target_pairs={{2,0},{4,2},{6,4},{10,8},{12,10},{14,12},{18,16},{20,18},{22,20},{... | collective-permute-start | bytes 55304 | tf_op jit(solution)/shard_map/ppermute | solution.py:20
  22.0 6.2 %collective-permute-start.1 = (f32[9,8,256]{2,1,0:T(8,128)S(1)}, f32[9,8,256]{2,1,0:T(8,128)S(1)}, u32[]{:S(2)}, u32[]{:S(2)}) collective-permute-start(f32[9,8,256]{2,1,0:T(8,128)S(1)} %get-tuple-element.26), channel_id=1, source_target_pairs={{0,8},{2,10},{4,12},{6,14},{8,16},{10,18},{12,20},{14,22},{16,24},... | collective-permute-start | bytes 221192 | tf_op jit(solution)/shard_map/ppermute | solution.py:20
  25.5 6.2 %collective-permute-start.6 = (f32[9,8,256]{2,1,0:T(8,128)S(1)}, f32[9,8,256]{2,1,0:T(8,128)S(1)}, u32[]{:S(2)}, u32[]{:S(2)}) collective-permute-start(f32[9,8,256]{2,1,0:T(8,128)S(1)} %get-tuple-element.27), channel_id=1, source_target_pairs={{8,0},{10,2},{12,4},{14,6},{16,8},{18,10},{20,12},{22,14},{24,16},... | collective-permute-start | bytes 221192 | tf_op jit(solution)/shard_map/ppermute | solution.py:20
  43.5 1.7 %copy-start.1 = (f32[8,32,128]{2,1,0:T(8,128)}, f32[8,32,128]{2,1,0:T(8,128)S(1)}, u32[]{:S(2)}) copy-start(f32[8,32,128]{2,1,0:T(8,128)S(1)} %fusion.71) | copy-start | bytes 393220

commit v3 on v0

v3 whole, which is shorter than its diff:
```python
import jax
import jax.numpy as jnp
from jax import lax
from jax.experimental import pallas as pl
from jax.experimental.pallas import tpu as pltpu
from jax.sharding import PartitionSpec as P

SWEEPS = 4
DAMPING = 0.8
HALO = 8
LANE_PAD = 128
HI = lax.Precision.HIGHEST


def exchange(block, axis, dim, width):
    count = lax.axis_size(axis)
    forward = [(i, i + 1) for i in range(count - 1)]
    backward = [(target, source) for source, target in forward]
    low = lax.ppermute(
        lax.slice_in_dim(block, block.shape[dim] - width, None, axis=dim), axis, forward
    )
    high = lax.ppermute(lax.slice_in_dim(block, 0, width, axis=dim), axis, backward)
    return low, high


def periodic_halo(block, width):
    low, high = exchange(block, "gx", 1, width)
    block = jnp.concatenate([block, high, low], axis=1)
    low, high = exchange(block, "gy", 2, width)
    gap = jnp.zeros(block.shape[:2] + (LANE_PAD - 2 * width,), block.dtype)
    return jnp.concatenate([block, high, gap, low], axis=2)


def neighbours(v):
    rows, cols = v.shape
    return (
        pltpu.roll(v, rows - 1, 0),
        pltpu.roll(v, 1, 0),
        pltpu.roll(v, cols - 1, 1),
        pltpu.roll(v, 1, 1),
    )


def couplings(perm):
    linkage = tuple(
        jnp.where(beside > 0.0, 2.0 * perm * beside / (perm + beside), 2.0 * perm)
        for beside in neighbours(perm)
    )
    diagonal = linkage[0] + linkage[1] + linkage[2] + linkage[3]
    return linkage, diagonal


def operator(linkage, diagonal, current):
    beside_all = neighbours(current)
    return diagonal * current - (
        linkage[0] * beside_all[0]
        + linkage[1] * beside_all[1]
        + linkage[2] * beside_all[2]
        + linkage[3] * beside_all[3]
    )


def dot(a, b):
    return jnp.dot(a, b, precision=HI, preferred_element_type=jnp.float32)


def smooth_kernel(
    levels_ref, src_ref, cls_ref, mask_ref, cmask_ref, rx_ref, ry_ref, ex_ref, ey_ref,
    sol_ref, corr_ref,
):
    s = pl.program_id(0)
    classes = cls_ref[0]
    valid = mask_ref[...] > 0.5
    perm = jnp.zeros(classes.shape, jnp.float32)
    for category in range(levels_ref.shape[1]):
        perm = perm + jnp.where(classes == float(category), levels_ref[s, category], 0.0)
    perm = jnp.where(valid, perm, 0.0)
    source = src_ref[0]
    linkage, diagonal = couplings(perm)
    safe_diagonal = jnp.where(valid, diagonal, 1.0)
    current = DAMPING * source / safe_diagonal
    for sweep_index in range(SWEEPS):
        residual = source - operator(linkage, diagonal, current)
        if sweep_index + 1 < SWEEPS:
            current = current + DAMPING * residual / safe_diagonal
    rx = rx_ref[...]
    ry = ry_ref[...]
    coarse_rhs = dot(dot(rx, residual), ry)
    coarse_perm = 0.25 * dot(dot(rx, perm), ry)
    coarse_valid = cmask_ref[...] > 0.5
    coarse_links, coarse_diagonal = couplings(coarse_perm)
    coarse_safe = jnp.where(coarse_valid, coarse_diagonal, 1.0)
    first = DAMPING * coarse_rhs / coarse_safe
    correction = (
        first
        + DAMPING * (coarse_rhs - operator(coarse_links, coarse_diagonal, first)) / coarse_safe
    )
    rows, cols = sol_ref.shape[1], sol_ref.shape[2]
    own = correction[: rows // 2, : cols // 2]
    corr_ref[0] = own
    sol_ref[0] = current[:rows, :cols] + dot(dot(ex_ref[...], own), ey_ref[...])


def offsets(n, wrap_at):
    f = jnp.arange(n, dtype=jnp.int32)
    return jnp.where(f < wrap_at, f, f - n)


def region(n, own, halo, wrap_at, index, count):
    g = offsets(n, wrap_at)
    near = (g >= -halo) & (g < own + halo)
    glob = g + index * own
    return near & (glob >= 0) & (glob < count * own)


def shards(source, sample_seeds, perm_levels, perm_classes):
    h = HALO
    count, rows, cols = source.shape
    ext_x, ext_y = rows + 2 * h, cols + LANE_PAD
    coarse_x = ext_x // 2
    coarse_y = -(-(ext_y // 2) // 128) * 128
    stacked = jnp.concatenate([source, perm_classes.astype(jnp.float32)[None]], axis=0)
    wide = periodic_halo(stacked, h)

    gx, gy = lax.axis_index("gx"), lax.axis_index("gy")
    nx, ny = lax.axis_size("gx"), lax.axis_size("gy")
    fine_r = region(ext_x, rows, h, rows + h, gx, nx)
    fine_c = region(ext_y, cols, h, cols + LANE_PAD // 2, gy, ny)
    mask = (fine_r[:, None] & fine_c[None, :]).astype(jnp.float32)
    coarse_r = region(coarse_x, rows // 2, h // 2, rows // 2 + h // 2, gx, nx)
    coarse_c = region(coarse_y, cols // 2, h // 2, cols // 2 + LANE_PAD // 4, gy, ny)
    cmask = (coarse_r[:, None] & coarse_c[None, :]).astype(jnp.float32)

    fr = jnp.arange(ext_x, dtype=jnp.int32)
    rx = (fr[None, :] // 2 == jnp.arange(coarse_x, dtype=jnp.int32)[:, None]).astype(jnp.float32)
    gcol = offsets(ext_y, cols + LANE_PAD // 2)
    near = (gcol >= -h) & (gcol < cols + h)
    target = jnp.mod(jnp.floor_divide(gcol, 2), coarse_y)
    ry = near[:, None] & (target[:, None] == jnp.arange(coarse_y, dtype=jnp.int32)[None, :])
    ry = ry.astype(jnp.float32)
    ex = (
        jnp.arange(rows, dtype=jnp.int32)[:, None] // 2
        == jnp.arange(rows // 2, dtype=jnp.int32)[None, :]
    ).astype(jnp.float32)
    ey = (
        jnp.arange(cols, dtype=jnp.int32)[None, :] // 2
        == jnp.arange(cols // 2, dtype=jnp.int32)[:, None]
    ).astype(jnp.float32)

    choose = (
        sample_seeds[:, None] == jnp.arange(perm_levels.shape[0], dtype=jnp.int32)[None, :]
    ).astype(jnp.float32)
    sample_levels = jnp.sum(choose[:, :, None] * perm_levels[None, :, :], axis=1)

    full = lambda shape: pl.BlockSpec(shape, lambda s: (0,) * len(shape))
    solution_block, correction_block = pl.pallas_call(
        smooth_kernel,
        grid=(count,),
        in_specs=[
            pl.BlockSpec(memory_space=pltpu.MemorySpace.SMEM),
            pl.BlockSpec((1, ext_x, ext_y), lambda s: (s, 0, 0)),
            pl.BlockSpec((1, ext_x, ext_y), lambda s: (count, 0, 0)),
            full((ext_x, ext_y)),
            full((coarse_x, coarse_y)),
            full((coarse_x, ext_x)),
            full((ext_y, coarse_y)),
            full((rows, rows // 2)),
            full((cols // 2, cols)),
        ],
        out_specs=[
            pl.BlockSpec((1, rows, cols), lambda s: (s, 0, 0)),
            pl.BlockSpec((1, rows // 2, cols // 2), lambda s: (s, 0, 0)),
        ],
        out_shape=[
            jax.ShapeDtypeStruct((count, rows, cols), jnp.float32),
            jax.ShapeDtypeStruct((count, rows // 2, cols // 2), jnp.float32),
        ],
    )(sample_levels, wide, wide, mask, cmask, rx, ry, ex, ey)
    return solution_block, correction_block


def solution(mesh):
    placed = (P("sa", "gx", "gy"), P("sa"), P("sa", None), P("gx", "gy"))
    return jax.shard_map(
        shards,
        mesh=mesh,
        in_specs=placed,
        out_specs=(P("sa", "gx", "gy"), P("sa", "gx", "gy")),
        check_vma=False,
    )
```

time: 247 us -> 43.5 us (0.18)
  other arithmetic: 92.9 us -> 8.14 us
  local copies, waits for them, and re-layouts: 66 us -> 0.26 us
  starting transfers between devices: 63.8 us -> 10.2 us
  Pallas kernels: 0 us -> 18.1 us
  waiting for transfers between devices: 20.7 us -> 5.64 us
    ppermute x24 -> x4, starting transfers between devices: 63.8 us -> 10.2 us  [the longest x2 5.91 us: exchange(): lax.ppermute(lax.slice_in_dim(block, block.shape[dim] - width, None, axis...]
    reduce_sum x3 -> x1, other arithmetic: 50.5 us -> 0.67 us  [shards(): jnp.sum(choose[:, :, None] * perm_levels[None, :, :], axis=1)]
    add x6 -> x0, other arithmetic: 18.4 us -> none  [the longest x3 16.8 us: shards(): current = current + DAMPING * residual / diagonal]
    pallas_call x0 -> x1, Pallas kernels: none -> 18.1 us  [shards(): pl.pallas_call(smooth_kernel, grid=(count,), in_specs=[pl.BlockSpec(memor...]
    slice x18 -> x1, local copies, waits for them, and re-layouts: 17.5 us -> 0.16 us  [exchange(): lax.slice_in_dim(block, 0, width, axis=dim)]
    ppermute x24 -> x4, waiting for transfers between devices: 20.7 us -> 5.64 us  [the longest x2 3.82 us: exchange(): lax.ppermute(lax.slice_in_dim(block, block.shape[dim] - width, None, axis...]
    ppermute x10 -> x0, local copies, waits for them, and re-layouts: 11.8 us -> none  [the longest x5 5.97 us: with_halo(): lax.ppermute(lax.slice_in_dim(block, 0, width, axis=dim), axis, backward)]
    reshape x2 -> x0, local copies, waits for them, and re-layouts: 11.8 us -> none  [the longest x1 11.5 us: restrict(): values.reshape(values.shape[0], values.shape[1] // 2, 2, values.shape[2]...]
  transfers between devices with their start and end apart: 24 -> 4, of which waited for: 11 -> 2; matrix products, arithmetic and copies ran while one was open for 31% -> 12% of each run, Pallas kernels for 0% -> 0%
where the time goes in v3:
time: 43.5 us; the launch traced here: 43.1 us
  Pallas kernels  18.1 us (42%)
  starting transfers between devices  10.2 us (23%)
  other arithmetic  8.14 us (19%)
  waiting for transfers between devices  5.64 us (13%)
  between operations  0.79 us (2%)
    pallas_call x1, Pallas kernels, shards(): pl.pallas_call(smooth_kernel, grid=(count,), in_specs=[pl.BlockSpec(memor...  18.1 us
    ppermute x2, starting transfers between devices, exchange(): lax.ppermute(lax.slice_in_dim(block, block.shape[dim] - width, None, axis...  5.91 us
    ppermute x2, starting transfers between devices, exchange(): lax.ppermute(lax.slice_in_dim(block, 0, width, axis=dim), axis, backward)  4.28 us
    ppermute x2, waiting for transfers between devices, exchange(): lax.ppermute(lax.slice_in_dim(block, block.shape[dim] - width, None, axis...  3.82 us
    ppermute x2, waiting for transfers between devices, exchange(): lax.ppermute(lax.slice_in_dim(block, 0, width, axis=dim), axis, backward)  1.82 us
    concatenate x1, other arithmetic, periodic_halo(): return jnp.concatenate([block, high, gap, low], axis=2)  1.18 us
    convert_element_type x1, other arithmetic, shards(): ry = ry.astype(jnp.float32)  0.93 us
    broadcast_in_dim x1, other arithmetic, shards(): perm_classes.astype(jnp.float32)[None]  0.91 us
  transfers between devices with their start and end apart: 4, of which 2 were waited for; matrix products, arithmetic and copies ran while one was open for 12% of the time, Pallas kernels for 0%

profile of v3, /device:TPU:18, one launch (start us, length us, event | category | flops | bytes accessed | tf_op | source)
XLA Modules:
  0.0 43.1 jit_solution(4928553127600228535)
XLA Ops:
  0.6 0.0 copy-start
  0.6 0.0 copy-start.2
  0.7 0.9 %convert_bitcast_fusion = f32[1,64,256]{2,1,0:T(8,128)S(1)} fusion(s32[64,256]{1,0:T(8,128)} %param.7), kind=kLoop, calls=%fused_computation.10 | loop fusion | flops 16384 | bytes 131072 | tf_op jit(solution)/shard_map/broadcast_in_dim | solution.py:122
  1.6 0.9 %pad_maximum_fusion.3 = (f32[9,8,256]{2,1,0:T(8,128)S(1)}, f32[9,8,256]{2,1,0:T(8,128)S(1)}) fusion(f32[1,64,256]{2,1,0:T(8,128)S(1)} %convert_bitcast_fusion, f32[8,64,256]{2,1,0:T(8,128)} %param.4), kind=kLoop, calls=%fused_computation.9 | loop fusion | flops 36864 | bytes 737280 | tf_op jit(solution)/shard_map/slice | solution.py:22
  2.4 2.4 %collective-permute-start = (f32[9,8,256]{2,1,0:T(8,128)S(1)}, f32[9,8,256]{2,1,0:T(8,128)S(1)}, u32[]{:S(2)}, u32[]{:S(2)}) collective-permute-start(f32[9,8,256]{2,1,0:T(8,128)S(1)} %get-tuple-element.4), channel_id=1, source_target_pairs={{8,0},{16,8},{24,16},{9,1},{17,9},{25,17},{10,2},{18,10},{26,18},{... | collective-permute-start | bytes 221192 | tf_op jit(solution)/shard_map/ppermute | solution.py:22
  4.8 3.5 %collective-permute-start.1 = (f32[9,8,256]{2,1,0:T(8,128)S(1)}, f32[9,8,256]{2,1,0:T(8,128)S(1)}, u32[]{:S(2)}, u32[]{:S(2)}) collective-permute-start(f32[9,8,256]{2,1,0:T(8,128)S(1)} %get-tuple-element.5), channel_id=1, source_target_pairs={{0,8},{8,16},{16,24},{1,9},{9,17},{17,25},{2,10},{10,18},{18,26},{... | collective-permute-start | bytes 221192 | tf_op jit(solution)/shard_map/ppermute | solution.py:19
  8.5 0.7 %fusion.2.ey_ref = f32[128,256]{1,0:T(8,128)} fusion(s32[256]{0:T(256)S(1)} %and_select_fusion), kind=kLoop, calls=%fused_computation.6 | loop fusion | flops 65536 | bytes 132096 | tf_op jit(solution)/shard_map/convert_element_type | solution.py:148
  9.1 0.7 %fusion.3.ex_ref = f32[64,32]{1,0:T(8,128)} fusion(s32[64]{0:T(128)S(1)} %and_select_fusion.1), kind=kLoop, calls=%fused_computation.14 | loop fusion | flops 4096 | bytes 8448 | tf_op jit(solution)/shard_map/convert_element_type | solution.py:144
  9.8 0.6 %fusion.4.rx_ref = f32[40,80]{1,0:T(8,128)} fusion(s32[80]{0:T(128)S(1)} %and_select_fusion.2), kind=kLoop, calls=%fused_computation.16 | loop fusion | flops 6400 | bytes 13120 | tf_op jit(solution)/shard_map/convert_element_type | solution.py:135
  10.4 0.7 %and_convert_fusion.mask_ref = f32[80,384]{1,0:T(8,128)} fusion(pred[384]{0:T(512)(128)(4,1)S(1)} %fusion.15, pred[80]{0:T(512)(128)(4,1)S(1)} %compare_and_fusion.2), kind=kLoop, calls=%fused_computation.7 | loop fusion | flops 61440 | bytes 123344 | tf_op jit(solution)/shard_map/convert_element_type | solution.py:129
  11.1 0.7 %and_convert_fusion.1.cmask_ref = f32[40,256]{1,0:T(8,128)} fusion(pred[256]{0:T(512)(128)(4,1)S(1)} %compare_and_fusion, pred[40]{0:T(512)(128)(4,1)S(1)} %compare_and_fusion.1), kind=kLoop, calls=%fused_computation.11 | loop fusion | flops 20480 | bytes 41256 | tf_op jit(solution)/shard_map/convert_element_type | solution.py:132
  11.8 0.9 %fusion.1.ry_ref = f32[384,256]{1,0:T(8,128)} fusion(s32[384]{0:T(512)S(1)} %add_select_fusion, pred[384]{0:T(512)(128)(4,1)S(1)} %fusion.16), kind=kLoop, calls=%fused_computation.4 | loop fusion | flops 294912 | bytes 395136 | tf_op jit(solution)/shard_map/convert_element_type | solution.py:140
  12.8 0.0 copy-done.2
  12.8 0.1 fusion.5
  12.8 0.0 collective-permute-done
  12.8 0.0 collective-permute-done.1
  12.8 0.0 copy-done
  12.8 0.1 pad_maximum_fusion.1
  12.9 0.0 copy-start.1
  12.9 0.2 fusion.18
  13.1 1.9 %collective-permute-start.2 = (f32[9,80,8]{2,1,0:T(8,128)S(1)}, f32[9,80,8]{2,1,0:T(8,128)S(1)}, u32[]{:S(2)}, u32[]{:S(2)}) collective-permute-start(f32[9,80,8]{2,1,0:T(8,128)S(1)} %get-tuple-element.2), channel_id=1, source_target_pairs={{2,0},{4,2},{6,4},{3,1},{5,3},{7,5},{10,8},{12,10},{14,12},{11,9},... | collective-permute-start | bytes 69128 | tf_op jit(solution)/shard_map/ppermute | solution.py:22
  15.0 2.4 %collective-permute-start.3 = (f32[9,80,8]{2,1,0:T(8,128)S(1)}, f32[9,80,8]{2,1,0:T(8,128)S(1)}, u32[]{:S(2)}, u32[]{:S(2)}) collective-permute-start(f32[9,80,8]{2,1,0:T(8,128)S(1)} %get-tuple-element.3), channel_id=1, source_target_pairs={{0,2},{2,4},{4,6},{1,3},{3,5},{5,7},{8,10},{10,12},{12,14},{9,11},... | collective-permute-start | bytes 69128 | tf_op jit(solution)/shard_map/ppermute | solution.py:19
  17.4 0.0 copy-done.1
  17.4 0.7 %multiply_reduce_fusion.levels_ref = f32[8,8]{1,0:T(8,128)} fusion(f32[8,8]{1,0:T(8,128)S(1)} %copy-done.1, f32[8,8]{1,0:T(8,128)S(1)} %fusion.5), kind=kLoop, calls=%fused_computation.13 | loop fusion | flops 960 | bytes 768 | tf_op jit(solution)/shard_map/reduce_sum | solution.py:153
  18.1 0.1 pad.5.clone
  18.2 1.8 %collective-permute-done.2 = f32[9,80,8]{2,1,0:T(8,128)S(1)} collective-permute-done((f32[9,80,8]{2,1,0:T(8,128)S(1)}, f32[9,80,8]{2,1,0:T(8,128)S(1)}, u32[]{:S(2)}, u32[]{:S(2)}) %collective-permute-start.2) | collective-permute-done | bytes 23072 | tf_op jit(solution)/shard_map/ppermute | solution.py:22
  20.0 3.8 %collective-permute-done.3 = f32[9,80,8]{2,1,0:T(8,128)S(1)} collective-permute-done((f32[9,80,8]{2,1,0:T(8,128)S(1)}, f32[9,80,8]{2,1,0:T(8,128)S(1)}, u32[]{:S(2)}, u32[]{:S(2)}) %collective-permute-start.3) | collective-permute-done | bytes 23072 | tf_op jit(solution)/shard_map/ppermute | solution.py:19
  23.8 1.2 %pad_maximum_fusion.src_ref.cls_ref = f32[9,80,384]{2,1,0:T(8,128)} fusion(f32[9,80,8]{2,1,0:T(8,128)S(1)} %collective-permute-done.3, f32[9,80,8]{2,1,0:T(8,128)S(1)} %collective-permute-done.2, f32[9,8,256]{2,1,0:T(8,128)S(1)} %collective-permute-done.1, f32[9,8,256]{2,1,0:T(8,128)S(1)} %collective-permute-done, f32[1,64,256]{2,1,0:T(8,128)S(1)} %convert_bitcast_fusion, ...), kind=kLoop, calls=%fused_computation | loop fusion | flops 1658880 | bytes 1890816 | tf_op jit(solution)/shard_map/concatenate | solution.py:31
  25.0 18.1 %shard_map.59 = (f32[8,64,256]{2,1,0:T(8,128)}, f32[8,32,128]{2,1,0:T(8,128)}) custom-call(f32[8,8]{1,0:T(8,128)} %multiply_reduce_fusion.levels_ref, f32[9,80,384]{2,1,0:T(8,128)} %pad_maximum_fusion.src_ref.cls_ref, f32[9,80,384]{2,1,0:T(8,128)} %pad_maximum_fusion.src_ref.cls_ref, f32[80,384]{1,0:T(8,128)} %and_convert_fusion.mask_ref, ...), custom_call_target="tpu_custom_call" | custom-call | tf_op jit(solution)/shard_map/pallas_call | solution.py:156
  (10 shorter events, 0.1 us)
Async XLA Ops:
  0.6 12.2 %copy-start = (f32[8,64,256]{2,1,0:T(8,128)S(1)}, f32[8,64,256]{2,1,0:T(8,128)}, u32[]{:S(2)}) copy-start(f32[8,64,256]{2,1,0:T(8,128)} %param.4) | copy-start | bytes 1572868
  0.6 12.1 %copy-start.2 = (s32[8]{0:T(128)S(1)}, s32[8]{0:T(128)}, u32[]{:S(2)}) copy-start(s32[8]{0:T(128)} %param.5) | copy-start | bytes 100
  2.4 10.4 %collective-permute-start = (f32[9,8,256]{2,1,0:T(8,128)S(1)}, f32[9,8,256]{2,1,0:T(8,128)S(1)}, u32[]{:S(2)}, u32[]{:S(2)}) collective-permute-start(f32[9,8,256]{2,1,0:T(8,128)S(1)} %get-tuple-element.4), channel_id=1, source_target_pairs={{8,0},{16,8},{24,16},{9,1},{17,9},{25,17},{10,2},{18,10},{26,18},{... | collective-permute-start | bytes 221192 | tf_op jit(solution)/shard_map/ppermute | solution.py:22
  4.8 8.0 %collective-permute-start.1 = (f32[9,8,256]{2,1,0:T(8,128)S(1)}, f32[9,8,256]{2,1,0:T(8,128)S(1)}, u32[]{:S(2)}, u32[]{:S(2)}) collective-permute-start(f32[9,8,256]{2,1,0:T(8,128)S(1)} %get-tuple-element.5), channel_id=1, source_target_pairs={{0,8},{8,16},{16,24},{1,9},{9,17},{17,25},{2,10},{10,18},{18,26},{... | collective-permute-start | bytes 221192 | tf_op jit(solution)/shard_map/ppermute | solution.py:19
  12.9 4.5 %copy-start.1 = (f32[8,8]{1,0:T(8,128)S(1)}, f32[8,8]{1,0:T(8,128)}, u32[]{:S(2)}) copy-start(f32[8,8]{1,0:T(8,128)} %param.6) | copy-start | bytes 772
  13.1 6.9 %collective-permute-start.2 = (f32[9,80,8]{2,1,0:T(8,128)S(1)}, f32[9,80,8]{2,1,0:T(8,128)S(1)}, u32[]{:S(2)}, u32[]{:S(2)}) collective-permute-start(f32[9,80,8]{2,1,0:T(8,128)S(1)} %get-tuple-element.2), channel_id=1, source_target_pairs={{2,0},{4,2},{6,4},{3,1},{5,3},{7,5},{10,8},{12,10},{14,12},{11,9},... | collective-permute-start | bytes 69128 | tf_op jit(solution)/shard_map/ppermute | solution.py:22
  15.0 8.8 %collective-permute-start.3 = (f32[9,80,8]{2,1,0:T(8,128)S(1)}, f32[9,80,8]{2,1,0:T(8,128)S(1)}, u32[]{:S(2)}, u32[]{:S(2)}) collective-permute-start(f32[9,80,8]{2,1,0:T(8,128)S(1)} %get-tuple-element.3), channel_id=1, source_target_pairs={{0,2},{2,4},{4,6},{1,3},{3,5},{5,7},{8,10},{10,12},{12,14},{9,11},... | collective-permute-start | bytes 69128 | tf_op jit(solution)/shard_map/ppermute | solution.py:19

commit v4 on v3

v4 whole, which is shorter than its diff:
```python
import jax
import jax.numpy as jnp
from jax import lax
from jax.experimental import pallas as pl
from jax.experimental.pallas import tpu as pltpu
from jax.sharding import PartitionSpec as P

SWEEPS = 4
DAMPING = 0.8
HALO = 8
LANE_PAD = 128
HI = lax.Precision.HIGHEST


def exchange(block, axis, dim, width):
    count = lax.axis_size(axis)
    forward = [(i, i + 1) for i in range(count - 1)]
    backward = [(target, source) for source, target in forward]
    low = lax.ppermute(
        lax.slice_in_dim(block, block.shape[dim] - width, None, axis=dim), axis, forward
    )
    high = lax.ppermute(lax.slice_in_dim(block, 0, width, axis=dim), axis, backward)
    return low, high


def periodic_halo(block, width):
    low, high = exchange(block, "gx", 1, width)
    block = jnp.concatenate([block, high, low], axis=1)
    low, high = exchange(block, "gy", 2, width)
    gap = jnp.zeros(block.shape[:2] + (LANE_PAD - 2 * width,), block.dtype)
    return jnp.concatenate([block, high, gap, low], axis=2)


def rolled(v, step):
    rows, cols = v.shape
    return (
        pltpu.roll(v, rows - step, 0),
        pltpu.roll(v, step, 0),
        pltpu.roll(v, cols - step, 1),
        pltpu.roll(v, step, 1),
    )


def couplings(perm, step):
    down, up, right, left = rolled(perm, step)
    rows, cols = perm.shape
    twice = 2.0 * perm
    south = twice * down / (perm + down)
    east = twice * right / (perm + right)
    linkage = (
        jnp.where(down > 0.0, south, twice),
        jnp.where(up > 0.0, pltpu.roll(south, step, 0), twice),
        jnp.where(right > 0.0, east, twice),
        jnp.where(left > 0.0, pltpu.roll(east, step, 1), twice),
    )
    diagonal = linkage[0] + linkage[1] + linkage[2] + linkage[3]
    return linkage, diagonal


def operator(linkage, diagonal, current, step):
    beside_all = rolled(current, step)
    return diagonal * current - (
        linkage[0] * beside_all[0]
        + linkage[1] * beside_all[1]
        + linkage[2] * beside_all[2]
        + linkage[3] * beside_all[3]
    )


def smooth_kernel(levels_ref, src_ref, cls_ref, mask_ref, cmask_ref, sy_ref, sol_ref, corr_ref, spare):
    s = pl.program_id(0)
    classes = cls_ref[0]
    valid = mask_ref[...] > 0.5
    ext_x, ext_y = classes.shape
    perm = jnp.zeros(classes.shape, jnp.float32)
    for category in range(levels_ref.shape[1]):
        perm = perm + jnp.where(classes == float(category), levels_ref[s, category], 0.0)
    perm = jnp.where(valid, perm, 0.0)
    source = src_ref[0]
    linkage, diagonal = couplings(perm, 1)
    inverse = 1.0 / jnp.where(valid, diagonal, 1.0)
    current = (DAMPING * source) * inverse
    for sweep_index in range(SWEEPS):
        residual = source - operator(linkage, diagonal, current, 1)
        if sweep_index + 1 < SWEEPS:
            current = current + (DAMPING * residual) * inverse
    pairs = residual + pltpu.roll(residual, ext_x - 1, 0)
    coarse_rhs = pairs + pltpu.roll(pairs, ext_y - 1, 1)
    pairs = perm + pltpu.roll(perm, ext_x - 1, 0)
    coarse_perm = 0.25 * (pairs + pltpu.roll(pairs, ext_y - 1, 1))
    coarse_valid = cmask_ref[...] > 0.5
    coarse_links, coarse_diagonal = couplings(coarse_perm, 2)
    coarse_inverse = 1.0 / jnp.where(coarse_valid, coarse_diagonal, 1.0)
    first = (DAMPING * coarse_rhs) * coarse_inverse
    correction = first + (
        DAMPING * (coarse_rhs - operator(coarse_links, coarse_diagonal, first, 2))
    ) * coarse_inverse
    rows, cols = sol_ref.shape[1], sol_ref.shape[2]
    odd_row = (lax.broadcasted_iota(jnp.int32, classes.shape, 0) & 1) == 1
    odd_col = (lax.broadcasted_iota(jnp.int32, classes.shape, 1) & 1) == 1
    spread = jnp.where(odd_row, pltpu.roll(correction, 1, 0), correction)
    spread = jnp.where(odd_col, pltpu.roll(spread, 1, 1), spread)
    sol_ref[0] = current[:rows, :cols] + spread[:rows, :cols]
    pieces = []
    for k in range(cols // 128):
        spare[k] = correction[:, k * 128 : (k + 1) * 128]
        pieces.append(spare[k, pl.ds(0, rows // 2, stride=2), :])
    even_rows = jnp.concatenate(pieces, axis=1)
    corr_ref[0] = jnp.dot(even_rows, sy_ref[...], precision=HI, preferred_element_type=jnp.float32)


def offsets(n, wrap_at):
    f = jnp.arange(n, dtype=jnp.int32)
    return jnp.where(f < wrap_at, f, f - n)


def region(n, own, halo, wrap_at, index, count):
    g = offsets(n, wrap_at)
    near = (g >= -halo) & (g < own + halo)
    glob = g + index * own
    return near & (glob >= 0) & (glob < count * own)


def shards(source, sample_seeds, perm_levels, perm_classes):
    h = HALO
    count, rows, cols = source.shape
    ext_x, ext_y = rows + 2 * h, cols + LANE_PAD
    stacked = jnp.concatenate([source, perm_classes.astype(jnp.float32)[None]], axis=0)
    wide = periodic_halo(stacked, h)

    gx, gy = lax.axis_index("gx"), lax.axis_index("gy")
    nx, ny = lax.axis_size("gx"), lax.axis_size("gy")
    fine_r = region(ext_x, rows, h, rows + h, gx, nx)
    fine_c = region(ext_y, cols, h, cols + LANE_PAD // 2, gy, ny)
    mask = (fine_r[:, None] & fine_c[None, :]).astype(jnp.float32)
    fr = jnp.arange(ext_x, dtype=jnp.int32)
    fc = jnp.arange(ext_y, dtype=jnp.int32)
    even = ((fr[:, None] & 1) == 0) & ((fc[None, :] & 1) == 0)
    cmask = ((fine_r[:, None] & fine_c[None, :]) & even).astype(jnp.float32)
    sy = (fc[:cols, None] == 2 * jnp.arange(cols // 2, dtype=jnp.int32)[None, :]).astype(jnp.float32)

    choose = (
        sample_seeds[:, None] == jnp.arange(perm_levels.shape[0], dtype=jnp.int32)[None, :]
    ).astype(jnp.float32)
    sample_levels = jnp.sum(choose[:, :, None] * perm_levels[None, :, :], axis=1)

    full = lambda shape: pl.BlockSpec(shape, lambda s: (0,) * len(shape))
    solution_block, correction_block = pl.pallas_call(
        smooth_kernel,
        grid=(count,),
        in_specs=[
            pl.BlockSpec(memory_space=pltpu.MemorySpace.SMEM),
            pl.BlockSpec((1, ext_x, ext_y), lambda s: (s, 0, 0)),
            pl.BlockSpec((1, ext_x, ext_y), lambda s: (count, 0, 0)),
            full((ext_x, ext_y)),
            full((ext_x, ext_y)),
            full((cols, cols // 2)),
        ],
        out_specs=[
            pl.BlockSpec((1, rows, cols), lambda s: (s, 0, 0)),
            pl.BlockSpec((1, rows // 2, cols // 2), lambda s: (s, 0, 0)),
        ],
        out_shape=[
            jax.ShapeDtypeStruct((count, rows, cols), jnp.float32),
            jax.ShapeDtypeStruct((count, rows // 2, cols // 2), jnp.float32),
        ],
        scratch_shapes=[pltpu.VMEM((cols // 128, ext_x, 128), jnp.float32)],
    )(sample_levels, wide, wide, mask, cmask, sy)
    return solution_block, correction_block


def solution(mesh):
    placed = (P("sa", "gx", "gy"), P("sa"), P("sa", None), P("gx", "gy"))
    return jax.shard_map(
        shards,
        mesh=mesh,
        in_specs=placed,
        out_specs=(P("sa", "gx", "gy"), P("sa", "gx", "gy")),
        check_vma=False,
    )
```

time: 43.5 us -> 35.5 us (0.82)
  Pallas kernels: 18.1 us -> 12 us
  other arithmetic: 8.14 us -> 5.35 us
  waiting for transfers between devices: 5.64 us -> 6.68 us
    pallas_call x1, Pallas kernels: 18.1 us -> 12 us  [shards(): pl.pallas_call(smooth_kernel, grid=(count,), in_specs=[pl.BlockSpec(memor...]
    convert_element_type x6 -> x2, other arithmetic: 4.29 us -> 1.55 us  [the longest x1 0.8 us: shards(): cmask = (fine_r[:, None] & fine_c[None, :] & even).astype(jnp.float32)]
    ppermute x2, waiting for transfers between devices: 3.82 us -> 4.87 us  [exchange(): lax.ppermute(lax.slice_in_dim(block, block.shape[dim] - width, None, axis...]
  transfers between devices with their start and end apart: 4 -> 4, of which waited for: 2 -> 3; matrix products, arithmetic and copies ran while one was open for 12% -> 7% of each run, Pallas kernels for 0% -> 0%
where the time goes in v4:
time: 35.5 us; the launch traced here: 35.2 us
  Pallas kernels  12 us (34%)
  starting transfers between devices  10.2 us (29%)
  waiting for transfers between devices  6.68 us (19%)
  other arithmetic  5.35 us (15%)
  between operations  0.76 us (2%)
    pallas_call x1, Pallas kernels, shards(): pl.pallas_call(smooth_kernel, grid=(count,), in_specs=[pl.BlockSpec(memor...  12 us
    ppermute x2, starting transfers between devices, exchange(): lax.ppermute(lax.slice_in_dim(block, block.shape[dim] - width, None, axis...  5.91 us
    ppermute x2, waiting for transfers between devices, exchange(): lax.ppermute(lax.slice_in_dim(block, block.shape[dim] - width, None, axis...  4.87 us
    ppermute x2, starting transfers between devices, exchange(): lax.ppermute(lax.slice_in_dim(block, 0, width, axis=dim), axis, backward)  4.28 us
    ppermute x2, waiting for transfers between devices, exchange(): lax.ppermute(lax.slice_in_dim(block, 0, width, axis=dim), axis, backward)  1.81 us
    concatenate x1, other arithmetic, periodic_halo(): return jnp.concatenate([block, high, gap, low], axis=2)  1.18 us
    broadcast_in_dim x1, other arithmetic, shards(): perm_classes.astype(jnp.float32)[None]  0.91 us
    slice x1, other arithmetic, exchange(): lax.slice_in_dim(block, 0, width, axis=dim)  0.88 us
  transfers between devices with their start and end apart: 4, of which 3 were waited for; matrix products, arithmetic and copies ran while one was open for 7% of the time, Pallas kernels for 0%

profile of v4, /device:TPU:18, one launch (start us, length us, event | category | flops | bytes accessed | tf_op | source)
XLA Modules:
  0.0 35.2 jit_solution(17418692703558607805)
XLA Ops:
  0.6 0.0 copy-start
  0.6 0.0 copy-start.2
  0.7 0.9 %convert_bitcast_fusion = f32[1,64,256]{2,1,0:T(8,128)S(1)} fusion(s32[64,256]{1,0:T(8,128)} %param.7), kind=kLoop, calls=%fused_computation.8 | loop fusion | flops 16384 | bytes 131072 | tf_op jit(solution)/shard_map/broadcast_in_dim | solution.py:128
  1.6 0.9 %pad_maximum_fusion.3 = (f32[9,8,256]{2,1,0:T(8,128)S(1)}, f32[9,8,256]{2,1,0:T(8,128)S(1)}) fusion(f32[1,64,256]{2,1,0:T(8,128)S(1)} %convert_bitcast_fusion, f32[8,64,256]{2,1,0:T(8,128)} %param.4), kind=kLoop, calls=%fused_computation.7 | loop fusion | flops 36864 | bytes 737280 | tf_op jit(solution)/shard_map/slice | solution.py:22
  2.4 2.4 %collective-permute-start = (f32[9,8,256]{2,1,0:T(8,128)S(1)}, f32[9,8,256]{2,1,0:T(8,128)S(1)}, u32[]{:S(2)}, u32[]{:S(2)}) collective-permute-start(f32[9,8,256]{2,1,0:T(8,128)S(1)} %get-tuple-element.4), channel_id=1, source_target_pairs={{8,0},{16,8},{24,16},{9,1},{17,9},{25,17},{10,2},{18,10},{26,18},{... | collective-permute-start | bytes 221192 | tf_op jit(solution)/shard_map/ppermute | solution.py:22
  4.8 3.5 %collective-permute-start.1 = (f32[9,8,256]{2,1,0:T(8,128)S(1)}, f32[9,8,256]{2,1,0:T(8,128)S(1)}, u32[]{:S(2)}, u32[]{:S(2)}) collective-permute-start(f32[9,8,256]{2,1,0:T(8,128)S(1)} %get-tuple-element.5), channel_id=1, source_target_pairs={{0,8},{8,16},{16,24},{1,9},{9,17},{17,25},{2,10},{10,18},{18,26},{... | collective-permute-start | bytes 221192 | tf_op jit(solution)/shard_map/ppermute | solution.py:19
  8.4 0.7 %compare_convert_fusion.sy_ref = f32[256,128]{1,0:T(8,128)} fusion(s32[128]{0:T(128)S(1)} %iota_multiply_fusion, s32[256]{0:T(256)S(1)} %slice.19), kind=kLoop, calls=%fused_computation.4 | loop fusion | flops 65536 | bytes 132608 | tf_op jit(solution)/shard_map/convert_element_type | solution.py:140
  9.1 0.8 %fusion = (f32[80,384]{1,0:T(8,128)}, f32[80,384]{1,0:T(8,128)}) fusion(pred[384]{0:T(512)(128)(4,1)S(1)} %get-tuple-element.8, pred[384]{0:T(512)(128)(4,1)S(1)} %get-tuple-element.9, pred[80]{0:T(512)(128)(4,1)S(1)} %get-tuple-element.11, pred[80]{0:T(512)(128)(4,1)S(1)} %get-tuple-element.10), kind=kLoop, calls=%fused_computation.5 | loop fusion | flops 153600 | bytes 246688 | tf_op jit(solution)/shard_map/convert_element_type | solution.py:139
  9.9 0.0 copy-done.2
  9.9 0.1 fusion.1
  10.0 0.0 collective-permute-done
  10.0 1.0 %collective-permute-done.1 = f32[9,8,256]{2,1,0:T(8,128)S(1)} collective-permute-done((f32[9,8,256]{2,1,0:T(8,128)S(1)}, f32[9,8,256]{2,1,0:T(8,128)S(1)}, u32[]{:S(2)}, u32[]{:S(2)}) %collective-permute-start.1) | collective-permute-done | bytes 73760 | tf_op jit(solution)/shard_map/ppermute | solution.py:19
  11.1 0.0 copy-done
  11.1 0.1 pad_maximum_fusion.1
  11.1 0.0 copy-start.1
  11.1 0.2 fusion.10
  11.3 1.9 %collective-permute-start.2 = (f32[9,80,8]{2,1,0:T(8,128)S(1)}, f32[9,80,8]{2,1,0:T(8,128)S(1)}, u32[]{:S(2)}, u32[]{:S(2)}) collective-permute-start(f32[9,80,8]{2,1,0:T(8,128)S(1)} %get-tuple-element.2), channel_id=1, source_target_pairs={{2,0},{4,2},{6,4},{3,1},{5,3},{7,5},{10,8},{12,10},{14,12},{11,9},... | collective-permute-start | bytes 69128 | tf_op jit(solution)/shard_map/ppermute | solution.py:22
  13.2 2.4 %collective-permute-start.3 = (f32[9,80,8]{2,1,0:T(8,128)S(1)}, f32[9,80,8]{2,1,0:T(8,128)S(1)}, u32[]{:S(2)}, u32[]{:S(2)}) collective-permute-start(f32[9,80,8]{2,1,0:T(8,128)S(1)} %get-tuple-element.3), channel_id=1, source_target_pairs={{0,2},{2,4},{4,6},{1,3},{3,5},{5,7},{8,10},{10,12},{12,14},{9,11},... | collective-permute-start | bytes 69128 | tf_op jit(solution)/shard_map/ppermute | solution.py:19
  15.7 0.0 copy-done.1
  15.7 0.7 %multiply_reduce_fusion.levels_ref = f32[8,8]{1,0:T(8,128)} fusion(f32[8,8]{1,0:T(8,128)S(1)} %copy-done.1, f32[8,8]{1,0:T(8,128)S(1)} %fusion.1), kind=kLoop, calls=%fused_computation.9 | loop fusion | flops 960 | bytes 768 | tf_op jit(solution)/shard_map/reduce_sum | solution.py:145
  16.3 0.1 pad.5.clone
  16.4 1.8 %collective-permute-done.2 = f32[9,80,8]{2,1,0:T(8,128)S(1)} collective-permute-done((f32[9,80,8]{2,1,0:T(8,128)S(1)}, f32[9,80,8]{2,1,0:T(8,128)S(1)}, u32[]{:S(2)}, u32[]{:S(2)}) %collective-permute-start.2) | collective-permute-done | bytes 23072 | tf_op jit(solution)/shard_map/ppermute | solution.py:22
  18.2 3.8 %collective-permute-done.3 = f32[9,80,8]{2,1,0:T(8,128)S(1)} collective-permute-done((f32[9,80,8]{2,1,0:T(8,128)S(1)}, f32[9,80,8]{2,1,0:T(8,128)S(1)}, u32[]{:S(2)}, u32[]{:S(2)}) %collective-permute-start.3) | collective-permute-done | bytes 23072 | tf_op jit(solution)/shard_map/ppermute | solution.py:19
  22.1 1.2 %pad_maximum_fusion.src_ref.cls_ref = f32[9,80,384]{2,1,0:T(8,128)} fusion(f32[9,80,8]{2,1,0:T(8,128)S(1)} %collective-permute-done.3, f32[9,80,8]{2,1,0:T(8,128)S(1)} %collective-permute-done.2, f32[9,8,256]{2,1,0:T(8,128)S(1)} %collective-permute-done.1, f32[9,8,256]{2,1,0:T(8,128)S(1)} %collective-permute-done, f32[1,64,256]{2,1,0:T(8,128)S(1)} %convert_bitcast_fusion, ...), kind=kLoop, calls=%fused_computation | loop fusion | flops 1658880 | bytes 1890816 | tf_op jit(solution)/shard_map/concatenate | solution.py:31
  23.2 12.0 %shard_map.59 = (f32[8,64,256]{2,1,0:T(8,128)}, f32[8,32,128]{2,1,0:T(8,128)}) custom-call(f32[8,8]{1,0:T(8,128)} %multiply_reduce_fusion.levels_ref, f32[9,80,384]{2,1,0:T(8,128)} %pad_maximum_fusion.src_ref.cls_ref, f32[9,80,384]{2,1,0:T(8,128)} %pad_maximum_fusion.src_ref.cls_ref, f32[80,384]{1,0:T(8,128)} %get-tuple-element.7.mask_ref, ...), custom_call_target="tpu_custom_call" | custom-call | tf_op jit(solution)/shard_map/pallas_call | solution.py:148
  (6 shorter events, 0.0 us)
Async XLA Ops:
  0.6 10.4 %copy-start = (f32[8,64,256]{2,1,0:T(8,128)S(1)}, f32[8,64,256]{2,1,0:T(8,128)}, u32[]{:S(2)}) copy-start(f32[8,64,256]{2,1,0:T(8,128)} %param.4) | copy-start | bytes 1572868
  0.6 9.3 %copy-start.2 = (s32[8]{0:T(128)S(1)}, s32[8]{0:T(128)}, u32[]{:S(2)}) copy-start(s32[8]{0:T(128)} %param.5) | copy-start | bytes 100
  2.4 7.6 %collective-permute-start = (f32[9,8,256]{2,1,0:T(8,128)S(1)}, f32[9,8,256]{2,1,0:T(8,128)S(1)}, u32[]{:S(2)}, u32[]{:S(2)}) collective-permute-start(f32[9,8,256]{2,1,0:T(8,128)S(1)} %get-tuple-element.4), channel_id=1, source_target_pairs={{8,0},{16,8},{24,16},{9,1},{17,9},{25,17},{10,2},{18,10},{26,18},{... | collective-permute-start | bytes 221192 | tf_op jit(solution)/shard_map/ppermute | solution.py:22
  4.8 6.2 %collective-permute-start.1 = (f32[9,8,256]{2,1,0:T(8,128)S(1)}, f32[9,8,256]{2,1,0:T(8,128)S(1)}, u32[]{:S(2)}, u32[]{:S(2)}) collective-permute-start(f32[9,8,256]{2,1,0:T(8,128)S(1)} %get-tuple-element.5), channel_id=1, source_target_pairs={{0,8},{8,16},{16,24},{1,9},{9,17},{17,25},{2,10},{10,18},{18,26},{... | collective-permute-start | bytes 221192 | tf_op jit(solution)/shard_map/ppermute | solution.py:19
  11.1 4.5 %copy-start.1 = (f32[8,8]{1,0:T(8,128)S(1)}, f32[8,8]{1,0:T(8,128)}, u32[]{:S(2)}) copy-start(f32[8,8]{1,0:T(8,128)} %param.6) | copy-start | bytes 772
  11.3 6.9 %collective-permute-start.2 = (f32[9,80,8]{2,1,0:T(8,128)S(1)}, f32[9,80,8]{2,1,0:T(8,128)S(1)}, u32[]{:S(2)}, u32[]{:S(2)}) collective-permute-start(f32[9,80,8]{2,1,0:T(8,128)S(1)} %get-tuple-element.2), channel_id=1, source_target_pairs={{2,0},{4,2},{6,4},{3,1},{5,3},{7,5},{10,8},{12,10},{14,12},{11,9},... | collective-permute-start | bytes 69128 | tf_op jit(solution)/shard_map/ppermute | solution.py:22
  13.2 8.8 %collective-permute-start.3 = (f32[9,80,8]{2,1,0:T(8,128)S(1)}, f32[9,80,8]{2,1,0:T(8,128)S(1)}, u32[]{:S(2)}, u32[]{:S(2)}) collective-permute-start(f32[9,80,8]{2,1,0:T(8,128)S(1)} %get-tuple-element.3), channel_id=1, source_target_pairs={{0,2},{2,4},{4,6},{1,3},{3,5},{5,7},{8,10},{10,12},{12,14},{9,11},... | collective-permute-start | bytes 69128 | tf_op jit(solution)/shard_map/ppermute | solution.py:19

commit v5 on v4

v5 whole, which is shorter than its diff:
```python
import jax
import jax.numpy as jnp
from jax import lax
from jax.experimental import pallas as pl
from jax.experimental.pallas import tpu as pltpu
from jax.sharding import PartitionSpec as P

SWEEPS = 4
DAMPING = 0.8
HALO = 8
LANE_PAD = 128
HI = lax.Precision.HIGHEST


def halo_pieces(source, classes, width):
    stack = lambda a, b: jnp.concatenate([a, b[None]], axis=0)
    low = lax.ppermute(
        stack(source[:, -width:, :], classes[-width:, :]), "gx",
        [(i, i + 1) for i in range(lax.axis_size("gx") - 1)],
    )
    high = lax.ppermute(
        stack(source[:, :width, :], classes[:width, :]), "gx",
        [(i + 1, i) for i in range(lax.axis_size("gx") - 1)],
    )
    rows_halo = jnp.concatenate([high, low], axis=1)
    last = jnp.concatenate([stack(source[:, :, -width:], classes[:, -width:]), rows_halo[:, :, -width:]], axis=1)
    first = jnp.concatenate([stack(source[:, :, :width], classes[:, :width]), rows_halo[:, :, :width]], axis=1)
    low = lax.ppermute(last, "gy", [(i, i + 1) for i in range(lax.axis_size("gy") - 1)])
    high = lax.ppermute(first, "gy", [(i + 1, i) for i in range(lax.axis_size("gy") - 1)])
    gap = jnp.zeros(high.shape[:2] + (LANE_PAD - 2 * width,), high.dtype)
    return rows_halo, jnp.concatenate([high, gap, low], axis=2)


def rolled(v, step):
    rows, cols = v.shape
    return (
        pltpu.roll(v, rows - step, 0),
        pltpu.roll(v, step, 0),
        pltpu.roll(v, cols - step, 1),
        pltpu.roll(v, step, 1),
    )


def couplings(perm, step):
    down, up, right, left = rolled(perm, step)
    rows, cols = perm.shape
    twice = 2.0 * perm
    south = twice * down / (perm + down)
    east = twice * right / (perm + right)
    linkage = (
        jnp.where(down > 0.0, south, twice),
        jnp.where(up > 0.0, pltpu.roll(south, step, 0), twice),
        jnp.where(right > 0.0, east, twice),
        jnp.where(left > 0.0, pltpu.roll(east, step, 1), twice),
    )
    diagonal = linkage[0] + linkage[1] + linkage[2] + linkage[3]
    return linkage, diagonal


def operator(linkage, diagonal, current, step):
    beside_all = rolled(current, step)
    return diagonal * current - (
        linkage[0] * beside_all[0]
        + linkage[1] * beside_all[1]
        + linkage[2] * beside_all[2]
        + linkage[3] * beside_all[3]
    )


def inside(shape, own_x, own_y, place_ref):
    ext_x, ext_y = shape
    r = lax.broadcasted_iota(jnp.int32, shape, 0)
    c = lax.broadcasted_iota(jnp.int32, shape, 1)
    g_r = jnp.where(r < own_x + HALO, r, r - ext_x)
    g_c = jnp.where(c < own_y + LANE_PAD // 2, c, c - ext_y)
    glob_r = g_r + place_ref[0] * own_x
    glob_c = g_c + place_ref[1] * own_y
    near = (g_c >= -HALO) & (g_c < own_y + HALO)
    return (
        near
        & (glob_r >= 0) & (glob_r < place_ref[2] * own_x)
        & (glob_c >= 0) & (glob_c < place_ref[3] * own_y)
    ), r, c


def smooth_kernel(
    levels_ref, place_ref, src_ref, cls_ref, rows_ref, crows_ref, tile_ref, ctile_ref,
    sol_ref, corr_ref, source_ext, classes_ext, mask_ext, cmask_ext, spare,
):
    s = pl.program_id(0)
    rows, cols = sol_ref.shape[1], sol_ref.shape[2]
    ext_x, ext_y = source_ext.shape

    @pl.when(s == 0)
    def _():
        valid, r, c = inside((ext_x, ext_y), rows, cols, place_ref)
        even = ((r & 1) == 0) & ((c & 1) == 0)
        mask_ext[...] = valid.astype(jnp.float32)
        cmask_ext[...] = (valid & even).astype(jnp.float32)
        classes_ext[:rows, :cols] = cls_ref[...]
        classes_ext[rows:, :cols] = crows_ref[0].astype(jnp.int32)
        classes_ext[:, cols:] = ctile_ref[0].astype(jnp.int32)

    source_ext[:rows, :cols] = src_ref[0]
    source_ext[rows:, :cols] = rows_ref[0]
    source_ext[:, cols:] = tile_ref[0]
    source = source_ext[...]
    classes = classes_ext[...]
    valid = mask_ext[...] > 0.5
    level = [levels_ref[s, category] for category in range(levels_ref.shape[1])]
    bit0 = (classes & 1) != 0
    bit1 = (classes & 2) != 0
    bit2 = (classes & 4) != 0
    low = jnp.where(bit1, jnp.where(bit0, level[3], level[2]), jnp.where(bit0, level[1], level[0]))
    high = jnp.where(bit1, jnp.where(bit0, level[7], level[6]), jnp.where(bit0, level[5], level[4]))
    perm = jnp.where(valid, jnp.where(bit2, high, low), 0.0)
    linkage, diagonal = couplings(perm, 1)
    inverse = 1.0 / jnp.where(valid, diagonal, 1.0)
    current = (DAMPING * source) * inverse
    for sweep_index in range(SWEEPS):
        residual = source - operator(linkage, diagonal, current, 1)
        if sweep_index + 1 < SWEEPS:
            current = current + (DAMPING * residual) * inverse
    pairs = residual + pltpu.roll(residual, ext_x - 1, 0)
    coarse_rhs = pairs + pltpu.roll(pairs, ext_y - 1, 1)
    pairs = perm + pltpu.roll(perm, ext_x - 1, 0)
    coarse_perm = 0.25 * (pairs + pltpu.roll(pairs, ext_y - 1, 1))
    coarse_valid = cmask_ext[...] > 0.5
    coarse_links, coarse_diagonal = couplings(coarse_perm, 2)
    coarse_inverse = 1.0 / jnp.where(coarse_valid, coarse_diagonal, 1.0)
    first = (DAMPING * coarse_rhs) * coarse_inverse
    correction = first + (
        DAMPING * (coarse_rhs - operator(coarse_links, coarse_diagonal, first, 2))
    ) * coarse_inverse
    odd_row = (lax.broadcasted_iota(jnp.int32, (ext_x, ext_y), 0) & 1) == 1
    odd_col = (lax.broadcasted_iota(jnp.int32, (ext_x, ext_y), 1) & 1) == 1
    spread = jnp.where(odd_row, pltpu.roll(correction, 1, 0), correction)
    spread = jnp.where(odd_col, pltpu.roll(spread, 1, 1), spread)
    sol_ref[0] = current[:rows, :cols] + spread[:rows, :cols]
    pieces = []
    for k in range(cols // 128):
        spare[k] = correction[:, k * 128 : (k + 1) * 128]
        pieces.append(spare[k, pl.ds(0, rows // 2, stride=2), :])
    even_rows = jnp.concatenate(pieces, axis=1)
    pick = (
        lax.broadcasted_iota(jnp.int32, (cols, cols // 2), 0)
        == 2 * lax.broadcasted_iota(jnp.int32, (cols, cols // 2), 1)
    ).astype(jnp.float32)
    corr_ref[0] = jnp.dot(even_rows, pick, precision=HI, preferred_element_type=jnp.float32)


def shards(source, sample_seeds, perm_levels, perm_classes):
    h = HALO
    count, rows, cols = source.shape
    ext_x, ext_y = rows + 2 * h, cols + LANE_PAD
    rows_halo, lane_tile = halo_pieces(source, perm_classes.astype(jnp.float32), h)
    place = jnp.stack(
        [lax.axis_index("gx"), lax.axis_index("gy"), lax.axis_size("gx"), lax.axis_size("gy")]
    ).astype(jnp.int32)
    choose = (
        sample_seeds[:, None] == jnp.arange(perm_levels.shape[0], dtype=jnp.int32)[None, :]
    ).astype(jnp.float32)
    sample_levels = jnp.sum(choose[:, :, None] * perm_levels[None, :, :], axis=1)

    smem = pl.BlockSpec(memory_space=pltpu.MemorySpace.SMEM)
    solution_block, correction_block = pl.pallas_call(
        smooth_kernel,
        grid=(count,),
        in_specs=[
            smem,
            smem,
            pl.BlockSpec((1, rows, cols), lambda s: (s, 0, 0)),
            pl.BlockSpec((rows, cols), lambda s: (0, 0)),
            pl.BlockSpec((1, 2 * h, cols), lambda s: (s, 0, 0)),
            pl.BlockSpec((1, 2 * h, cols), lambda s: (count, 0, 0)),
            pl.BlockSpec((1, ext_x, LANE_PAD), lambda s: (s, 0, 0)),
            pl.BlockSpec((1, ext_x, LANE_PAD), lambda s: (count, 0, 0)),
        ],
        out_specs=[
            pl.BlockSpec((1, rows, cols), lambda s: (s, 0, 0)),
            pl.BlockSpec((1, rows // 2, cols // 2), lambda s: (s, 0, 0)),
        ],
        out_shape=[
            jax.ShapeDtypeStruct((count, rows, cols), jnp.float32),
            jax.ShapeDtypeStruct((count, rows // 2, cols // 2), jnp.float32),
        ],
        scratch_shapes=[
            pltpu.VMEM((ext_x, ext_y), jnp.float32),
            pltpu.VMEM((ext_x, ext_y), jnp.int32),
            pltpu.VMEM((ext_x, ext_y), jnp.float32),
            pltpu.VMEM((ext_x, ext_y), jnp.float32),
            pltpu.VMEM((cols // 128, ext_x, 128), jnp.float32),
        ],
        compiler_params=pltpu.CompilerParams(dimension_semantics=("arbitrary",)),
    )(sample_levels, place, source, perm_classes, rows_halo, rows_halo, lane_tile, lane_tile)
    return solution_block, correction_block


def solution(mesh):
    placed = (P("sa", "gx", "gy"), P("sa"), P("sa", None), P("gx", "gy"))
    return jax.shard_map(
        shards,
        mesh=mesh,
        in_specs=placed,
        out_specs=(P("sa", "gx", "gy"), P("sa", "gx", "gy")),
        check_vma=False,
    )
```

time: 35.5 us -> 35.8 us (level)
  local copies, waits for them, and re-layouts: 0.26 us -> 2.45 us
  other arithmetic: 5.35 us -> 3.25 us
    unnamed x6 -> x9, local copies, waits for them, and re-layouts: 0.02 us -> 1.19 us
    slice x2 -> x3, local copies, waits for them, and re-layouts: 0.16 us -> 1.1 us  [the longest x1 0.88 us: halo_pieces(): source[:, -width:, :]]
    broadcast_in_dim x1 -> x0, other arithmetic: 0.91 us -> none  [shards(): perm_classes.astype(jnp.float32)[None]]
    slice x1 -> x0, other arithmetic: 0.88 us -> none  [exchange(): lax.slice_in_dim(block, 0, width, axis=dim)]
    convert_element_type x2 -> x1, other arithmetic: 1.55 us -> 0.9 us  [shards(): perm_classes.astype(jnp.float32)]
    another operation x0 -> x1, other arithmetic: none -> 0.63 us  [shards(): jnp.stack([lax.axis_index('gx'), lax.axis_index('gy'), lax.axis_size('gx'...]
    concatenate x2 -> x5, other arithmetic: 1.24 us -> 0.97 us  [the longest x1 0.9 us: halo_pieces(): return (rows_halo, jnp.concatenate([high, gap, low], axis=2))]
  transfers between devices with their start and end apart: 4 -> 4, of which waited for: 3 -> 3; matrix products, arithmetic and copies ran while one was open for 7% -> 5% of each run, Pallas kernels for 0% -> 0%
where the time goes in v5:
time: 35.8 us; the launch traced here: 35.5 us
  Pallas kernels  12 us (34%)
  starting transfers between devices  10.2 us (28%)
  waiting for transfers between devices  6.84 us (19%)
  other arithmetic  3.25 us (9%)
  local copies, waits for them, and re-layouts  2.45 us (7%)
  between operations  0.74 us (2%)
    pallas_call x1, Pallas kernels, shards(): pl.pallas_call(smooth_kernel, grid=(count,), in_specs=[smem, smem, pl.Blo...  12 us
    ppermute x1, waiting for transfers between devices, halo_pieces(): lax.ppermute(last, 'gy', [(i, i + 1) for i in range(lax.axis_size('gy') -...  3.86 us
    ppermute x1, starting transfers between devices, halo_pieces(): lax.ppermute(stack(source[:, -width:, :], classes[-width:, :]), 'gx', [(i...  3.48 us
    ppermute x1, starting transfers between devices, halo_pieces(): lax.ppermute(last, 'gy', [(i, i + 1) for i in range(lax.axis_size('gy') -...  2.42 us
    ppermute x1, starting transfers between devices, halo_pieces(): lax.ppermute(stack(source[:, :width, :], classes[:width, :]), 'gx', [(i +...  2.36 us
    ppermute x1, starting transfers between devices, halo_pieces(): lax.ppermute(first, 'gy', [(i + 1, i) for i in range(lax.axis_size('gy')...  1.92 us
    ppermute x1, waiting for transfers between devices, halo_pieces(): lax.ppermute(first, 'gy', [(i + 1, i) for i in range(lax.axis_size('gy')...  1.82 us
    unnamed x9, local copies, waits for them, and re-layouts  1.19 us
  transfers between devices with their start and end apart: 4, of which 3 were waited for; matrix products, arithmetic and copies ran while one was open for 5% of the time, Pallas kernels for 0%

profile of v5, /device:TPU:18, one launch (start us, length us, event | category | flops | bytes accessed | tf_op | source)
XLA Modules:
  0.0 35.5 jit_solution(8014355682906110874)
XLA Ops:
  0.6 0.0 copy-start
  0.6 0.9 %convert_element_type.11 = f32[64,256]{1,0:T(8,128)S(1)} convert(s32[64,256]{1,0:T(8,128)} %cls_ref.1) | non-fusion elementwise | flops 16384 | bytes 131072 | tf_op jit(solution)/shard_map/convert_element_type | solution.py:156
  1.6 0.9 %fusion.2 = (f32[8,8,256]{2,1,0:T(8,128)S(1)}, f32[8,8,256]{2,1,0:T(8,128)S(1)}) fusion(f32[8,64,256]{2,1,0:T(8,128)} %src_ref.1), kind=kLoop, calls=%fused_computation.16 | loop fusion | bytes 262144 | tf_op jit(solution)/shard_map/slice | solution.py:18
  2.5 2.4 %collective-permute-start = (f32[9,8,256]{2,1,0:T(8,128)S(1)}, f32[9,8,256]{2,1,0:T(8,128)S(1)}, u32[]{:S(2)}, u32[]{:S(2)}) collective-permute-start(f32[9,8,256]{2,1,0:T(8,128)S(1)} %pad_maximum_fusion.3), channel_id=1, source_target_pairs={{8,0},{16,8},{24,16},{9,1},{17,9},{25,17},{10,2},{18,10},{26,18},{... | collective-permute-start | bytes 221192 | tf_op jit(solution)/shard_map/ppermute | solution.py:21
  4.8 3.5 %collective-permute-start.1 = (f32[9,8,256]{2,1,0:T(8,128)S(1)}, f32[9,8,256]{2,1,0:T(8,128)S(1)}, u32[]{:S(2)}, u32[]{:S(2)}) collective-permute-start(f32[9,8,256]{2,1,0:T(8,128)S(1)} %pad_maximum_fusion.4), channel_id=1, source_target_pairs={{0,8},{8,16},{16,24},{1,9},{9,17},{17,25},{2,10},{10,18},{18,26},{... | collective-permute-start | bytes 221192 | tf_op jit(solution)/shard_map/ppermute | solution.py:17
  8.3 0.1 slice_bitcast_fusion.1
  8.4 0.0 copy-done
  8.4 0.0 copy-start.3
  8.4 0.1 fusion.1
  8.5 0.0 copy-start.2
  8.6 0.5 %copy-done.3 = s32[8]{0:T(128)S(1)} copy-done((s32[8]{0:T(128)S(1)}, s32[8]{0:T(128)}, u32[]{:S(2)}) %copy-start.3) | copy-done | bytes 56
  9.1 0.1 fusion
  9.1 0.1 copy-done.2
  9.2 0.7 %multiply_reduce_fusion.levels_ref = f32[8,8]{1,0:T(8,128)} fusion(f32[8,8]{1,0:T(8,128)S(1)} %copy-done.2, f32[8,8]{1,0:T(8,128)S(1)} %fusion), kind=kLoop, calls=%fused_computation.7 | loop fusion | flops 960 | bytes 768 | tf_op jit(solution)/shard_map/reduce_sum | solution.py:163
  9.9 0.0 collective-permute-done
  9.9 1.1 %collective-permute-done.1 = f32[9,8,256]{2,1,0:T(8,128)S(1)} collective-permute-done((f32[9,8,256]{2,1,0:T(8,128)S(1)}, f32[9,8,256]{2,1,0:T(8,128)S(1)}, u32[]{:S(2)}, u32[]{:S(2)}) %collective-permute-start.1) | collective-permute-done | bytes 73760 | tf_op jit(solution)/shard_map/ppermute | solution.py:17
  11.1 0.0 copy-start.1
  11.1 0.1 fusion.3
  11.2 0.6 %copy-done.1 = f32[9,16,256]{2,1,0:T(8,128)} copy-done((f32[9,16,256]{2,1,0:T(8,128)}, f32[9,16,256]{2,1,0:T(8,128)S(1)}, u32[]{:S(2)}) %copy-start.1) | copy-done | bytes 147480
  11.8 1.9 %collective-permute-start.2 = (f32[9,80,8]{2,1,0:T(8,128)S(1)}, f32[9,80,8]{2,1,0:T(8,128)S(1)}, u32[]{:S(2)}, u32[]{:S(2)}) collective-permute-start(f32[9,80,8]{2,1,0:T(8,128)S(1)} %pad_maximum_fusion), channel_id=1, source_target_pairs={{2,0},{4,2},{6,4},{3,1},{5,3},{7,5},{10,8},{12,10},{14,12},{11,9},... | collective-permute-start | bytes 69128 | tf_op jit(solution)/shard_map/ppermute | solution.py:29
  13.7 2.4 %collective-permute-start.3 = (f32[9,80,8]{2,1,0:T(8,128)S(1)}, f32[9,80,8]{2,1,0:T(8,128)S(1)}, u32[]{:S(2)}, u32[]{:S(2)}) collective-permute-start(f32[9,80,8]{2,1,0:T(8,128)S(1)} %pad_maximum_fusion.1), channel_id=1, source_target_pairs={{0,2},{2,4},{4,6},{1,3},{3,5},{5,7},{8,10},{10,12},{12,14},{9,11},... | collective-permute-start | bytes 69128 | tf_op jit(solution)/shard_map/ppermute | solution.py:28
  16.2 0.6 %pad_add_fusion.place_ref = s32[4]{0:T(128)} fusion(s32[2]{0:T(128)S(1)} %broadcast.18, s32[1]{0:T(128)} %bitcast.1, s32[1]{0:T(128)} %bitcast), kind=kLoop, calls=%fused_computation.14 | loop fusion | flops 8 | bytes 32 | tf_op jit(solution)/shard_map/stack | solution.py:157
  16.8 0.1 pad.1.clone
  16.9 1.8 %collective-permute-done.2 = f32[9,80,8]{2,1,0:T(8,128)S(1)} collective-permute-done((f32[9,80,8]{2,1,0:T(8,128)S(1)}, f32[9,80,8]{2,1,0:T(8,128)S(1)}, u32[]{:S(2)}, u32[]{:S(2)}) %collective-permute-start.2) | collective-permute-done | bytes 23072 | tf_op jit(solution)/shard_map/ppermute | solution.py:29
  18.7 3.9 %collective-permute-done.3 = f32[9,80,8]{2,1,0:T(8,128)S(1)} collective-permute-done((f32[9,80,8]{2,1,0:T(8,128)S(1)}, f32[9,80,8]{2,1,0:T(8,128)S(1)}, u32[]{:S(2)}, u32[]{:S(2)}) %collective-permute-start.3) | collective-permute-done | bytes 23072 | tf_op jit(solution)/shard_map/ppermute | solution.py:28
  22.6 0.9 %pad_maximum_fusion.2.tile_ref.ctile_ref = f32[9,80,128]{2,1,0:T(8,128)} fusion(f32[9,80,8]{2,1,0:T(8,128)S(1)} %collective-permute-done.3, f32[9,80,8]{2,1,0:T(8,128)S(1)} %collective-permute-done.2, f32[128]{0:T(128)S(1)} %pad.1.clone), kind=kLoop, calls=%fused_computation.2 | loop fusion | flops 184320 | bytes 415232 | tf_op jit(solution)/shard_map/concatenate | solution.py:31
  23.5 12.0 %shard_map.59 = (f32[8,64,256]{2,1,0:T(8,128)}, f32[8,32,128]{2,1,0:T(8,128)}) custom-call(f32[8,8]{1,0:T(8,128)} %multiply_reduce_fusion.levels_ref, s32[4]{0:T(128)} %pad_add_fusion.place_ref, f32[8,64,256]{2,1,0:T(8,128)} %src_ref.1, s32[64,256]{1,0:T(8,128)} %cls_ref.1, f32[9,16,256]{2,1,0:T(8,128)} %copy-done.1, f32[9,16,256]{2,1,0:T(8,128)} %copy-done.1, ...), custom_call_target="tpu_custom_call" | custom-call | tf_op jit(solution)/shard_map/pallas_call | solution.py:166
  (9 shorter events, 0.1 us)
Async XLA Ops:
  0.6 7.8 %copy-start = (f32[8,64,256]{2,1,0:T(8,128)S(1)}, f32[8,64,256]{2,1,0:T(8,128)}, u32[]{:S(2)}) copy-start(f32[8,64,256]{2,1,0:T(8,128)} %src_ref.1) | copy-start | bytes 1572868
  2.5 7.5 %collective-permute-start = (f32[9,8,256]{2,1,0:T(8,128)S(1)}, f32[9,8,256]{2,1,0:T(8,128)S(1)}, u32[]{:S(2)}, u32[]{:S(2)}) collective-permute-start(f32[9,8,256]{2,1,0:T(8,128)S(1)} %pad_maximum_fusion.3), channel_id=1, source_target_pairs={{8,0},{16,8},{24,16},{9,1},{17,9},{25,17},{10,2},{18,10},{26,18},{... | collective-permute-start | bytes 221192 | tf_op jit(solution)/shard_map/ppermute | solution.py:21
  4.8 6.2 %collective-permute-start.1 = (f32[9,8,256]{2,1,0:T(8,128)S(1)}, f32[9,8,256]{2,1,0:T(8,128)S(1)}, u32[]{:S(2)}, u32[]{:S(2)}) collective-permute-start(f32[9,8,256]{2,1,0:T(8,128)S(1)} %pad_maximum_fusion.4), channel_id=1, source_target_pairs={{0,8},{8,16},{16,24},{1,9},{9,17},{17,25},{2,10},{10,18},{18,26},{... | collective-permute-start | bytes 221192 | tf_op jit(solution)/shard_map/ppermute | solution.py:17
  8.4 0.7 %copy-start.3 = (s32[8]{0:T(128)S(1)}, s32[8]{0:T(128)}, u32[]{:S(2)}) copy-start(s32[8]{0:T(128)} %param.5) | copy-start | bytes 100
  8.5 0.7 %copy-start.2 = (f32[8,8]{1,0:T(8,128)S(1)}, f32[8,8]{1,0:T(8,128)}, u32[]{:S(2)}) copy-start(f32[8,8]{1,0:T(8,128)} %param.6) | copy-start | bytes 772
  11.1 0.7 %copy-start.1 = (f32[9,16,256]{2,1,0:T(8,128)}, f32[9,16,256]{2,1,0:T(8,128)S(1)}, u32[]{:S(2)}) copy-start(f32[9,16,256]{2,1,0:T(8,128)S(1)} %constant_dynamic-update-slice_fusion.rows_ref.crows_ref) | copy-start | bytes 442372
  11.8 6.9 %collective-permute-start.2 = (f32[9,80,8]{2,1,0:T(8,128)S(1)}, f32[9,80,8]{2,1,0:T(8,128)S(1)}, u32[]{:S(2)}, u32[]{:S(2)}) collective-permute-start(f32[9,80,8]{2,1,0:T(8,128)S(1)} %pad_maximum_fusion), channel_id=1, source_target_pairs={{2,0},{4,2},{6,4},{3,1},{5,3},{7,5},{10,8},{12,10},{14,12},{11,9},... | collective-permute-start | bytes 69128 | tf_op jit(solution)/shard_map/ppermute | solution.py:29
  13.7 8.8 %collective-permute-start.3 = (f32[9,80,8]{2,1,0:T(8,128)S(1)}, f32[9,80,8]{2,1,0:T(8,128)S(1)}, u32[]{:S(2)}, u32[]{:S(2)}) collective-permute-start(f32[9,80,8]{2,1,0:T(8,128)S(1)} %pad_maximum_fusion.1), channel_id=1, source_target_pairs={{0,2},{2,4},{4,6},{1,3},{3,5},{5,7},{8,10},{10,12},{12,14},{9,11},... | collective-permute-start | bytes 69128 | tf_op jit(solution)/shard_map/ppermute | solution.py:28

commit v6 on v5

v6 whole, which is shorter than its diff:
```python
import jax
import jax.numpy as jnp
from jax import lax
from jax.experimental import pallas as pl
from jax.experimental.pallas import tpu as pltpu
from jax.sharding import PartitionSpec as P

SWEEPS = 4
DAMPING = 0.8
HALO = 8
LANE_PAD = 128
HI = lax.Precision.HIGHEST


def halo_pieces(source, codes, width):
    stack = lambda a, b: jnp.concatenate([a, b[None]], axis=0)
    low = lax.ppermute(
        stack(source[:, -width:, :], codes[-width:, :]), "gx",
        [(i, i + 1) for i in range(lax.axis_size("gx") - 1)],
    )
    high = lax.ppermute(
        stack(source[:, :width, :], codes[:width, :]), "gx",
        [(i + 1, i) for i in range(lax.axis_size("gx") - 1)],
    )
    rows_halo = jnp.concatenate([high, low], axis=1)

    def packed(strip, halo_strip):
        planes = jnp.concatenate([strip, halo_strip], axis=1)
        count, rows, _ = planes.shape
        flat = jnp.transpose(planes, (1, 0, 2)).reshape(rows, count * width)
        return jnp.pad(flat, ((0, 0), (0, LANE_PAD - count * width)))

    last = packed(stack(source[:, :, -width:], codes[:, -width:]), rows_halo[:, :, -width:])
    first = packed(stack(source[:, :, :width], codes[:, :width]), rows_halo[:, :, :width])
    low = lax.ppermute(last, "gy", [(i, i + 1) for i in range(lax.axis_size("gy") - 1)])
    high = lax.ppermute(first, "gy", [(i + 1, i) for i in range(lax.axis_size("gy") - 1)])
    return rows_halo, high, low


def rolled(v, step):
    rows, cols = v.shape
    return (
        pltpu.roll(v, rows - step, 0),
        pltpu.roll(v, step, 0),
        pltpu.roll(v, cols - step, 1),
        pltpu.roll(v, step, 1),
    )


def couplings(perm, step):
    down, up, right, left = rolled(perm, step)
    rows, cols = perm.shape
    twice = 2.0 * perm
    south = twice * down / (perm + down)
    east = twice * right / (perm + right)
    linkage = (
        jnp.where(down > 0.0, south, twice),
        jnp.where(up > 0.0, pltpu.roll(south, step, 0), twice),
        jnp.where(right > 0.0, east, twice),
        jnp.where(left > 0.0, pltpu.roll(east, step, 1), twice),
    )
    diagonal = linkage[0] + linkage[1] + linkage[2] + linkage[3]
    return linkage, diagonal


def operator(linkage, diagonal, current, step):
    beside_all = rolled(current, step)
    return diagonal * current - (
        linkage[0] * beside_all[0]
        + linkage[1] * beside_all[1]
        + linkage[2] * beside_all[2]
        + linkage[3] * beside_all[3]
    )


def lane_tile(high_ref, low_ref, plane):
    high = high_ref[...]
    low = low_ref[...]
    lane = lax.broadcasted_iota(jnp.int32, high.shape, 1)
    after = pltpu.roll(high, (LANE_PAD - HALO * plane) % LANE_PAD, 1)
    before = pltpu.roll(low, (LANE_PAD - HALO - HALO * plane) % LANE_PAD, 1)
    return jnp.where(lane < HALO, after, jnp.where(lane >= LANE_PAD - HALO, before, 0.0))


def smooth_kernel(
    seeds_ref, levels_ref, src_ref, cls_ref, rows_ref, crows_ref, high_ref, low_ref,
    sol_ref, corr_ref, source_ext, codes_ext, spare,
):
    s = pl.program_id(0)
    count = pl.num_programs(0)
    rows, cols = sol_ref.shape[1], sol_ref.shape[2]
    ext_x, ext_y = source_ext.shape

    @pl.when(s == 0)
    def _():
        codes_ext[:rows, :cols] = cls_ref[...] + 1
        codes_ext[rows:, :cols] = crows_ref[0].astype(jnp.int32)
        codes_ext[:, cols:] = lane_tile(high_ref, low_ref, count).astype(jnp.int32)

    source_ext[:rows, :cols] = src_ref[0]
    source_ext[rows:, :cols] = rows_ref[0]
    source_ext[:, cols:] = lane_tile(high_ref, low_ref, s)
    source = source_ext[...]
    codes = codes_ext[...]
    valid = codes > 0
    classes = codes - 1
    seed = seeds_ref[s]
    level = [levels_ref[seed, category] for category in range(levels_ref.shape[1])]
    bit0 = (classes & 1) != 0
    bit1 = (classes & 2) != 0
    bit2 = (classes & 4) != 0
    low = jnp.where(bit1, jnp.where(bit0, level[3], level[2]), jnp.where(bit0, level[1], level[0]))
    high = jnp.where(bit1, jnp.where(bit0, level[7], level[6]), jnp.where(bit0, level[5], level[4]))
    perm = jnp.where(valid, jnp.where(bit2, high, low), 0.0)
    linkage, diagonal = couplings(perm, 1)
    inverse = 1.0 / jnp.where(valid, diagonal, 1.0)
    current = (DAMPING * source) * inverse
    for sweep_index in range(SWEEPS):
        residual = source - operator(linkage, diagonal, current, 1)
        if sweep_index + 1 < SWEEPS:
            current = current + (DAMPING * residual) * inverse
    pairs = residual + pltpu.roll(residual, ext_x - 1, 0)
    coarse_rhs = pairs + pltpu.roll(pairs, ext_y - 1, 1)
    pairs = perm + pltpu.roll(perm, ext_x - 1, 0)
    coarse_perm = 0.25 * (pairs + pltpu.roll(pairs, ext_y - 1, 1))
    odd_row = (lax.broadcasted_iota(jnp.int32, (ext_x, ext_y), 0) & 1) == 1
    odd_col = (lax.broadcasted_iota(jnp.int32, (ext_x, ext_y), 1) & 1) == 1
    coarse_valid = valid & jnp.logical_not(odd_row | odd_col)
    coarse_links, coarse_diagonal = couplings(coarse_perm, 2)
    coarse_inverse = 1.0 / jnp.where(coarse_valid, coarse_diagonal, 1.0)
    first = (DAMPING * coarse_rhs) * coarse_inverse
    correction = first + (
        DAMPING * (coarse_rhs - operator(coarse_links, coarse_diagonal, first, 2))
    ) * coarse_inverse
    spread = jnp.where(odd_row, pltpu.roll(correction, 1, 0), correction)
    spread = jnp.where(odd_col, pltpu.roll(spread, 1, 1), spread)
    sol_ref[0] = current[:rows, :cols] + spread[:rows, :cols]
    pieces = []
    for k in range(cols // 128):
        spare[k] = correction[:, k * 128 : (k + 1) * 128]
        pieces.append(spare[k, pl.ds(0, rows // 2, stride=2), :])
    even_rows = jnp.concatenate(pieces, axis=1)
    pick = (
        lax.broadcasted_iota(jnp.int32, (cols, cols // 2), 0)
        == 2 * lax.broadcasted_iota(jnp.int32, (cols, cols // 2), 1)
    ).astype(jnp.float32)
    corr_ref[0] = jnp.dot(even_rows, pick, precision=HI, preferred_element_type=jnp.float32)


def shards(source, sample_seeds, perm_levels, perm_classes):
    h = HALO
    count, rows, cols = source.shape
    ext_x, ext_y = rows + 2 * h, cols + LANE_PAD
    rows_halo, high, low = halo_pieces(source, (perm_classes + 1).astype(jnp.float32), h)
    smem = pl.BlockSpec(memory_space=pltpu.MemorySpace.SMEM)
    whole = lambda shape: pl.BlockSpec(shape, lambda s: (0,) * len(shape))
    solution_block, correction_block = pl.pallas_call(
        smooth_kernel,
        grid=(count,),
        in_specs=[
            smem,
            smem,
            pl.BlockSpec((1, rows, cols), lambda s: (s, 0, 0)),
            whole((rows, cols)),
            pl.BlockSpec((1, 2 * h, cols), lambda s: (s, 0, 0)),
            pl.BlockSpec((1, 2 * h, cols), lambda s: (count, 0, 0)),
            whole((ext_x, LANE_PAD)),
            whole((ext_x, LANE_PAD)),
        ],
        out_specs=[
            pl.BlockSpec((1, rows, cols), lambda s: (s, 0, 0)),
            pl.BlockSpec((1, rows // 2, cols // 2), lambda s: (s, 0, 0)),
        ],
        out_shape=[
            jax.ShapeDtypeStruct((count, rows, cols), jnp.float32),
            jax.ShapeDtypeStruct((count, rows // 2, cols // 2), jnp.float32),
        ],
        scratch_shapes=[
            pltpu.VMEM((ext_x, ext_y), jnp.float32),
            pltpu.VMEM((ext_x, ext_y), jnp.int32),
            pltpu.VMEM((cols // 128, ext_x, 128), jnp.float32),
        ],
        compiler_params=pltpu.CompilerParams(dimension_semantics=("arbitrary",)),
    )(sample_seeds, perm_levels, source, perm_classes, rows_halo, rows_halo, high, low)
    return solution_block, correction_block


def solution(mesh):
    placed = (P("sa", "gx", "gy"), P("sa"), P("sa", None), P("gx", "gy"))
    return jax.shard_map(
        shards,
        mesh=mesh,
        in_specs=placed,
        out_specs=(P("sa", "gx", "gy"), P("sa", "gx", "gy")),
        check_vma=False,
    )
```

time: 35.8 us -> 32.7 us (0.913)
  other arithmetic: 3.25 us -> 1.09 us
  waiting for transfers between devices: 6.84 us -> 5.03 us
  local copies, waits for them, and re-layouts: 2.45 us -> 3.12 us
    ppermute x1, waiting for transfers between devices: 1.82 us -> 0.01 us  [halo_pieces(): lax.ppermute(first, 'gy', [(i + 1, i) for i in range(lax.axis_size('gy')...]
    ppermute x2, waiting for transfers between devices: 1.15 us -> 2.14 us  [the longest x1 2.13 us: halo_pieces(): lax.ppermute(stack(source[:, -width:, :], codes[-width:, :]), 'gx', [(i,...]
    ppermute x1, waiting for transfers between devices: 3.86 us -> 2.89 us  [halo_pieces(): lax.ppermute(last, 'gy', [(i, i + 1) for i in range(lax.axis_size('gy') -...]
    concatenate x3 -> x0, other arithmetic: 0.95 us -> none  [the longest x1 0.9 us: halo_pieces(): return (rows_halo, jnp.concatenate([high, gap, low], axis=2))]
    reduce_sum x1 -> x0, other arithmetic: 0.68 us -> none  [shards(): jnp.sum(choose[:, :, None] * perm_levels[None, :, :], axis=1)]
    another operation x1 -> x0, other arithmetic: 0.63 us -> none  [shards(): jnp.stack([lax.axis_index('gx'), lax.axis_index('gy'), lax.axis_size('gx'...]
    unnamed x9 -> x11, local copies, waits for them, and re-layouts: 1.19 us -> 1.48 us
    convert_element_type x2 -> x1, other arithmetic: 0.98 us -> 0.91 us  [shards(): (perm_classes + 1).astype(jnp.float32)]
  transfers between devices with their start and end apart: 4 -> 4, of which waited for: 3 -> 2; matrix products, arithmetic and copies ran while one was open for 5% -> 2% of each run, Pallas kernels for 0% -> 0%
where the time goes in v6:
time: 32.7 us; the launch traced here: 32.4 us
  Pallas kernels  12.2 us (37%)
  starting transfers between devices  10.2 us (31%)
  waiting for transfers between devices  5.03 us (15%)
  local copies, waits for them, and re-layouts  3.12 us (10%)
  other arithmetic  1.09 us (3%)
  between operations  0.77 us (2%)
    pallas_call x1, Pallas kernels, shards(): pl.pallas_call(smooth_kernel, grid=(count,), in_specs=[smem, smem, pl.Blo...  12.2 us
    ppermute x1, starting transfers between devices, halo_pieces(): lax.ppermute(stack(source[:, -width:, :], codes[-width:, :]), 'gx', [(i,...  3.48 us
    ppermute x1, waiting for transfers between devices, halo_pieces(): lax.ppermute(last, 'gy', [(i, i + 1) for i in range(lax.axis_size('gy') -...  2.89 us
    ppermute x1, starting transfers between devices, halo_pieces(): lax.ppermute(last, 'gy', [(i, i + 1) for i in range(lax.axis_size('gy') -...  2.4 us
    ppermute x1, starting transfers between devices, halo_pieces(): lax.ppermute(stack(source[:, :width, :], codes[:width, :]), 'gx', [(i + 1...  2.36 us
    ppermute x1, waiting for transfers between devices, halo_pieces(): lax.ppermute(stack(source[:, -width:, :], codes[-width:, :]), 'gx', [(i,...  2.13 us
    ppermute x1, starting transfers between devices, halo_pieces(): lax.ppermute(first, 'gy', [(i + 1, i) for i in range(lax.axis_size('gy')...  1.92 us
    unnamed x11, local copies, waits for them, and re-layouts  1.48 us
  transfers between devices with their start and end apart: 4, of which 2 were waited for; matrix products, arithmetic and copies ran while one was open for 2% of the time, Pallas kernels for 0%

profile of v6, /device:TPU:18, one launch (start us, length us, event | category | flops | bytes accessed | tf_op | source)
XLA Modules:
  0.0 32.4 jit_solution(5665021682849233315)
XLA Ops:
  0.6 0.0 copy-start
  0.6 0.9 %add_convert_fusion = f32[64,256]{1,0:T(8,128)S(1)} fusion(s32[64,256]{1,0:T(8,128)} %cls_ref.1), kind=kLoop, calls=%fused_computation.2 | loop fusion | flops 32768 | bytes 131072 | tf_op jit(solution)/shard_map/convert_element_type | solution.py:154
  1.6 0.9 %fusion.1 = (f32[8,8,256]{2,1,0:T(8,128)S(1)}, f32[8,8,256]{2,1,0:T(8,128)S(1)}) fusion(f32[8,64,256]{2,1,0:T(8,128)} %src_ref.1), kind=kLoop, calls=%fused_computation.12 | loop fusion | bytes 262144 | tf_op jit(solution)/shard_map/slice | solution.py:18
  2.5 2.4 %collective-permute-start = (f32[9,8,256]{2,1,0:T(8,128)S(1)}, f32[9,8,256]{2,1,0:T(8,128)S(1)}, u32[]{:S(2)}, u32[]{:S(2)}) collective-permute-start(f32[9,8,256]{2,1,0:T(8,128)S(1)} %pad_maximum_fusion), channel_id=1, source_target_pairs={{8,0},{16,8},{24,16},{9,1},{17,9},{25,17},{10,2},{18,10},{26,18},{... | collective-permute-start | bytes 221192 | tf_op jit(solution)/shard_map/ppermute | solution.py:21
  4.8 3.5 %collective-permute-start.1 = (f32[9,8,256]{2,1,0:T(8,128)S(1)}, f32[9,8,256]{2,1,0:T(8,128)S(1)}, u32[]{:S(2)}, u32[]{:S(2)}) collective-permute-start(f32[9,8,256]{2,1,0:T(8,128)S(1)} %pad_maximum_fusion.1), channel_id=1, source_target_pairs={{0,8},{8,16},{16,24},{1,9},{9,17},{17,25},{2,10},{10,18},{18,26},{... | collective-permute-start | bytes 221192 | tf_op jit(solution)/shard_map/ppermute | solution.py:17
  8.3 0.0 copy-done
  8.3 0.1 fusion
  8.5 0.1 slice_bitcast_fusion
  8.5 0.1 copy.13
  8.6 0.1 copy.9
  8.7 0.1 copy.17
  8.8 0.1 copy.16
  8.9 0.0 collective-permute-done
  9.0 2.1 %collective-permute-done.1 = f32[9,8,256]{2,1,0:T(8,128)S(1)} collective-permute-done((f32[9,8,256]{2,1,0:T(8,128)S(1)}, f32[9,8,256]{2,1,0:T(8,128)S(1)}, u32[]{:S(2)}, u32[]{:S(2)}) %collective-permute-start.1) | collective-permute-done | bytes 73760 | tf_op jit(solution)/shard_map/ppermute | solution.py:17
  11.1 0.0 copy-start.1
  11.1 0.1 fusion.2
  11.2 0.6 %copy-done.1 = f32[9,16,256]{2,1,0:T(8,128)} copy-done((f32[9,16,256]{2,1,0:T(8,128)}, f32[9,16,256]{2,1,0:T(8,128)S(1)}, u32[]{:S(2)}) %copy-start.1) | copy-done | bytes 147480
  11.8 0.1 copy.14
  11.8 0.1 copy.10
  11.9 0.1 maximum_bitcast_fusion.1
  12.0 0.1 copy.15
  12.1 0.1 maximum_bitcast_fusion
  12.2 0.1 copy.11
  12.3 1.9 %collective-permute-start.2 = (f32[80,128]{1,0:T(8,128)S(1)}, f32[80,128]{1,0:T(8,128)S(1)}, u32[]{:S(2)}, u32[]{:S(2)}) collective-permute-start(f32[80,128]{1,0:T(8,128)S(1)} %pad.7), channel_id=1, source_target_pairs={{2,0},{4,2},{6,4},{3,1},{5,3},{7,5},{10,8},{12,10},{14,12},{11,9},... | collective-permute-start | bytes 122888 | tf_op jit(solution)/shard_map/ppermute | solution.py:36
  14.2 2.4 %collective-permute-start.3 = (f32[80,128]{1,0:T(8,128)S(1)}, f32[80,128]{1,0:T(8,128)S(1)}, u32[]{:S(2)}, u32[]{:S(2)}) collective-permute-start(f32[80,128]{1,0:T(8,128)S(1)} %pad.8), channel_id=1, source_target_pairs={{0,2},{2,4},{4,6},{1,3},{3,5},{5,7},{8,10},{10,12},{12,14},{9,11},... | collective-permute-start | bytes 122888 | tf_op jit(solution)/shard_map/ppermute | solution.py:35
  16.6 0.0 collective-permute-done.2.high_ref
  16.6 0.0 copy-start.2
  16.7 2.9 %collective-permute-done.3.low_ref = f32[80,128]{1,0:T(8,128)S(1)} collective-permute-done((f32[80,128]{1,0:T(8,128)S(1)}, f32[80,128]{1,0:T(8,128)S(1)}, u32[]{:S(2)}, u32[]{:S(2)}) %collective-permute-start.3) | collective-permute-done | bytes 40992 | tf_op jit(solution)/shard_map/ppermute | solution.py:35
  19.5 0.0 copy-done.2
  19.5 0.0 copy-start.3
  19.6 0.6 %copy-done.3 = f32[80,128]{1,0:T(8,128)} copy-done((f32[80,128]{1,0:T(8,128)}, f32[80,128]{1,0:T(8,128)S(1)}, u32[]{:S(2)}) %copy-start.3) | copy-done | bytes 40984
  20.2 12.2 %shard_map.59 = (f32[8,64,256]{2,1,0:T(8,128)}, f32[8,32,128]{2,1,0:T(8,128)}) custom-call(s32[8]{0:T(128)} %seeds_ref.1, f32[8,8]{1,0:T(8,128)} %levels_ref.1, f32[8,64,256]{2,1,0:T(8,128)} %src_ref.1, s32[64,256]{1,0:T(8,128)} %cls_ref.1, f32[9,16,256]{2,1,0:T(8,128)} %copy-done.1, f32[9,16,256]{2,1,0:T(8,128)} %copy-done.1, f32[80,128]{1,0:T(8,128)} %copy-done.2, ...), custom_call_target="tpu_custom_call" | custom-call | tf_op jit(solution)/shard_map/pallas_call | solution.py:157
  (7 shorter events, 0.1 us)
Async XLA Ops:
  0.6 7.7 %copy-start = (f32[8,64,256]{2,1,0:T(8,128)S(1)}, f32[8,64,256]{2,1,0:T(8,128)}, u32[]{:S(2)}) copy-start(f32[8,64,256]{2,1,0:T(8,128)} %src_ref.1) | copy-start | bytes 1572868
  2.5 6.5 %collective-permute-start = (f32[9,8,256]{2,1,0:T(8,128)S(1)}, f32[9,8,256]{2,1,0:T(8,128)S(1)}, u32[]{:S(2)}, u32[]{:S(2)}) collective-permute-start(f32[9,8,256]{2,1,0:T(8,128)S(1)} %pad_maximum_fusion), channel_id=1, source_target_pairs={{8,0},{16,8},{24,16},{9,1},{17,9},{25,17},{10,2},{18,10},{26,18},{... | collective-permute-start | bytes 221192 | tf_op jit(solution)/shard_map/ppermute | solution.py:21
  4.8 6.2 %collective-permute-start.1 = (f32[9,8,256]{2,1,0:T(8,128)S(1)}, f32[9,8,256]{2,1,0:T(8,128)S(1)}, u32[]{:S(2)}, u32[]{:S(2)}) collective-permute-start(f32[9,8,256]{2,1,0:T(8,128)S(1)} %pad_maximum_fusion.1), channel_id=1, source_target_pairs={{0,8},{8,16},{16,24},{1,9},{9,17},{17,25},{2,10},{10,18},{18,26},{... | collective-permute-start | bytes 221192 | tf_op jit(solution)/shard_map/ppermute | solution.py:17
  11.1 0.7 %copy-start.1 = (f32[9,16,256]{2,1,0:T(8,128)}, f32[9,16,256]{2,1,0:T(8,128)S(1)}, u32[]{:S(2)}) copy-start(f32[9,16,256]{2,1,0:T(8,128)S(1)} %constant_dynamic-update-slice_fusion.rows_ref.crows_ref) | copy-start | bytes 442372
  12.3 4.3 %collective-permute-start.2 = (f32[80,128]{1,0:T(8,128)S(1)}, f32[80,128]{1,0:T(8,128)S(1)}, u32[]{:S(2)}, u32[]{:S(2)}) collective-permute-start(f32[80,128]{1,0:T(8,128)S(1)} %pad.7), channel_id=1, source_target_pairs={{2,0},{4,2},{6,4},{3,1},{5,3},{7,5},{10,8},{12,10},{14,12},{11,9},... | collective-permute-start | bytes 122888 | tf_op jit(solution)/shard_map/ppermute | solution.py:36
  14.2 5.3 %collective-permute-start.3 = (f32[80,128]{1,0:T(8,128)S(1)}, f32[80,128]{1,0:T(8,128)S(1)}, u32[]{:S(2)}, u32[]{:S(2)}) collective-permute-start(f32[80,128]{1,0:T(8,128)S(1)} %pad.8), channel_id=1, source_target_pairs={{0,2},{2,4},{4,6},{1,3},{3,5},{5,7},{8,10},{10,12},{12,14},{9,11},... | collective-permute-start | bytes 122888 | tf_op jit(solution)/shard_map/ppermute | solution.py:35
  16.6 2.9 %copy-start.2 = (f32[80,128]{1,0:T(8,128)}, f32[80,128]{1,0:T(8,128)S(1)}, u32[]{:S(2)}) copy-start(f32[80,128]{1,0:T(8,128)S(1)} %collective-permute-done.2.high_ref) | copy-start | bytes 122884
  19.5 0.6 %copy-start.3 = (f32[80,128]{1,0:T(8,128)}, f32[80,128]{1,0:T(8,128)S(1)}, u32[]{:S(2)}) copy-start(f32[80,128]{1,0:T(8,128)S(1)} %collective-permute-done.3.low_ref) | copy-start | bytes 122884

commit v7 on v6

--- a/solution.py
+++ b/solution.py
@@ -39,25 +39,25 @@
 
 def rolled(v, step):
     rows, cols = v.shape
+    down, across = step
     return (
-        pltpu.roll(v, rows - step, 0),
-        pltpu.roll(v, step, 0),
-        pltpu.roll(v, cols - step, 1),
-        pltpu.roll(v, step, 1),
+        pltpu.roll(v, rows - down, 0),
+        pltpu.roll(v, down, 0),
+        pltpu.roll(v, cols - across, 1),
+        pltpu.roll(v, across, 1),
     )
 
 
 def couplings(perm, step):
     down, up, right, left = rolled(perm, step)
-    rows, cols = perm.shape
     twice = 2.0 * perm
     south = twice * down / (perm + down)
     east = twice * right / (perm + right)
     linkage = (
         jnp.where(down > 0.0, south, twice),
-        jnp.where(up > 0.0, pltpu.roll(south, step, 0), twice),
+        jnp.where(up > 0.0, pltpu.roll(south, step[0], 0), twice),
         jnp.where(right > 0.0, east, twice),
-        jnp.where(left > 0.0, pltpu.roll(east, step, 1), twice),
+        jnp.where(left > 0.0, pltpu.roll(east, step[1], 1), twice),
     )
     diagonal = linkage[0] + linkage[1] + linkage[2] + linkage[3]
     return linkage, diagonal
@@ -84,7 +84,7 @@
 
 def smooth_kernel(
     seeds_ref, levels_ref, src_ref, cls_ref, rows_ref, crows_ref, high_ref, low_ref,
-    sol_ref, corr_ref, source_ext, codes_ext, spare,
+    sol_ref, corr_ref, source_ext, codes_ext, spare, wide,
 ):
     s = pl.program_id(0)
     count = pl.num_programs(0)
@@ -112,39 +112,45 @@
     low = jnp.where(bit1, jnp.where(bit0, level[3], level[2]), jnp.where(bit0, level[1], level[0]))
     high = jnp.where(bit1, jnp.where(bit0, level[7], level[6]), jnp.where(bit0, level[5], level[4]))
     perm = jnp.where(valid, jnp.where(bit2, high, low), 0.0)
-    linkage, diagonal = couplings(perm, 1)
+    linkage, diagonal = couplings(perm, (1, 1))
     inverse = 1.0 / jnp.where(valid, diagonal, 1.0)
     current = (DAMPING * source) * inverse
     for sweep_index in range(SWEEPS):
-        residual = source - operator(linkage, diagonal, current, 1)
+        residual = source - operator(linkage, diagonal, current, (1, 1))
         if sweep_index + 1 < SWEEPS:
             current = current + (DAMPING * residual) * inverse
+
+    def even_rows(v):
+        pieces = []
+        for k in range(ext_y // 128):
+            spare[k] = v[:, k * 128 : (k + 1) * 128]
+            pieces.append(spare[k, pl.ds(0, ext_x // 2, stride=2), :])
+        return jnp.concatenate(pieces, axis=1)
+
     pairs = residual + pltpu.roll(residual, ext_x - 1, 0)
-    coarse_rhs = pairs + pltpu.roll(pairs, ext_y - 1, 1)
+    coarse_rhs = even_rows(pairs + pltpu.roll(pairs, ext_y - 1, 1))
     pairs = perm + pltpu.roll(perm, ext_x - 1, 0)
-    coarse_perm = 0.25 * (pairs + pltpu.roll(pairs, ext_y - 1, 1))
-    odd_row = (lax.broadcasted_iota(jnp.int32, (ext_x, ext_y), 0) & 1) == 1
-    odd_col = (lax.broadcasted_iota(jnp.int32, (ext_x, ext_y), 1) & 1) == 1
-    coarse_valid = valid & jnp.logical_not(odd_row | odd_col)
-    coarse_links, coarse_diagonal = couplings(coarse_perm, 2)
-    coarse_inverse = 1.0 / jnp.where(coarse_valid, coarse_diagonal, 1.0)
+    coarse_perm = 0.25 * even_rows(pairs + pltpu.roll(pairs, ext_y - 1, 1))
+    coarse_links, coarse_diagonal = couplings(coarse_perm, (1, 2))
+    coarse_inverse = 1.0 / jnp.where(coarse_perm > 0.0, coarse_diagonal, 1.0)
     first = (DAMPING * coarse_rhs) * coarse_inverse
     correction = first + (
-        DAMPING * (coarse_rhs - operator(coarse_links, coarse_diagonal, first, 2))
+        DAMPING * (coarse_rhs - operator(coarse_links, coarse_diagonal, first, (1, 2)))
     ) * coarse_inverse
-    spread = jnp.where(odd_row, pltpu.roll(correction, 1, 0), correction)
-    spread = jnp.where(odd_col, pltpu.roll(spread, 1, 1), spread)
-    sol_ref[0] = current[:rows, :cols] + spread[:rows, :cols]
-    pieces = []
-    for k in range(cols // 128):
-        spare[k] = correction[:, k * 128 : (k + 1) * 128]
-        pieces.append(spare[k, pl.ds(0, rows // 2, stride=2), :])
-    even_rows = jnp.concatenate(pieces, axis=1)
+    own = correction[: rows // 2, :cols]
     pick = (
         lax.broadcasted_iota(jnp.int32, (cols, cols // 2), 0)
         == 2 * lax.broadcasted_iota(jnp.int32, (cols, cols // 2), 1)
     ).astype(jnp.float32)
-    corr_ref[0] = jnp.dot(even_rows, pick, precision=HI, preferred_element_type=jnp.float32)
+    corr_ref[0] = jnp.dot(own, pick, precision=HI, preferred_element_type=jnp.float32)
+    for k in range(cols // 128):
+        piece = own[:, k * 128 : (k + 1) * 128]
+        wide[k, pl.ds(0, rows // 2, stride=2), :] = piece
+        wide[k, pl.ds(1, rows // 2, stride=2), :] = piece
+    spread = jnp.concatenate([wide[k] for k in range(cols // 128)], axis=1)
+    odd_col = (lax.broadcasted_iota(jnp.int32, (rows, cols), 1) & 1) == 1
+    spread = jnp.where(odd_col, pltpu.roll(spread, 1, 1), spread)
+    sol_ref[0] = current[:rows, :cols] + spread
 
 
 def shards(source, sample_seeds, perm_levels, perm_classes):
@@ -178,7 +184,8 @@
         scratch_shapes=[
             pltpu.VMEM((ext_x, ext_y), jnp.float32),
             pltpu.VMEM((ext_x, ext_y), jnp.int32),
-            pltpu.VMEM((cols // 128, ext_x, 128), jnp.float32),
+            pltpu.VMEM((ext_y // 128, ext_x, 128), jnp.float32),
+            pltpu.VMEM((cols // 128, rows, 128), jnp.float32),
         ],
         compiler_params=pltpu.CompilerParams(dimension_semantics=("arbitrary",)),
     )(sample_seeds, perm_levels, source, perm_classes, rows_halo, rows_halo, high, low)

time: 32.7 us -> 31.5 us (0.963)
  Pallas kernels: 12.2 us -> 11.1 us
    pallas_call x1, Pallas kernels: 12.2 us -> 11.1 us  [shards(): pl.pallas_call(smooth_kernel, grid=(count,), in_specs=[smem, smem, pl.Blo...]
where the time goes in v7:
time: 31.5 us; the launch traced here: 31.2 us
  Pallas kernels  11.1 us (35%)
  starting transfers between devices  10.2 us (32%)
  waiting for transfers between devices  5.03 us (16%)
  local copies, waits for them, and re-layouts  3.12 us (10%)
  other arithmetic  1.09 us (3%)
  between operations  0.77 us (2%)
    pallas_call x1, Pallas kernels, shards(): pl.pallas_call(smooth_kernel, grid=(count,), in_specs=[smem, smem, pl.Blo...  11.1 us
    ppermute x1, starting transfers between devices, halo_pieces(): lax.ppermute(stack(source[:, -width:, :], codes[-width:, :]), 'gx', [(i,...  3.48 us
    ppermute x1, waiting for transfers between devices, halo_pieces(): lax.ppermute(last, 'gy', [(i, i + 1) for i in range(lax.axis_size('gy') -...  2.89 us
    ppermute x1, starting transfers between devices, halo_pieces(): lax.ppermute(last, 'gy', [(i, i + 1) for i in range(lax.axis_size('gy') -...  2.4 us
    ppermute x1, starting transfers between devices, halo_pieces(): lax.ppermute(stack(source[:, :width, :], codes[:width, :]), 'gx', [(i + 1...  2.36 us
    ppermute x1, waiting for transfers between devices, halo_pieces(): lax.ppermute(stack(source[:, -width:, :], codes[-width:, :]), 'gx', [(i,...  2.13 us
    ppermute x1, starting transfers between devices, halo_pieces(): lax.ppermute(first, 'gy', [(i + 1, i) for i in range(lax.axis_size('gy')...  1.92 us
    unnamed x11, local copies, waits for them, and re-layouts  1.48 us
  transfers between devices with their start and end apart: 4, of which 2 were waited for; matrix products, arithmetic and copies ran while one was open for 2% of the time, Pallas kernels for 0%

profile of v7, /device:TPU:18, one launch (start us, length us, event | category | flops | bytes accessed | tf_op | source)
XLA Modules:
  0.0 31.2 jit_solution(11295995149906672138)
XLA Ops:
  0.6 0.0 copy-start
  0.6 0.9 %add_convert_fusion = f32[64,256]{1,0:T(8,128)S(1)} fusion(s32[64,256]{1,0:T(8,128)} %cls_ref.1), kind=kLoop, calls=%fused_computation.2 | loop fusion | flops 32768 | bytes 131072 | tf_op jit(solution)/shard_map/convert_element_type | solution.py:160
  1.6 0.9 %fusion.1 = (f32[8,8,256]{2,1,0:T(8,128)S(1)}, f32[8,8,256]{2,1,0:T(8,128)S(1)}) fusion(f32[8,64,256]{2,1,0:T(8,128)} %src_ref.1), kind=kLoop, calls=%fused_computation.12 | loop fusion | bytes 262144 | tf_op jit(solution)/shard_map/slice | solution.py:18
  2.5 2.4 %collective-permute-start = (f32[9,8,256]{2,1,0:T(8,128)S(1)}, f32[9,8,256]{2,1,0:T(8,128)S(1)}, u32[]{:S(2)}, u32[]{:S(2)}) collective-permute-start(f32[9,8,256]{2,1,0:T(8,128)S(1)} %pad_maximum_fusion), channel_id=1, source_target_pairs={{8,0},{16,8},{24,16},{9,1},{17,9},{25,17},{10,2},{18,10},{26,18},{... | collective-permute-start | bytes 221192 | tf_op jit(solution)/shard_map/ppermute | solution.py:21
  4.8 3.5 %collective-permute-start.1 = (f32[9,8,256]{2,1,0:T(8,128)S(1)}, f32[9,8,256]{2,1,0:T(8,128)S(1)}, u32[]{:S(2)}, u32[]{:S(2)}) collective-permute-start(f32[9,8,256]{2,1,0:T(8,128)S(1)} %pad_maximum_fusion.1), channel_id=1, source_target_pairs={{0,8},{8,16},{16,24},{1,9},{9,17},{17,25},{2,10},{10,18},{18,26},{... | collective-permute-start | bytes 221192 | tf_op jit(solution)/shard_map/ppermute | solution.py:17
  8.3 0.0 copy-done
  8.3 0.1 fusion
  8.5 0.1 slice_bitcast_fusion
  8.5 0.1 copy.13
  8.6 0.1 copy.9
  8.7 0.1 copy.17
  8.8 0.1 copy.16
  8.9 0.0 collective-permute-done
  9.0 2.1 %collective-permute-done.1 = f32[9,8,256]{2,1,0:T(8,128)S(1)} collective-permute-done((f32[9,8,256]{2,1,0:T(8,128)S(1)}, f32[9,8,256]{2,1,0:T(8,128)S(1)}, u32[]{:S(2)}, u32[]{:S(2)}) %collective-permute-start.1) | collective-permute-done | bytes 73760 | tf_op jit(solution)/shard_map/ppermute | solution.py:17
  11.1 0.0 copy-start.1
  11.1 0.1 fusion.2
  11.2 0.6 %copy-done.1 = f32[9,16,256]{2,1,0:T(8,128)} copy-done((f32[9,16,256]{2,1,0:T(8,128)}, f32[9,16,256]{2,1,0:T(8,128)S(1)}, u32[]{:S(2)}) %copy-start.1) | copy-done | bytes 147480
  11.8 0.1 copy.14
  11.8 0.1 copy.10
  11.9 0.1 maximum_bitcast_fusion.1
  12.0 0.1 copy.15
  12.1 0.1 maximum_bitcast_fusion
  12.2 0.1 copy.11
  12.3 1.9 %collective-permute-start.2 = (f32[80,128]{1,0:T(8,128)S(1)}, f32[80,128]{1,0:T(8,128)S(1)}, u32[]{:S(2)}, u32[]{:S(2)}) collective-permute-start(f32[80,128]{1,0:T(8,128)S(1)} %pad.7), channel_id=1, source_target_pairs={{2,0},{4,2},{6,4},{3,1},{5,3},{7,5},{10,8},{12,10},{14,12},{11,9},... | collective-permute-start | bytes 122888 | tf_op jit(solution)/shard_map/ppermute | solution.py:36
  14.2 2.4 %collective-permute-start.3 = (f32[80,128]{1,0:T(8,128)S(1)}, f32[80,128]{1,0:T(8,128)S(1)}, u32[]{:S(2)}, u32[]{:S(2)}) collective-permute-start(f32[80,128]{1,0:T(8,128)S(1)} %pad.8), channel_id=1, source_target_pairs={{0,2},{2,4},{4,6},{1,3},{3,5},{5,7},{8,10},{10,12},{12,14},{9,11},... | collective-permute-start | bytes 122888 | tf_op jit(solution)/shard_map/ppermute | solution.py:35
  16.6 0.0 collective-permute-done.2.high_ref
  16.6 0.0 copy-start.2
  16.7 2.9 %collective-permute-done.3.low_ref = f32[80,128]{1,0:T(8,128)S(1)} collective-permute-done((f32[80,128]{1,0:T(8,128)S(1)}, f32[80,128]{1,0:T(8,128)S(1)}, u32[]{:S(2)}, u32[]{:S(2)}) %collective-permute-start.3) | collective-permute-done | bytes 40992 | tf_op jit(solution)/shard_map/ppermute | solution.py:35
  19.5 0.0 copy-done.2
  19.5 0.0 copy-start.3
  19.6 0.6 %copy-done.3 = f32[80,128]{1,0:T(8,128)} copy-done((f32[80,128]{1,0:T(8,128)}, f32[80,128]{1,0:T(8,128)S(1)}, u32[]{:S(2)}) %copy-start.3) | copy-done | bytes 40984
  20.2 11.1 %shard_map.59 = (f32[8,64,256]{2,1,0:T(8,128)}, f32[8,32,128]{2,1,0:T(8,128)}) custom-call(s32[8]{0:T(128)} %seeds_ref.1, f32[8,8]{1,0:T(8,128)} %levels_ref.1, f32[8,64,256]{2,1,0:T(8,128)} %src_ref.1, s32[64,256]{1,0:T(8,128)} %cls_ref.1, f32[9,16,256]{2,1,0:T(8,128)} %copy-done.1, f32[9,16,256]{2,1,0:T(8,128)} %copy-done.1, f32[80,128]{1,0:T(8,128)} %copy-done.2, ...), custom_call_target="tpu_custom_call" | custom-call | tf_op jit(solution)/shard_map/pallas_call | solution.py:163
  (7 shorter events, 0.1 us)
Async XLA Ops:
  0.6 7.7 %copy-start = (f32[8,64,256]{2,1,0:T(8,128)S(1)}, f32[8,64,256]{2,1,0:T(8,128)}, u32[]{:S(2)}) copy-start(f32[8,64,256]{2,1,0:T(8,128)} %src_ref.1) | copy-start | bytes 1572868
  2.5 6.5 %collective-permute-start = (f32[9,8,256]{2,1,0:T(8,128)S(1)}, f32[9,8,256]{2,1,0:T(8,128)S(1)}, u32[]{:S(2)}, u32[]{:S(2)}) collective-permute-start(f32[9,8,256]{2,1,0:T(8,128)S(1)} %pad_maximum_fusion), channel_id=1, source_target_pairs={{8,0},{16,8},{24,16},{9,1},{17,9},{25,17},{10,2},{18,10},{26,18},{... | collective-permute-start | bytes 221192 | tf_op jit(solution)/shard_map/ppermute | solution.py:21
  4.8 6.2 %collective-permute-start.1 = (f32[9,8,256]{2,1,0:T(8,128)S(1)}, f32[9,8,256]{2,1,0:T(8,128)S(1)}, u32[]{:S(2)}, u32[]{:S(2)}) collective-permute-start(f32[9,8,256]{2,1,0:T(8,128)S(1)} %pad_maximum_fusion.1), channel_id=1, source_target_pairs={{0,8},{8,16},{16,24},{1,9},{9,17},{17,25},{2,10},{10,18},{18,26},{... | collective-permute-start | bytes 221192 | tf_op jit(solution)/shard_map/ppermute | solution.py:17
  11.1 0.7 %copy-start.1 = (f32[9,16,256]{2,1,0:T(8,128)}, f32[9,16,256]{2,1,0:T(8,128)S(1)}, u32[]{:S(2)}) copy-start(f32[9,16,256]{2,1,0:T(8,128)S(1)} %constant_dynamic-update-slice_fusion.rows_ref.crows_ref) | copy-start | bytes 442372
  12.3 4.3 %collective-permute-start.2 = (f32[80,128]{1,0:T(8,128)S(1)}, f32[80,128]{1,0:T(8,128)S(1)}, u32[]{:S(2)}, u32[]{:S(2)}) collective-permute-start(f32[80,128]{1,0:T(8,128)S(1)} %pad.7), channel_id=1, source_target_pairs={{2,0},{4,2},{6,4},{3,1},{5,3},{7,5},{10,8},{12,10},{14,12},{11,9},... | collective-permute-start | bytes 122888 | tf_op jit(solution)/shard_map/ppermute | solution.py:36
  14.2 5.3 %collective-permute-start.3 = (f32[80,128]{1,0:T(8,128)S(1)}, f32[80,128]{1,0:T(8,128)S(1)}, u32[]{:S(2)}, u32[]{:S(2)}) collective-permute-start(f32[80,128]{1,0:T(8,128)S(1)} %pad.8), channel_id=1, source_target_pairs={{0,2},{2,4},{4,6},{1,3},{3,5},{5,7},{8,10},{10,12},{12,14},{9,11},... | collective-permute-start | bytes 122888 | tf_op jit(solution)/shard_map/ppermute | solution.py:35
  16.6 2.9 %copy-start.2 = (f32[80,128]{1,0:T(8,128)}, f32[80,128]{1,0:T(8,128)S(1)}, u32[]{:S(2)}) copy-start(f32[80,128]{1,0:T(8,128)S(1)} %collective-permute-done.2.high_ref) | copy-start | bytes 122884
  19.5 0.6 %copy-start.3 = (f32[80,128]{1,0:T(8,128)}, f32[80,128]{1,0:T(8,128)S(1)}, u32[]{:S(2)}) copy-start(f32[80,128]{1,0:T(8,128)S(1)} %collective-permute-done.3.low_ref) | copy-start | bytes 122884

commit v8 on v7

--- a/solution.py
+++ b/solution.py
@@ -10,16 +10,17 @@
 HALO = 8
 LANE_PAD = 128
 HI = lax.Precision.HIGHEST
-
-
-def halo_pieces(source, codes, width):
-    stack = lambda a, b: jnp.concatenate([a, b[None]], axis=0)
+PER_STEP = 2
+
+
+def halo_pieces(source, classes, width):
+    stack = lambda a, b: jnp.concatenate([a, (b + 1).astype(a.dtype)[None]], axis=0)
     low = lax.ppermute(
-        stack(source[:, -width:, :], codes[-width:, :]), "gx",
+        stack(source[:, -width:, :], classes[-width:, :]), "gx",
         [(i, i + 1) for i in range(lax.axis_size("gx") - 1)],
     )
     high = lax.ppermute(
-        stack(source[:, :width, :], codes[:width, :]), "gx",
+        stack(source[:, :width, :], classes[:width, :]), "gx",
         [(i + 1, i) for i in range(lax.axis_size("gx") - 1)],
     )
     rows_halo = jnp.concatenate([high, low], axis=1)
@@ -30,8 +31,8 @@
         flat = jnp.transpose(planes, (1, 0, 2)).reshape(rows, count * width)
         return jnp.pad(flat, ((0, 0), (0, LANE_PAD - count * width)))
 
-    last = packed(stack(source[:, :, -width:], codes[:, -width:]), rows_halo[:, :, -width:])
-    first = packed(stack(source[:, :, :width], codes[:, :width]), rows_halo[:, :, :width])
+    last = packed(stack(source[:, :, -width:], classes[:, -width:]), rows_halo[:, :, -width:])
+    first = packed(stack(source[:, :, :width], classes[:, :width]), rows_halo[:, :, :width])
     low = lax.ppermute(last, "gy", [(i, i + 1) for i in range(lax.axis_size("gy") - 1)])
     high = lax.ppermute(first, "gy", [(i + 1, i) for i in range(lax.axis_size("gy") - 1)])
     return rows_halo, high, low
@@ -87,7 +88,7 @@
     sol_ref, corr_ref, source_ext, codes_ext, spare, wide,
 ):
     s = pl.program_id(0)
-    count = pl.num_programs(0)
+    count = PER_STEP * pl.num_programs(0)
     rows, cols = sol_ref.shape[1], sol_ref.shape[2]
     ext_x, ext_y = source_ext.shape
 
@@ -97,14 +98,27 @@
         codes_ext[rows:, :cols] = crows_ref[0].astype(jnp.int32)
         codes_ext[:, cols:] = lane_tile(high_ref, low_ref, count).astype(jnp.int32)
 
-    source_ext[:rows, :cols] = src_ref[0]
-    source_ext[rows:, :cols] = rows_ref[0]
-    source_ext[:, cols:] = lane_tile(high_ref, low_ref, s)
+    for j in range(PER_STEP):
+        one_sample(
+            PER_STEP * s + j, j, seeds_ref, levels_ref, src_ref, rows_ref, high_ref, low_ref,
+            sol_ref, corr_ref, source_ext, codes_ext, spare, wide,
+        )
+
+
+def one_sample(
+    plane, j, seeds_ref, levels_ref, src_ref, rows_ref, high_ref, low_ref,
+    sol_ref, corr_ref, source_ext, codes_ext, spare, wide,
+):
+    rows, cols = sol_ref.shape[1], sol_ref.shape[2]
+    ext_x, ext_y = source_ext.shape
+    source_ext[:rows, :cols] = src_ref[j]
+    source_ext[rows:, :cols] = rows_ref[j]
+    source_ext[:, cols:] = lane_tile(high_ref, low_ref, plane)
     source = source_ext[...]
     codes = codes_ext[...]
     valid = codes > 0
     classes = codes - 1
-    seed = seeds_ref[s]
+    seed = seeds_ref[plane]
     level = [levels_ref[seed, category] for category in range(levels_ref.shape[1])]
     bit0 = (classes & 1) != 0
     bit1 = (classes & 2) != 0
@@ -142,7 +156,7 @@
         lax.broadcasted_iota(jnp.int32, (cols, cols // 2), 0)
         == 2 * lax.broadcasted_iota(jnp.int32, (cols, cols // 2), 1)
     ).astype(jnp.float32)
-    corr_ref[0] = jnp.dot(own, pick, precision=HI, preferred_element_type=jnp.float32)
+    corr_ref[j] = jnp.dot(own, pick, precision=HI, preferred_element_type=jnp.float32)
     for k in range(cols // 128):
         piece = own[:, k * 128 : (k + 1) * 128]
         wide[k, pl.ds(0, rows // 2, stride=2), :] = piece
@@ -150,32 +164,32 @@
     spread = jnp.concatenate([wide[k] for k in range(cols // 128)], axis=1)
     odd_col = (lax.broadcasted_iota(jnp.int32, (rows, cols), 1) & 1) == 1
     spread = jnp.where(odd_col, pltpu.roll(spread, 1, 1), spread)
-    sol_ref[0] = current[:rows, :cols] + spread
+    sol_ref[j] = current[:rows, :cols] + spread
 
 
 def shards(source, sample_seeds, perm_levels, perm_classes):
     h = HALO
     count, rows, cols = source.shape
     ext_x, ext_y = rows + 2 * h, cols + LANE_PAD
-    rows_halo, high, low = halo_pieces(source, (perm_classes + 1).astype(jnp.float32), h)
+    rows_halo, high, low = halo_pieces(source, perm_classes, h)
     smem = pl.BlockSpec(memory_space=pltpu.MemorySpace.SMEM)
     whole = lambda shape: pl.BlockSpec(shape, lambda s: (0,) * len(shape))
     solution_block, correction_block = pl.pallas_call(
         smooth_kernel,
-        grid=(count,),
+        grid=(count // PER_STEP,),
         in_specs=[
             smem,
             smem,
-            pl.BlockSpec((1, rows, cols), lambda s: (s, 0, 0)),
+            pl.BlockSpec((PER_STEP, rows, cols), lambda s: (s, 0, 0)),
             whole((rows, cols)),
-            pl.BlockSpec((1, 2 * h, cols), lambda s: (s, 0, 0)),
+            pl.BlockSpec((PER_STEP, 2 * h, cols), lambda s: (s, 0, 0)),
             pl.BlockSpec((1, 2 * h, cols), lambda s: (count, 0, 0)),
             whole((ext_x, LANE_PAD)),
             whole((ext_x, LANE_PAD)),
         ],
         out_specs=[
-            pl.BlockSpec((1, rows, cols), lambda s: (s, 0, 0)),
-            pl.BlockSpec((1, rows // 2, cols // 2), lambda s: (s, 0, 0)),
+            pl.BlockSpec((PER_STEP, rows, cols), lambda s: (s, 0, 0)),
+            pl.BlockSpec((PER_STEP, rows // 2, cols // 2), lambda s: (s, 0, 0)),
         ],
         out_shape=[
             jax.ShapeDtypeStruct((count, rows, cols), jnp.float32),

time: 31.5 us -> 30.4 us (0.965)
  Pallas kernels: 11.1 us -> 10.1 us
    pallas_call x1, Pallas kernels: 11.1 us -> 10.1 us  [shards(): pl.pallas_call(smooth_kernel, grid=(count // PER_STEP,), in_specs=[smem,...]
    convert_element_type x1 -> x0, other arithmetic: 0.91 us -> none  [shards(): (perm_classes + 1).astype(jnp.float32)]
    broadcast_in_dim x0 -> x3, other arithmetic: none -> 0.79 us  [halo_pieces(): (b + 1).astype(a.dtype)[None]]
    unnamed x11 -> x15, local copies, waits for them, and re-layouts: 1.48 us -> 1.59 us
where the time goes in v8:
time: 30.4 us; the launch traced here: 30.1 us
  starting transfers between devices  10.2 us (34%)
  Pallas kernels  10.1 us (33%)
  waiting for transfers between devices  5.01 us (16%)
  local copies, waits for them, and re-layouts  3.1 us (10%)
  other arithmetic  0.98 us (3%)
  between operations  0.78 us (3%)
    pallas_call x1, Pallas kernels, shards(): pl.pallas_call(smooth_kernel, grid=(count // PER_STEP,), in_specs=[smem,...  10.1 us
    ppermute x1, starting transfers between devices, halo_pieces(): lax.ppermute(stack(source[:, -width:, :], classes[-width:, :]), 'gx', [(i...  3.48 us
    ppermute x1, waiting for transfers between devices, halo_pieces(): lax.ppermute(last, 'gy', [(i, i + 1) for i in range(lax.axis_size('gy') -...  2.89 us
    ppermute x1, starting transfers between devices, halo_pieces(): lax.ppermute(last, 'gy', [(i, i + 1) for i in range(lax.axis_size('gy') -...  2.4 us
    ppermute x1, starting transfers between devices, halo_pieces(): lax.ppermute(stack(source[:, :width, :], classes[:width, :]), 'gx', [(i +...  2.36 us
    ppermute x1, waiting for transfers between devices, halo_pieces(): lax.ppermute(stack(source[:, -width:, :], classes[-width:, :]), 'gx', [(i...  2.12 us
    ppermute x1, starting transfers between devices, halo_pieces(): lax.ppermute(first, 'gy', [(i + 1, i) for i in range(lax.axis_size('gy')...  1.92 us
    unnamed x15, local copies, waits for them, and re-layouts  1.59 us
  transfers between devices with their start and end apart: 4, of which 2 were waited for; matrix products, arithmetic and copies ran while one was open for 2% of the time, Pallas kernels for 0%

profile of v8, /device:TPU:18, one launch (start us, length us, event | category | flops | bytes accessed | tf_op | source)
XLA Modules:
  0.0 30.1 jit_solution(7508114833506826097)
XLA Ops:
  0.6 0.0 copy-start
  0.6 0.8 %convert_bitcast_fusion = (f32[1,8,256]{2,1,0:T(8,128)S(1)}, f32[1,8,256]{2,1,0:T(8,128)S(1)}) fusion(s32[64,256]{1,0:T(8,128)} %cls_ref.1), kind=kLoop, calls=%fused_computation.4 | loop fusion | flops 8192 | bytes 32768 | tf_op jit(solution)/shard_map/broadcast_in_dim | solution.py:17
  1.4 0.9 %fusion.1 = (f32[8,8,256]{2,1,0:T(8,128)S(1)}, f32[8,8,256]{2,1,0:T(8,128)S(1)}) fusion(f32[8,64,256]{2,1,0:T(8,128)} %src_ref.1), kind=kLoop, calls=%fused_computation.11 | loop fusion | bytes 262144 | tf_op jit(solution)/shard_map/slice | solution.py:19
  2.3 2.4 %collective-permute-start = (f32[9,8,256]{2,1,0:T(8,128)S(1)}, f32[9,8,256]{2,1,0:T(8,128)S(1)}, u32[]{:S(2)}, u32[]{:S(2)}) collective-permute-start(f32[9,8,256]{2,1,0:T(8,128)S(1)} %pad_maximum_fusion), channel_id=1, source_target_pairs={{8,0},{16,8},{24,16},{9,1},{17,9},{25,17},{10,2},{18,10},{26,18},{... | collective-permute-start | bytes 221192 | tf_op jit(solution)/shard_map/ppermute | solution.py:22
  4.7 0.0 copy-start.2
  4.7 3.5 %collective-permute-start.1 = (f32[9,8,256]{2,1,0:T(8,128)S(1)}, f32[9,8,256]{2,1,0:T(8,128)S(1)}, u32[]{:S(2)}, u32[]{:S(2)}) collective-permute-start(f32[9,8,256]{2,1,0:T(8,128)S(1)} %pad_maximum_fusion.1), channel_id=1, source_target_pairs={{0,8},{8,16},{16,24},{1,9},{9,17},{17,25},{2,10},{10,18},{18,26},{... | collective-permute-start | bytes 221192 | tf_op jit(solution)/shard_map/ppermute | solution.py:18
  8.2 0.0 copy-done.2
  8.2 0.1 fusion.3
  8.3 0.0 copy-done
  8.3 0.1 fusion
  8.4 0.1 copy.19
  8.5 0.1 copy.17
  8.6 0.1 copy.18
  8.7 0.1 copy.16
  8.8 0.0 collective-permute-done
  8.8 2.1 %collective-permute-done.1 = f32[9,8,256]{2,1,0:T(8,128)S(1)} collective-permute-done((f32[9,8,256]{2,1,0:T(8,128)S(1)}, f32[9,8,256]{2,1,0:T(8,128)S(1)}, u32[]{:S(2)}, u32[]{:S(2)}) %collective-permute-start.1) | collective-permute-done | bytes 73760 | tf_op jit(solution)/shard_map/ppermute | solution.py:18
  11.0 0.0 copy-start.1
  11.0 0.1 fusion.2
  11.1 0.6 %copy-done.1 = f32[9,16,256]{2,1,0:T(8,128)} copy-done((f32[9,16,256]{2,1,0:T(8,128)}, f32[9,16,256]{2,1,0:T(8,128)S(1)}, u32[]{:S(2)}) %copy-start.1) | copy-done | bytes 147480
  11.6 0.1 copy.14
  11.7 0.1 copy.10
  11.8 0.1 maximum_bitcast_fusion.1
  11.9 0.1 copy.15
  12.0 0.1 maximum_bitcast_fusion
  12.0 0.1 copy.11
  12.2 1.9 %collective-permute-start.2 = (f32[80,128]{1,0:T(8,128)S(1)}, f32[80,128]{1,0:T(8,128)S(1)}, u32[]{:S(2)}, u32[]{:S(2)}) collective-permute-start(f32[80,128]{1,0:T(8,128)S(1)} %pad.7), channel_id=1, source_target_pairs={{2,0},{4,2},{6,4},{3,1},{5,3},{7,5},{10,8},{12,10},{14,12},{11,9},... | collective-permute-start | bytes 122888 | tf_op jit(solution)/shard_map/ppermute | solution.py:37
  14.1 2.4 %collective-permute-start.3 = (f32[80,128]{1,0:T(8,128)S(1)}, f32[80,128]{1,0:T(8,128)S(1)}, u32[]{:S(2)}, u32[]{:S(2)}) collective-permute-start(f32[80,128]{1,0:T(8,128)S(1)} %pad.8), channel_id=1, source_target_pairs={{0,2},{2,4},{4,6},{1,3},{3,5},{5,7},{8,10},{10,12},{12,14},{9,11},... | collective-permute-start | bytes 122888 | tf_op jit(solution)/shard_map/ppermute | solution.py:36
  16.5 0.0 collective-permute-done.2.high_ref
  16.5 0.0 copy-start.3
  16.5 2.9 %collective-permute-done.3.low_ref = f32[80,128]{1,0:T(8,128)S(1)} collective-permute-done((f32[80,128]{1,0:T(8,128)S(1)}, f32[80,128]{1,0:T(8,128)S(1)}, u32[]{:S(2)}, u32[]{:S(2)}) %collective-permute-start.3) | collective-permute-done | bytes 40992 | tf_op jit(solution)/shard_map/ppermute | solution.py:36
  19.4 0.0 copy-done.3
  19.4 0.0 copy-start.4
  19.4 0.6 %copy-done.4 = f32[80,128]{1,0:T(8,128)} copy-done((f32[80,128]{1,0:T(8,128)}, f32[80,128]{1,0:T(8,128)S(1)}, u32[]{:S(2)}) %copy-start.4) | copy-done | bytes 40984
  20.0 10.1 %shard_map.59 = (f32[8,64,256]{2,1,0:T(8,128)}, f32[8,32,128]{2,1,0:T(8,128)}) custom-call(s32[8]{0:T(128)} %seeds_ref.1, f32[8,8]{1,0:T(8,128)} %levels_ref.1, f32[8,64,256]{2,1,0:T(8,128)} %src_ref.1, s32[64,256]{1,0:T(8,128)} %cls_ref.1, f32[9,16,256]{2,1,0:T(8,128)} %copy-done.1, f32[9,16,256]{2,1,0:T(8,128)} %copy-done.1, f32[80,128]{1,0:T(8,128)} %copy-done.3, ...), custom_call_target="tpu_custom_call" | custom-call | tf_op jit(solution)/shard_map/pallas_call | solution.py:177
  (8 shorter events, 0.1 us)
Async XLA Ops:
  0.6 7.7 %copy-start = (f32[8,64,256]{2,1,0:T(8,128)S(1)}, f32[8,64,256]{2,1,0:T(8,128)}, u32[]{:S(2)}) copy-start(f32[8,64,256]{2,1,0:T(8,128)} %src_ref.1) | copy-start | bytes 1572868
  2.3 6.5 %collective-permute-start = (f32[9,8,256]{2,1,0:T(8,128)S(1)}, f32[9,8,256]{2,1,0:T(8,128)S(1)}, u32[]{:S(2)}, u32[]{:S(2)}) collective-permute-start(f32[9,8,256]{2,1,0:T(8,128)S(1)} %pad_maximum_fusion), channel_id=1, source_target_pairs={{8,0},{16,8},{24,16},{9,1},{17,9},{25,17},{10,2},{18,10},{26,18},{... | collective-permute-start | bytes 221192 | tf_op jit(solution)/shard_map/ppermute | solution.py:22
  4.7 3.5 %copy-start.2 = (s32[64,256]{1,0:T(8,128)S(1)}, s32[64,256]{1,0:T(8,128)}, u32[]{:S(2)}) copy-start(s32[64,256]{1,0:T(8,128)} %cls_ref.1) | copy-start | bytes 196612
  4.7 6.2 %collective-permute-start.1 = (f32[9,8,256]{2,1,0:T(8,128)S(1)}, f32[9,8,256]{2,1,0:T(8,128)S(1)}, u32[]{:S(2)}, u32[]{:S(2)}) collective-permute-start(f32[9,8,256]{2,1,0:T(8,128)S(1)} %pad_maximum_fusion.1), channel_id=1, source_target_pairs={{0,8},{8,16},{16,24},{1,9},{9,17},{17,25},{2,10},{10,18},{18,26},{... | collective-permute-start | bytes 221192 | tf_op jit(solution)/shard_map/ppermute | solution.py:18
  11.0 0.7 %copy-start.1 = (f32[9,16,256]{2,1,0:T(8,128)}, f32[9,16,256]{2,1,0:T(8,128)S(1)}, u32[]{:S(2)}) copy-start(f32[9,16,256]{2,1,0:T(8,128)S(1)} %constant_dynamic-update-slice_fusion.rows_ref.crows_ref) | copy-start | bytes 442372
  12.2 4.3 %collective-permute-start.2 = (f32[80,128]{1,0:T(8,128)S(1)}, f32[80,128]{1,0:T(8,128)S(1)}, u32[]{:S(2)}, u32[]{:S(2)}) collective-permute-start(f32[80,128]{1,0:T(8,128)S(1)} %pad.7), channel_id=1, source_target_pairs={{2,0},{4,2},{6,4},{3,1},{5,3},{7,5},{10,8},{12,10},{14,12},{11,9},... | collective-permute-start | bytes 122888 | tf_op jit(solution)/shard_map/ppermute | solution.py:37
  14.1 5.3 %collective-permute-start.3 = (f32[80,128]{1,0:T(8,128)S(1)}, f32[80,128]{1,0:T(8,128)S(1)}, u32[]{:S(2)}, u32[]{:S(2)}) collective-permute-start(f32[80,128]{1,0:T(8,128)S(1)} %pad.8), channel_id=1, source_target_pairs={{0,2},{2,4},{4,6},{1,3},{3,5},{5,7},{8,10},{10,12},{12,14},{9,11},... | collective-permute-start | bytes 122888 | tf_op jit(solution)/shard_map/ppermute | solution.py:36
  16.5 2.9 %copy-start.3 = (f32[80,128]{1,0:T(8,128)}, f32[80,128]{1,0:T(8,128)S(1)}, u32[]{:S(2)}) copy-start(f32[80,128]{1,0:T(8,128)S(1)} %collective-permute-done.2.high_ref) | copy-start | bytes 122884
  19.4 0.6 %copy-start.4 = (f32[80,128]{1,0:T(8,128)}, f32[80,128]{1,0:T(8,128)S(1)}, u32[]{:S(2)}) copy-start(f32[80,128]{1,0:T(8,128)S(1)} %collective-permute-done.3.low_ref) | copy-start | bytes 122884

commit v9 on v8

--- a/solution.py
+++ b/solution.py
@@ -84,7 +84,7 @@
 
 
 def smooth_kernel(
-    seeds_ref, levels_ref, src_ref, cls_ref, rows_ref, crows_ref, high_ref, low_ref,
+    seeds_ref, levels_ref, src_ref, cls_ref, rows_ref, high_ref, low_ref,
     sol_ref, corr_ref, source_ext, codes_ext, spare, wide,
 ):
     s = pl.program_id(0)
@@ -95,7 +95,7 @@
     @pl.when(s == 0)
     def _():
         codes_ext[:rows, :cols] = cls_ref[...] + 1
-        codes_ext[rows:, :cols] = crows_ref[0].astype(jnp.int32)
+        codes_ext[rows:, :cols] = rows_ref[count].astype(jnp.int32)
         codes_ext[:, cols:] = lane_tile(high_ref, low_ref, count).astype(jnp.int32)
 
     for j in range(PER_STEP):
@@ -112,7 +112,7 @@
     rows, cols = sol_ref.shape[1], sol_ref.shape[2]
     ext_x, ext_y = source_ext.shape
     source_ext[:rows, :cols] = src_ref[j]
-    source_ext[rows:, :cols] = rows_ref[j]
+    source_ext[rows:, :cols] = rows_ref[plane]
     source_ext[:, cols:] = lane_tile(high_ref, low_ref, plane)
     source = source_ext[...]
     codes = codes_ext[...]
@@ -173,6 +173,7 @@
     ext_x, ext_y = rows + 2 * h, cols + LANE_PAD
     rows_halo, high, low = halo_pieces(source, perm_classes, h)
     smem = pl.BlockSpec(memory_space=pltpu.MemorySpace.SMEM)
+    vmem = pl.BlockSpec(memory_space=pltpu.MemorySpace.VMEM)
     whole = lambda shape: pl.BlockSpec(shape, lambda s: (0,) * len(shape))
     solution_block, correction_block = pl.pallas_call(
         smooth_kernel,
@@ -182,10 +183,9 @@
             smem,
             pl.BlockSpec((PER_STEP, rows, cols), lambda s: (s, 0, 0)),
             whole((rows, cols)),
-            pl.BlockSpec((PER_STEP, 2 * h, cols), lambda s: (s, 0, 0)),
-            pl.BlockSpec((1, 2 * h, cols), lambda s: (count, 0, 0)),
-            whole((ext_x, LANE_PAD)),
-            whole((ext_x, LANE_PAD)),
+            vmem,
+            vmem,
+            vmem,
         ],
         out_specs=[
             pl.BlockSpec((PER_STEP, rows, cols), lambda s: (s, 0, 0)),
@@ -202,7 +202,7 @@
             pltpu.VMEM((cols // 128, rows, 128), jnp.float32),
         ],
         compiler_params=pltpu.CompilerParams(dimension_semantics=("arbitrary",)),
-    )(sample_seeds, perm_levels, source, perm_classes, rows_halo, rows_halo, high, low)
+    )(sample_seeds, perm_levels, source, perm_classes, rows_halo, high, low)
     return solution_block, correction_block
 
 

time: 30.4 us -> 30.4 us (level)
  no operation moved by 1% of the time
where the time goes in v9:
time: 30.4 us; the launch traced here: 30.1 us
  starting transfers between devices  10.2 us (34%)
  Pallas kernels  10.1 us (33%)
  waiting for transfers between devices  5.01 us (16%)
  local copies, waits for them, and re-layouts  3.1 us (10%)
  other arithmetic  0.98 us (3%)
  between operations  0.78 us (3%)
    pallas_call x1, Pallas kernels, shards(): pl.pallas_call(smooth_kernel, grid=(count // PER_STEP,), in_specs=[smem,...  10.1 us
    ppermute x1, starting transfers between devices, halo_pieces(): lax.ppermute(stack(source[:, -width:, :], classes[-width:, :]), 'gx', [(i...  3.48 us
    ppermute x1, waiting for transfers between devices, halo_pieces(): lax.ppermute(last, 'gy', [(i, i + 1) for i in range(lax.axis_size('gy') -...  2.89 us
    ppermute x1, starting transfers between devices, halo_pieces(): lax.ppermute(last, 'gy', [(i, i + 1) for i in range(lax.axis_size('gy') -...  2.4 us
    ppermute x1, starting transfers between devices, halo_pieces(): lax.ppermute(stack(source[:, :width, :], classes[:width, :]), 'gx', [(i +...  2.36 us
    ppermute x1, waiting for transfers between devices, halo_pieces(): lax.ppermute(stack(source[:, -width:, :], classes[-width:, :]), 'gx', [(i...  2.12 us
    ppermute x1, starting transfers between devices, halo_pieces(): lax.ppermute(first, 'gy', [(i + 1, i) for i in range(lax.axis_size('gy')...  1.92 us
    unnamed x15, local copies, waits for them, and re-layouts  1.59 us
  transfers between devices with their start and end apart: 4, of which 2 were waited for; matrix products, arithmetic and copies ran while one was open for 2% of the time, Pallas kernels for 0%

profile of v9, /device:TPU:18, one launch (start us, length us, event | category | flops | bytes accessed | tf_op | source)
XLA Modules:
  0.0 30.1 jit_solution(8396242235358025341)
XLA Ops:
  0.6 0.0 copy-start
  0.6 0.8 %convert_bitcast_fusion = (f32[1,8,256]{2,1,0:T(8,128)S(1)}, f32[1,8,256]{2,1,0:T(8,128)S(1)}) fusion(s32[64,256]{1,0:T(8,128)} %cls_ref.1), kind=kLoop, calls=%fused_computation.4 | loop fusion | flops 8192 | bytes 32768 | tf_op jit(solution)/shard_map/broadcast_in_dim | solution.py:17
  1.4 0.9 %fusion.1 = (f32[8,8,256]{2,1,0:T(8,128)S(1)}, f32[8,8,256]{2,1,0:T(8,128)S(1)}) fusion(f32[8,64,256]{2,1,0:T(8,128)} %src_ref.1), kind=kLoop, calls=%fused_computation.11 | loop fusion | bytes 262144 | tf_op jit(solution)/shard_map/slice | solution.py:19
  2.3 2.4 %collective-permute-start = (f32[9,8,256]{2,1,0:T(8,128)S(1)}, f32[9,8,256]{2,1,0:T(8,128)S(1)}, u32[]{:S(2)}, u32[]{:S(2)}) collective-permute-start(f32[9,8,256]{2,1,0:T(8,128)S(1)} %pad_maximum_fusion), channel_id=1, source_target_pairs={{8,0},{16,8},{24,16},{9,1},{17,9},{25,17},{10,2},{18,10},{26,18},{... | collective-permute-start | bytes 221192 | tf_op jit(solution)/shard_map/ppermute | solution.py:22
  4.7 0.0 copy-start.2
  4.7 3.5 %collective-permute-start.1 = (f32[9,8,256]{2,1,0:T(8,128)S(1)}, f32[9,8,256]{2,1,0:T(8,128)S(1)}, u32[]{:S(2)}, u32[]{:S(2)}) collective-permute-start(f32[9,8,256]{2,1,0:T(8,128)S(1)} %pad_maximum_fusion.1), channel_id=1, source_target_pairs={{0,8},{8,16},{16,24},{1,9},{9,17},{17,25},{2,10},{10,18},{18,26},{... | collective-permute-start | bytes 221192 | tf_op jit(solution)/shard_map/ppermute | solution.py:18
  8.2 0.0 copy-done.2
  8.2 0.1 fusion.3
  8.3 0.0 copy-done
  8.3 0.1 fusion
  8.4 0.1 copy.19
  8.5 0.1 copy.17
  8.6 0.1 copy.18
  8.7 0.1 copy.16
  8.8 0.0 collective-permute-done
  8.8 2.1 %collective-permute-done.1 = f32[9,8,256]{2,1,0:T(8,128)S(1)} collective-permute-done((f32[9,8,256]{2,1,0:T(8,128)S(1)}, f32[9,8,256]{2,1,0:T(8,128)S(1)}, u32[]{:S(2)}, u32[]{:S(2)}) %collective-permute-start.1) | collective-permute-done | bytes 73760 | tf_op jit(solution)/shard_map/ppermute | solution.py:18
  11.0 0.0 copy-start.1
  11.0 0.1 fusion.2
  11.1 0.6 %copy-done.1 = f32[9,16,256]{2,1,0:T(8,128)} copy-done((f32[9,16,256]{2,1,0:T(8,128)}, f32[9,16,256]{2,1,0:T(8,128)S(1)}, u32[]{:S(2)}) %copy-start.1) | copy-done | bytes 147480
  11.6 0.1 copy.14
  11.7 0.1 copy.10
  11.8 0.1 maximum_bitcast_fusion.1
  11.9 0.1 copy.15
  12.0 0.1 maximum_bitcast_fusion
  12.0 0.1 copy.11
  12.2 1.9 %collective-permute-start.2 = (f32[80,128]{1,0:T(8,128)S(1)}, f32[80,128]{1,0:T(8,128)S(1)}, u32[]{:S(2)}, u32[]{:S(2)}) collective-permute-start(f32[80,128]{1,0:T(8,128)S(1)} %pad.7), channel_id=1, source_target_pairs={{2,0},{4,2},{6,4},{3,1},{5,3},{7,5},{10,8},{12,10},{14,12},{11,9},... | collective-permute-start | bytes 122888 | tf_op jit(solution)/shard_map/ppermute | solution.py:37
  14.1 2.4 %collective-permute-start.3 = (f32[80,128]{1,0:T(8,128)S(1)}, f32[80,128]{1,0:T(8,128)S(1)}, u32[]{:S(2)}, u32[]{:S(2)}) collective-permute-start(f32[80,128]{1,0:T(8,128)S(1)} %pad.8), channel_id=1, source_target_pairs={{0,2},{2,4},{4,6},{1,3},{3,5},{5,7},{8,10},{10,12},{12,14},{9,11},... | collective-permute-start | bytes 122888 | tf_op jit(solution)/shard_map/ppermute | solution.py:36
  16.5 0.0 collective-permute-done.2.high_ref
  16.5 0.0 copy-start.3
  16.5 2.9 %collective-permute-done.3.low_ref = f32[80,128]{1,0:T(8,128)S(1)} collective-permute-done((f32[80,128]{1,0:T(8,128)S(1)}, f32[80,128]{1,0:T(8,128)S(1)}, u32[]{:S(2)}, u32[]{:S(2)}) %collective-permute-start.3) | collective-permute-done | bytes 40992 | tf_op jit(solution)/shard_map/ppermute | solution.py:36
  19.4 0.0 copy-done.3
  19.4 0.0 copy-start.4
  19.4 0.6 %copy-done.4 = f32[80,128]{1,0:T(8,128)} copy-done((f32[80,128]{1,0:T(8,128)}, f32[80,128]{1,0:T(8,128)S(1)}, u32[]{:S(2)}) %copy-start.4) | copy-done | bytes 40984
  20.0 10.1 %shard_map.59 = (f32[8,64,256]{2,1,0:T(8,128)}, f32[8,32,128]{2,1,0:T(8,128)}) custom-call(s32[8]{0:T(128)} %seeds_ref.1, f32[8,8]{1,0:T(8,128)} %levels_ref.1, f32[8,64,256]{2,1,0:T(8,128)} %src_ref.1, s32[64,256]{1,0:T(8,128)} %cls_ref.1, f32[9,16,256]{2,1,0:T(8,128)} %copy-done.1, f32[80,128]{1,0:T(8,128)} %copy-done.3, f32[80,128]{1,0:T(8,128)} %copy-done.4), custom_call_target="tpu_custom_call" | custom-call | tf_op jit(solution)/shard_map/pallas_call | solution.py:178
  (8 shorter events, 0.1 us)
Async XLA Ops:
  0.6 7.7 %copy-start = (f32[8,64,256]{2,1,0:T(8,128)S(1)}, f32[8,64,256]{2,1,0:T(8,128)}, u32[]{:S(2)}) copy-start(f32[8,64,256]{2,1,0:T(8,128)} %src_ref.1) | copy-start | bytes 1572868
  2.3 6.5 %collective-permute-start = (f32[9,8,256]{2,1,0:T(8,128)S(1)}, f32[9,8,256]{2,1,0:T(8,128)S(1)}, u32[]{:S(2)}, u32[]{:S(2)}) collective-permute-start(f32[9,8,256]{2,1,0:T(8,128)S(1)} %pad_maximum_fusion), channel_id=1, source_target_pairs={{8,0},{16,8},{24,16},{9,1},{17,9},{25,17},{10,2},{18,10},{26,18},{... | collective-permute-start | bytes 221192 | tf_op jit(solution)/shard_map/ppermute | solution.py:22
  4.7 3.5 %copy-start.2 = (s32[64,256]{1,0:T(8,128)S(1)}, s32[64,256]{1,0:T(8,128)}, u32[]{:S(2)}) copy-start(s32[64,256]{1,0:T(8,128)} %cls_ref.1) | copy-start | bytes 196612
  4.7 6.2 %collective-permute-start.1 = (f32[9,8,256]{2,1,0:T(8,128)S(1)}, f32[9,8,256]{2,1,0:T(8,128)S(1)}, u32[]{:S(2)}, u32[]{:S(2)}) collective-permute-start(f32[9,8,256]{2,1,0:T(8,128)S(1)} %pad_maximum_fusion.1), channel_id=1, source_target_pairs={{0,8},{8,16},{16,24},{1,9},{9,17},{17,25},{2,10},{10,18},{18,26},{... | collective-permute-start | bytes 221192 | tf_op jit(solution)/shard_map/ppermute | solution.py:18
  11.0 0.7 %copy-start.1 = (f32[9,16,256]{2,1,0:T(8,128)}, f32[9,16,256]{2,1,0:T(8,128)S(1)}, u32[]{:S(2)}) copy-start(f32[9,16,256]{2,1,0:T(8,128)S(1)} %constant_dynamic-update-slice_fusion.rows_ref) | copy-start | bytes 442372
  12.2 4.3 %collective-permute-start.2 = (f32[80,128]{1,0:T(8,128)S(1)}, f32[80,128]{1,0:T(8,128)S(1)}, u32[]{:S(2)}, u32[]{:S(2)}) collective-permute-start(f32[80,128]{1,0:T(8,128)S(1)} %pad.7), channel_id=1, source_target_pairs={{2,0},{4,2},{6,4},{3,1},{5,3},{7,5},{10,8},{12,10},{14,12},{11,9},... | collective-permute-start | bytes 122888 | tf_op jit(solution)/shard_map/ppermute | solution.py:37
  14.1 5.3 %collective-permute-start.3 = (f32[80,128]{1,0:T(8,128)S(1)}, f32[80,128]{1,0:T(8,128)S(1)}, u32[]{:S(2)}, u32[]{:S(2)}) collective-permute-start(f32[80,128]{1,0:T(8,128)S(1)} %pad.8), channel_id=1, source_target_pairs={{0,2},{2,4},{4,6},{1,3},{3,5},{5,7},{8,10},{10,12},{12,14},{9,11},... | collective-permute-start | bytes 122888 | tf_op jit(solution)/shard_map/ppermute | solution.py:36
  16.5 2.9 %copy-start.3 = (f32[80,128]{1,0:T(8,128)}, f32[80,128]{1,0:T(8,128)S(1)}, u32[]{:S(2)}) copy-start(f32[80,128]{1,0:T(8,128)S(1)} %collective-permute-done.2.high_ref) | copy-start | bytes 122884
  19.4 0.6 %copy-start.4 = (f32[80,128]{1,0:T(8,128)}, f32[80,128]{1,0:T(8,128)S(1)}, u32[]{:S(2)}) copy-start(f32[80,128]{1,0:T(8,128)S(1)} %collective-permute-done.3.low_ref) | copy-start | bytes 122884

commit v10 on v9

--- a/solution.py
+++ b/solution.py
@@ -10,7 +10,7 @@
 HALO = 8
 LANE_PAD = 128
 HI = lax.Precision.HIGHEST
-PER_STEP = 2
+PER_STEP = 4
 
 
 def halo_pieces(source, classes, width):
@@ -74,58 +74,72 @@
     )
 
 
-def lane_tile(high_ref, low_ref, plane):
+def lane_tiles(high_ref, low_ref, plane):
     high = high_ref[...]
     low = low_ref[...]
     lane = lax.broadcasted_iota(jnp.int32, high.shape, 1)
     after = pltpu.roll(high, (LANE_PAD - HALO * plane) % LANE_PAD, 1)
     before = pltpu.roll(low, (LANE_PAD - HALO - HALO * plane) % LANE_PAD, 1)
-    return jnp.where(lane < HALO, after, jnp.where(lane >= LANE_PAD - HALO, before, 0.0))
+    zero = jnp.zeros_like(high)
+    return jnp.where(lane < HALO, after, zero), jnp.where(lane >= LANE_PAD - HALO, before, zero)
+
+
+def base_layout(own, halo_rows, after, before, width):
+    top = jnp.concatenate([own, halo_rows], axis=0)
+    gap = jnp.zeros((top.shape[0], width - top.shape[1] - 2 * LANE_PAD), top.dtype)
+    return jnp.concatenate([top, after, gap, before], axis=1)
 
 
 def smooth_kernel(
     seeds_ref, levels_ref, src_ref, cls_ref, rows_ref, high_ref, low_ref,
-    sol_ref, corr_ref, source_ext, codes_ext, spare, wide,
+    sol_ref, corr_ref, codes_pk, spare, wide,
 ):
     s = pl.program_id(0)
     count = PER_STEP * pl.num_programs(0)
     rows, cols = sol_ref.shape[1], sol_ref.shape[2]
-    ext_x, ext_y = source_ext.shape
+    ext_x, width = codes_pk.shape
+    span = cols + 2 * HALO
+    lane = lax.broadcasted_iota(jnp.int32, (ext_x, width), 1)
+
+    def packed(pieces):
+        out = None
+        for j, piece in enumerate(pieces):
+            moved = pltpu.roll(piece, (j * span + HALO) % width, 1)
+            out = moved if out is None else jnp.where(lane >= j * span, moved, out)
+        return out
 
     @pl.when(s == 0)
     def _():
-        codes_ext[:rows, :cols] = cls_ref[...] + 1
-        codes_ext[rows:, :cols] = rows_ref[count].astype(jnp.int32)
-        codes_ext[:, cols:] = lane_tile(high_ref, low_ref, count).astype(jnp.int32)
-
+        after, before = lane_tiles(high_ref, low_ref, count)
+        own = base_layout(
+            cls_ref[...] + 1, rows_ref[count].astype(jnp.int32),
+            after.astype(jnp.int32), before.astype(jnp.int32), width,
+        )
+        codes_pk[...] = packed([own] * PER_STEP)
+
+    pieces = []
     for j in range(PER_STEP):
-        one_sample(
-            PER_STEP * s + j, j, seeds_ref, levels_ref, src_ref, rows_ref, high_ref, low_ref,
-            sol_ref, corr_ref, source_ext, codes_ext, spare, wide,
-        )
-
-
-def one_sample(
-    plane, j, seeds_ref, levels_ref, src_ref, rows_ref, high_ref, low_ref,
-    sol_ref, corr_ref, source_ext, codes_ext, spare, wide,
-):
-    rows, cols = sol_ref.shape[1], sol_ref.shape[2]
-    ext_x, ext_y = source_ext.shape
-    source_ext[:rows, :cols] = src_ref[j]
-    source_ext[rows:, :cols] = rows_ref[plane]
-    source_ext[:, cols:] = lane_tile(high_ref, low_ref, plane)
-    source = source_ext[...]
-    codes = codes_ext[...]
+        plane = PER_STEP * s + j
+        after, before = lane_tiles(high_ref, low_ref, plane)
+        pieces.append(base_layout(src_ref[j], rows_ref[plane], after, before, width))
+    source = packed(pieces)
+    codes = codes_pk[...]
     valid = codes > 0
-    classes = codes - 1
-    seed = seeds_ref[plane]
-    level = [levels_ref[seed, category] for category in range(levels_ref.shape[1])]
+    classes = (codes - 1).reshape(ext_x // 8, 8, width)
+    row_lane = lax.broadcasted_iota(jnp.int32, (8, width), 1)
+    level = []
+    for category in range(levels_ref.shape[1]):
+        row = jnp.full((8, width), levels_ref[seeds_ref[PER_STEP * s], category], jnp.float32)
+        for j in range(1, PER_STEP):
+            pick_level = levels_ref[seeds_ref[PER_STEP * s + j], category]
+            row = jnp.where(row_lane >= j * span, pick_level, row)
+        level.append(row[None])
     bit0 = (classes & 1) != 0
     bit1 = (classes & 2) != 0
     bit2 = (classes & 4) != 0
     low = jnp.where(bit1, jnp.where(bit0, level[3], level[2]), jnp.where(bit0, level[1], level[0]))
     high = jnp.where(bit1, jnp.where(bit0, level[7], level[6]), jnp.where(bit0, level[5], level[4]))
-    perm = jnp.where(valid, jnp.where(bit2, high, low), 0.0)
+    perm = jnp.where(valid, jnp.where(bit2, high, low).reshape(ext_x, width), 0.0)
     linkage, diagonal = couplings(perm, (1, 1))
     inverse = 1.0 / jnp.where(valid, diagonal, 1.0)
     current = (DAMPING * source) * inverse
@@ -135,42 +149,45 @@
             current = current + (DAMPING * residual) * inverse
 
     def even_rows(v):
-        pieces = []
-        for k in range(ext_y // 128):
+        parts = []
+        for k in range(width // 128):
             spare[k] = v[:, k * 128 : (k + 1) * 128]
-            pieces.append(spare[k, pl.ds(0, ext_x // 2, stride=2), :])
-        return jnp.concatenate(pieces, axis=1)
+            parts.append(spare[k, pl.ds(0, ext_x // 2, stride=2), :])
+        return jnp.concatenate(parts, axis=1)
 
     pairs = residual + pltpu.roll(residual, ext_x - 1, 0)
-    coarse_rhs = even_rows(pairs + pltpu.roll(pairs, ext_y - 1, 1))
+    coarse_rhs = even_rows(pairs + pltpu.roll(pairs, width - 1, 1))
     pairs = perm + pltpu.roll(perm, ext_x - 1, 0)
-    coarse_perm = 0.25 * even_rows(pairs + pltpu.roll(pairs, ext_y - 1, 1))
+    coarse_perm = 0.25 * even_rows(pairs + pltpu.roll(pairs, width - 1, 1))
     coarse_links, coarse_diagonal = couplings(coarse_perm, (1, 2))
     coarse_inverse = 1.0 / jnp.where(coarse_perm > 0.0, coarse_diagonal, 1.0)
     first = (DAMPING * coarse_rhs) * coarse_inverse
     correction = first + (
         DAMPING * (coarse_rhs - operator(coarse_links, coarse_diagonal, first, (1, 2)))
     ) * coarse_inverse
-    own = correction[: rows // 2, :cols]
     pick = (
         lax.broadcasted_iota(jnp.int32, (cols, cols // 2), 0)
         == 2 * lax.broadcasted_iota(jnp.int32, (cols, cols // 2), 1)
     ).astype(jnp.float32)
-    corr_ref[j] = jnp.dot(own, pick, precision=HI, preferred_element_type=jnp.float32)
-    for k in range(cols // 128):
-        piece = own[:, k * 128 : (k + 1) * 128]
-        wide[k, pl.ds(0, rows // 2, stride=2), :] = piece
-        wide[k, pl.ds(1, rows // 2, stride=2), :] = piece
-    spread = jnp.concatenate([wide[k] for k in range(cols // 128)], axis=1)
     odd_col = (lax.broadcasted_iota(jnp.int32, (rows, cols), 1) & 1) == 1
-    spread = jnp.where(odd_col, pltpu.roll(spread, 1, 1), spread)
-    sol_ref[j] = current[:rows, :cols] + spread
+    for j in range(PER_STEP):
+        back = (width - j * span - HALO) % width
+        own = pltpu.roll(correction, back, 1)[: rows // 2, :cols]
+        corr_ref[j] = jnp.dot(own, pick, precision=HI, preferred_element_type=jnp.float32)
+        for k in range(cols // 128):
+            piece = own[:, k * 128 : (k + 1) * 128]
+            wide[k, pl.ds(0, rows // 2, stride=2), :] = piece
+            wide[k, pl.ds(1, rows // 2, stride=2), :] = piece
+        spread = jnp.concatenate([wide[k] for k in range(cols // 128)], axis=1)
+        spread = jnp.where(odd_col, pltpu.roll(spread, 1, 1), spread)
+        sol_ref[j] = pltpu.roll(current, back, 1)[:rows, :cols] + spread
 
 
 def shards(source, sample_seeds, perm_levels, perm_classes):
     h = HALO
     count, rows, cols = source.shape
-    ext_x, ext_y = rows + 2 * h, cols + LANE_PAD
+    ext_x = rows + 2 * h
+    width = -(-(PER_STEP * (cols + 2 * h)) // 128) * 128
     rows_halo, high, low = halo_pieces(source, perm_classes, h)
     smem = pl.BlockSpec(memory_space=pltpu.MemorySpace.SMEM)
     vmem = pl.BlockSpec(memory_space=pltpu.MemorySpace.VMEM)
@@ -196,9 +213,8 @@
             jax.ShapeDtypeStruct((count, rows // 2, cols // 2), jnp.float32),
         ],
         scratch_shapes=[
-            pltpu.VMEM((ext_x, ext_y), jnp.float32),
-            pltpu.VMEM((ext_x, ext_y), jnp.int32),
-            pltpu.VMEM((ext_y // 128, ext_x, 128), jnp.float32),
+            pltpu.VMEM((ext_x, width), jnp.int32),
+            pltpu.VMEM((width // 128, ext_x, 128), jnp.float32),
             pltpu.VMEM((cols // 128, rows, 128), jnp.float32),
         ],
         compiler_params=pltpu.CompilerParams(dimension_semantics=("arbitrary",)),

time: 30.4 us -> 29 us (0.954)
  Pallas kernels: 10.1 us -> 8.71 us
    pallas_call x1, Pallas kernels: 10.1 us -> 8.71 us  [shards(): pl.pallas_call(smooth_kernel, grid=(count // PER_STEP,), in_specs=[smem,...]
where the time goes in v10:
time: 29 us; the launch traced here: 28.7 us
  starting transfers between devices  10.2 us (35%)
  Pallas kernels  8.71 us (30%)
  waiting for transfers between devices  5.01 us (17%)
  local copies, waits for them, and re-layouts  3.1 us (11%)
  other arithmetic  0.98 us (3%)
  between operations  0.78 us (3%)
    pallas_call x1, Pallas kernels, shards(): pl.pallas_call(smooth_kernel, grid=(count // PER_STEP,), in_specs=[smem,...  8.71 us
    ppermute x1, starting transfers between devices, halo_pieces(): lax.ppermute(stack(source[:, -width:, :], classes[-width:, :]), 'gx', [(i...  3.48 us
    ppermute x1, waiting for transfers between devices, halo_pieces(): lax.ppermute(last, 'gy', [(i, i + 1) for i in range(lax.axis_size('gy') -...  2.89 us
    ppermute x1, starting transfers between devices, halo_pieces(): lax.ppermute(last, 'gy', [(i, i + 1) for i in range(lax.axis_size('gy') -...  2.4 us
    ppermute x1, starting transfers between devices, halo_pieces(): lax.ppermute(stack(source[:, :width, :], classes[:width, :]), 'gx', [(i +...  2.36 us
    ppermute x1, waiting for transfers between devices, halo_pieces(): lax.ppermute(stack(source[:, -width:, :], classes[-width:, :]), 'gx', [(i...  2.12 us
    ppermute x1, starting transfers between devices, halo_pieces(): lax.ppermute(first, 'gy', [(i + 1, i) for i in range(lax.axis_size('gy')...  1.92 us
    unnamed x15, local copies, waits for them, and re-layouts  1.59 us
  transfers between devices with their start and end apart: 4, of which 2 were waited for; matrix products, arithmetic and copies ran while one was open for 2% of the time, Pallas kernels for 0%

profile of v10, /device:TPU:18, one launch (start us, length us, event | category | flops | bytes accessed | tf_op | source)
XLA Modules:
  0.0 28.7 jit_solution(15212880482796361543)
XLA Ops:
  0.6 0.0 copy-start
  0.6 0.8 %convert_bitcast_fusion = (f32[1,8,256]{2,1,0:T(8,128)S(1)}, f32[1,8,256]{2,1,0:T(8,128)S(1)}) fusion(s32[64,256]{1,0:T(8,128)} %cls_ref.1), kind=kLoop, calls=%fused_computation.4 | loop fusion | flops 8192 | bytes 32768 | tf_op jit(solution)/shard_map/broadcast_in_dim | solution.py:17
  1.4 0.9 %fusion.1 = (f32[8,8,256]{2,1,0:T(8,128)S(1)}, f32[8,8,256]{2,1,0:T(8,128)S(1)}) fusion(f32[8,64,256]{2,1,0:T(8,128)} %src_ref.1), kind=kLoop, calls=%fused_computation.11 | loop fusion | bytes 262144 | tf_op jit(solution)/shard_map/slice | solution.py:19
  2.3 2.4 %collective-permute-start = (f32[9,8,256]{2,1,0:T(8,128)S(1)}, f32[9,8,256]{2,1,0:T(8,128)S(1)}, u32[]{:S(2)}, u32[]{:S(2)}) collective-permute-start(f32[9,8,256]{2,1,0:T(8,128)S(1)} %pad_maximum_fusion), channel_id=1, source_target_pairs={{8,0},{16,8},{24,16},{9,1},{17,9},{25,17},{10,2},{18,10},{26,18},{... | collective-permute-start | bytes 221192 | tf_op jit(solution)/shard_map/ppermute | solution.py:22
  4.7 0.0 copy-start.2
  4.7 3.5 %collective-permute-start.1 = (f32[9,8,256]{2,1,0:T(8,128)S(1)}, f32[9,8,256]{2,1,0:T(8,128)S(1)}, u32[]{:S(2)}, u32[]{:S(2)}) collective-permute-start(f32[9,8,256]{2,1,0:T(8,128)S(1)} %pad_maximum_fusion.1), channel_id=1, source_target_pairs={{0,8},{8,16},{16,24},{1,9},{9,17},{17,25},{2,10},{10,18},{18,26},{... | collective-permute-start | bytes 221192 | tf_op jit(solution)/shard_map/ppermute | solution.py:18
  8.2 0.0 copy-done.2
  8.2 0.1 fusion.3
  8.3 0.0 copy-done
  8.3 0.1 fusion
  8.4 0.1 copy.19
  8.5 0.1 copy.17
  8.6 0.1 copy.18
  8.7 0.1 copy.16
  8.8 0.0 collective-permute-done
  8.8 2.1 %collective-permute-done.1 = f32[9,8,256]{2,1,0:T(8,128)S(1)} collective-permute-done((f32[9,8,256]{2,1,0:T(8,128)S(1)}, f32[9,8,256]{2,1,0:T(8,128)S(1)}, u32[]{:S(2)}, u32[]{:S(2)}) %collective-permute-start.1) | collective-permute-done | bytes 73760 | tf_op jit(solution)/shard_map/ppermute | solution.py:18
  11.0 0.0 copy-start.1
  11.0 0.1 fusion.2
  11.1 0.6 %copy-done.1 = f32[9,16,256]{2,1,0:T(8,128)} copy-done((f32[9,16,256]{2,1,0:T(8,128)}, f32[9,16,256]{2,1,0:T(8,128)S(1)}, u32[]{:S(2)}) %copy-start.1) | copy-done | bytes 147480
  11.6 0.1 copy.14
  11.7 0.1 copy.10
  11.8 0.1 maximum_bitcast_fusion.1
  11.9 0.1 copy.15
  12.0 0.1 maximum_bitcast_fusion
  12.0 0.1 copy.11
  12.2 1.9 %collective-permute-start.2 = (f32[80,128]{1,0:T(8,128)S(1)}, f32[80,128]{1,0:T(8,128)S(1)}, u32[]{:S(2)}, u32[]{:S(2)}) collective-permute-start(f32[80,128]{1,0:T(8,128)S(1)} %pad.7), channel_id=1, source_target_pairs={{2,0},{4,2},{6,4},{3,1},{5,3},{7,5},{10,8},{12,10},{14,12},{11,9},... | collective-permute-start | bytes 122888 | tf_op jit(solution)/shard_map/ppermute | solution.py:37
  14.1 2.4 %collective-permute-start.3 = (f32[80,128]{1,0:T(8,128)S(1)}, f32[80,128]{1,0:T(8,128)S(1)}, u32[]{:S(2)}, u32[]{:S(2)}) collective-permute-start(f32[80,128]{1,0:T(8,128)S(1)} %pad.8), channel_id=1, source_target_pairs={{0,2},{2,4},{4,6},{1,3},{3,5},{5,7},{8,10},{10,12},{12,14},{9,11},... | collective-permute-start | bytes 122888 | tf_op jit(solution)/shard_map/ppermute | solution.py:36
  16.5 0.0 collective-permute-done.2.high_ref
  16.5 0.0 copy-start.3
  16.5 2.9 %collective-permute-done.3.low_ref = f32[80,128]{1,0:T(8,128)S(1)} collective-permute-done((f32[80,128]{1,0:T(8,128)S(1)}, f32[80,128]{1,0:T(8,128)S(1)}, u32[]{:S(2)}, u32[]{:S(2)}) %collective-permute-start.3) | collective-permute-done | bytes 40992 | tf_op jit(solution)/shard_map/ppermute | solution.py:36
  19.4 0.0 copy-done.3
  19.4 0.0 copy-start.4
  19.4 0.6 %copy-done.4 = f32[80,128]{1,0:T(8,128)} copy-done((f32[80,128]{1,0:T(8,128)}, f32[80,128]{1,0:T(8,128)S(1)}, u32[]{:S(2)}) %copy-start.4) | copy-done | bytes 40984
  20.0 8.7 %shard_map.59 = (f32[8,64,256]{2,1,0:T(8,128)}, f32[8,32,128]{2,1,0:T(8,128)}) custom-call(s32[8]{0:T(128)} %seeds_ref.1, f32[8,8]{1,0:T(8,128)} %levels_ref.1, f32[8,64,256]{2,1,0:T(8,128)} %src_ref.1, s32[64,256]{1,0:T(8,128)} %cls_ref.1, f32[9,16,256]{2,1,0:T(8,128)} %copy-done.1, f32[80,128]{1,0:T(8,128)} %copy-done.3, f32[80,128]{1,0:T(8,128)} %copy-done.4), custom_call_target="tpu_custom_call" | custom-call | tf_op jit(solution)/shard_map/pallas_call | solution.py:195
  (8 shorter events, 0.1 us)
Async XLA Ops:
  0.6 7.7 %copy-start = (f32[8,64,256]{2,1,0:T(8,128)S(1)}, f32[8,64,256]{2,1,0:T(8,128)}, u32[]{:S(2)}) copy-start(f32[8,64,256]{2,1,0:T(8,128)} %src_ref.1) | copy-start | bytes 1572868
  2.3 6.5 %collective-permute-start = (f32[9,8,256]{2,1,0:T(8,128)S(1)}, f32[9,8,256]{2,1,0:T(8,128)S(1)}, u32[]{:S(2)}, u32[]{:S(2)}) collective-permute-start(f32[9,8,256]{2,1,0:T(8,128)S(1)} %pad_maximum_fusion), channel_id=1, source_target_pairs={{8,0},{16,8},{24,16},{9,1},{17,9},{25,17},{10,2},{18,10},{26,18},{... | collective-permute-start | bytes 221192 | tf_op jit(solution)/shard_map/ppermute | solution.py:22
  4.7 3.5 %copy-start.2 = (s32[64,256]{1,0:T(8,128)S(1)}, s32[64,256]{1,0:T(8,128)}, u32[]{:S(2)}) copy-start(s32[64,256]{1,0:T(8,128)} %cls_ref.1) | copy-start | bytes 196612
  4.7 6.2 %collective-permute-start.1 = (f32[9,8,256]{2,1,0:T(8,128)S(1)}, f32[9,8,256]{2,1,0:T(8,128)S(1)}, u32[]{:S(2)}, u32[]{:S(2)}) collective-permute-start(f32[9,8,256]{2,1,0:T(8,128)S(1)} %pad_maximum_fusion.1), channel_id=1, source_target_pairs={{0,8},{8,16},{16,24},{1,9},{9,17},{17,25},{2,10},{10,18},{18,26},{... | collective-permute-start | bytes 221192 | tf_op jit(solution)/shard_map/ppermute | solution.py:18
  11.0 0.7 %copy-start.1 = (f32[9,16,256]{2,1,0:T(8,128)}, f32[9,16,256]{2,1,0:T(8,128)S(1)}, u32[]{:S(2)}) copy-start(f32[9,16,256]{2,1,0:T(8,128)S(1)} %constant_dynamic-update-slice_fusion.rows_ref) | copy-start | bytes 442372
  12.2 4.3 %collective-permute-start.2 = (f32[80,128]{1,0:T(8,128)S(1)}, f32[80,128]{1,0:T(8,128)S(1)}, u32[]{:S(2)}, u32[]{:S(2)}) collective-permute-start(f32[80,128]{1,0:T(8,128)S(1)} %pad.7), channel_id=1, source_target_pairs={{2,0},{4,2},{6,4},{3,1},{5,3},{7,5},{10,8},{12,10},{14,12},{11,9},... | collective-permute-start | bytes 122888 | tf_op jit(solution)/shard_map/ppermute | solution.py:37
  14.1 5.3 %collective-permute-start.3 = (f32[80,128]{1,0:T(8,128)S(1)}, f32[80,128]{1,0:T(8,128)S(1)}, u32[]{:S(2)}, u32[]{:S(2)}) collective-permute-start(f32[80,128]{1,0:T(8,128)S(1)} %pad.8), channel_id=1, source_target_pairs={{0,2},{2,4},{4,6},{1,3},{3,5},{5,7},{8,10},{10,12},{12,14},{9,11},... | collective-permute-start | bytes 122888 | tf_op jit(solution)/shard_map/ppermute | solution.py:36
  16.5 2.9 %copy-start.3 = (f32[80,128]{1,0:T(8,128)}, f32[80,128]{1,0:T(8,128)S(1)}, u32[]{:S(2)}) copy-start(f32[80,128]{1,0:T(8,128)S(1)} %collective-permute-done.2.high_ref) | copy-start | bytes 122884
  19.4 0.6 %copy-start.4 = (f32[80,128]{1,0:T(8,128)}, f32[80,128]{1,0:T(8,128)S(1)}, u32[]{:S(2)}) copy-start(f32[80,128]{1,0:T(8,128)S(1)} %collective-permute-done.3.low_ref) | copy-start | bytes 122884

commit v11 on v10

--- a/solution.py
+++ b/solution.py
@@ -13,16 +13,40 @@
 PER_STEP = 4
 
 
+def edge_rows_kernel(bottom_ref, top_ref, cls_bottom_ref, cls_top_ref, low_ref, high_ref):
+    count = bottom_ref.shape[0]
+    low_ref[:count] = bottom_ref[...]
+    low_ref[count] = (cls_bottom_ref[...] + 1).astype(jnp.float32)
+    high_ref[:count] = top_ref[...]
+    high_ref[count] = (cls_top_ref[...] + 1).astype(jnp.float32)
+
+
+def edge_rows(source, classes, width):
+    count, rows, cols = source.shape
+    last = rows // width - 1
+    piece = jax.ShapeDtypeStruct((count + 1, width, cols), jnp.float32)
+    return pl.pallas_call(
+        edge_rows_kernel,
+        grid=(1,),
+        in_specs=[
+            pl.BlockSpec((count, width, cols), lambda i: (0, last, 0)),
+            pl.BlockSpec((count, width, cols), lambda i: (0, 0, 0)),
+            pl.BlockSpec((width, cols), lambda i: (last, 0)),
+            pl.BlockSpec((width, cols), lambda i: (0, 0)),
+        ],
+        out_specs=[
+            pl.BlockSpec((count + 1, width, cols), lambda i: (0, 0, 0)),
+            pl.BlockSpec((count + 1, width, cols), lambda i: (0, 0, 0)),
+        ],
+        out_shape=[piece, piece],
+    )(source, source, classes, classes)
+
+
 def halo_pieces(source, classes, width):
     stack = lambda a, b: jnp.concatenate([a, (b + 1).astype(a.dtype)[None]], axis=0)
-    low = lax.ppermute(
-        stack(source[:, -width:, :], classes[-width:, :]), "gx",
-        [(i, i + 1) for i in range(lax.axis_size("gx") - 1)],
-    )
-    high = lax.ppermute(
-        stack(source[:, :width, :], classes[:width, :]), "gx",
-        [(i + 1, i) for i in range(lax.axis_size("gx") - 1)],
-    )
+    bottom, top = edge_rows(source, classes, width)
+    low = lax.ppermute(bottom, "gx", [(i, i + 1) for i in range(lax.axis_size("gx") - 1)])
+    high = lax.ppermute(top, "gx", [(i + 1, i) for i in range(lax.axis_size("gx") - 1)])
     rows_halo = jnp.concatenate([high, low], axis=1)
 
     def packed(strip, halo_strip):

time: 29 us -> 29.1 us (level)
  Pallas kernels: 8.71 us -> 10.3 us
  local copies, waits for them, and re-layouts: 3.1 us -> 2.23 us
  other arithmetic: 0.98 us -> 0.19 us
    pallas_call x0 -> x1, Pallas kernels: none -> 1.6 us  [edge_rows(): pl.pallas_call(edge_rows_kernel, grid=(1,), in_specs=[pl.BlockSpec((count...]
    slice x1 -> x0, local copies, waits for them, and re-layouts: 0.88 us -> none  [halo_pieces(): source[:, -width:, :]]
    broadcast_in_dim x3 -> x2, other arithmetic: 0.79 us -> 0.01 us  [halo_pieces(): (b + 1).astype(a.dtype)[None]]
where the time goes in v11:
time: 29.1 us; the launch traced here: 28.9 us
  Pallas kernels  10.3 us (35%)
  starting transfers between devices  10.2 us (35%)
  waiting for transfers between devices  5.22 us (18%)
  local copies, waits for them, and re-layouts  2.23 us (8%)
  between operations  0.76 us (3%)
    pallas_call x1, Pallas kernels, shards(): pl.pallas_call(smooth_kernel, grid=(count // PER_STEP,), in_specs=[smem,...  8.71 us
    ppermute x1, starting transfers between devices, halo_pieces(): lax.ppermute(bottom, 'gx', [(i, i + 1) for i in range(lax.axis_size('gx')...  3.48 us
    ppermute x1, waiting for transfers between devices, halo_pieces(): lax.ppermute(last, 'gy', [(i, i + 1) for i in range(lax.axis_size('gy') -...  2.89 us
    ppermute x1, starting transfers between devices, halo_pieces(): lax.ppermute(last, 'gy', [(i, i + 1) for i in range(lax.axis_size('gy') -...  2.4 us
    ppermute x1, starting transfers between devices, halo_pieces(): lax.ppermute(top, 'gx', [(i + 1, i) for i in range(lax.axis_size('gx') -...  2.35 us
    ppermute x1, waiting for transfers between devices, halo_pieces(): lax.ppermute(bottom, 'gx', [(i, i + 1) for i in range(lax.axis_size('gx')...  2.33 us
    ppermute x1, starting transfers between devices, halo_pieces(): lax.ppermute(first, 'gy', [(i + 1, i) for i in range(lax.axis_size('gy')...  1.92 us
    pallas_call x1, Pallas kernels, edge_rows(): pl.pallas_call(edge_rows_kernel, grid=(1,), in_specs=[pl.BlockSpec((count...  1.6 us
  transfers between devices with their start and end apart: 4, of which 2 were waited for; matrix products, arithmetic and copies ran while one was open for 2% of the time, Pallas kernels for 0%

profile of v11, /device:TPU:18, one launch (start us, length us, event | category | flops | bytes accessed | tf_op | source)
XLA Modules:
  0.0 28.9 jit_solution(17981353980706316449)
XLA Ops:
  0.6 0.0 copy-start.1
  0.6 0.0 copy-start
  0.7 1.6 %shard_map.59 = (f32[9,8,256]{2,1,0:T(8,128)}, f32[9,8,256]{2,1,0:T(8,128)}) custom-call(f32[8,64,256]{2,1,0:T(8,128)} %src_ref.1, f32[8,64,256]{2,1,0:T(8,128)} %src_ref.1, s32[64,256]{1,0:T(8,128)} %cls_ref.1, s32[64,256]{1,0:T(8,128)} %cls_ref.1), custom_call_target="tpu_custom_call" | custom-call | tf_op jit(solution)/shard_map/pallas_call | solution.py:28
  2.3 2.3 %collective-permute-start = (f32[9,8,256]{2,1,0:T(8,128)}, f32[9,8,256]{2,1,0:T(8,128)S(1)}, u32[]{:S(2)}, u32[]{:S(2)}) collective-permute-start(f32[9,8,256]{2,1,0:T(8,128)} %get-tuple-element.4), channel_id=1, source_target_pairs={{8,0},{16,8},{24,16},{9,1},{17,9},{25,17},{10,2},{18,10},{26,18},{... | collective-permute-start | bytes 221192 | tf_op jit(solution)/shard_map/ppermute | solution.py:49
  4.6 3.5 %collective-permute-start.1 = (f32[9,8,256]{2,1,0:T(8,128)}, f32[9,8,256]{2,1,0:T(8,128)S(1)}, u32[]{:S(2)}, u32[]{:S(2)}) collective-permute-start(f32[9,8,256]{2,1,0:T(8,128)} %get-tuple-element.5), channel_id=1, source_target_pairs={{0,8},{8,16},{16,24},{1,9},{9,17},{17,25},{2,10},{10,18},{18,26},{... | collective-permute-start | bytes 221192 | tf_op jit(solution)/shard_map/ppermute | solution.py:48
  8.1 0.0 copy-done.1
  8.1 0.1 fusion.2
  8.2 0.0 copy-done
  8.2 0.1 fusion
  8.3 0.1 copy.19
  8.4 0.1 copy.17
  8.5 0.1 copy.18
  8.6 0.1 copy.16
  8.7 0.0 collective-permute-done
  8.7 2.3 %collective-permute-done.1 = f32[9,8,256]{2,1,0:T(8,128)S(1)} collective-permute-done((f32[9,8,256]{2,1,0:T(8,128)}, f32[9,8,256]{2,1,0:T(8,128)S(1)}, u32[]{:S(2)}, u32[]{:S(2)}) %collective-permute-start.1) | collective-permute-done | bytes 73760 | tf_op jit(solution)/shard_map/ppermute | solution.py:48
  11.1 0.0 copy-start.2
  11.1 0.1 fusion.1
  11.2 0.6 %copy-done.2 = f32[9,16,256]{2,1,0:T(8,128)} copy-done((f32[9,16,256]{2,1,0:T(8,128)}, f32[9,16,256]{2,1,0:T(8,128)S(1)}, u32[]{:S(2)}) %copy-start.2) | copy-done | bytes 147480
  11.7 0.1 copy.14
  11.8 0.1 copy.10
  11.9 0.1 maximum_bitcast_fusion.1
  12.0 0.1 copy.15
  12.1 0.1 maximum_bitcast_fusion
  12.2 0.1 copy.11
  12.3 1.9 %collective-permute-start.2 = (f32[80,128]{1,0:T(8,128)S(1)}, f32[80,128]{1,0:T(8,128)S(1)}, u32[]{:S(2)}, u32[]{:S(2)}) collective-permute-start(f32[80,128]{1,0:T(8,128)S(1)} %pad.7), channel_id=1, source_target_pairs={{2,0},{4,2},{6,4},{3,1},{5,3},{7,5},{10,8},{12,10},{14,12},{11,9},... | collective-permute-start | bytes 122888 | tf_op jit(solution)/shard_map/ppermute | solution.py:61
  14.2 2.4 %collective-permute-start.3 = (f32[80,128]{1,0:T(8,128)S(1)}, f32[80,128]{1,0:T(8,128)S(1)}, u32[]{:S(2)}, u32[]{:S(2)}) collective-permute-start(f32[80,128]{1,0:T(8,128)S(1)} %pad.8), channel_id=1, source_target_pairs={{0,2},{2,4},{4,6},{1,3},{3,5},{5,7},{8,10},{10,12},{12,14},{9,11},... | collective-permute-start | bytes 122888 | tf_op jit(solution)/shard_map/ppermute | solution.py:60
  16.6 0.0 collective-permute-done.2.high_ref
  16.6 0.0 copy-start.3
  16.6 2.9 %collective-permute-done.3.low_ref = f32[80,128]{1,0:T(8,128)S(1)} collective-permute-done((f32[80,128]{1,0:T(8,128)S(1)}, f32[80,128]{1,0:T(8,128)S(1)}, u32[]{:S(2)}, u32[]{:S(2)}) %collective-permute-start.3) | collective-permute-done | bytes 40992 | tf_op jit(solution)/shard_map/ppermute | solution.py:60
  19.5 0.0 copy-done.3
  19.5 0.0 copy-start.4
  19.5 0.6 %copy-done.4 = f32[80,128]{1,0:T(8,128)} copy-done((f32[80,128]{1,0:T(8,128)}, f32[80,128]{1,0:T(8,128)S(1)}, u32[]{:S(2)}) %copy-start.4) | copy-done | bytes 40984
  20.2 8.7 %shard_map.60 = (f32[8,64,256]{2,1,0:T(8,128)}, f32[8,32,128]{2,1,0:T(8,128)}) custom-call(s32[8]{0:T(128)} %seeds_ref.1, f32[8,8]{1,0:T(8,128)} %levels_ref.1, f32[8,64,256]{2,1,0:T(8,128)} %src_ref.1, s32[64,256]{1,0:T(8,128)} %cls_ref.1, f32[9,16,256]{2,1,0:T(8,128)} %copy-done.2, f32[80,128]{1,0:T(8,128)} %copy-done.3, f32[80,128]{1,0:T(8,128)} %copy-done.4), custom_call_target="tpu_custom_call" | custom-call | tf_op jit(solution)/shard_map/pallas_call | solution.py:219
  (6 shorter events, 0.0 us)
Async XLA Ops:
  0.6 7.5 %copy-start.1 = (s32[64,256]{1,0:T(8,128)S(1)}, s32[64,256]{1,0:T(8,128)}, u32[]{:S(2)}) copy-start(s32[64,256]{1,0:T(8,128)} %cls_ref.1) | copy-start | bytes 196612
  0.6 7.5 %copy-start = (f32[8,64,256]{2,1,0:T(8,128)S(1)}, f32[8,64,256]{2,1,0:T(8,128)}, u32[]{:S(2)}) copy-start(f32[8,64,256]{2,1,0:T(8,128)} %src_ref.1) | copy-start | bytes 1572868
  2.3 6.5 %collective-permute-start = (f32[9,8,256]{2,1,0:T(8,128)}, f32[9,8,256]{2,1,0:T(8,128)S(1)}, u32[]{:S(2)}, u32[]{:S(2)}) collective-permute-start(f32[9,8,256]{2,1,0:T(8,128)} %get-tuple-element.4), channel_id=1, source_target_pairs={{8,0},{16,8},{24,16},{9,1},{17,9},{25,17},{10,2},{18,10},{26,18},{... | collective-permute-start | bytes 221192 | tf_op jit(solution)/shard_map/ppermute | solution.py:49
  4.6 6.5 %collective-permute-start.1 = (f32[9,8,256]{2,1,0:T(8,128)}, f32[9,8,256]{2,1,0:T(8,128)S(1)}, u32[]{:S(2)}, u32[]{:S(2)}) collective-permute-start(f32[9,8,256]{2,1,0:T(8,128)} %get-tuple-element.5), channel_id=1, source_target_pairs={{0,8},{8,16},{16,24},{1,9},{9,17},{17,25},{2,10},{10,18},{18,26},{... | collective-permute-start | bytes 221192 | tf_op jit(solution)/shard_map/ppermute | solution.py:48
  11.1 0.7 %copy-start.2 = (f32[9,16,256]{2,1,0:T(8,128)}, f32[9,16,256]{2,1,0:T(8,128)S(1)}, u32[]{:S(2)}) copy-start(f32[9,16,256]{2,1,0:T(8,128)S(1)} %constant_dynamic-update-slice_fusion.rows_ref) | copy-start | bytes 442372
  12.3 4.3 %collective-permute-start.2 = (f32[80,128]{1,0:T(8,128)S(1)}, f32[80,128]{1,0:T(8,128)S(1)}, u32[]{:S(2)}, u32[]{:S(2)}) collective-permute-start(f32[80,128]{1,0:T(8,128)S(1)} %pad.7), channel_id=1, source_target_pairs={{2,0},{4,2},{6,4},{3,1},{5,3},{7,5},{10,8},{12,10},{14,12},{11,9},... | collective-permute-start | bytes 122888 | tf_op jit(solution)/shard_map/ppermute | solution.py:61
  14.2 5.3 %collective-permute-start.3 = (f32[80,128]{1,0:T(8,128)S(1)}, f32[80,128]{1,0:T(8,128)S(1)}, u32[]{:S(2)}, u32[]{:S(2)}) collective-permute-start(f32[80,128]{1,0:T(8,128)S(1)} %pad.8), channel_id=1, source_target_pairs={{0,2},{2,4},{4,6},{1,3},{3,5},{5,7},{8,10},{10,12},{12,14},{9,11},... | collective-permute-start | bytes 122888 | tf_op jit(solution)/shard_map/ppermute | solution.py:60
  16.6 2.9 %copy-start.3 = (f32[80,128]{1,0:T(8,128)}, f32[80,128]{1,0:T(8,128)S(1)}, u32[]{:S(2)}) copy-start(f32[80,128]{1,0:T(8,128)S(1)} %collective-permute-done.2.high_ref) | copy-start | bytes 122884
  19.5 0.6 %copy-start.4 = (f32[80,128]{1,0:T(8,128)}, f32[80,128]{1,0:T(8,128)S(1)}, u32[]{:S(2)}) copy-start(f32[80,128]{1,0:T(8,128)S(1)} %collective-permute-done.3.low_ref) | copy-start | bytes 122884

commit v12 on v10

--- a/solution.py
+++ b/solution.py
@@ -13,15 +13,22 @@
 PER_STEP = 4
 
 
+def swap_exchange(last, first, axis):
+    n = lax.axis_size(axis)
+    even = lax.axis_index(axis) % 2 == 0
+    inner = [(k, k ^ 1) for k in range(n) if k ^ 1 < n]
+    outer = [(k, k + 1) for k in range(1, n - 1, 2)] + [(k + 1, k) for k in range(1, n - 1, 2)]
+    one = lax.ppermute(jnp.where(even, last, first), axis, inner)
+    two = lax.ppermute(jnp.where(even, first, last), axis, outer)
+    return jnp.where(even, two, one), jnp.where(even, one, two)
+
+
 def halo_pieces(source, classes, width):
     stack = lambda a, b: jnp.concatenate([a, (b + 1).astype(a.dtype)[None]], axis=0)
-    low = lax.ppermute(
-        stack(source[:, -width:, :], classes[-width:, :]), "gx",
-        [(i, i + 1) for i in range(lax.axis_size("gx") - 1)],
-    )
-    high = lax.ppermute(
-        stack(source[:, :width, :], classes[:width, :]), "gx",
-        [(i + 1, i) for i in range(lax.axis_size("gx") - 1)],
+    low, high = swap_exchange(
+        stack(source[:, -width:, :], classes[-width:, :]),
+        stack(source[:, :width, :], classes[:width, :]),
+        "gx",
     )
     rows_halo = jnp.concatenate([high, low], axis=1)
 
@@ -33,8 +40,7 @@
 
     last = packed(stack(source[:, :, -width:], classes[:, -width:]), rows_halo[:, :, -width:])
     first = packed(stack(source[:, :, :width], classes[:, :width]), rows_halo[:, :, :width])
-    low = lax.ppermute(last, "gy", [(i, i + 1) for i in range(lax.axis_size("gy") - 1)])
-    high = lax.ppermute(first, "gy", [(i + 1, i) for i in range(lax.axis_size("gy") - 1)])
+    low, high = swap_exchange(last, first, "gy")
     return rows_halo, high, low
 
 

time: 29 us -> 25.8 us (0.89)
  starting transfers between devices: 10.2 us -> 5.54 us
  other arithmetic: 0.98 us -> 2.4 us
  waiting for transfers between devices: 5.01 us -> 6.34 us
  local copies, waits for them, and re-layouts: 3.1 us -> 1.81 us
    ppermute x4, starting transfers between devices: 10.2 us -> 5.54 us  [the longest x2 3.83 us: swap_exchange(): two = lax.ppermute(jnp.where(even, first, last), axis, outer)]
    ppermute x4, waiting for transfers between devices: 5.01 us -> 6.34 us  [the longest x2 6.09 us: swap_exchange(): two = lax.ppermute(jnp.where(even, first, last), axis, outer)]
    unnamed x15 -> x8, local copies, waits for them, and re-layouts: 1.59 us -> 0.38 us
    concatenate x2, other arithmetic: 0.01 us -> 0.76 us  [halo_pieces(): rows_halo = jnp.concatenate([high, low], axis=1)]
    select_n x0 -> x4, other arithmetic: none -> 0.68 us  [the longest x2 0.65 us: swap_exchange(): return (jnp.where(even, two, one), jnp.where(even, one, two))]
  transfers between devices with their start and end apart: 4 -> 4, of which waited for: 2 -> 3; matrix products, arithmetic and copies ran while one was open for 2% -> 5% of each run, Pallas kernels for 0% -> 0%
where the time goes in v12:
time: 25.8 us; the launch traced here: 25.5 us
  Pallas kernels  8.71 us (34%)
  waiting for transfers between devices  6.34 us (25%)
  starting transfers between devices  5.54 us (21%)
  other arithmetic  2.4 us (9%)
  local copies, waits for them, and re-layouts  1.81 us (7%)
  between operations  0.74 us (3%)
    pallas_call x1, Pallas kernels, shards(): pl.pallas_call(smooth_kernel, grid=(count // PER_STEP,), in_specs=[smem,...  8.71 us
    ppermute x2, waiting for transfers between devices, swap_exchange(): two = lax.ppermute(jnp.where(even, first, last), axis, outer)  6.09 us
    ppermute x2, starting transfers between devices, swap_exchange(): two = lax.ppermute(jnp.where(even, first, last), axis, outer)  3.83 us
    ppermute x2, starting transfers between devices, swap_exchange(): one = lax.ppermute(jnp.where(even, last, first), axis, inner)  1.71 us
    slice x1, local copies, waits for them, and re-layouts, halo_pieces(): source[:, -width:, :]  0.88 us
    broadcast_in_dim x3, other arithmetic, halo_pieces(): (b + 1).astype(a.dtype)[None]  0.79 us
    concatenate x2, other arithmetic, halo_pieces(): rows_halo = jnp.concatenate([high, low], axis=1)  0.76 us
    select_n x2, other arithmetic, swap_exchange(): return (jnp.where(even, two, one), jnp.where(even, one, two))  0.65 us
  transfers between devices with their start and end apart: 4, of which 3 were waited for; matrix products, arithmetic and copies ran while one was open for 5% of the time, Pallas kernels for 0%

profile of v12, /device:TPU:18, one launch (start us, length us, event | category | flops | bytes accessed | tf_op | source)
XLA Modules:
  0.0 25.5 jit_solution(5992248710530226472)
XLA Ops:
  0.6 0.0 copy-start
  0.7 0.8 %convert_bitcast_fusion.1 = (f32[1,8,256]{2,1,0:T(8,128)S(1)}, f32[1,8,256]{2,1,0:T(8,128)S(1)}) fusion(s32[64,256]{1,0:T(8,128)} %cls_ref.1), kind=kLoop, calls=%fused_computation.20 | loop fusion | flops 8192 | bytes 32768 | tf_op jit(solution)/shard_map/broadcast_in_dim | solution.py:27
  1.4 0.9 %fusion.5 = (f32[8,8,256]{2,1,0:T(8,128)S(1)}, f32[8,8,256]{2,1,0:T(8,128)S(1)}) fusion(f32[8,64,256]{2,1,0:T(8,128)} %src_ref.1), kind=kLoop, calls=%fused_computation.24 | loop fusion | bytes 262144 | tf_op jit(solution)/shard_map/slice | solution.py:29
  2.3 0.0 copy-start.1
  2.3 1.6 %collective-permute-start = (f32[9,8,256]{2,1,0:T(8,128)S(1)}, f32[9,8,256]{2,1,0:T(8,128)S(1)}, u32[]{:S(2)}, u32[]{:S(2)}) collective-permute-start(f32[9,8,256]{2,1,0:T(8,128)S(1)} %get-tuple-element.10), channel_id=1, source_target_pairs={{0,8},{8,0},{16,24},{24,16},{1,9},{9,1},{17,25},{25,17},{2,10},{10... | collective-permute-start | bytes 221192 | tf_op jit(solution)/shard_map/ppermute | solution.py:21
  4.0 1.9 %collective-permute-start.1 = (f32[9,8,256]{2,1,0:T(8,128)S(1)}, f32[9,8,256]{2,1,0:T(8,128)S(1)}, u32[]{:S(2)}, u32[]{:S(2)}) collective-permute-start(f32[9,8,256]{2,1,0:T(8,128)S(1)} %get-tuple-element.11), channel_id=1, source_target_pairs={{8,16},{16,8},{9,17},{17,9},{10,18},{18,10},{11,19},{19,11},{12,20... | collective-permute-start | bytes 221192 | tf_op jit(solution)/shard_map/ppermute | solution.py:22
  5.9 0.0 copy-done.1
  5.9 0.1 fusion.6
  6.0 0.0 copy-done
  6.0 0.1 fusion.4
  6.1 0.1 copy.17
  6.2 0.1 copy.19
  6.3 0.1 copy.16
  6.4 0.1 copy.18
  6.5 0.2 collective-permute-done
  6.8 3.5 %collective-permute-done.1 = f32[9,8,256]{2,1,0:T(8,128)S(1)} collective-permute-done((f32[9,8,256]{2,1,0:T(8,128)S(1)}, f32[9,8,256]{2,1,0:T(8,128)S(1)}, u32[]{:S(2)}, u32[]{:S(2)}) %collective-permute-start.1) | collective-permute-done | bytes 73760 | tf_op jit(solution)/shard_map/ppermute | solution.py:22
  10.2 0.1 fusion
  10.3 0.1 copy.10
  10.4 0.1 copy.14
  10.5 0.1 maximum_bitcast_fusion
  10.6 0.1 copy.11
  10.7 0.1 maximum_bitcast_fusion.1
  10.8 0.1 copy.15
  10.9 1.9 %collective-permute-start.3 = (f32[80,128]{1,0:T(8,128)S(1)}, f32[80,128]{1,0:T(8,128)S(1)}, u32[]{:S(2)}, u32[]{:S(2)}) collective-permute-start(f32[80,128]{1,0:T(8,128)S(1)} %get-tuple-element.14), channel_id=1, source_target_pairs={{2,4},{4,2},{3,5},{5,3},{10,12},{12,10},{11,13},{13,11},{18,20},{2... | collective-permute-start | bytes 122888 | tf_op jit(solution)/shard_map/ppermute | solution.py:22
  12.8 0.1 collective-permute-start.2
  12.9 0.7 %pad_maximum_fusion.rows_ref = f32[9,16,256]{2,1,0:T(8,128)} fusion(f32[9,8,256]{2,1,0:T(8,128)S(1)} %get-tuple-element.9, f32[9,8,256]{2,1,0:T(8,128)S(1)} %get-tuple-element.8), kind=kLoop, calls=%fused_computation.2 | loop fusion | flops 36864 | bytes 294912 | tf_op jit(solution)/shard_map/concatenate | solution.py:33
  13.6 2.6 %collective-permute-done.3 = f32[80,128]{1,0:T(8,128)S(1)} collective-permute-done((f32[80,128]{1,0:T(8,128)S(1)}, f32[80,128]{1,0:T(8,128)S(1)}, u32[]{:S(2)}, u32[]{:S(2)}) %collective-permute-start.3) | collective-permute-done | bytes 40992 | tf_op jit(solution)/shard_map/ppermute | solution.py:22
  16.2 0.0 collective-permute-done.2
  16.2 0.6 %broadcast_select_fusion.2 = (f32[80,128]{1,0:T(8,128)}, f32[80,128]{1,0:T(8,128)}) fusion(f32[80,128]{1,0:T(8,128)S(1)} %collective-permute-done.3, f32[80,128]{1,0:T(8,128)S(1)} %collective-permute-done.2, pred[]{:T(512)S(6)} %eq.10), kind=kLoop, calls=%fused_computation.17 | loop fusion | flops 20480 | bytes 163841 | tf_op jit(solution)/shard_map/jit(_where)/select_n | solution.py:23
  16.8 8.7 %shard_map.59 = (f32[8,64,256]{2,1,0:T(8,128)}, f32[8,32,128]{2,1,0:T(8,128)}) custom-call(s32[8]{0:T(128)} %seeds_ref.1, f32[8,8]{1,0:T(8,128)} %levels_ref.1, f32[8,64,256]{2,1,0:T(8,128)} %src_ref.1, s32[64,256]{1,0:T(8,128)} %cls_ref.1, f32[9,16,256]{2,1,0:T(8,128)} %pad_maximum_fusion.rows_ref, f32[80,128]{1,0:T(8,128)} %get-tuple-element.13.high_ref, ...), custom_call_target="tpu_custom_call" | custom-call | tf_op jit(solution)/shard_map/pallas_call | solution.py:201
  (5 shorter events, 0.1 us)
Async XLA Ops:
  0.6 5.4 %copy-start = (f32[8,64,256]{2,1,0:T(8,128)S(1)}, f32[8,64,256]{2,1,0:T(8,128)}, u32[]{:S(2)}) copy-start(f32[8,64,256]{2,1,0:T(8,128)} %src_ref.1) | copy-start | bytes 1572868
  2.3 3.6 %copy-start.1 = (s32[64,256]{1,0:T(8,128)S(1)}, s32[64,256]{1,0:T(8,128)}, u32[]{:S(2)}) copy-start(s32[64,256]{1,0:T(8,128)} %cls_ref.1) | copy-start | bytes 196612
  2.3 4.4 %collective-permute-start = (f32[9,8,256]{2,1,0:T(8,128)S(1)}, f32[9,8,256]{2,1,0:T(8,128)S(1)}, u32[]{:S(2)}, u32[]{:S(2)}) collective-permute-start(f32[9,8,256]{2,1,0:T(8,128)S(1)} %get-tuple-element.10), channel_id=1, source_target_pairs={{0,8},{8,0},{16,24},{24,16},{1,9},{9,1},{17,25},{25,17},{2,10},{10... | collective-permute-start | bytes 221192 | tf_op jit(solution)/shard_map/ppermute | solution.py:21
  4.0 6.2 %collective-permute-start.1 = (f32[9,8,256]{2,1,0:T(8,128)S(1)}, f32[9,8,256]{2,1,0:T(8,128)S(1)}, u32[]{:S(2)}, u32[]{:S(2)}) collective-permute-start(f32[9,8,256]{2,1,0:T(8,128)S(1)} %get-tuple-element.11), channel_id=1, source_target_pairs={{8,16},{16,8},{9,17},{17,9},{10,18},{18,10},{11,19},{19,11},{12,20... | collective-permute-start | bytes 221192 | tf_op jit(solution)/shard_map/ppermute | solution.py:22
  10.9 5.3 %collective-permute-start.3 = (f32[80,128]{1,0:T(8,128)S(1)}, f32[80,128]{1,0:T(8,128)S(1)}, u32[]{:S(2)}, u32[]{:S(2)}) collective-permute-start(f32[80,128]{1,0:T(8,128)S(1)} %get-tuple-element.14), channel_id=1, source_target_pairs={{2,4},{4,2},{3,5},{5,3},{10,12},{12,10},{11,13},{13,11},{18,20},{2... | collective-permute-start | bytes 122888 | tf_op jit(solution)/shard_map/ppermute | solution.py:22
  12.8 3.4 %collective-permute-start.2 = (f32[80,128]{1,0:T(8,128)S(1)}, f32[80,128]{1,0:T(8,128)S(1)}, u32[]{:S(2)}, u32[]{:S(2)}) collective-permute-start(f32[80,128]{1,0:T(8,128)S(1)} %get-tuple-element.15), channel_id=1, source_target_pairs={{0,2},{2,0},{4,6},{6,4},{1,3},{3,1},{5,7},{7,5},{8,10},{10,8},{12,... | collective-permute-start | bytes 122888 | tf_op jit(solution)/shard_map/ppermute | solution.py:21

commit v13 on v12

--- a/solution.py
+++ b/solution.py
@@ -20,17 +20,19 @@
     outer = [(k, k + 1) for k in range(1, n - 1, 2)] + [(k + 1, k) for k in range(1, n - 1, 2)]
     one = lax.ppermute(jnp.where(even, last, first), axis, inner)
     two = lax.ppermute(jnp.where(even, first, last), axis, outer)
-    return jnp.where(even, two, one), jnp.where(even, one, two)
+    return one, two, even
 
 
 def halo_pieces(source, classes, width):
     stack = lambda a, b: jnp.concatenate([a, (b + 1).astype(a.dtype)[None]], axis=0)
-    low, high = swap_exchange(
+    one_x, two_x, even_x = swap_exchange(
         stack(source[:, -width:, :], classes[-width:, :]),
         stack(source[:, :width, :], classes[:width, :]),
         "gx",
     )
-    rows_halo = jnp.concatenate([high, low], axis=1)
+    rows_halo = jnp.where(
+        even_x, jnp.concatenate([one_x, two_x], axis=1), jnp.concatenate([two_x, one_x], axis=1)
+    )
 
     def packed(strip, halo_strip):
         planes = jnp.concatenate([strip, halo_strip], axis=1)
@@ -40,8 +42,9 @@
 
     last = packed(stack(source[:, :, -width:], classes[:, -width:]), rows_halo[:, :, -width:])
     first = packed(stack(source[:, :, :width], classes[:, :width]), rows_halo[:, :, :width])
-    low, high = swap_exchange(last, first, "gy")
-    return rows_halo, high, low
+    one_y, two_y, even_y = swap_exchange(last, first, "gy")
+    parity = jnp.stack([even_x, even_y]).astype(jnp.int32)
+    return one_x, two_x, one_y, two_y, parity
 
 
 def rolled(v, step):
@@ -80,9 +83,7 @@
     )
 
 
-def lane_tiles(high_ref, low_ref, plane):
-    high = high_ref[...]
-    low = low_ref[...]
+def lane_tiles(high, low, plane):
     lane = lax.broadcasted_iota(jnp.int32, high.shape, 1)
     after = pltpu.roll(high, (LANE_PAD - HALO * plane) % LANE_PAD, 1)
     before = pltpu.roll(low, (LANE_PAD - HALO - HALO * plane) % LANE_PAD, 1)
@@ -97,7 +98,7 @@
 
 
 def smooth_kernel(
-    seeds_ref, levels_ref, src_ref, cls_ref, rows_ref, high_ref, low_ref,
+    seeds_ref, levels_ref, parity_ref, src_ref, cls_ref, one_x, two_x, one_y, two_y,
     sol_ref, corr_ref, codes_pk, spare, wide,
 ):
     s = pl.program_id(0)
@@ -106,6 +107,15 @@
     ext_x, width = codes_pk.shape
     span = cols + 2 * HALO
     lane = lax.broadcasted_iota(jnp.int32, (ext_x, width), 1)
+    even_x = parity_ref[0] == 1
+    even_y = parity_ref[1] == 1
+    high_y = jnp.where(even_y, one_y[...], two_y[...])
+    low_y = jnp.where(even_y, two_y[...], one_y[...])
+
+    def halo_rows(plane):
+        after = jnp.where(even_x, one_x[plane], two_x[plane])
+        before = jnp.where(even_x, two_x[plane], one_x[plane])
+        return jnp.concatenate([after, before], axis=0)
 
     def packed(pieces):
         out = None
@@ -116,9 +126,9 @@
 
     @pl.when(s == 0)
     def _():
-        after, before = lane_tiles(high_ref, low_ref, count)
+        after, before = lane_tiles(high_y, low_y, count)
         own = base_layout(
-            cls_ref[...] + 1, rows_ref[count].astype(jnp.int32),
+            cls_ref[...] + 1, halo_rows(count).astype(jnp.int32),
             after.astype(jnp.int32), before.astype(jnp.int32), width,
         )
         codes_pk[...] = packed([own] * PER_STEP)
@@ -126,8 +136,8 @@
     pieces = []
     for j in range(PER_STEP):
         plane = PER_STEP * s + j
-        after, before = lane_tiles(high_ref, low_ref, plane)
-        pieces.append(base_layout(src_ref[j], rows_ref[plane], after, before, width))
+        after, before = lane_tiles(high_y, low_y, plane)
+        pieces.append(base_layout(src_ref[j], halo_rows(plane), after, before, width))
     source = packed(pieces)
     codes = codes_pk[...]
     valid = codes > 0
@@ -194,7 +204,7 @@
     count, rows, cols = source.shape
     ext_x = rows + 2 * h
     width = -(-(PER_STEP * (cols + 2 * h)) // 128) * 128
-    rows_halo, high, low = halo_pieces(source, perm_classes, h)
+    one_x, two_x, one_y, two_y, parity = halo_pieces(source, perm_classes, h)
     smem = pl.BlockSpec(memory_space=pltpu.MemorySpace.SMEM)
     vmem = pl.BlockSpec(memory_space=pltpu.MemorySpace.VMEM)
     whole = lambda shape: pl.BlockSpec(shape, lambda s: (0,) * len(shape))
@@ -204,8 +214,10 @@
         in_specs=[
             smem,
             smem,
+            smem,
             pl.BlockSpec((PER_STEP, rows, cols), lambda s: (s, 0, 0)),
             whole((rows, cols)),
+            vmem,
             vmem,
             vmem,
             vmem,
@@ -224,7 +236,7 @@
             pltpu.VMEM((cols // 128, rows, 128), jnp.float32),
         ],
         compiler_params=pltpu.CompilerParams(dimension_semantics=("arbitrary",)),
-    )(sample_seeds, perm_levels, source, perm_classes, rows_halo, high, low)
+    )(sample_seeds, perm_levels, parity, source, perm_classes, one_x, two_x, one_y, two_y)
     return solution_block, correction_block
 
 

time: 25.8 us -> 27.5 us (1.066)
  the two profiles are of different devices: /device:TPU:18 before, /device:TPU:1 now
where the time goes in v13:
time: 27.5 us; the launch traced here: 27.3 us
  starting transfers between devices  10.3 us (37%)
  Pallas kernels  8.8 us (32%)
  local copies, waits for them, and re-layouts  3.71 us (13%)
  waiting for transfers between devices  2.15 us (8%)
  other arithmetic  1.58 us (6%)
  between operations  0.74 us (3%)
    pallas_call x1, Pallas kernels, shards(): pl.pallas_call(smooth_kernel, grid=(count // PER_STEP,), in_specs=[smem,...  8.8 us
    ppermute x2, starting transfers between devices, swap_exchange(): two = lax.ppermute(jnp.where(even, first, last), axis, outer)  5.49 us
    ppermute x2, starting transfers between devices, swap_exchange(): one = lax.ppermute(jnp.where(even, last, first), axis, inner)  4.8 us
    unnamed x16, local copies, waits for them, and re-layouts  2.22 us
    ppermute x2, waiting for transfers between devices, swap_exchange(): one = lax.ppermute(jnp.where(even, last, first), axis, inner)  1.14 us
    ppermute x2, waiting for transfers between devices, swap_exchange(): two = lax.ppermute(jnp.where(even, first, last), axis, outer)  1.02 us
    slice x1, local copies, waits for them, and re-layouts, halo_pieces(): source[:, -width:, :]  0.88 us
    broadcast_in_dim x3, other arithmetic, halo_pieces(): (b + 1).astype(a.dtype)[None]  0.79 us
  transfers between devices with their start and end apart: 4, of which 2 were waited for; matrix products, arithmetic and copies ran while one was open for 4% of the time, Pallas kernels for 0%

profile of v13, /device:TPU:1, one launch (start us, length us, event | category | flops | bytes accessed | tf_op | source)
XLA Modules:
  0.0 27.3 jit_solution(14133314064428638543)
XLA Ops:
  0.6 0.0 copy-start
  0.7 0.8 %convert_bitcast_fusion.1 = (f32[1,8,256]{2,1,0:T(8,128)S(1)}, f32[1,8,256]{2,1,0:T(8,128)S(1)}) fusion(s32[64,256]{1,0:T(8,128)} %cls_ref.1), kind=kLoop, calls=%fused_computation.10 | loop fusion | flops 8192 | bytes 32768 | tf_op jit(solution)/shard_map/broadcast_in_dim | solution.py:27
  1.4 0.9 %fusion.3 = (f32[8,8,256]{2,1,0:T(8,128)S(1)}, f32[8,8,256]{2,1,0:T(8,128)S(1)}) fusion(f32[8,64,256]{2,1,0:T(8,128)} %src_ref.1), kind=kLoop, calls=%fused_computation.15 | loop fusion | bytes 262144 | tf_op jit(solution)/shard_map/slice | solution.py:29
  2.3 0.0 copy-start.1
  2.3 0.7 %collective-permute-start.1 = (f32[9,8,256]{2,1,0:T(8,128)S(1)}, f32[9,8,256]{2,1,0:T(8,128)S(1)}, u32[]{:S(2)}, u32[]{:S(2)}) collective-permute-start(f32[9,8,256]{2,1,0:T(8,128)S(1)} %get-tuple-element.8), channel_id=1, source_target_pairs={{8,16},{16,8},{9,17},{17,9},{10,18},{18,10},{11,19},{19,11},{12,20... | collective-permute-start | bytes 221192 | tf_op jit(solution)/shard_map/ppermute | solution.py:22
  3.0 4.7 %collective-permute-start = (f32[9,8,256]{2,1,0:T(8,128)S(1)}, f32[9,8,256]{2,1,0:T(8,128)S(1)}, u32[]{:S(2)}, u32[]{:S(2)}) collective-permute-start(f32[9,8,256]{2,1,0:T(8,128)S(1)} %get-tuple-element.9), channel_id=1, source_target_pairs={{0,8},{8,0},{16,24},{24,16},{1,9},{9,1},{17,25},{25,17},{2,10},{10... | collective-permute-start | bytes 221192 | tf_op jit(solution)/shard_map/ppermute | solution.py:21
  7.8 0.0 copy-done.1
  7.8 0.1 fusion.5
  7.8 0.0 copy-done
  7.8 0.1 fusion.2
  8.0 0.1 copy.17
  8.0 0.1 copy.19
  8.1 0.1 copy.16
  8.2 0.1 copy.18
  8.4 0.0 collective-permute-done.1.two_x
  8.4 0.0 copy-start.2
  8.4 1.1 %collective-permute-done.one_x = f32[9,8,256]{2,1,0:T(8,128)S(1)} collective-permute-done((f32[9,8,256]{2,1,0:T(8,128)S(1)}, f32[9,8,256]{2,1,0:T(8,128)S(1)}, u32[]{:S(2)}, u32[]{:S(2)}) %collective-permute-start) | collective-permute-done | bytes 73760 | tf_op jit(solution)/shard_map/ppermute | solution.py:21
  9.5 0.0 copy-start.3
  9.5 0.0 copy-done.2
  9.5 0.6 %copy-done.3 = f32[9,8,256]{2,1,0:T(8,128)} copy-done((f32[9,8,256]{2,1,0:T(8,128)}, f32[9,8,256]{2,1,0:T(8,128)S(1)}, u32[]{:S(2)}) %copy-start.3) | copy-done | bytes 73752
  10.1 0.1 fusion.4
  10.2 0.1 copy.10
  10.3 0.1 copy.14
  10.4 0.1 maximum_bitcast_fusion
  10.5 0.1 copy.11
  10.6 0.1 maximum_bitcast_fusion.1
  10.6 0.1 copy.15
  10.8 4.8 %collective-permute-start.3 = (f32[80,128]{1,0:T(8,128)S(1)}, f32[80,128]{1,0:T(8,128)S(1)}, u32[]{:S(2)}, u32[]{:S(2)}) collective-permute-start(f32[80,128]{1,0:T(8,128)S(1)} %get-tuple-element.10), channel_id=1, source_target_pairs={{2,4},{4,2},{3,5},{5,3},{10,12},{12,10},{11,13},{13,11},{18,20},{2... | collective-permute-start | bytes 122888 | tf_op jit(solution)/shard_map/ppermute | solution.py:22
  15.6 0.1 collective-permute-start.2
  15.7 0.6 %add_convert_fusion.parity_ref = s32[2]{0:T(128)} fusion(pred[1]{0:T(512)(128)(4,1)} %bitcast.1, pred[1]{0:T(512)(128)(4,1)} %bitcast), kind=kLoop, calls=%fused_computation.13 | loop fusion | flops 4 | bytes 10 | tf_op jit(solution)/shard_map/convert_element_type | solution.py:46
  16.3 1.0 %collective-permute-done.3.two_y = f32[80,128]{1,0:T(8,128)S(1)} collective-permute-done((f32[80,128]{1,0:T(8,128)S(1)}, f32[80,128]{1,0:T(8,128)S(1)}, u32[]{:S(2)}, u32[]{:S(2)}) %collective-permute-start.3) | collective-permute-done | bytes 40992 | tf_op jit(solution)/shard_map/ppermute | solution.py:22
  17.3 0.0 copy-start.4
  17.3 0.0 collective-permute-done.2.one_y
  17.3 0.6 %copy-done.4 = f32[80,128]{1,0:T(8,128)} copy-done((f32[80,128]{1,0:T(8,128)}, f32[80,128]{1,0:T(8,128)S(1)}, u32[]{:S(2)}) %copy-start.4) | copy-done | bytes 40984
  17.9 0.0 copy-start.5
  17.9 0.6 %copy-done.5 = f32[80,128]{1,0:T(8,128)} copy-done((f32[80,128]{1,0:T(8,128)}, f32[80,128]{1,0:T(8,128)S(1)}, u32[]{:S(2)}) %copy-start.5) | copy-done | bytes 40984
  18.5 8.8 %shard_map.59 = (f32[8,64,256]{2,1,0:T(8,128)}, f32[8,32,128]{2,1,0:T(8,128)}) custom-call(s32[8]{0:T(128)} %seeds_ref.1, f32[8,8]{1,0:T(8,128)} %levels_ref.1, s32[2]{0:T(128)} %add_convert_fusion.parity_ref, f32[8,64,256]{2,1,0:T(8,128)} %src_ref.1, s32[64,256]{1,0:T(8,128)} %cls_ref.1, f32[9,8,256]{2,1,0:T(8,128)} %copy-done.3, f32[9,8,256]{2,1,0:T(8,128)} %copy-done.2, ...), custom_call_target="tpu_custom_call" | custom-call | tf_op jit(solution)/shard_map/pallas_call | solution.py:211
  (5 shorter events, 0.1 us)
Async XLA Ops:
  0.6 7.2 %copy-start = (f32[8,64,256]{2,1,0:T(8,128)S(1)}, f32[8,64,256]{2,1,0:T(8,128)}, u32[]{:S(2)}) copy-start(f32[8,64,256]{2,1,0:T(8,128)} %src_ref.1) | copy-start | bytes 1572868
  2.3 5.4 %copy-start.1 = (s32[64,256]{1,0:T(8,128)S(1)}, s32[64,256]{1,0:T(8,128)}, u32[]{:S(2)}) copy-start(s32[64,256]{1,0:T(8,128)} %cls_ref.1) | copy-start | bytes 196612
  2.3 6.0 %collective-permute-start.1 = (f32[9,8,256]{2,1,0:T(8,128)S(1)}, f32[9,8,256]{2,1,0:T(8,128)S(1)}, u32[]{:S(2)}, u32[]{:S(2)}) collective-permute-start(f32[9,8,256]{2,1,0:T(8,128)S(1)} %get-tuple-element.8), channel_id=1, source_target_pairs={{8,16},{16,8},{9,17},{17,9},{10,18},{18,10},{11,19},{19,11},{12,20... | collective-permute-start | bytes 221192 | tf_op jit(solution)/shard_map/ppermute | solution.py:22
  3.0 6.5 %collective-permute-start = (f32[9,8,256]{2,1,0:T(8,128)S(1)}, f32[9,8,256]{2,1,0:T(8,128)S(1)}, u32[]{:S(2)}, u32[]{:S(2)}) collective-permute-start(f32[9,8,256]{2,1,0:T(8,128)S(1)} %get-tuple-element.9), channel_id=1, source_target_pairs={{0,8},{8,0},{16,24},{24,16},{1,9},{9,1},{17,25},{25,17},{2,10},{10... | collective-permute-start | bytes 221192 | tf_op jit(solution)/shard_map/ppermute | solution.py:21
  8.4 1.2 %copy-start.2 = (f32[9,8,256]{2,1,0:T(8,128)}, f32[9,8,256]{2,1,0:T(8,128)S(1)}, u32[]{:S(2)}) copy-start(f32[9,8,256]{2,1,0:T(8,128)S(1)} %collective-permute-done.1.two_x) | copy-start | bytes 221188
  9.5 0.6 %copy-start.3 = (f32[9,8,256]{2,1,0:T(8,128)}, f32[9,8,256]{2,1,0:T(8,128)S(1)}, u32[]{:S(2)}) copy-start(f32[9,8,256]{2,1,0:T(8,128)S(1)} %collective-permute-done.one_x) | copy-start | bytes 221188
  10.8 6.5 %collective-permute-start.3 = (f32[80,128]{1,0:T(8,128)S(1)}, f32[80,128]{1,0:T(8,128)S(1)}, u32[]{:S(2)}, u32[]{:S(2)}) collective-permute-start(f32[80,128]{1,0:T(8,128)S(1)} %get-tuple-element.10), channel_id=1, source_target_pairs={{2,4},{4,2},{3,5},{5,3},{10,12},{12,10},{11,13},{13,11},{18,20},{2... | collective-permute-start | bytes 122888 | tf_op jit(solution)/shard_map/ppermute | solution.py:22
  15.6 1.7 %collective-permute-start.2 = (f32[80,128]{1,0:T(8,128)S(1)}, f32[80,128]{1,0:T(8,128)S(1)}, u32[]{:S(2)}, u32[]{:S(2)}) collective-permute-start(f32[80,128]{1,0:T(8,128)S(1)} %get-tuple-element.11), channel_id=1, source_target_pairs={{0,2},{2,0},{4,6},{6,4},{1,3},{3,1},{5,7},{7,5},{8,10},{10,8},{12,... | collective-permute-start | bytes 122888 | tf_op jit(solution)/shard_map/ppermute | solution.py:21
  17.3 0.6 %copy-start.4 = (f32[80,128]{1,0:T(8,128)}, f32[80,128]{1,0:T(8,128)S(1)}, u32[]{:S(2)}) copy-start(f32[80,128]{1,0:T(8,128)S(1)} %collective-permute-done.3.two_y) | copy-start | bytes 122884
  17.9 0.6 %copy-start.5 = (f32[80,128]{1,0:T(8,128)}, f32[80,128]{1,0:T(8,128)S(1)}, u32[]{:S(2)}) copy-start(f32[80,128]{1,0:T(8,128)S(1)} %collective-permute-done.2.one_y) | copy-start | bytes 122884

commit v14 on v12

--- a/solution.py
+++ b/solution.py
@@ -20,27 +20,38 @@
     outer = [(k, k + 1) for k in range(1, n - 1, 2)] + [(k + 1, k) for k in range(1, n - 1, 2)]
     one = lax.ppermute(jnp.where(even, last, first), axis, inner)
     two = lax.ppermute(jnp.where(even, first, last), axis, outer)
-    return jnp.where(even, two, one), jnp.where(even, one, two)
+    return one, two, even
 
 
 def halo_pieces(source, classes, width):
+    count, rows, cols = source.shape
     stack = lambda a, b: jnp.concatenate([a, (b + 1).astype(a.dtype)[None]], axis=0)
-    low, high = swap_exchange(
-        stack(source[:, -width:, :], classes[-width:, :]),
-        stack(source[:, :width, :], classes[:width, :]),
+
+    def packed(planes):
+        flat = jnp.transpose(planes, (1, 0, 2)).reshape(rows, (count + 1) * width)
+        return jnp.pad(flat, ((0, 0), (0, LANE_PAD - (count + 1) * width)))
+
+    one_y, two_y, even_y = swap_exchange(
+        packed(stack(source[:, :, -width:], classes[:, -width:])),
+        packed(stack(source[:, :, :width], classes[:, :width])),
+        "gy",
+    )
+    high = jnp.where(even_y, one_y, two_y)
+    low = jnp.where(even_y, two_y, one_y)
+
+    def with_corners(planes, edge):
+        corner = jnp.concatenate([high[edge], low[edge]], axis=1)
+        corner = jnp.pad(corner, ((0, 0), (0, cols - 2 * LANE_PAD)))
+        return jnp.concatenate([planes, corner[None]], axis=0)
+
+    one_x, two_x, even_x = swap_exchange(
+        with_corners(stack(source[:, -width:, :], classes[-width:, :]), slice(rows - width, rows)),
+        with_corners(stack(source[:, :width, :], classes[:width, :]), slice(0, width)),
         "gx",
     )
-    rows_halo = jnp.concatenate([high, low], axis=1)
-
-    def packed(strip, halo_strip):
-        planes = jnp.concatenate([strip, halo_strip], axis=1)
-        count, rows, _ = planes.shape
-        flat = jnp.transpose(planes, (1, 0, 2)).reshape(rows, count * width)
-        return jnp.pad(flat, ((0, 0), (0, LANE_PAD - count * width)))
-
-    last = packed(stack(source[:, :, -width:], classes[:, -width:]), rows_halo[:, :, -width:])
-    first = packed(stack(source[:, :, :width], classes[:, :width]), rows_halo[:, :, :width])
-    low, high = swap_exchange(last, first, "gy")
+    rows_halo = jnp.where(
+        even_x, jnp.concatenate([one_x, two_x], axis=1), jnp.concatenate([two_x, one_x], axis=1)
+    )
     return rows_halo, high, low
 
 
@@ -80,9 +91,7 @@
     )
 
 
-def lane_tiles(high_ref, low_ref, plane):
-    high = high_ref[...]
-    low = low_ref[...]
+def lane_tiles(high, low, plane):
     lane = lax.broadcasted_iota(jnp.int32, high.shape, 1)
     after = pltpu.roll(high, (LANE_PAD - HALO * plane) % LANE_PAD, 1)
     before = pltpu.roll(low, (LANE_PAD - HALO - HALO * plane) % LANE_PAD, 1)
@@ -106,6 +115,9 @@
     ext_x, width = codes_pk.shape
     span = cols + 2 * HALO
     lane = lax.broadcasted_iota(jnp.int32, (ext_x, width), 1)
+    corner = rows_ref[count + 1]
+    high_y = jnp.concatenate([high_ref[...], corner[:, :LANE_PAD]], axis=0)
+    low_y = jnp.concatenate([low_ref[...], corner[:, LANE_PAD : 2 * LANE_PAD]], axis=0)
 
     def packed(pieces):
         out = None
@@ -116,7 +128,7 @@
 
     @pl.when(s == 0)
     def _():
-        after, before = lane_tiles(high_ref, low_ref, count)
+        after, before = lane_tiles(high_y, low_y, count)
         own = base_layout(
             cls_ref[...] + 1, rows_ref[count].astype(jnp.int32),
             after.astype(jnp.int32), before.astype(jnp.int32), width,
@@ -126,7 +138,7 @@
     pieces = []
     for j in range(PER_STEP):
         plane = PER_STEP * s + j
-        after, before = lane_tiles(high_ref, low_ref, plane)
+        after, before = lane_tiles(high_y, low_y, plane)
         pieces.append(base_layout(src_ref[j], rows_ref[plane], after, before, width))
     source = packed(pieces)
     codes = codes_pk[...]

time: 25.8 us -> 26.9 us (1.043)
  local copies, waits for them, and re-layouts: 1.81 us -> 4.01 us
  other arithmetic: 2.4 us -> 1.49 us
  waiting for transfers between devices: 6.34 us -> 5.49 us
  starting transfers between devices: 5.54 us -> 6.15 us
    ppermute x2, waiting for transfers between devices: 6.09 us -> 4.54 us  [swap_exchange(): two = lax.ppermute(jnp.where(even, first, last), axis, outer)]
    slice x1, local copies, waits for them, and re-layouts: 0.13 us -> 1.18 us  [halo_pieces(): source[:, :, -width:]]
    slice x1, local copies, waits for them, and re-layouts: 0.08 us -> 0.85 us  [halo_pieces(): classes[:, -width:]]
    concatenate x2 -> x0, other arithmetic: 0.76 us -> none  [halo_pieces(): rows_halo = jnp.concatenate([high, low], axis=1)]
    ppermute x2, waiting for transfers between devices: 0.25 us -> 0.95 us  [swap_exchange(): one = lax.ppermute(jnp.where(even, last, first), axis, inner)]
    ppermute x2, starting transfers between devices: 3.83 us -> 4.44 us  [swap_exchange(): two = lax.ppermute(jnp.where(even, first, last), axis, outer)]
    unnamed x8, local copies, waits for them, and re-layouts: 0.38 us -> 0.93 us
    select_n x3 -> x2, other arithmetic: 0.66 us -> 0.69 us  [the longest x1 0.68 us: halo_pieces(): jnp.where(even_x, jnp.concatenate([one_x, two_x], axis=1), jnp.concatenat...]
  transfers between devices with their start and end apart: 4 -> 4, of which waited for: 3 -> 3; matrix products, arithmetic and copies ran while one was open for 5% -> 6% of each run, Pallas kernels for 0% -> 0%
where the time goes in v14:
time: 26.9 us; the launch traced here: 26.6 us
  Pallas kernels  8.73 us (32%)
  starting transfers between devices  6.15 us (23%)
  waiting for transfers between devices  5.49 us (20%)
  local copies, waits for them, and re-layouts  4.01 us (15%)
  other arithmetic  1.49 us (6%)
  between operations  0.74 us (3%)
    pallas_call x1, Pallas kernels, shards(): pl.pallas_call(smooth_kernel, grid=(count // PER_STEP,), in_specs=[smem,...  8.73 us
    ppermute x2, waiting for transfers between devices, swap_exchange(): two = lax.ppermute(jnp.where(even, first, last), axis, outer)  4.54 us
    ppermute x2, starting transfers between devices, swap_exchange(): two = lax.ppermute(jnp.where(even, first, last), axis, outer)  4.44 us
    ppermute x2, starting transfers between devices, swap_exchange(): one = lax.ppermute(jnp.where(even, last, first), axis, inner)  1.71 us
    slice x1, local copies, waits for them, and re-layouts, halo_pieces(): source[:, :, -width:]  1.18 us
    ppermute x2, waiting for transfers between devices, swap_exchange(): one = lax.ppermute(jnp.where(even, last, first), axis, inner)  0.95 us
    unnamed x8, local copies, waits for them, and re-layouts  0.93 us
    slice x1, local copies, waits for them, and re-layouts, halo_pieces(): source[:, -width:, :]  0.89 us
  transfers between devices with their start and end apart: 4, of which 3 were waited for; matrix products, arithmetic and copies ran while one was open for 6% of the time, Pallas kernels for 0%

profile of v14, /device:TPU:18, one launch (start us, length us, event | category | flops | bytes accessed | tf_op | source)
XLA Modules:
  0.0 26.6 jit_solution(12776775152028557960)
XLA Ops:
  0.6 0.9 %fusion.4 = (s32[64,8]{1,0:T(8,128)S(1)}, s32[64,8]{1,0:T(8,128)S(1)}) fusion(s32[64,256]{1,0:T(8,128)} %cls_ref.1), kind=kLoop, calls=%fused_computation.19 | loop fusion | bytes 8192 | tf_op jit(solution)/shard_map/slice | solution.py:35
  1.5 0.1 copy.19
  1.6 0.1 copy.21
  1.6 1.2 %fusion.3 = (f32[8,64,8]{2,1,0:T(8,128)S(1)}, f32[8,64,8]{2,1,0:T(8,128)S(1)}) fusion(f32[8,64,256]{2,1,0:T(8,128)} %src_ref.1), kind=kLoop, calls=%fused_computation.18 | loop fusion | bytes 65536 | tf_op jit(solution)/shard_map/slice | solution.py:35
  2.8 0.1 copy.18
  2.9 0.1 copy.14
  3.0 0.1 copy.20
  3.2 0.1 copy.17
  3.3 0.1 collective-permute-start
  3.3 2.5 %collective-permute-start.1 = (f32[64,128]{1,0:T(8,128)S(1)}, f32[64,128]{1,0:T(8,128)S(1)}, u32[]{:S(2)}, u32[]{:S(2)}) collective-permute-start(f32[64,128]{1,0:T(8,128)S(1)} %get-tuple-element.13), channel_id=1, source_target_pairs={{2,4},{4,2},{3,5},{5,3},{10,12},{12,10},{11,13},{13,11},{18,20},{2... | collective-permute-start | bytes 98312 | tf_op jit(solution)/shard_map/ppermute | solution.py:22
  5.9 0.9 %fusion.2 = (f32[8,8,256]{2,1,0:T(8,128)S(1)}, f32[8,8,256]{2,1,0:T(8,128)S(1)}) fusion(f32[8,64,256]{2,1,0:T(8,128)} %src_ref.1), kind=kLoop, calls=%fused_computation.17 | loop fusion | bytes 262144 | tf_op jit(solution)/shard_map/slice | solution.py:48
  6.8 0.7 %convert_bitcast_fusion.1 = (f32[1,8,256]{2,1,0:T(8,128)S(1)}, f32[1,8,256]{2,1,0:T(8,128)S(1)}) fusion(s32[64,256]{1,0:T(8,128)} %cls_ref.1), kind=kLoop, calls=%fused_computation.14 | loop fusion | flops 8192 | bytes 32768 | tf_op jit(solution)/shard_map/broadcast_in_dim | solution.py:28
  7.5 0.0 collective-permute-done
  7.5 1.1 %collective-permute-done.1 = f32[64,128]{1,0:T(8,128)S(1)} collective-permute-done((f32[64,128]{1,0:T(8,128)S(1)}, f32[64,128]{1,0:T(8,128)S(1)}, u32[]{:S(2)}, u32[]{:S(2)}) %collective-permute-start.1) | collective-permute-done | bytes 32800 | tf_op jit(solution)/shard_map/ppermute | solution.py:22
  8.6 0.0 copy-start
  8.6 0.0 copy-start.1
  8.6 0.5 %copy-done = f32[64,128]{1,0:T(8,128)} copy-done((f32[64,128]{1,0:T(8,128)}, f32[64,128]{1,0:T(8,128)S(1)}, u32[]{:S(2)}) %copy-start) | copy-done | bytes 32792
  9.2 0.0 copy-done.1
  9.2 1.6 %collective-permute-start.2 = (f32[10,8,256]{2,1,0:T(8,128)S(1)}, f32[10,8,256]{2,1,0:T(8,128)S(1)}, u32[]{:S(2)}, u32[]{:S(2)}) collective-permute-start(f32[10,8,256]{2,1,0:T(8,128)S(1)} %get-tuple-element.6), channel_id=1, source_target_pairs={{0,8},{8,0},{16,24},{24,16},{1,9},{9,1},{17,25},{25,17},{2,10},{10... | collective-permute-start | bytes 245768 | tf_op jit(solution)/shard_map/ppermute | solution.py:21
  10.9 1.9 %collective-permute-start.3 = (f32[10,8,256]{2,1,0:T(8,128)S(1)}, f32[10,8,256]{2,1,0:T(8,128)S(1)}, u32[]{:S(2)}, u32[]{:S(2)}) collective-permute-start(f32[10,8,256]{2,1,0:T(8,128)S(1)} %get-tuple-element.7), channel_id=1, source_target_pairs={{8,16},{16,8},{9,17},{17,9},{10,18},{18,10},{11,19},{19,11},{12,20... | collective-permute-start | bytes 245768 | tf_op jit(solution)/shard_map/ppermute | solution.py:22
  12.8 0.9 %collective-permute-done.2 = f32[10,8,256]{2,1,0:T(8,128)S(1)} collective-permute-done((f32[10,8,256]{2,1,0:T(8,128)S(1)}, f32[10,8,256]{2,1,0:T(8,128)S(1)}, u32[]{:S(2)}, u32[]{:S(2)}) %collective-permute-start.2) | collective-permute-done | bytes 81952 | tf_op jit(solution)/shard_map/ppermute | solution.py:21
  13.7 3.5 %collective-permute-done.3 = f32[10,8,256]{2,1,0:T(8,128)S(1)} collective-permute-done((f32[10,8,256]{2,1,0:T(8,128)S(1)}, f32[10,8,256]{2,1,0:T(8,128)S(1)}, u32[]{:S(2)}, u32[]{:S(2)}) %collective-permute-start.3) | collective-permute-done | bytes 81952 | tf_op jit(solution)/shard_map/ppermute | solution.py:22
  17.2 0.7 %maximum_select_fusion.rows_ref = f32[10,16,256]{2,1,0:T(8,128)} fusion(f32[10,8,256]{2,1,0:T(8,128)S(1)} %collective-permute-done.3, f32[10,8,256]{2,1,0:T(8,128)S(1)} %collective-permute-done.2, pred[]{:T(512)S(6)} %eq.9), kind=kLoop, calls=%fused_computation | loop fusion | flops 122880 | bytes 327681 | tf_op jit(solution)/shard_map/jit(_where)/select_n | solution.py:52
  17.9 8.7 %shard_map.59 = (f32[8,64,256]{2,1,0:T(8,128)}, f32[8,32,128]{2,1,0:T(8,128)}) custom-call(s32[8]{0:T(128)} %seeds_ref.1, f32[8,8]{1,0:T(8,128)} %levels_ref.1, f32[8,64,256]{2,1,0:T(8,128)} %src_ref.1, s32[64,256]{1,0:T(8,128)} %cls_ref.1, f32[10,16,256]{2,1,0:T(8,128)} %maximum_select_fusion.rows_ref, f32[64,128]{1,0:T(8,128)} %copy-done, f32[64,128]{1,0:T(8,128)} %copy-done.1), custom_call_target="tpu_custom_call" | custom-call | tf_op jit(solution)/shard_map/pallas_call | solution.py:213
  (10 shorter events, 0.1 us)
Async XLA Ops:
  3.3 4.2 %collective-permute-start = (f32[64,128]{1,0:T(8,128)S(1)}, f32[64,128]{1,0:T(8,128)S(1)}, u32[]{:S(2)}, u32[]{:S(2)}) collective-permute-start(f32[64,128]{1,0:T(8,128)S(1)} %get-tuple-element.12), channel_id=1, source_target_pairs={{0,2},{2,0},{4,6},{6,4},{1,3},{3,1},{5,7},{7,5},{8,10},{10,8},{12,... | collective-permute-start | bytes 98312 | tf_op jit(solution)/shard_map/ppermute | solution.py:21
  3.3 5.2 %collective-permute-start.1 = (f32[64,128]{1,0:T(8,128)S(1)}, f32[64,128]{1,0:T(8,128)S(1)}, u32[]{:S(2)}, u32[]{:S(2)}) collective-permute-start(f32[64,128]{1,0:T(8,128)S(1)} %get-tuple-element.13), channel_id=1, source_target_pairs={{2,4},{4,2},{3,5},{5,3},{10,12},{12,10},{11,13},{13,11},{18,20},{2... | collective-permute-start | bytes 98312 | tf_op jit(solution)/shard_map/ppermute | solution.py:22
  8.6 0.6 %copy-start = (f32[64,128]{1,0:T(8,128)}, f32[64,128]{1,0:T(8,128)S(1)}, u32[]{:S(2)}) copy-start(f32[64,128]{1,0:T(8,128)S(1)} %get-tuple-element.10.high_ref) | copy-start | bytes 98308
  8.6 0.6 %copy-start.1 = (f32[64,128]{1,0:T(8,128)}, f32[64,128]{1,0:T(8,128)S(1)}, u32[]{:S(2)}) copy-start(f32[64,128]{1,0:T(8,128)S(1)} %get-tuple-element.11.low_ref) | copy-start | bytes 98308
  9.2 4.5 %collective-permute-start.2 = (f32[10,8,256]{2,1,0:T(8,128)S(1)}, f32[10,8,256]{2,1,0:T(8,128)S(1)}, u32[]{:S(2)}, u32[]{:S(2)}) collective-permute-start(f32[10,8,256]{2,1,0:T(8,128)S(1)} %get-tuple-element.6), channel_id=1, source_target_pairs={{0,8},{8,0},{16,24},{24,16},{1,9},{9,1},{17,25},{25,17},{2,10},{10... | collective-permute-start | bytes 245768 | tf_op jit(solution)/shard_map/ppermute | solution.py:21
  10.9 6.3 %collective-permute-start.3 = (f32[10,8,256]{2,1,0:T(8,128)S(1)}, f32[10,8,256]{2,1,0:T(8,128)S(1)}, u32[]{:S(2)}, u32[]{:S(2)}) collective-permute-start(f32[10,8,256]{2,1,0:T(8,128)S(1)} %get-tuple-element.7), channel_id=1, source_target_pairs={{8,16},{16,8},{9,17},{17,9},{10,18},{18,10},{11,19},{19,11},{12,20... | collective-permute-start | bytes 245768 | tf_op jit(solution)/shard_map/ppermute | solution.py:22

commit v15 on v12

--- a/solution.py
+++ b/solution.py
@@ -18,8 +18,8 @@
     even = lax.axis_index(axis) % 2 == 0
     inner = [(k, k ^ 1) for k in range(n) if k ^ 1 < n]
     outer = [(k, k + 1) for k in range(1, n - 1, 2)] + [(k + 1, k) for k in range(1, n - 1, 2)]
+    two = lax.ppermute(jnp.where(even, first, last), axis, outer)
     one = lax.ppermute(jnp.where(even, last, first), axis, inner)
-    two = lax.ppermute(jnp.where(even, first, last), axis, outer)
     return jnp.where(even, two, one), jnp.where(even, one, two)
 
 

time: 25.8 us -> 25.8 us (level)
  no operation moved by 1% of the time
where the time goes in v15:
time: 25.8 us; the launch traced here: 25.5 us
  Pallas kernels  8.71 us (34%)
  waiting for transfers between devices  6.34 us (25%)
  starting transfers between devices  5.54 us (21%)
  other arithmetic  2.4 us (9%)
  local copies, waits for them, and re-layouts  1.81 us (7%)
  between operations  0.74 us (3%)
    pallas_call x1, Pallas kernels, shards(): pl.pallas_call(smooth_kernel, grid=(count // PER_STEP,), in_specs=[smem,...  8.71 us
    ppermute x2, waiting for transfers between devices, swap_exchange(): two = lax.ppermute(jnp.where(even, first, last), axis, outer)  6.09 us
    ppermute x2, starting transfers between devices, swap_exchange(): two = lax.ppermute(jnp.where(even, first, last), axis, outer)  3.83 us
    ppermute x2, starting transfers between devices, swap_exchange(): one = lax.ppermute(jnp.where(even, last, first), axis, inner)  1.71 us
    slice x1, local copies, waits for them, and re-layouts, halo_pieces(): source[:, -width:, :]  0.88 us
    broadcast_in_dim x3, other arithmetic, halo_pieces(): (b + 1).astype(a.dtype)[None]  0.79 us
    concatenate x2, other arithmetic, halo_pieces(): rows_halo = jnp.concatenate([high, low], axis=1)  0.76 us
    select_n x2, other arithmetic, swap_exchange(): return (jnp.where(even, two, one), jnp.where(even, one, two))  0.65 us
  transfers between devices with their start and end apart: 4, of which 3 were waited for; matrix products, arithmetic and copies ran while one was open for 5% of the time, Pallas kernels for 0%

profile of v15, /device:TPU:18, one launch (start us, length us, event | category | flops | bytes accessed | tf_op | source)
XLA Modules:
  0.0 25.5 jit_solution(5992248710530226472)
XLA Ops:
  0.6 0.0 copy-start
  0.7 0.8 %convert_bitcast_fusion.1 = (f32[1,8,256]{2,1,0:T(8,128)S(1)}, f32[1,8,256]{2,1,0:T(8,128)S(1)}) fusion(s32[64,256]{1,0:T(8,128)} %cls_ref.1), kind=kLoop, calls=%fused_computation.20 | loop fusion | flops 8192 | bytes 32768 | tf_op jit(solution)/shard_map/broadcast_in_dim | solution.py:27
  1.4 0.9 %fusion.5 = (f32[8,8,256]{2,1,0:T(8,128)S(1)}, f32[8,8,256]{2,1,0:T(8,128)S(1)}) fusion(f32[8,64,256]{2,1,0:T(8,128)} %src_ref.1), kind=kLoop, calls=%fused_computation.24 | loop fusion | bytes 262144 | tf_op jit(solution)/shard_map/slice | solution.py:29
  2.3 0.0 copy-start.1
  2.3 1.6 %collective-permute-start = (f32[9,8,256]{2,1,0:T(8,128)S(1)}, f32[9,8,256]{2,1,0:T(8,128)S(1)}, u32[]{:S(2)}, u32[]{:S(2)}) collective-permute-start(f32[9,8,256]{2,1,0:T(8,128)S(1)} %get-tuple-element.10), channel_id=1, source_target_pairs={{0,8},{8,0},{16,24},{24,16},{1,9},{9,1},{17,25},{25,17},{2,10},{10... | collective-permute-start | bytes 221192 | tf_op jit(solution)/shard_map/ppermute | solution.py:22
  4.0 1.9 %collective-permute-start.1 = (f32[9,8,256]{2,1,0:T(8,128)S(1)}, f32[9,8,256]{2,1,0:T(8,128)S(1)}, u32[]{:S(2)}, u32[]{:S(2)}) collective-permute-start(f32[9,8,256]{2,1,0:T(8,128)S(1)} %get-tuple-element.11), channel_id=1, source_target_pairs={{8,16},{16,8},{9,17},{17,9},{10,18},{18,10},{11,19},{19,11},{12,20... | collective-permute-start | bytes 221192 | tf_op jit(solution)/shard_map/ppermute | solution.py:21
  5.9 0.0 copy-done.1
  5.9 0.1 fusion.6
  6.0 0.0 copy-done
  6.0 0.1 fusion.4
  6.1 0.1 copy.17
  6.2 0.1 copy.19
  6.3 0.1 copy.16
  6.4 0.1 copy.18
  6.5 0.2 collective-permute-done
  6.8 3.5 %collective-permute-done.1 = f32[9,8,256]{2,1,0:T(8,128)S(1)} collective-permute-done((f32[9,8,256]{2,1,0:T(8,128)S(1)}, f32[9,8,256]{2,1,0:T(8,128)S(1)}, u32[]{:S(2)}, u32[]{:S(2)}) %collective-permute-start.1) | collective-permute-done | bytes 73760 | tf_op jit(solution)/shard_map/ppermute | solution.py:21
  10.2 0.1 fusion
  10.3 0.1 copy.10
  10.4 0.1 copy.14
  10.5 0.1 maximum_bitcast_fusion
  10.6 0.1 copy.11
  10.7 0.1 maximum_bitcast_fusion.1
  10.8 0.1 copy.15
  10.9 1.9 %collective-permute-start.3 = (f32[80,128]{1,0:T(8,128)S(1)}, f32[80,128]{1,0:T(8,128)S(1)}, u32[]{:S(2)}, u32[]{:S(2)}) collective-permute-start(f32[80,128]{1,0:T(8,128)S(1)} %get-tuple-element.14), channel_id=1, source_target_pairs={{2,4},{4,2},{3,5},{5,3},{10,12},{12,10},{11,13},{13,11},{18,20},{2... | collective-permute-start | bytes 122888 | tf_op jit(solution)/shard_map/ppermute | solution.py:21
  12.8 0.1 collective-permute-start.2
  12.9 0.7 %pad_maximum_fusion.rows_ref = f32[9,16,256]{2,1,0:T(8,128)} fusion(f32[9,8,256]{2,1,0:T(8,128)S(1)} %get-tuple-element.9, f32[9,8,256]{2,1,0:T(8,128)S(1)} %get-tuple-element.8), kind=kLoop, calls=%fused_computation.2 | loop fusion | flops 36864 | bytes 294912 | tf_op jit(solution)/shard_map/concatenate | solution.py:33
  13.6 2.6 %collective-permute-done.3 = f32[80,128]{1,0:T(8,128)S(1)} collective-permute-done((f32[80,128]{1,0:T(8,128)S(1)}, f32[80,128]{1,0:T(8,128)S(1)}, u32[]{:S(2)}, u32[]{:S(2)}) %collective-permute-start.3) | collective-permute-done | bytes 40992 | tf_op jit(solution)/shard_map/ppermute | solution.py:21
  16.2 0.0 collective-permute-done.2
  16.2 0.6 %broadcast_select_fusion.2 = (f32[80,128]{1,0:T(8,128)}, f32[80,128]{1,0:T(8,128)}) fusion(f32[80,128]{1,0:T(8,128)S(1)} %collective-permute-done.3, f32[80,128]{1,0:T(8,128)S(1)} %collective-permute-done.2, pred[]{:T(512)S(6)} %eq.10), kind=kLoop, calls=%fused_computation.17 | loop fusion | flops 20480 | bytes 163841 | tf_op jit(solution)/shard_map/jit(_where)/select_n | solution.py:23
  16.8 8.7 %shard_map.59 = (f32[8,64,256]{2,1,0:T(8,128)}, f32[8,32,128]{2,1,0:T(8,128)}) custom-call(s32[8]{0:T(128)} %seeds_ref.1, f32[8,8]{1,0:T(8,128)} %levels_ref.1, f32[8,64,256]{2,1,0:T(8,128)} %src_ref.1, s32[64,256]{1,0:T(8,128)} %cls_ref.1, f32[9,16,256]{2,1,0:T(8,128)} %pad_maximum_fusion.rows_ref, f32[80,128]{1,0:T(8,128)} %get-tuple-element.13.high_ref, ...), custom_call_target="tpu_custom_call" | custom-call | tf_op jit(solution)/shard_map/pallas_call | solution.py:201
  (5 shorter events, 0.1 us)
Async XLA Ops:
  0.6 5.4 %copy-start = (f32[8,64,256]{2,1,0:T(8,128)S(1)}, f32[8,64,256]{2,1,0:T(8,128)}, u32[]{:S(2)}) copy-start(f32[8,64,256]{2,1,0:T(8,128)} %src_ref.1) | copy-start | bytes 1572868
  2.3 3.6 %copy-start.1 = (s32[64,256]{1,0:T(8,128)S(1)}, s32[64,256]{1,0:T(8,128)}, u32[]{:S(2)}) copy-start(s32[64,256]{1,0:T(8,128)} %cls_ref.1) | copy-start | bytes 196612
  2.3 4.4 %collective-permute-start = (f32[9,8,256]{2,1,0:T(8,128)S(1)}, f32[9,8,256]{2,1,0:T(8,128)S(1)}, u32[]{:S(2)}, u32[]{:S(2)}) collective-permute-start(f32[9,8,256]{2,1,0:T(8,128)S(1)} %get-tuple-element.10), channel_id=1, source_target_pairs={{0,8},{8,0},{16,24},{24,16},{1,9},{9,1},{17,25},{25,17},{2,10},{10... | collective-permute-start | bytes 221192 | tf_op jit(solution)/shard_map/ppermute | solution.py:22
  4.0 6.2 %collective-permute-start.1 = (f32[9,8,256]{2,1,0:T(8,128)S(1)}, f32[9,8,256]{2,1,0:T(8,128)S(1)}, u32[]{:S(2)}, u32[]{:S(2)}) collective-permute-start(f32[9,8,256]{2,1,0:T(8,128)S(1)} %get-tuple-element.11), channel_id=1, source_target_pairs={{8,16},{16,8},{9,17},{17,9},{10,18},{18,10},{11,19},{19,11},{12,20... | collective-permute-start | bytes 221192 | tf_op jit(solution)/shard_map/ppermute | solution.py:21
  10.9 5.3 %collective-permute-start.3 = (f32[80,128]{1,0:T(8,128)S(1)}, f32[80,128]{1,0:T(8,128)S(1)}, u32[]{:S(2)}, u32[]{:S(2)}) collective-permute-start(f32[80,128]{1,0:T(8,128)S(1)} %get-tuple-element.14), channel_id=1, source_target_pairs={{2,4},{4,2},{3,5},{5,3},{10,12},{12,10},{11,13},{13,11},{18,20},{2... | collective-permute-start | bytes 122888 | tf_op jit(solution)/shard_map/ppermute | solution.py:21
  12.8 3.4 %collective-permute-start.2 = (f32[80,128]{1,0:T(8,128)S(1)}, f32[80,128]{1,0:T(8,128)S(1)}, u32[]{:S(2)}, u32[]{:S(2)}) collective-permute-start(f32[80,128]{1,0:T(8,128)S(1)} %get-tuple-element.15), channel_id=1, source_target_pairs={{0,2},{2,0},{4,6},{6,4},{1,3},{3,1},{5,7},{7,5},{8,10},{10,8},{12,... | collective-permute-start | bytes 122888 | tf_op jit(solution)/shard_map/ppermute | solution.py:22

commit v16 on v12

--- a/solution.py
+++ b/solution.py
@@ -40,8 +40,14 @@
 
     last = packed(stack(source[:, :, -width:], classes[:, -width:]), rows_halo[:, :, -width:])
     first = packed(stack(source[:, :, :width], classes[:, :width]), rows_halo[:, :, :width])
-    low, high = swap_exchange(last, first, "gy")
-    return rows_halo, high, low
+    n = lax.axis_size("gy")
+    even = lax.axis_index("gy") % 2 == 0
+    one = lax.ppermute(jnp.where(even, last, first), "gy", [(k, k ^ 1) for k in range(n) if k ^ 1 < n])
+    two = lax.ppermute(
+        jnp.where(even, first, last), "gy",
+        [(k, k + 1) for k in range(1, n - 1, 2)] + [(k + 1, k) for k in range(1, n - 1, 2)],
+    )
+    return rows_halo, one, two, even.astype(jnp.int32)[None]
 
 
 def rolled(v, step):
@@ -80,9 +86,7 @@
     )
 
 
-def lane_tiles(high_ref, low_ref, plane):
-    high = high_ref[...]
-    low = low_ref[...]
+def lane_tiles(high, low, plane):
     lane = lax.broadcasted_iota(jnp.int32, high.shape, 1)
     after = pltpu.roll(high, (LANE_PAD - HALO * plane) % LANE_PAD, 1)
     before = pltpu.roll(low, (LANE_PAD - HALO - HALO * plane) % LANE_PAD, 1)
@@ -97,7 +101,7 @@
 
 
 def smooth_kernel(
-    seeds_ref, levels_ref, src_ref, cls_ref, rows_ref, high_ref, low_ref,
+    seeds_ref, levels_ref, parity_ref, src_ref, cls_ref, rows_ref, one_ref, two_ref,
     sol_ref, corr_ref, codes_pk, spare, wide,
 ):
     s = pl.program_id(0)
@@ -106,6 +110,9 @@
     ext_x, width = codes_pk.shape
     span = cols + 2 * HALO
     lane = lax.broadcasted_iota(jnp.int32, (ext_x, width), 1)
+    even_y = parity_ref[0] == 1
+    high_y = jnp.where(even_y, one_ref[...], two_ref[...])
+    low_y = jnp.where(even_y, two_ref[...], one_ref[...])
 
     def packed(pieces):
         out = None
@@ -116,7 +123,7 @@
 
     @pl.when(s == 0)
     def _():
-        after, before = lane_tiles(high_ref, low_ref, count)
+        after, before = lane_tiles(high_y, low_y, count)
         own = base_layout(
             cls_ref[...] + 1, rows_ref[count].astype(jnp.int32),
             after.astype(jnp.int32), before.astype(jnp.int32), width,
@@ -126,7 +133,7 @@
     pieces = []
     for j in range(PER_STEP):
         plane = PER_STEP * s + j
-        after, before = lane_tiles(high_ref, low_ref, plane)
+        after, before = lane_tiles(high_y, low_y, plane)
         pieces.append(base_layout(src_ref[j], rows_ref[plane], after, before, width))
     source = packed(pieces)
     codes = codes_pk[...]
@@ -194,7 +201,7 @@
     count, rows, cols = source.shape
     ext_x = rows + 2 * h
     width = -(-(PER_STEP * (cols + 2 * h)) // 128) * 128
-    rows_halo, high, low = halo_pieces(source, perm_classes, h)
+    rows_halo, one, two, parity = halo_pieces(source, perm_classes, h)
     smem = pl.BlockSpec(memory_space=pltpu.MemorySpace.SMEM)
     vmem = pl.BlockSpec(memory_space=pltpu.MemorySpace.VMEM)
     whole = lambda shape: pl.BlockSpec(shape, lambda s: (0,) * len(shape))
@@ -204,6 +211,7 @@
         in_specs=[
             smem,
             smem,
+            smem,
             pl.BlockSpec((PER_STEP, rows, cols), lambda s: (s, 0, 0)),
             whole((rows, cols)),
             vmem,
@@ -224,7 +232,7 @@
             pltpu.VMEM((cols // 128, rows, 128), jnp.float32),
         ],
         compiler_params=pltpu.CompilerParams(dimension_semantics=("arbitrary",)),
-    )(sample_seeds, perm_levels, source, perm_classes, rows_halo, high, low)
+    )(sample_seeds, perm_levels, parity, source, perm_classes, rows_halo, one, two)
     return solution_block, correction_block
 
 

time: 25.8 us -> 25.8 us (level)
  other arithmetic: 2.4 us -> 1.76 us
  local copies, waits for them, and re-layouts: 1.81 us -> 2.44 us
    ppermute x0 -> x2, waiting for transfers between devices: none -> 2.64 us  [the longest x1 2.64 us: halo_pieces(): lax.ppermute(jnp.where(even, first, last), 'gy', [(k, k + 1) for k in ran...]
    ppermute x2 -> x1, waiting for transfers between devices: 6.09 us -> 3.46 us  [swap_exchange(): two = lax.ppermute(jnp.where(even, first, last), axis, outer)]
    ppermute x0 -> x2, starting transfers between devices: none -> 1.99 us  [the longest x1 1.92 us: halo_pieces(): lax.ppermute(jnp.where(even, first, last), 'gy', [(k, k + 1) for k in ran...]
    ppermute x2 -> x1, starting transfers between devices: 3.83 us -> 1.91 us  [swap_exchange(): two = lax.ppermute(jnp.where(even, first, last), axis, outer)]
    unnamed x8 -> x12, local copies, waits for them, and re-layouts: 0.38 us -> 1.02 us
    select_n x2 -> x1, other arithmetic: 0.65 us -> 0.01 us  [swap_exchange(): return (jnp.where(even, two, one), jnp.where(even, one, two))]
    ppermute x2 -> x1, starting transfers between devices: 1.71 us -> 1.64 us  [swap_exchange(): one = lax.ppermute(jnp.where(even, last, first), axis, inner)]
where the time goes in v16:
time: 25.8 us; the launch traced here: 25.6 us
  Pallas kernels  8.73 us (34%)
  waiting for transfers between devices  6.35 us (25%)
  starting transfers between devices  5.54 us (21%)
  local copies, waits for them, and re-layouts  2.44 us (9%)
  other arithmetic  1.76 us (7%)
  between operations  0.74 us (3%)
    pallas_call x1, Pallas kernels, shards(): pl.pallas_call(smooth_kernel, grid=(count // PER_STEP,), in_specs=[smem,...  8.73 us
    ppermute x1, waiting for transfers between devices, swap_exchange(): two = lax.ppermute(jnp.where(even, first, last), axis, outer)  3.46 us
    ppermute x1, waiting for transfers between devices, halo_pieces(): lax.ppermute(jnp.where(even, first, last), 'gy', [(k, k + 1) for k in ran...  2.64 us
    ppermute x1, starting transfers between devices, halo_pieces(): lax.ppermute(jnp.where(even, first, last), 'gy', [(k, k + 1) for k in ran...  1.92 us
    ppermute x1, starting transfers between devices, swap_exchange(): two = lax.ppermute(jnp.where(even, first, last), axis, outer)  1.91 us
    ppermute x1, starting transfers between devices, swap_exchange(): one = lax.ppermute(jnp.where(even, last, first), axis, inner)  1.64 us
    unnamed x12, local copies, waits for them, and re-layouts  1.02 us
    slice x1, local copies, waits for them, and re-layouts, halo_pieces(): source[:, -width:, :]  0.88 us
  transfers between devices with their start and end apart: 4, of which 3 were waited for; matrix products, arithmetic and copies ran while one was open for 5% of the time, Pallas kernels for 0%

profile of v16, /device:TPU:18, one launch (start us, length us, event | category | flops | bytes accessed | tf_op | source)
XLA Modules:
  0.0 25.6 jit_solution(18178508648624770198)
XLA Ops:
  0.6 0.0 copy-start
  0.7 0.8 %convert_bitcast_fusion.1 = (f32[1,8,256]{2,1,0:T(8,128)S(1)}, f32[1,8,256]{2,1,0:T(8,128)S(1)}) fusion(s32[64,256]{1,0:T(8,128)} %cls_ref.1), kind=kLoop, calls=%fused_computation.18 | loop fusion | flops 8192 | bytes 32768 | tf_op jit(solution)/shard_map/broadcast_in_dim | solution.py:27
  1.4 0.9 %fusion.5 = (f32[8,8,256]{2,1,0:T(8,128)S(1)}, f32[8,8,256]{2,1,0:T(8,128)S(1)}) fusion(f32[8,64,256]{2,1,0:T(8,128)} %src_ref.1), kind=kLoop, calls=%fused_computation.22 | loop fusion | bytes 262144 | tf_op jit(solution)/shard_map/slice | solution.py:29
  2.3 0.0 copy-start.1
  2.3 1.6 %collective-permute-start = (f32[9,8,256]{2,1,0:T(8,128)S(1)}, f32[9,8,256]{2,1,0:T(8,128)S(1)}, u32[]{:S(2)}, u32[]{:S(2)}) collective-permute-start(f32[9,8,256]{2,1,0:T(8,128)S(1)} %get-tuple-element.10), channel_id=1, source_target_pairs={{0,8},{8,0},{16,24},{24,16},{1,9},{9,1},{17,25},{25,17},{2,10},{10... | collective-permute-start | bytes 221192 | tf_op jit(solution)/shard_map/ppermute | solution.py:21
  4.0 1.9 %collective-permute-start.1 = (f32[9,8,256]{2,1,0:T(8,128)S(1)}, f32[9,8,256]{2,1,0:T(8,128)S(1)}, u32[]{:S(2)}, u32[]{:S(2)}) collective-permute-start(f32[9,8,256]{2,1,0:T(8,128)S(1)} %get-tuple-element.11), channel_id=1, source_target_pairs={{8,16},{16,8},{9,17},{17,9},{10,18},{18,10},{11,19},{19,11},{12,20... | collective-permute-start | bytes 221192 | tf_op jit(solution)/shard_map/ppermute | solution.py:22
  5.9 0.0 copy-done.1
  5.9 0.1 fusion.6
  6.0 0.0 copy-done
  6.0 0.1 fusion.4
  6.1 0.1 copy.17
  6.2 0.1 copy.19
  6.3 0.1 copy.16
  6.4 0.1 copy.18
  6.5 0.2 collective-permute-done
  6.8 3.5 %collective-permute-done.1 = f32[9,8,256]{2,1,0:T(8,128)S(1)} collective-permute-done((f32[9,8,256]{2,1,0:T(8,128)S(1)}, f32[9,8,256]{2,1,0:T(8,128)S(1)}, u32[]{:S(2)}, u32[]{:S(2)}) %collective-permute-start.1) | collective-permute-done | bytes 73760 | tf_op jit(solution)/shard_map/ppermute | solution.py:22
  10.2 0.1 fusion
  10.3 0.1 copy.10
  10.4 0.1 copy.14
  10.5 0.1 maximum_bitcast_fusion
  10.6 0.1 copy.11
  10.7 0.1 maximum_bitcast_fusion.1
  10.8 0.1 copy.15
  10.9 1.9 %collective-permute-start.3 = (f32[80,128]{1,0:T(8,128)S(1)}, f32[80,128]{1,0:T(8,128)S(1)}, u32[]{:S(2)}, u32[]{:S(2)}) collective-permute-start(f32[80,128]{1,0:T(8,128)S(1)} %get-tuple-element.12), channel_id=1, source_target_pairs={{2,4},{4,2},{3,5},{5,3},{10,12},{12,10},{11,13},{13,11},{18,20},{2... | collective-permute-start | bytes 122888 | tf_op jit(solution)/shard_map/ppermute | solution.py:46
  12.8 0.1 collective-permute-start.2
  12.9 0.7 %pad_maximum_fusion.rows_ref = f32[9,16,256]{2,1,0:T(8,128)} fusion(f32[9,8,256]{2,1,0:T(8,128)S(1)} %get-tuple-element.9, f32[9,8,256]{2,1,0:T(8,128)S(1)} %get-tuple-element.8), kind=kLoop, calls=%fused_computation.2 | loop fusion | flops 36864 | bytes 294912 | tf_op jit(solution)/shard_map/concatenate | solution.py:33
  13.6 2.6 %collective-permute-done.3.two_ref = f32[80,128]{1,0:T(8,128)S(1)} collective-permute-done((f32[80,128]{1,0:T(8,128)S(1)}, f32[80,128]{1,0:T(8,128)S(1)}, u32[]{:S(2)}, u32[]{:S(2)}) %collective-permute-start.3) | collective-permute-done | bytes 40992 | tf_op jit(solution)/shard_map/ppermute | solution.py:46
  16.2 0.0 copy-start.2
  16.2 0.0 collective-permute-done.2.one_ref
  16.2 0.0 copy-start.3
  16.2 0.6 %copy-done.2 = f32[80,128]{1,0:T(8,128)} copy-done((f32[80,128]{1,0:T(8,128)}, f32[80,128]{1,0:T(8,128)S(1)}, u32[]{:S(2)}) %copy-start.2) | copy-done | bytes 40984
  16.8 0.0 copy-done.3
  16.8 8.7 %shard_map.59 = (f32[8,64,256]{2,1,0:T(8,128)}, f32[8,32,128]{2,1,0:T(8,128)}) custom-call(s32[8]{0:T(128)} %seeds_ref.1, f32[8,8]{1,0:T(8,128)} %levels_ref.1, s32[1]{0:T(128)} %bitcast.parity_ref, f32[8,64,256]{2,1,0:T(8,128)} %src_ref.1, s32[64,256]{1,0:T(8,128)} %cls_ref.1, f32[9,16,256]{2,1,0:T(8,128)} %pad_maximum_fusion.rows_ref, ...), custom_call_target="tpu_custom_call" | custom-call | tf_op jit(solution)/shard_map/pallas_call | solution.py:208
  (5 shorter events, 0.1 us)
Async XLA Ops:
  0.6 5.4 %copy-start = (f32[8,64,256]{2,1,0:T(8,128)S(1)}, f32[8,64,256]{2,1,0:T(8,128)}, u32[]{:S(2)}) copy-start(f32[8,64,256]{2,1,0:T(8,128)} %src_ref.1) | copy-start | bytes 1572868
  2.3 3.6 %copy-start.1 = (s32[64,256]{1,0:T(8,128)S(1)}, s32[64,256]{1,0:T(8,128)}, u32[]{:S(2)}) copy-start(s32[64,256]{1,0:T(8,128)} %cls_ref.1) | copy-start | bytes 196612
  2.3 4.4 %collective-permute-start = (f32[9,8,256]{2,1,0:T(8,128)S(1)}, f32[9,8,256]{2,1,0:T(8,128)S(1)}, u32[]{:S(2)}, u32[]{:S(2)}) collective-permute-start(f32[9,8,256]{2,1,0:T(8,128)S(1)} %get-tuple-element.10), channel_id=1, source_target_pairs={{0,8},{8,0},{16,24},{24,16},{1,9},{9,1},{17,25},{25,17},{2,10},{10... | collective-permute-start | bytes 221192 | tf_op jit(solution)/shard_map/ppermute | solution.py:21
  4.0 6.2 %collective-permute-start.1 = (f32[9,8,256]{2,1,0:T(8,128)S(1)}, f32[9,8,256]{2,1,0:T(8,128)S(1)}, u32[]{:S(2)}, u32[]{:S(2)}) collective-permute-start(f32[9,8,256]{2,1,0:T(8,128)S(1)} %get-tuple-element.11), channel_id=1, source_target_pairs={{8,16},{16,8},{9,17},{17,9},{10,18},{18,10},{11,19},{19,11},{12,20... | collective-permute-start | bytes 221192 | tf_op jit(solution)/shard_map/ppermute | solution.py:22
  10.9 5.3 %collective-permute-start.3 = (f32[80,128]{1,0:T(8,128)S(1)}, f32[80,128]{1,0:T(8,128)S(1)}, u32[]{:S(2)}, u32[]{:S(2)}) collective-permute-start(f32[80,128]{1,0:T(8,128)S(1)} %get-tuple-element.12), channel_id=1, source_target_pairs={{2,4},{4,2},{3,5},{5,3},{10,12},{12,10},{11,13},{13,11},{18,20},{2... | collective-permute-start | bytes 122888 | tf_op jit(solution)/shard_map/ppermute | solution.py:46
  12.8 3.4 %collective-permute-start.2 = (f32[80,128]{1,0:T(8,128)S(1)}, f32[80,128]{1,0:T(8,128)S(1)}, u32[]{:S(2)}, u32[]{:S(2)}) collective-permute-start(f32[80,128]{1,0:T(8,128)S(1)} %get-tuple-element.13), channel_id=1, source_target_pairs={{0,2},{2,0},{4,6},{6,4},{1,3},{3,1},{5,7},{7,5},{8,10},{10,8},{12,... | collective-permute-start | bytes 122888 | tf_op jit(solution)/shard_map/ppermute | solution.py:45
  16.2 0.6 %copy-start.2 = (f32[80,128]{1,0:T(8,128)}, f32[80,128]{1,0:T(8,128)S(1)}, u32[]{:S(2)}) copy-start(f32[80,128]{1,0:T(8,128)S(1)} %collective-permute-done.3.two_ref) | copy-start | bytes 122884
  16.2 0.6 %copy-start.3 = (f32[80,128]{1,0:T(8,128)}, f32[80,128]{1,0:T(8,128)S(1)}, u32[]{:S(2)}) copy-start(f32[80,128]{1,0:T(8,128)S(1)} %collective-permute-done.2.one_ref) | copy-start | bytes 122884

commit v17 on v16

--- a/solution.py
+++ b/solution.py
@@ -40,6 +40,7 @@
 
     last = packed(stack(source[:, :, -width:], classes[:, -width:]), rows_halo[:, :, -width:])
     first = packed(stack(source[:, :, :width], classes[:, :width]), rows_halo[:, :, :width])
+    rows_halo, last, first = lax.optimization_barrier((rows_halo, last, first))
     n = lax.axis_size("gy")
     even = lax.axis_index("gy") % 2 == 0
     one = lax.ppermute(jnp.where(even, last, first), "gy", [(k, k ^ 1) for k in range(n) if k ^ 1 < n])

time: 25.8 us -> 26.5 us (1.027)
  waiting for transfers between devices: 6.35 us -> 7.02 us
    ppermute x1, waiting for transfers between devices: 2.64 us -> 3.31 us  [halo_pieces(): lax.ppermute(jnp.where(even, first, last), 'gy', [(k, k + 1) for k in ran...]
  transfers between devices with their start and end apart: 4 -> 4, of which waited for: 3 -> 3; matrix products, arithmetic and copies ran while one was open for 5% -> 2% of each run, Pallas kernels for 0% -> 0%
where the time goes in v17:
time: 26.5 us; the launch traced here: 26.3 us
  Pallas kernels  8.73 us (33%)
  waiting for transfers between devices  7.02 us (26%)
  starting transfers between devices  5.54 us (21%)
  local copies, waits for them, and re-layouts  2.46 us (9%)
  other arithmetic  1.76 us (7%)
  between operations  0.76 us (3%)
    pallas_call x1, Pallas kernels, shards(): pl.pallas_call(smooth_kernel, grid=(count // PER_STEP,), in_specs=[smem,...  8.73 us
    ppermute x1, waiting for transfers between devices, swap_exchange(): two = lax.ppermute(jnp.where(even, first, last), axis, outer)  3.46 us
    ppermute x1, waiting for transfers between devices, halo_pieces(): lax.ppermute(jnp.where(even, first, last), 'gy', [(k, k + 1) for k in ran...  3.31 us
    ppermute x1, starting transfers between devices, halo_pieces(): lax.ppermute(jnp.where(even, first, last), 'gy', [(k, k + 1) for k in ran...  1.92 us
    ppermute x1, starting transfers between devices, swap_exchange(): two = lax.ppermute(jnp.where(even, first, last), axis, outer)  1.91 us
    ppermute x1, starting transfers between devices, swap_exchange(): one = lax.ppermute(jnp.where(even, last, first), axis, inner)  1.64 us
    unnamed x12, local copies, waits for them, and re-layouts  1.02 us
    slice x1, local copies, waits for them, and re-layouts, halo_pieces(): source[:, -width:, :]  0.88 us
  transfers between devices with their start and end apart: 4, of which 3 were waited for; matrix products, arithmetic and copies ran while one was open for 2% of the time, Pallas kernels for 0%

profile of v17, /device:TPU:18, one launch (start us, length us, event | category | flops | bytes accessed | tf_op | source)
XLA Modules:
  0.0 26.3 jit_solution(15399522616109897140)
XLA Ops:
  0.6 0.0 copy-start
  0.7 0.8 %convert_bitcast_fusion.1 = (f32[1,8,256]{2,1,0:T(8,128)S(1)}, f32[1,8,256]{2,1,0:T(8,128)S(1)}) fusion(s32[64,256]{1,0:T(8,128)} %cls_ref.1), kind=kLoop, calls=%fused_computation.18 | loop fusion | flops 8192 | bytes 32768 | tf_op jit(solution)/shard_map/broadcast_in_dim | solution.py:27
  1.4 0.9 %fusion.5 = (f32[8,8,256]{2,1,0:T(8,128)S(1)}, f32[8,8,256]{2,1,0:T(8,128)S(1)}) fusion(f32[8,64,256]{2,1,0:T(8,128)} %src_ref.1), kind=kLoop, calls=%fused_computation.22 | loop fusion | bytes 262144 | tf_op jit(solution)/shard_map/slice | solution.py:29
  2.3 0.0 copy-start.1
  2.3 1.6 %collective-permute-start = (f32[9,8,256]{2,1,0:T(8,128)S(1)}, f32[9,8,256]{2,1,0:T(8,128)S(1)}, u32[]{:S(2)}, u32[]{:S(2)}) collective-permute-start(f32[9,8,256]{2,1,0:T(8,128)S(1)} %get-tuple-element.16), channel_id=1, source_target_pairs={{0,8},{8,0},{16,24},{24,16},{1,9},{9,1},{17,25},{25,17},{2,10},{10... | collective-permute-start | bytes 221192 | tf_op jit(solution)/shard_map/ppermute | solution.py:21
  4.0 1.9 %collective-permute-start.1 = (f32[9,8,256]{2,1,0:T(8,128)S(1)}, f32[9,8,256]{2,1,0:T(8,128)S(1)}, u32[]{:S(2)}, u32[]{:S(2)}) collective-permute-start(f32[9,8,256]{2,1,0:T(8,128)S(1)} %get-tuple-element.17), channel_id=1, source_target_pairs={{8,16},{16,8},{9,17},{17,9},{10,18},{18,10},{11,19},{19,11},{12,20... | collective-permute-start | bytes 221192 | tf_op jit(solution)/shard_map/ppermute | solution.py:22
  5.9 0.0 copy-done.1
  5.9 0.1 fusion.6
  6.0 0.0 copy-done
  6.0 0.1 fusion.4
  6.1 0.1 copy.19
  6.2 0.1 copy.17
  6.3 0.1 copy.18
  6.4 0.1 copy.16
  6.5 0.2 collective-permute-done
  6.8 3.5 %collective-permute-done.1 = f32[9,8,256]{2,1,0:T(8,128)S(1)} collective-permute-done((f32[9,8,256]{2,1,0:T(8,128)S(1)}, f32[9,8,256]{2,1,0:T(8,128)S(1)}, u32[]{:S(2)}, u32[]{:S(2)}) %collective-permute-start.1) | collective-permute-done | bytes 73760 | tf_op jit(solution)/shard_map/ppermute | solution.py:22
  10.2 0.7 %pad_maximum_fusion.rows_ref = f32[9,16,256]{2,1,0:T(8,128)} fusion(f32[9,8,256]{2,1,0:T(8,128)S(1)} %get-tuple-element.15, f32[9,8,256]{2,1,0:T(8,128)S(1)} %get-tuple-element.14), kind=kLoop, calls=%fused_computation.2 | loop fusion | flops 36864 | bytes 294912 | tf_op jit(solution)/shard_map/concatenate | solution.py:33
  10.9 0.1 fusion.1
  11.0 0.1 copy.14
  11.1 0.1 copy.10
  11.2 0.1 maximum_bitcast_fusion.1
  11.3 0.1 copy.15
  11.3 0.1 maximum_bitcast_fusion
  11.4 0.1 copy.11
  11.6 1.9 %collective-permute-start.3 = (f32[80,128]{1,0:T(8,128)S(1)}, f32[80,128]{1,0:T(8,128)S(1)}, u32[]{:S(2)}, u32[]{:S(2)}) collective-permute-start(f32[80,128]{1,0:T(8,128)S(1)} %get-tuple-element.18), channel_id=1, source_target_pairs={{2,4},{4,2},{3,5},{5,3},{10,12},{12,10},{11,13},{13,11},{18,20},{2... | collective-permute-start | bytes 122888 | tf_op jit(solution)/shard_map/ppermute | solution.py:47
  13.5 0.1 collective-permute-start.2
  13.6 3.3 %collective-permute-done.3.two_ref = f32[80,128]{1,0:T(8,128)S(1)} collective-permute-done((f32[80,128]{1,0:T(8,128)S(1)}, f32[80,128]{1,0:T(8,128)S(1)}, u32[]{:S(2)}, u32[]{:S(2)}) %collective-permute-start.3) | collective-permute-done | bytes 40992 | tf_op jit(solution)/shard_map/ppermute | solution.py:47
  16.9 0.0 copy-start.2
  16.9 0.0 collective-permute-done.2.one_ref
  16.9 0.0 copy-start.3
  16.9 0.6 %copy-done.2 = f32[80,128]{1,0:T(8,128)} copy-done((f32[80,128]{1,0:T(8,128)}, f32[80,128]{1,0:T(8,128)S(1)}, u32[]{:S(2)}) %copy-start.2) | copy-done | bytes 40984
  17.5 0.0 copy-done.3
  17.5 8.7 %shard_map.59 = (f32[8,64,256]{2,1,0:T(8,128)}, f32[8,32,128]{2,1,0:T(8,128)}) custom-call(s32[8]{0:T(128)} %seeds_ref.1, f32[8,8]{1,0:T(8,128)} %levels_ref.1, s32[1]{0:T(128)} %bitcast.parity_ref, f32[8,64,256]{2,1,0:T(8,128)} %src_ref.1, s32[64,256]{1,0:T(8,128)} %cls_ref.1, f32[9,16,256]{2,1,0:T(8,128)} %pad_maximum_fusion.rows_ref, ...), custom_call_target="tpu_custom_call" | custom-call | tf_op jit(solution)/shard_map/pallas_call | solution.py:209
  (7 shorter events, 0.1 us)
Async XLA Ops:
  0.6 5.4 %copy-start = (f32[8,64,256]{2,1,0:T(8,128)S(1)}, f32[8,64,256]{2,1,0:T(8,128)}, u32[]{:S(2)}) copy-start(f32[8,64,256]{2,1,0:T(8,128)} %src_ref.1) | copy-start | bytes 1572868
  2.3 3.6 %copy-start.1 = (s32[64,256]{1,0:T(8,128)S(1)}, s32[64,256]{1,0:T(8,128)}, u32[]{:S(2)}) copy-start(s32[64,256]{1,0:T(8,128)} %cls_ref.1) | copy-start | bytes 196612
  2.3 4.4 %collective-permute-start = (f32[9,8,256]{2,1,0:T(8,128)S(1)}, f32[9,8,256]{2,1,0:T(8,128)S(1)}, u32[]{:S(2)}, u32[]{:S(2)}) collective-permute-start(f32[9,8,256]{2,1,0:T(8,128)S(1)} %get-tuple-element.16), channel_id=1, source_target_pairs={{0,8},{8,0},{16,24},{24,16},{1,9},{9,1},{17,25},{25,17},{2,10},{10... | collective-permute-start | bytes 221192 | tf_op jit(solution)/shard_map/ppermute | solution.py:21
  4.0 6.2 %collective-permute-start.1 = (f32[9,8,256]{2,1,0:T(8,128)S(1)}, f32[9,8,256]{2,1,0:T(8,128)S(1)}, u32[]{:S(2)}, u32[]{:S(2)}) collective-permute-start(f32[9,8,256]{2,1,0:T(8,128)S(1)} %get-tuple-element.17), channel_id=1, source_target_pairs={{8,16},{16,8},{9,17},{17,9},{10,18},{18,10},{11,19},{19,11},{12,20... | collective-permute-start | bytes 221192 | tf_op jit(solution)/shard_map/ppermute | solution.py:22
  11.6 5.3 %collective-permute-start.3 = (f32[80,128]{1,0:T(8,128)S(1)}, f32[80,128]{1,0:T(8,128)S(1)}, u32[]{:S(2)}, u32[]{:S(2)}) collective-permute-start(f32[80,128]{1,0:T(8,128)S(1)} %get-tuple-element.18), channel_id=1, source_target_pairs={{2,4},{4,2},{3,5},{5,3},{10,12},{12,10},{11,13},{13,11},{18,20},{2... | collective-permute-start | bytes 122888 | tf_op jit(solution)/shard_map/ppermute | solution.py:47
  13.5 3.4 %collective-permute-start.2 = (f32[80,128]{1,0:T(8,128)S(1)}, f32[80,128]{1,0:T(8,128)S(1)}, u32[]{:S(2)}, u32[]{:S(2)}) collective-permute-start(f32[80,128]{1,0:T(8,128)S(1)} %get-tuple-element.19), channel_id=1, source_target_pairs={{0,2},{2,0},{4,6},{6,4},{1,3},{3,1},{5,7},{7,5},{8,10},{10,8},{12,... | collective-permute-start | bytes 122888 | tf_op jit(solution)/shard_map/ppermute | solution.py:46
  16.9 0.6 %copy-start.2 = (f32[80,128]{1,0:T(8,128)}, f32[80,128]{1,0:T(8,128)S(1)}, u32[]{:S(2)}) copy-start(f32[80,128]{1,0:T(8,128)S(1)} %collective-permute-done.3.two_ref) | copy-start | bytes 122884
  16.9 0.6 %copy-start.3 = (f32[80,128]{1,0:T(8,128)}, f32[80,128]{1,0:T(8,128)S(1)}, u32[]{:S(2)}) copy-start(f32[80,128]{1,0:T(8,128)S(1)} %collective-permute-done.2.one_ref) | copy-start | bytes 122884

commit v18 on v12

--- a/solution.py
+++ b/solution.py
@@ -10,7 +10,7 @@
 HALO = 8
 LANE_PAD = 128
 HI = lax.Precision.HIGHEST
-PER_STEP = 4
+PER_STEP = 8
 
 
 def swap_exchange(last, first, axis):

time: 25.8 us -> 24.9 us (0.965)
  Pallas kernels: 8.71 us -> 7.78 us
    pallas_call x1, Pallas kernels: 8.71 us -> 7.78 us  [shards(): pl.pallas_call(smooth_kernel, grid=(count // PER_STEP,), in_specs=[smem,...]
where the time goes in v18:
time: 24.9 us; the launch traced here: 24.6 us
  Pallas kernels  7.78 us (31%)
  waiting for transfers between devices  6.34 us (25%)
  starting transfers between devices  5.54 us (22%)
  other arithmetic  2.4 us (10%)
  local copies, waits for them, and re-layouts  1.81 us (7%)
  between operations  0.74 us (3%)
    pallas_call x1, Pallas kernels, shards(): pl.pallas_call(smooth_kernel, grid=(count // PER_STEP,), in_specs=[smem,...  7.78 us
    ppermute x2, waiting for transfers between devices, swap_exchange(): two = lax.ppermute(jnp.where(even, first, last), axis, outer)  6.09 us
    ppermute x2, starting transfers between devices, swap_exchange(): two = lax.ppermute(jnp.where(even, first, last), axis, outer)  3.83 us
    ppermute x2, starting transfers between devices, swap_exchange(): one = lax.ppermute(jnp.where(even, last, first), axis, inner)  1.71 us
    slice x1, local copies, waits for them, and re-layouts, halo_pieces(): source[:, -width:, :]  0.88 us
    broadcast_in_dim x3, other arithmetic, halo_pieces(): (b + 1).astype(a.dtype)[None]  0.79 us
    concatenate x2, other arithmetic, halo_pieces(): rows_halo = jnp.concatenate([high, low], axis=1)  0.76 us
    select_n x2, other arithmetic, swap_exchange(): return (jnp.where(even, two, one), jnp.where(even, one, two))  0.65 us
  transfers between devices with their start and end apart: 4, of which 3 were waited for; matrix products, arithmetic and copies ran while one was open for 5% of the time, Pallas kernels for 0%

profile of v18, /device:TPU:18, one launch (start us, length us, event | category | flops | bytes accessed | tf_op | source)
XLA Modules:
  0.0 24.6 jit_solution(8024386269941510507)
XLA Ops:
  0.6 0.0 copy-start
  0.7 0.8 %convert_bitcast_fusion.1 = (f32[1,8,256]{2,1,0:T(8,128)S(1)}, f32[1,8,256]{2,1,0:T(8,128)S(1)}) fusion(s32[64,256]{1,0:T(8,128)} %cls_ref.1), kind=kLoop, calls=%fused_computation.20 | loop fusion | flops 8192 | bytes 32768 | tf_op jit(solution)/shard_map/broadcast_in_dim | solution.py:27
  1.4 0.9 %fusion.5 = (f32[8,8,256]{2,1,0:T(8,128)S(1)}, f32[8,8,256]{2,1,0:T(8,128)S(1)}) fusion(f32[8,64,256]{2,1,0:T(8,128)} %src_ref.1), kind=kLoop, calls=%fused_computation.24 | loop fusion | bytes 262144 | tf_op jit(solution)/shard_map/slice | solution.py:29
  2.3 0.0 copy-start.1
  2.3 1.6 %collective-permute-start = (f32[9,8,256]{2,1,0:T(8,128)S(1)}, f32[9,8,256]{2,1,0:T(8,128)S(1)}, u32[]{:S(2)}, u32[]{:S(2)}) collective-permute-start(f32[9,8,256]{2,1,0:T(8,128)S(1)} %get-tuple-element.10), channel_id=1, source_target_pairs={{0,8},{8,0},{16,24},{24,16},{1,9},{9,1},{17,25},{25,17},{2,10},{10... | collective-permute-start | bytes 221192 | tf_op jit(solution)/shard_map/ppermute | solution.py:21
  4.0 1.9 %collective-permute-start.1 = (f32[9,8,256]{2,1,0:T(8,128)S(1)}, f32[9,8,256]{2,1,0:T(8,128)S(1)}, u32[]{:S(2)}, u32[]{:S(2)}) collective-permute-start(f32[9,8,256]{2,1,0:T(8,128)S(1)} %get-tuple-element.11), channel_id=1, source_target_pairs={{8,16},{16,8},{9,17},{17,9},{10,18},{18,10},{11,19},{19,11},{12,20... | collective-permute-start | bytes 221192 | tf_op jit(solution)/shard_map/ppermute | solution.py:22
  5.9 0.0 copy-done.1
  5.9 0.1 fusion.6
  6.0 0.0 copy-done
  6.0 0.1 fusion.4
  6.1 0.1 copy.17
  6.2 0.1 copy.19
  6.3 0.1 copy.16
  6.4 0.1 copy.18
  6.5 0.2 %collective-permute-done = f32[9,8,256]{2,1,0:T(8,128)S(1)} collective-permute-done((f32[9,8,256]{2,1,0:T(8,128)S(1)}, f32[9,8,256]{2,1,0:T(8,128)S(1)}, u32[]{:S(2)}, u32[]{:S(2)}) %collective-permute-start) | collective-permute-done | bytes 73760 | tf_op jit(solution)/shard_map/ppermute | solution.py:21
  6.8 3.5 %collective-permute-done.1 = f32[9,8,256]{2,1,0:T(8,128)S(1)} collective-permute-done((f32[9,8,256]{2,1,0:T(8,128)S(1)}, f32[9,8,256]{2,1,0:T(8,128)S(1)}, u32[]{:S(2)}, u32[]{:S(2)}) %collective-permute-start.1) | collective-permute-done | bytes 73760 | tf_op jit(solution)/shard_map/ppermute | solution.py:22
  10.2 0.1 fusion
  10.3 0.1 copy.10
  10.4 0.1 copy.14
  10.5 0.1 maximum_bitcast_fusion
  10.6 0.1 copy.11
  10.7 0.1 maximum_bitcast_fusion.1
  10.8 0.1 copy.15
  10.9 1.9 %collective-permute-start.3 = (f32[80,128]{1,0:T(8,128)S(1)}, f32[80,128]{1,0:T(8,128)S(1)}, u32[]{:S(2)}, u32[]{:S(2)}) collective-permute-start(f32[80,128]{1,0:T(8,128)S(1)} %get-tuple-element.14), channel_id=1, source_target_pairs={{2,4},{4,2},{3,5},{5,3},{10,12},{12,10},{11,13},{13,11},{18,20},{2... | collective-permute-start | bytes 122888 | tf_op jit(solution)/shard_map/ppermute | solution.py:22
  12.8 0.1 collective-permute-start.2
  12.9 0.7 %pad_maximum_fusion.rows_ref = f32[9,16,256]{2,1,0:T(8,128)} fusion(f32[9,8,256]{2,1,0:T(8,128)S(1)} %get-tuple-element.9, f32[9,8,256]{2,1,0:T(8,128)S(1)} %get-tuple-element.8), kind=kLoop, calls=%fused_computation.2 | loop fusion | flops 36864 | bytes 294912 | tf_op jit(solution)/shard_map/concatenate | solution.py:33
  13.6 2.6 %collective-permute-done.3 = f32[80,128]{1,0:T(8,128)S(1)} collective-permute-done((f32[80,128]{1,0:T(8,128)S(1)}, f32[80,128]{1,0:T(8,128)S(1)}, u32[]{:S(2)}, u32[]{:S(2)}) %collective-permute-start.3) | collective-permute-done | bytes 40992 | tf_op jit(solution)/shard_map/ppermute | solution.py:22
  16.2 0.0 collective-permute-done.2
  16.2 0.6 %broadcast_select_fusion.2 = (f32[80,128]{1,0:T(8,128)}, f32[80,128]{1,0:T(8,128)}) fusion(f32[80,128]{1,0:T(8,128)S(1)} %collective-permute-done.3, f32[80,128]{1,0:T(8,128)S(1)} %collective-permute-done.2, pred[]{:T(512)S(6)} %eq.10), kind=kLoop, calls=%fused_computation.17 | loop fusion | flops 20480 | bytes 163841 | tf_op jit(solution)/shard_map/jit(_where)/select_n | solution.py:23
  16.8 7.8 %shard_map.59 = (f32[8,64,256]{2,1,0:T(8,128)}, f32[8,32,128]{2,1,0:T(8,128)}) custom-call(s32[8]{0:T(128)} %seeds_ref.1, f32[8,8]{1,0:T(8,128)} %levels_ref.1, f32[8,64,256]{2,1,0:T(8,128)} %src_ref.1, s32[64,256]{1,0:T(8,128)} %cls_ref.1, f32[9,16,256]{2,1,0:T(8,128)} %pad_maximum_fusion.rows_ref, f32[80,128]{1,0:T(8,128)} %get-tuple-element.13.high_ref, ...), custom_call_target="tpu_custom_call" | custom-call | tf_op jit(solution)/shard_map/pallas_call | solution.py:201
  (5 shorter events, 0.1 us)
Async XLA Ops:
  0.6 5.4 %copy-start = (f32[8,64,256]{2,1,0:T(8,128)S(1)}, f32[8,64,256]{2,1,0:T(8,128)}, u32[]{:S(2)}) copy-start(f32[8,64,256]{2,1,0:T(8,128)} %src_ref.1) | copy-start | bytes 1572868
  2.3 3.6 %copy-start.1 = (s32[64,256]{1,0:T(8,128)S(1)}, s32[64,256]{1,0:T(8,128)}, u32[]{:S(2)}) copy-start(s32[64,256]{1,0:T(8,128)} %cls_ref.1) | copy-start | bytes 196612
  2.3 4.4 %collective-permute-start = (f32[9,8,256]{2,1,0:T(8,128)S(1)}, f32[9,8,256]{2,1,0:T(8,128)S(1)}, u32[]{:S(2)}, u32[]{:S(2)}) collective-permute-start(f32[9,8,256]{2,1,0:T(8,128)S(1)} %get-tuple-element.10), channel_id=1, source_target_pairs={{0,8},{8,0},{16,24},{24,16},{1,9},{9,1},{17,25},{25,17},{2,10},{10... | collective-permute-start | bytes 221192 | tf_op jit(solution)/shard_map/ppermute | solution.py:21
  4.0 6.2 %collective-permute-start.1 = (f32[9,8,256]{2,1,0:T(8,128)S(1)}, f32[9,8,256]{2,1,0:T(8,128)S(1)}, u32[]{:S(2)}, u32[]{:S(2)}) collective-permute-start(f32[9,8,256]{2,1,0:T(8,128)S(1)} %get-tuple-element.11), channel_id=1, source_target_pairs={{8,16},{16,8},{9,17},{17,9},{10,18},{18,10},{11,19},{19,11},{12,20... | collective-permute-start | bytes 221192 | tf_op jit(solution)/shard_map/ppermute | solution.py:22
  10.9 5.3 %collective-permute-start.3 = (f32[80,128]{1,0:T(8,128)S(1)}, f32[80,128]{1,0:T(8,128)S(1)}, u32[]{:S(2)}, u32[]{:S(2)}) collective-permute-start(f32[80,128]{1,0:T(8,128)S(1)} %get-tuple-element.14), channel_id=1, source_target_pairs={{2,4},{4,2},{3,5},{5,3},{10,12},{12,10},{11,13},{13,11},{18,20},{2... | collective-permute-start | bytes 122888 | tf_op jit(solution)/shard_map/ppermute | solution.py:22
  12.8 3.4 %collective-permute-start.2 = (f32[80,128]{1,0:T(8,128)S(1)}, f32[80,128]{1,0:T(8,128)S(1)}, u32[]{:S(2)}, u32[]{:S(2)}) collective-permute-start(f32[80,128]{1,0:T(8,128)S(1)} %get-tuple-element.15), channel_id=1, source_target_pairs={{0,2},{2,0},{4,6},{6,4},{1,3},{3,1},{5,7},{7,5},{8,10},{10,8},{12,... | collective-permute-start | bytes 122888 | tf_op jit(solution)/shard_map/ppermute | solution.py:21

commit v19 on v16

--- a/solution.py
+++ b/solution.py
@@ -10,7 +10,7 @@
 HALO = 8
 LANE_PAD = 128
 HI = lax.Precision.HIGHEST
-PER_STEP = 4
+PER_STEP = 8
 
 
 def swap_exchange(last, first, axis):

time: 25.8 us -> 24.9 us (0.965)
  Pallas kernels: 8.73 us -> 7.78 us
    pallas_call x1, Pallas kernels: 8.73 us -> 7.78 us  [shards(): pl.pallas_call(smooth_kernel, grid=(count // PER_STEP,), in_specs=[smem,...]
where the time goes in v19:
time: 24.9 us; the launch traced here: 24.6 us
  Pallas kernels  7.78 us (31%)
  waiting for transfers between devices  6.35 us (26%)
  starting transfers between devices  5.54 us (22%)
  local copies, waits for them, and re-layouts  2.44 us (10%)
  other arithmetic  1.76 us (7%)
  between operations  0.74 us (3%)
    pallas_call x1, Pallas kernels, shards(): pl.pallas_call(smooth_kernel, grid=(count // PER_STEP,), in_specs=[smem,...  7.78 us
    ppermute x1, waiting for transfers between devices, swap_exchange(): two = lax.ppermute(jnp.where(even, first, last), axis, outer)  3.46 us
    ppermute x1, waiting for transfers between devices, halo_pieces(): lax.ppermute(jnp.where(even, first, last), 'gy', [(k, k + 1) for k in ran...  2.64 us
    ppermute x1, starting transfers between devices, halo_pieces(): lax.ppermute(jnp.where(even, first, last), 'gy', [(k, k + 1) for k in ran...  1.92 us
    ppermute x1, starting transfers between devices, swap_exchange(): two = lax.ppermute(jnp.where(even, first, last), axis, outer)  1.91 us
    ppermute x1, starting transfers between devices, swap_exchange(): one = lax.ppermute(jnp.where(even, last, first), axis, inner)  1.64 us
    unnamed x12, local copies, waits for them, and re-layouts  1.02 us
    slice x1, local copies, waits for them, and re-layouts, halo_pieces(): source[:, -width:, :]  0.88 us
  transfers between devices with their start and end apart: 4, of which 3 were waited for; matrix products, arithmetic and copies ran while one was open for 5% of the time, Pallas kernels for 0%

profile of v19, /device:TPU:18, one launch (start us, length us, event | category | flops | bytes accessed | tf_op | source)
XLA Modules:
  0.0 24.6 jit_solution(10581748645392622476)
XLA Ops:
  0.6 0.0 copy-start
  0.7 0.8 %convert_bitcast_fusion.1 = (f32[1,8,256]{2,1,0:T(8,128)S(1)}, f32[1,8,256]{2,1,0:T(8,128)S(1)}) fusion(s32[64,256]{1,0:T(8,128)} %cls_ref.1), kind=kLoop, calls=%fused_computation.18 | loop fusion | flops 8192 | bytes 32768 | tf_op jit(solution)/shard_map/broadcast_in_dim | solution.py:27
  1.4 0.9 %fusion.5 = (f32[8,8,256]{2,1,0:T(8,128)S(1)}, f32[8,8,256]{2,1,0:T(8,128)S(1)}) fusion(f32[8,64,256]{2,1,0:T(8,128)} %src_ref.1), kind=kLoop, calls=%fused_computation.22 | loop fusion | bytes 262144 | tf_op jit(solution)/shard_map/slice | solution.py:29
  2.3 0.0 copy-start.1
  2.3 1.6 %collective-permute-start = (f32[9,8,256]{2,1,0:T(8,128)S(1)}, f32[9,8,256]{2,1,0:T(8,128)S(1)}, u32[]{:S(2)}, u32[]{:S(2)}) collective-permute-start(f32[9,8,256]{2,1,0:T(8,128)S(1)} %get-tuple-element.10), channel_id=1, source_target_pairs={{0,8},{8,0},{16,24},{24,16},{1,9},{9,1},{17,25},{25,17},{2,10},{10... | collective-permute-start | bytes 221192 | tf_op jit(solution)/shard_map/ppermute | solution.py:21
  4.0 1.9 %collective-permute-start.1 = (f32[9,8,256]{2,1,0:T(8,128)S(1)}, f32[9,8,256]{2,1,0:T(8,128)S(1)}, u32[]{:S(2)}, u32[]{:S(2)}) collective-permute-start(f32[9,8,256]{2,1,0:T(8,128)S(1)} %get-tuple-element.11), channel_id=1, source_target_pairs={{8,16},{16,8},{9,17},{17,9},{10,18},{18,10},{11,19},{19,11},{12,20... | collective-permute-start | bytes 221192 | tf_op jit(solution)/shard_map/ppermute | solution.py:22
  5.9 0.0 copy-done.1
  5.9 0.1 fusion.6
  6.0 0.0 copy-done
  6.0 0.1 fusion.4
  6.1 0.1 copy.17
  6.2 0.1 copy.19
  6.3 0.1 copy.16
  6.4 0.1 copy.18
  6.5 0.2 %collective-permute-done = f32[9,8,256]{2,1,0:T(8,128)S(1)} collective-permute-done((f32[9,8,256]{2,1,0:T(8,128)S(1)}, f32[9,8,256]{2,1,0:T(8,128)S(1)}, u32[]{:S(2)}, u32[]{:S(2)}) %collective-permute-start) | collective-permute-done | bytes 73760 | tf_op jit(solution)/shard_map/ppermute | solution.py:21
  6.8 3.5 %collective-permute-done.1 = f32[9,8,256]{2,1,0:T(8,128)S(1)} collective-permute-done((f32[9,8,256]{2,1,0:T(8,128)S(1)}, f32[9,8,256]{2,1,0:T(8,128)S(1)}, u32[]{:S(2)}, u32[]{:S(2)}) %collective-permute-start.1) | collective-permute-done | bytes 73760 | tf_op jit(solution)/shard_map/ppermute | solution.py:22
  10.2 0.1 fusion
  10.3 0.1 copy.10
  10.4 0.1 copy.14
  10.5 0.1 maximum_bitcast_fusion
  10.6 0.1 copy.11
  10.7 0.1 maximum_bitcast_fusion.1
  10.8 0.1 copy.15
  10.9 1.9 %collective-permute-start.3 = (f32[80,128]{1,0:T(8,128)S(1)}, f32[80,128]{1,0:T(8,128)S(1)}, u32[]{:S(2)}, u32[]{:S(2)}) collective-permute-start(f32[80,128]{1,0:T(8,128)S(1)} %get-tuple-element.12), channel_id=1, source_target_pairs={{2,4},{4,2},{3,5},{5,3},{10,12},{12,10},{11,13},{13,11},{18,20},{2... | collective-permute-start | bytes 122888 | tf_op jit(solution)/shard_map/ppermute | solution.py:46
  12.8 0.1 collective-permute-start.2
  12.9 0.7 %pad_maximum_fusion.rows_ref = f32[9,16,256]{2,1,0:T(8,128)} fusion(f32[9,8,256]{2,1,0:T(8,128)S(1)} %get-tuple-element.9, f32[9,8,256]{2,1,0:T(8,128)S(1)} %get-tuple-element.8), kind=kLoop, calls=%fused_computation.2 | loop fusion | flops 36864 | bytes 294912 | tf_op jit(solution)/shard_map/concatenate | solution.py:33
  13.6 2.6 %collective-permute-done.3.two_ref = f32[80,128]{1,0:T(8,128)S(1)} collective-permute-done((f32[80,128]{1,0:T(8,128)S(1)}, f32[80,128]{1,0:T(8,128)S(1)}, u32[]{:S(2)}, u32[]{:S(2)}) %collective-permute-start.3) | collective-permute-done | bytes 40992 | tf_op jit(solution)/shard_map/ppermute | solution.py:46
  16.2 0.0 copy-start.2
  16.2 0.0 collective-permute-done.2.one_ref
  16.2 0.0 copy-start.3
  16.2 0.6 %copy-done.2 = f32[80,128]{1,0:T(8,128)} copy-done((f32[80,128]{1,0:T(8,128)}, f32[80,128]{1,0:T(8,128)S(1)}, u32[]{:S(2)}) %copy-start.2) | copy-done | bytes 40984
  16.8 0.0 copy-done.3
  16.8 7.8 %shard_map.59 = (f32[8,64,256]{2,1,0:T(8,128)}, f32[8,32,128]{2,1,0:T(8,128)}) custom-call(s32[8]{0:T(128)} %seeds_ref.1, f32[8,8]{1,0:T(8,128)} %levels_ref.1, s32[1]{0:T(128)} %bitcast.parity_ref, f32[8,64,256]{2,1,0:T(8,128)} %src_ref.1, s32[64,256]{1,0:T(8,128)} %cls_ref.1, f32[9,16,256]{2,1,0:T(8,128)} %pad_maximum_fusion.rows_ref, ...), custom_call_target="tpu_custom_call" | custom-call | tf_op jit(solution)/shard_map/pallas_call | solution.py:208
  (5 shorter events, 0.1 us)
Async XLA Ops:
  0.6 5.4 %copy-start = (f32[8,64,256]{2,1,0:T(8,128)S(1)}, f32[8,64,256]{2,1,0:T(8,128)}, u32[]{:S(2)}) copy-start(f32[8,64,256]{2,1,0:T(8,128)} %src_ref.1) | copy-start | bytes 1572868
  2.3 3.6 %copy-start.1 = (s32[64,256]{1,0:T(8,128)S(1)}, s32[64,256]{1,0:T(8,128)}, u32[]{:S(2)}) copy-start(s32[64,256]{1,0:T(8,128)} %cls_ref.1) | copy-start | bytes 196612
  2.3 4.4 %collective-permute-start = (f32[9,8,256]{2,1,0:T(8,128)S(1)}, f32[9,8,256]{2,1,0:T(8,128)S(1)}, u32[]{:S(2)}, u32[]{:S(2)}) collective-permute-start(f32[9,8,256]{2,1,0:T(8,128)S(1)} %get-tuple-element.10), channel_id=1, source_target_pairs={{0,8},{8,0},{16,24},{24,16},{1,9},{9,1},{17,25},{25,17},{2,10},{10... | collective-permute-start | bytes 221192 | tf_op jit(solution)/shard_map/ppermute | solution.py:21
  4.0 6.2 %collective-permute-start.1 = (f32[9,8,256]{2,1,0:T(8,128)S(1)}, f32[9,8,256]{2,1,0:T(8,128)S(1)}, u32[]{:S(2)}, u32[]{:S(2)}) collective-permute-start(f32[9,8,256]{2,1,0:T(8,128)S(1)} %get-tuple-element.11), channel_id=1, source_target_pairs={{8,16},{16,8},{9,17},{17,9},{10,18},{18,10},{11,19},{19,11},{12,20... | collective-permute-start | bytes 221192 | tf_op jit(solution)/shard_map/ppermute | solution.py:22
  10.9 5.3 %collective-permute-start.3 = (f32[80,128]{1,0:T(8,128)S(1)}, f32[80,128]{1,0:T(8,128)S(1)}, u32[]{:S(2)}, u32[]{:S(2)}) collective-permute-start(f32[80,128]{1,0:T(8,128)S(1)} %get-tuple-element.12), channel_id=1, source_target_pairs={{2,4},{4,2},{3,5},{5,3},{10,12},{12,10},{11,13},{13,11},{18,20},{2... | collective-permute-start | bytes 122888 | tf_op jit(solution)/shard_map/ppermute | solution.py:46
  12.8 3.4 %collective-permute-start.2 = (f32[80,128]{1,0:T(8,128)S(1)}, f32[80,128]{1,0:T(8,128)S(1)}, u32[]{:S(2)}, u32[]{:S(2)}) collective-permute-start(f32[80,128]{1,0:T(8,128)S(1)} %get-tuple-element.13), channel_id=1, source_target_pairs={{0,2},{2,0},{4,6},{6,4},{1,3},{3,1},{5,7},{7,5},{8,10},{10,8},{12,... | collective-permute-start | bytes 122888 | tf_op jit(solution)/shard_map/ppermute | solution.py:45
  16.2 0.6 %copy-start.2 = (f32[80,128]{1,0:T(8,128)}, f32[80,128]{1,0:T(8,128)S(1)}, u32[]{:S(2)}) copy-start(f32[80,128]{1,0:T(8,128)S(1)} %collective-permute-done.3.two_ref) | copy-start | bytes 122884
  16.2 0.6 %copy-start.3 = (f32[80,128]{1,0:T(8,128)}, f32[80,128]{1,0:T(8,128)S(1)}, u32[]{:S(2)}) copy-start(f32[80,128]{1,0:T(8,128)S(1)} %collective-permute-done.2.one_ref) | copy-start | bytes 122884

commit v20 on v18

--- a/solution.py
+++ b/solution.py
@@ -147,12 +147,12 @@
     high = jnp.where(bit1, jnp.where(bit0, level[7], level[6]), jnp.where(bit0, level[5], level[4]))
     perm = jnp.where(valid, jnp.where(bit2, high, low).reshape(ext_x, width), 0.0)
     linkage, diagonal = couplings(perm, (1, 1))
-    inverse = 1.0 / jnp.where(valid, diagonal, 1.0)
-    current = (DAMPING * source) * inverse
+    inverse = DAMPING / jnp.where(valid, diagonal, 1.0)
+    current = source * inverse
     for sweep_index in range(SWEEPS):
         residual = source - operator(linkage, diagonal, current, (1, 1))
         if sweep_index + 1 < SWEEPS:
-            current = current + (DAMPING * residual) * inverse
+            current = current + residual * inverse
 
     def even_rows(v):
         parts = []
@@ -166,10 +166,10 @@
     pairs = perm + pltpu.roll(perm, ext_x - 1, 0)
     coarse_perm = 0.25 * even_rows(pairs + pltpu.roll(pairs, width - 1, 1))
     coarse_links, coarse_diagonal = couplings(coarse_perm, (1, 2))
-    coarse_inverse = 1.0 / jnp.where(coarse_perm > 0.0, coarse_diagonal, 1.0)
-    first = (DAMPING * coarse_rhs) * coarse_inverse
+    coarse_inverse = DAMPING / jnp.where(coarse_perm > 0.0, coarse_diagonal, 1.0)
+    first = coarse_rhs * coarse_inverse
     correction = first + (
-        DAMPING * (coarse_rhs - operator(coarse_links, coarse_diagonal, first, (1, 2)))
+        coarse_rhs - operator(coarse_links, coarse_diagonal, first, (1, 2))
     ) * coarse_inverse
     pick = (
         lax.broadcasted_iota(jnp.int32, (cols, cols // 2), 0)

time: 24.9 us -> 25 us (level)
  no operation moved by 1% of the time
where the time goes in v20:
time: 25 us; the launch traced here: 24.8 us
  Pallas kernels  7.92 us (32%)
  waiting for transfers between devices  6.34 us (25%)
  starting transfers between devices  5.54 us (22%)
  other arithmetic  2.4 us (10%)
  local copies, waits for them, and re-layouts  1.81 us (7%)
  between operations  0.74 us (3%)
    pallas_call x1, Pallas kernels, shards(): pl.pallas_call(smooth_kernel, grid=(count // PER_STEP,), in_specs=[smem,...  7.92 us
    ppermute x2, waiting for transfers between devices, swap_exchange(): two = lax.ppermute(jnp.where(even, first, last), axis, outer)  6.09 us
    ppermute x2, starting transfers between devices, swap_exchange(): two = lax.ppermute(jnp.where(even, first, last), axis, outer)  3.83 us
    ppermute x2, starting transfers between devices, swap_exchange(): one = lax.ppermute(jnp.where(even, last, first), axis, inner)  1.71 us
    slice x1, local copies, waits for them, and re-layouts, halo_pieces(): source[:, -width:, :]  0.88 us
    broadcast_in_dim x3, other arithmetic, halo_pieces(): (b + 1).astype(a.dtype)[None]  0.79 us
    concatenate x2, other arithmetic, halo_pieces(): rows_halo = jnp.concatenate([high, low], axis=1)  0.76 us
    select_n x2, other arithmetic, swap_exchange(): return (jnp.where(even, two, one), jnp.where(even, one, two))  0.65 us
  transfers between devices with their start and end apart: 4, of which 3 were waited for; matrix products, arithmetic and copies ran while one was open for 5% of the time, Pallas kernels for 0%

profile of v20, /device:TPU:18, one launch (start us, length us, event | category | flops | bytes accessed | tf_op | source)
XLA Modules:
  0.0 24.8 jit_solution(10632989167517582830)
XLA Ops:
  0.6 0.0 copy-start
  0.7 0.8 %convert_bitcast_fusion.1 = (f32[1,8,256]{2,1,0:T(8,128)S(1)}, f32[1,8,256]{2,1,0:T(8,128)S(1)}) fusion(s32[64,256]{1,0:T(8,128)} %cls_ref.1), kind=kLoop, calls=%fused_computation.20 | loop fusion | flops 8192 | bytes 32768 | tf_op jit(solution)/shard_map/broadcast_in_dim | solution.py:27
  1.4 0.9 %fusion.5 = (f32[8,8,256]{2,1,0:T(8,128)S(1)}, f32[8,8,256]{2,1,0:T(8,128)S(1)}) fusion(f32[8,64,256]{2,1,0:T(8,128)} %src_ref.1), kind=kLoop, calls=%fused_computation.24 | loop fusion | bytes 262144 | tf_op jit(solution)/shard_map/slice | solution.py:29
  2.3 0.0 copy-start.1
  2.3 1.6 %collective-permute-start = (f32[9,8,256]{2,1,0:T(8,128)S(1)}, f32[9,8,256]{2,1,0:T(8,128)S(1)}, u32[]{:S(2)}, u32[]{:S(2)}) collective-permute-start(f32[9,8,256]{2,1,0:T(8,128)S(1)} %get-tuple-element.10), channel_id=1, source_target_pairs={{0,8},{8,0},{16,24},{24,16},{1,9},{9,1},{17,25},{25,17},{2,10},{10... | collective-permute-start | bytes 221192 | tf_op jit(solution)/shard_map/ppermute | solution.py:21
  4.0 1.9 %collective-permute-start.1 = (f32[9,8,256]{2,1,0:T(8,128)S(1)}, f32[9,8,256]{2,1,0:T(8,128)S(1)}, u32[]{:S(2)}, u32[]{:S(2)}) collective-permute-start(f32[9,8,256]{2,1,0:T(8,128)S(1)} %get-tuple-element.11), channel_id=1, source_target_pairs={{8,16},{16,8},{9,17},{17,9},{10,18},{18,10},{11,19},{19,11},{12,20... | collective-permute-start | bytes 221192 | tf_op jit(solution)/shard_map/ppermute | solution.py:22
  5.9 0.0 copy-done.1
  5.9 0.1 fusion.6
  6.0 0.0 copy-done
  6.0 0.1 fusion.4
  6.1 0.1 copy.17
  6.2 0.1 copy.19
  6.3 0.1 copy.16
  6.4 0.1 copy.18
  6.5 0.2 collective-permute-done
  6.8 3.5 %collective-permute-done.1 = f32[9,8,256]{2,1,0:T(8,128)S(1)} collective-permute-done((f32[9,8,256]{2,1,0:T(8,128)S(1)}, f32[9,8,256]{2,1,0:T(8,128)S(1)}, u32[]{:S(2)}, u32[]{:S(2)}) %collective-permute-start.1) | collective-permute-done | bytes 73760 | tf_op jit(solution)/shard_map/ppermute | solution.py:22
  10.2 0.1 fusion
  10.3 0.1 copy.10
  10.4 0.1 copy.14
  10.5 0.1 maximum_bitcast_fusion
  10.6 0.1 copy.11
  10.7 0.1 maximum_bitcast_fusion.1
  10.8 0.1 copy.15
  10.9 1.9 %collective-permute-start.3 = (f32[80,128]{1,0:T(8,128)S(1)}, f32[80,128]{1,0:T(8,128)S(1)}, u32[]{:S(2)}, u32[]{:S(2)}) collective-permute-start(f32[80,128]{1,0:T(8,128)S(1)} %get-tuple-element.14), channel_id=1, source_target_pairs={{2,4},{4,2},{3,5},{5,3},{10,12},{12,10},{11,13},{13,11},{18,20},{2... | collective-permute-start | bytes 122888 | tf_op jit(solution)/shard_map/ppermute | solution.py:22
  12.8 0.1 collective-permute-start.2
  12.9 0.7 %pad_maximum_fusion.rows_ref = f32[9,16,256]{2,1,0:T(8,128)} fusion(f32[9,8,256]{2,1,0:T(8,128)S(1)} %get-tuple-element.9, f32[9,8,256]{2,1,0:T(8,128)S(1)} %get-tuple-element.8), kind=kLoop, calls=%fused_computation.2 | loop fusion | flops 36864 | bytes 294912 | tf_op jit(solution)/shard_map/concatenate | solution.py:33
  13.6 2.6 %collective-permute-done.3 = f32[80,128]{1,0:T(8,128)S(1)} collective-permute-done((f32[80,128]{1,0:T(8,128)S(1)}, f32[80,128]{1,0:T(8,128)S(1)}, u32[]{:S(2)}, u32[]{:S(2)}) %collective-permute-start.3) | collective-permute-done | bytes 40992 | tf_op jit(solution)/shard_map/ppermute | solution.py:22
  16.2 0.0 collective-permute-done.2
  16.2 0.6 %broadcast_select_fusion.2 = (f32[80,128]{1,0:T(8,128)}, f32[80,128]{1,0:T(8,128)}) fusion(f32[80,128]{1,0:T(8,128)S(1)} %collective-permute-done.3, f32[80,128]{1,0:T(8,128)S(1)} %collective-permute-done.2, pred[]{:T(512)S(6)} %eq.10), kind=kLoop, calls=%fused_computation.17 | loop fusion | flops 20480 | bytes 163841 | tf_op jit(solution)/shard_map/jit(_where)/select_n | solution.py:23
  16.8 7.9 %shard_map.59 = (f32[8,64,256]{2,1,0:T(8,128)}, f32[8,32,128]{2,1,0:T(8,128)}) custom-call(s32[8]{0:T(128)} %seeds_ref.1, f32[8,8]{1,0:T(8,128)} %levels_ref.1, f32[8,64,256]{2,1,0:T(8,128)} %src_ref.1, s32[64,256]{1,0:T(8,128)} %cls_ref.1, f32[9,16,256]{2,1,0:T(8,128)} %pad_maximum_fusion.rows_ref, f32[80,128]{1,0:T(8,128)} %get-tuple-element.13.high_ref, ...), custom_call_target="tpu_custom_call" | custom-call | tf_op jit(solution)/shard_map/pallas_call | solution.py:201
  (5 shorter events, 0.1 us)
Async XLA Ops:
  0.6 5.4 %copy-start = (f32[8,64,256]{2,1,0:T(8,128)S(1)}, f32[8,64,256]{2,1,0:T(8,128)}, u32[]{:S(2)}) copy-start(f32[8,64,256]{2,1,0:T(8,128)} %src_ref.1) | copy-start | bytes 1572868
  2.3 3.6 %copy-start.1 = (s32[64,256]{1,0:T(8,128)S(1)}, s32[64,256]{1,0:T(8,128)}, u32[]{:S(2)}) copy-start(s32[64,256]{1,0:T(8,128)} %cls_ref.1) | copy-start | bytes 196612
  2.3 4.4 %collective-permute-start = (f32[9,8,256]{2,1,0:T(8,128)S(1)}, f32[9,8,256]{2,1,0:T(8,128)S(1)}, u32[]{:S(2)}, u32[]{:S(2)}) collective-permute-start(f32[9,8,256]{2,1,0:T(8,128)S(1)} %get-tuple-element.10), channel_id=1, source_target_pairs={{0,8},{8,0},{16,24},{24,16},{1,9},{9,1},{17,25},{25,17},{2,10},{10... | collective-permute-start | bytes 221192 | tf_op jit(solution)/shard_map/ppermute | solution.py:21
  4.0 6.2 %collective-permute-start.1 = (f32[9,8,256]{2,1,0:T(8,128)S(1)}, f32[9,8,256]{2,1,0:T(8,128)S(1)}, u32[]{:S(2)}, u32[]{:S(2)}) collective-permute-start(f32[9,8,256]{2,1,0:T(8,128)S(1)} %get-tuple-element.11), channel_id=1, source_target_pairs={{8,16},{16,8},{9,17},{17,9},{10,18},{18,10},{11,19},{19,11},{12,20... | collective-permute-start | bytes 221192 | tf_op jit(solution)/shard_map/ppermute | solution.py:22
  10.9 5.3 %collective-permute-start.3 = (f32[80,128]{1,0:T(8,128)S(1)}, f32[80,128]{1,0:T(8,128)S(1)}, u32[]{:S(2)}, u32[]{:S(2)}) collective-permute-start(f32[80,128]{1,0:T(8,128)S(1)} %get-tuple-element.14), channel_id=1, source_target_pairs={{2,4},{4,2},{3,5},{5,3},{10,12},{12,10},{11,13},{13,11},{18,20},{2... | collective-permute-start | bytes 122888 | tf_op jit(solution)/shard_map/ppermute | solution.py:22
  12.8 3.4 %collective-permute-start.2 = (f32[80,128]{1,0:T(8,128)S(1)}, f32[80,128]{1,0:T(8,128)S(1)}, u32[]{:S(2)}, u32[]{:S(2)}) collective-permute-start(f32[80,128]{1,0:T(8,128)S(1)} %get-tuple-element.15), channel_id=1, source_target_pairs={{0,2},{2,0},{4,6},{6,4},{1,3},{3,1},{5,7},{7,5},{8,10},{10,8},{12,... | collective-permute-start | bytes 122888 | tf_op jit(solution)/shard_map/ppermute | solution.py:21

commit v21 on v18

--- a/solution.py
+++ b/solution.py
@@ -98,7 +98,7 @@
 
 def smooth_kernel(
     seeds_ref, levels_ref, src_ref, cls_ref, rows_ref, high_ref, low_ref,
-    sol_ref, corr_ref, codes_pk, spare, wide,
+    sol_ref, corr_ref, codes_pk, spare, wide, sol_v, corr_v, written,
 ):
     s = pl.program_id(0)
     count = PER_STEP * pl.num_programs(0)
@@ -176,17 +176,28 @@
         == 2 * lax.broadcasted_iota(jnp.int32, (cols, cols // 2), 1)
     ).astype(jnp.float32)
     odd_col = (lax.broadcasted_iota(jnp.int32, (rows, cols), 1) & 1) == 1
+    copies = []
     for j in range(PER_STEP):
         back = (width - j * span - HALO) % width
         own = pltpu.roll(correction, back, 1)[: rows // 2, :cols]
-        corr_ref[j] = jnp.dot(own, pick, precision=HI, preferred_element_type=jnp.float32)
+        corr_v[j] = jnp.dot(own, pick, precision=HI, preferred_element_type=jnp.float32)
+        copies.append(
+            pltpu.make_async_copy(corr_v.at[j], corr_ref.at[PER_STEP * s + j], written.at[0, j])
+        )
+        copies[-1].start()
         for k in range(cols // 128):
             piece = own[:, k * 128 : (k + 1) * 128]
             wide[k, pl.ds(0, rows // 2, stride=2), :] = piece
             wide[k, pl.ds(1, rows // 2, stride=2), :] = piece
         spread = jnp.concatenate([wide[k] for k in range(cols // 128)], axis=1)
         spread = jnp.where(odd_col, pltpu.roll(spread, 1, 1), spread)
-        sol_ref[j] = pltpu.roll(current, back, 1)[:rows, :cols] + spread
+        sol_v[j] = pltpu.roll(current, back, 1)[:rows, :cols] + spread
+        copies.append(
+            pltpu.make_async_copy(sol_v.at[j], sol_ref.at[PER_STEP * s + j], written.at[1, j])
+        )
+        copies[-1].start()
+    for copy in copies:
+        copy.wait()
 
 
 def shards(source, sample_seeds, perm_levels, perm_classes):
@@ -211,8 +222,8 @@
             vmem,
         ],
         out_specs=[
-            pl.BlockSpec((PER_STEP, rows, cols), lambda s: (s, 0, 0)),
-            pl.BlockSpec((PER_STEP, rows // 2, cols // 2), lambda s: (s, 0, 0)),
+            pl.BlockSpec(memory_space=pl.ANY),
+            pl.BlockSpec(memory_space=pl.ANY),
         ],
         out_shape=[
             jax.ShapeDtypeStruct((count, rows, cols), jnp.float32),
@@ -222,6 +233,9 @@
             pltpu.VMEM((ext_x, width), jnp.int32),
             pltpu.VMEM((width // 128, ext_x, 128), jnp.float32),
             pltpu.VMEM((cols // 128, rows, 128), jnp.float32),
+            pltpu.VMEM((PER_STEP, rows, cols), jnp.float32),
+            pltpu.VMEM((PER_STEP, rows // 2, cols // 2), jnp.float32),
+            pltpu.SemaphoreType.DMA((2, PER_STEP)),
         ],
         compiler_params=pltpu.CompilerParams(dimension_semantics=("arbitrary",)),
     )(sample_seeds, perm_levels, source, perm_classes, rows_halo, high, low)

time: 24.9 us -> 24.9 us (level)
  no operation moved by 1% of the time
where the time goes in v21:
time: 24.9 us; the launch traced here: 24.6 us
  Pallas kernels  7.75 us (31%)
  waiting for transfers between devices  6.34 us (25%)
  starting transfers between devices  5.54 us (22%)
  other arithmetic  2.4 us (10%)
  local copies, waits for them, and re-layouts  1.81 us (7%)
  between operations  0.74 us (3%)
    pallas_call x1, Pallas kernels, shards(): pl.pallas_call(smooth_kernel, grid=(count // PER_STEP,), in_specs=[smem,...  7.75 us
    ppermute x2, waiting for transfers between devices, swap_exchange(): two = lax.ppermute(jnp.where(even, first, last), axis, outer)  6.09 us
    ppermute x2, starting transfers between devices, swap_exchange(): two = lax.ppermute(jnp.where(even, first, last), axis, outer)  3.83 us
    ppermute x2, starting transfers between devices, swap_exchange(): one = lax.ppermute(jnp.where(even, last, first), axis, inner)  1.71 us
    slice x1, local copies, waits for them, and re-layouts, halo_pieces(): source[:, -width:, :]  0.88 us
    broadcast_in_dim x3, other arithmetic, halo_pieces(): (b + 1).astype(a.dtype)[None]  0.79 us
    concatenate x2, other arithmetic, halo_pieces(): rows_halo = jnp.concatenate([high, low], axis=1)  0.76 us
    select_n x2, other arithmetic, swap_exchange(): return (jnp.where(even, two, one), jnp.where(even, one, two))  0.65 us
  transfers between devices with their start and end apart: 4, of which 3 were waited for; matrix products, arithmetic and copies ran while one was open for 5% of the time, Pallas kernels for 0%

profile of v21, /device:TPU:18, one launch (start us, length us, event | category | flops | bytes accessed | tf_op | source)
XLA Modules:
  0.0 24.6 jit_solution(12402849004095725398)
XLA Ops:
  0.6 0.0 copy-start
  0.7 0.8 %convert_bitcast_fusion.1 = (f32[1,8,256]{2,1,0:T(8,128)S(1)}, f32[1,8,256]{2,1,0:T(8,128)S(1)}) fusion(s32[64,256]{1,0:T(8,128)} %cls_ref.1), kind=kLoop, calls=%fused_computation.20 | loop fusion | flops 8192 | bytes 32768 | tf_op jit(solution)/shard_map/broadcast_in_dim | solution.py:27
  1.4 0.9 %fusion.5 = (f32[8,8,256]{2,1,0:T(8,128)S(1)}, f32[8,8,256]{2,1,0:T(8,128)S(1)}) fusion(f32[8,64,256]{2,1,0:T(8,128)} %src_ref.1), kind=kLoop, calls=%fused_computation.24 | loop fusion | bytes 262144 | tf_op jit(solution)/shard_map/slice | solution.py:29
  2.3 0.0 copy-start.1
  2.3 1.6 %collective-permute-start = (f32[9,8,256]{2,1,0:T(8,128)S(1)}, f32[9,8,256]{2,1,0:T(8,128)S(1)}, u32[]{:S(2)}, u32[]{:S(2)}) collective-permute-start(f32[9,8,256]{2,1,0:T(8,128)S(1)} %get-tuple-element.10), channel_id=1, source_target_pairs={{0,8},{8,0},{16,24},{24,16},{1,9},{9,1},{17,25},{25,17},{2,10},{10... | collective-permute-start | bytes 221192 | tf_op jit(solution)/shard_map/ppermute | solution.py:21
  4.0 1.9 %collective-permute-start.1 = (f32[9,8,256]{2,1,0:T(8,128)S(1)}, f32[9,8,256]{2,1,0:T(8,128)S(1)}, u32[]{:S(2)}, u32[]{:S(2)}) collective-permute-start(f32[9,8,256]{2,1,0:T(8,128)S(1)} %get-tuple-element.11), channel_id=1, source_target_pairs={{8,16},{16,8},{9,17},{17,9},{10,18},{18,10},{11,19},{19,11},{12,20... | collective-permute-start | bytes 221192 | tf_op jit(solution)/shard_map/ppermute | solution.py:22
  5.9 0.0 copy-done.1
  5.9 0.1 fusion.6
  6.0 0.0 copy-done
  6.0 0.1 fusion.4
  6.1 0.1 copy.17
  6.2 0.1 copy.19
  6.3 0.1 copy.16
  6.4 0.1 copy.18
  6.5 0.2 %collective-permute-done = f32[9,8,256]{2,1,0:T(8,128)S(1)} collective-permute-done((f32[9,8,256]{2,1,0:T(8,128)S(1)}, f32[9,8,256]{2,1,0:T(8,128)S(1)}, u32[]{:S(2)}, u32[]{:S(2)}) %collective-permute-start) | collective-permute-done | bytes 73760 | tf_op jit(solution)/shard_map/ppermute | solution.py:21
  6.8 3.5 %collective-permute-done.1 = f32[9,8,256]{2,1,0:T(8,128)S(1)} collective-permute-done((f32[9,8,256]{2,1,0:T(8,128)S(1)}, f32[9,8,256]{2,1,0:T(8,128)S(1)}, u32[]{:S(2)}, u32[]{:S(2)}) %collective-permute-start.1) | collective-permute-done | bytes 73760 | tf_op jit(solution)/shard_map/ppermute | solution.py:22
  10.2 0.1 fusion
  10.3 0.1 copy.10
  10.4 0.1 copy.14
  10.5 0.1 maximum_bitcast_fusion
  10.6 0.1 copy.11
  10.7 0.1 maximum_bitcast_fusion.1
  10.8 0.1 copy.15
  10.9 1.9 %collective-permute-start.3 = (f32[80,128]{1,0:T(8,128)S(1)}, f32[80,128]{1,0:T(8,128)S(1)}, u32[]{:S(2)}, u32[]{:S(2)}) collective-permute-start(f32[80,128]{1,0:T(8,128)S(1)} %get-tuple-element.14), channel_id=1, source_target_pairs={{2,4},{4,2},{3,5},{5,3},{10,12},{12,10},{11,13},{13,11},{18,20},{2... | collective-permute-start | bytes 122888 | tf_op jit(solution)/shard_map/ppermute | solution.py:22
  12.8 0.1 collective-permute-start.2
  12.9 0.7 %pad_maximum_fusion.rows_ref = f32[9,16,256]{2,1,0:T(8,128)} fusion(f32[9,8,256]{2,1,0:T(8,128)S(1)} %get-tuple-element.9, f32[9,8,256]{2,1,0:T(8,128)S(1)} %get-tuple-element.8), kind=kLoop, calls=%fused_computation.2 | loop fusion | flops 36864 | bytes 294912 | tf_op jit(solution)/shard_map/concatenate | solution.py:33
  13.6 2.6 %collective-permute-done.3 = f32[80,128]{1,0:T(8,128)S(1)} collective-permute-done((f32[80,128]{1,0:T(8,128)S(1)}, f32[80,128]{1,0:T(8,128)S(1)}, u32[]{:S(2)}, u32[]{:S(2)}) %collective-permute-start.3) | collective-permute-done | bytes 40992 | tf_op jit(solution)/shard_map/ppermute | solution.py:22
  16.2 0.0 collective-permute-done.2
  16.2 0.6 %broadcast_select_fusion.2 = (f32[80,128]{1,0:T(8,128)}, f32[80,128]{1,0:T(8,128)}) fusion(f32[80,128]{1,0:T(8,128)S(1)} %collective-permute-done.3, f32[80,128]{1,0:T(8,128)S(1)} %collective-permute-done.2, pred[]{:T(512)S(6)} %eq.10), kind=kLoop, calls=%fused_computation.17 | loop fusion | flops 20480 | bytes 163841 | tf_op jit(solution)/shard_map/jit(_where)/select_n | solution.py:23
  16.8 7.8 %shard_map.59 = (f32[8,64,256]{2,1,0:T(8,128)}, f32[8,32,128]{2,1,0:T(8,128)}) custom-call(s32[8]{0:T(128)} %seeds_ref.1, f32[8,8]{1,0:T(8,128)} %levels_ref.1, f32[8,64,256]{2,1,0:T(8,128)} %src_ref.1, s32[64,256]{1,0:T(8,128)} %cls_ref.1, f32[9,16,256]{2,1,0:T(8,128)} %pad_maximum_fusion.rows_ref, f32[80,128]{1,0:T(8,128)} %get-tuple-element.13.high_ref, ...), custom_call_target="tpu_custom_call" | custom-call | tf_op jit(solution)/shard_map/pallas_call | solution.py:212
  (5 shorter events, 0.1 us)
Async XLA Ops:
  0.6 5.4 %copy-start = (f32[8,64,256]{2,1,0:T(8,128)S(1)}, f32[8,64,256]{2,1,0:T(8,128)}, u32[]{:S(2)}) copy-start(f32[8,64,256]{2,1,0:T(8,128)} %src_ref.1) | copy-start | bytes 1572868
  2.3 3.6 %copy-start.1 = (s32[64,256]{1,0:T(8,128)S(1)}, s32[64,256]{1,0:T(8,128)}, u32[]{:S(2)}) copy-start(s32[64,256]{1,0:T(8,128)} %cls_ref.1) | copy-start | bytes 196612
  2.3 4.4 %collective-permute-start = (f32[9,8,256]{2,1,0:T(8,128)S(1)}, f32[9,8,256]{2,1,0:T(8,128)S(1)}, u32[]{:S(2)}, u32[]{:S(2)}) collective-permute-start(f32[9,8,256]{2,1,0:T(8,128)S(1)} %get-tuple-element.10), channel_id=1, source_target_pairs={{0,8},{8,0},{16,24},{24,16},{1,9},{9,1},{17,25},{25,17},{2,10},{10... | collective-permute-start | bytes 221192 | tf_op jit(solution)/shard_map/ppermute | solution.py:21
  4.0 6.2 %collective-permute-start.1 = (f32[9,8,256]{2,1,0:T(8,128)S(1)}, f32[9,8,256]{2,1,0:T(8,128)S(1)}, u32[]{:S(2)}, u32[]{:S(2)}) collective-permute-start(f32[9,8,256]{2,1,0:T(8,128)S(1)} %get-tuple-element.11), channel_id=1, source_target_pairs={{8,16},{16,8},{9,17},{17,9},{10,18},{18,10},{11,19},{19,11},{12,20... | collective-permute-start | bytes 221192 | tf_op jit(solution)/shard_map/ppermute | solution.py:22
  10.9 5.3 %collective-permute-start.3 = (f32[80,128]{1,0:T(8,128)S(1)}, f32[80,128]{1,0:T(8,128)S(1)}, u32[]{:S(2)}, u32[]{:S(2)}) collective-permute-start(f32[80,128]{1,0:T(8,128)S(1)} %get-tuple-element.14), channel_id=1, source_target_pairs={{2,4},{4,2},{3,5},{5,3},{10,12},{12,10},{11,13},{13,11},{18,20},{2... | collective-permute-start | bytes 122888 | tf_op jit(solution)/shard_map/ppermute | solution.py:22
  12.8 3.4 %collective-permute-start.2 = (f32[80,128]{1,0:T(8,128)S(1)}, f32[80,128]{1,0:T(8,128)S(1)}, u32[]{:S(2)}, u32[]{:S(2)}) collective-permute-start(f32[80,128]{1,0:T(8,128)S(1)} %get-tuple-element.15), channel_id=1, source_target_pairs={{0,2},{2,0},{4,6},{6,4},{1,3},{3,1},{5,7},{7,5},{8,10},{10,8},{12,... | collective-permute-start | bytes 122888 | tf_op jit(solution)/shard_map/ppermute | solution.py:21

commit v22 on v21

--- a/solution.py
+++ b/solution.py
@@ -108,11 +108,19 @@
     lane = lax.broadcasted_iota(jnp.int32, (ext_x, width), 1)
 
     def packed(pieces):
-        out = None
-        for j, piece in enumerate(pieces):
-            moved = pltpu.roll(piece, (j * span + HALO) % width, 1)
-            out = moved if out is None else jnp.where(lane >= j * span, moved, out)
-        return out
+        moved = [pltpu.roll(piece, (j * span + HALO) % width, 1) for j, piece in enumerate(pieces)]
+        chunk_lane = lax.broadcasted_iota(jnp.int32, (ext_x, 128), 1)
+        chunks = []
+        for low_edge in range(0, width, 128):
+            first = min(low_edge // span, len(pieces) - 1)
+            out = moved[first][:, low_edge : low_edge + 128]
+            for j in range(first + 1, len(pieces)):
+                if j * span < low_edge + 128:
+                    out = jnp.where(
+                        chunk_lane >= j * span - low_edge, moved[j][:, low_edge : low_edge + 128], out
+                    )
+            chunks.append(out)
+        return jnp.concatenate(chunks, axis=1)
 
     @pl.when(s == 0)
     def _():
@@ -147,12 +155,12 @@
     high = jnp.where(bit1, jnp.where(bit0, level[7], level[6]), jnp.where(bit0, level[5], level[4]))
     perm = jnp.where(valid, jnp.where(bit2, high, low).reshape(ext_x, width), 0.0)
     linkage, diagonal = couplings(perm, (1, 1))
-    inverse = 1.0 / jnp.where(valid, diagonal, 1.0)
-    current = (DAMPING * source) * inverse
+    inverse = DAMPING / jnp.where(valid, diagonal, 1.0)
+    current = source * inverse
     for sweep_index in range(SWEEPS):
         residual = source - operator(linkage, diagonal, current, (1, 1))
         if sweep_index + 1 < SWEEPS:
-            current = current + (DAMPING * residual) * inverse
+            current = current + residual * inverse
 
     def even_rows(v):
         parts = []
@@ -166,10 +174,10 @@
     pairs = perm + pltpu.roll(perm, ext_x - 1, 0)
     coarse_perm = 0.25 * even_rows(pairs + pltpu.roll(pairs, width - 1, 1))
     coarse_links, coarse_diagonal = couplings(coarse_perm, (1, 2))
-    coarse_inverse = 1.0 / jnp.where(coarse_perm > 0.0, coarse_diagonal, 1.0)
-    first = (DAMPING * coarse_rhs) * coarse_inverse
+    coarse_inverse = DAMPING / jnp.where(coarse_perm > 0.0, coarse_diagonal, 1.0)
+    first = coarse_rhs * coarse_inverse
     correction = first + (
-        DAMPING * (coarse_rhs - operator(coarse_links, coarse_diagonal, first, (1, 2)))
+        coarse_rhs - operator(coarse_links, coarse_diagonal, first, (1, 2))
     ) * coarse_inverse
     pick = (
         lax.broadcasted_iota(jnp.int32, (cols, cols // 2), 0)

time: 24.9 us -> 25 us (level)
  no operation moved by 1% of the time
where the time goes in v22:
time: 25 us; the launch traced here: 24.7 us
  Pallas kernels  7.91 us (32%)
  waiting for transfers between devices  6.34 us (25%)
  starting transfers between devices  5.54 us (22%)
  other arithmetic  2.4 us (10%)
  local copies, waits for them, and re-layouts  1.81 us (7%)
  between operations  0.74 us (3%)
    pallas_call x1, Pallas kernels, shards(): pl.pallas_call(smooth_kernel, grid=(count // PER_STEP,), in_specs=[smem,...  7.91 us
    ppermute x2, waiting for transfers between devices, swap_exchange(): two = lax.ppermute(jnp.where(even, first, last), axis, outer)  6.09 us
    ppermute x2, starting transfers between devices, swap_exchange(): two = lax.ppermute(jnp.where(even, first, last), axis, outer)  3.83 us
    ppermute x2, starting transfers between devices, swap_exchange(): one = lax.ppermute(jnp.where(even, last, first), axis, inner)  1.71 us
    slice x1, local copies, waits for them, and re-layouts, halo_pieces(): source[:, -width:, :]  0.88 us
    broadcast_in_dim x3, other arithmetic, halo_pieces(): (b + 1).astype(a.dtype)[None]  0.79 us
    concatenate x2, other arithmetic, halo_pieces(): rows_halo = jnp.concatenate([high, low], axis=1)  0.76 us
    select_n x2, other arithmetic, swap_exchange(): return (jnp.where(even, two, one), jnp.where(even, one, two))  0.65 us
  transfers between devices with their start and end apart: 4, of which 3 were waited for; matrix products, arithmetic and copies ran while one was open for 5% of the time, Pallas kernels for 0%

profile of v22, /device:TPU:18, one launch (start us, length us, event | category | flops | bytes accessed | tf_op | source)
XLA Modules:
  0.0 24.7 jit_solution(16184719422384406079)
XLA Ops:
  0.6 0.0 copy-start
  0.7 0.8 %convert_bitcast_fusion.1 = (f32[1,8,256]{2,1,0:T(8,128)S(1)}, f32[1,8,256]{2,1,0:T(8,128)S(1)}) fusion(s32[64,256]{1,0:T(8,128)} %cls_ref.1), kind=kLoop, calls=%fused_computation.20 | loop fusion | flops 8192 | bytes 32768 | tf_op jit(solution)/shard_map/broadcast_in_dim | solution.py:27
  1.4 0.9 %fusion.5 = (f32[8,8,256]{2,1,0:T(8,128)S(1)}, f32[8,8,256]{2,1,0:T(8,128)S(1)}) fusion(f32[8,64,256]{2,1,0:T(8,128)} %src_ref.1), kind=kLoop, calls=%fused_computation.24 | loop fusion | bytes 262144 | tf_op jit(solution)/shard_map/slice | solution.py:29
  2.3 0.0 copy-start.1
  2.3 1.6 %collective-permute-start = (f32[9,8,256]{2,1,0:T(8,128)S(1)}, f32[9,8,256]{2,1,0:T(8,128)S(1)}, u32[]{:S(2)}, u32[]{:S(2)}) collective-permute-start(f32[9,8,256]{2,1,0:T(8,128)S(1)} %get-tuple-element.10), channel_id=1, source_target_pairs={{0,8},{8,0},{16,24},{24,16},{1,9},{9,1},{17,25},{25,17},{2,10},{10... | collective-permute-start | bytes 221192 | tf_op jit(solution)/shard_map/ppermute | solution.py:21
  4.0 1.9 %collective-permute-start.1 = (f32[9,8,256]{2,1,0:T(8,128)S(1)}, f32[9,8,256]{2,1,0:T(8,128)S(1)}, u32[]{:S(2)}, u32[]{:S(2)}) collective-permute-start(f32[9,8,256]{2,1,0:T(8,128)S(1)} %get-tuple-element.11), channel_id=1, source_target_pairs={{8,16},{16,8},{9,17},{17,9},{10,18},{18,10},{11,19},{19,11},{12,20... | collective-permute-start | bytes 221192 | tf_op jit(solution)/shard_map/ppermute | solution.py:22
  5.9 0.0 copy-done.1
  5.9 0.1 fusion.6
  6.0 0.0 copy-done
  6.0 0.1 fusion.4
  6.1 0.1 copy.17
  6.2 0.1 copy.19
  6.3 0.1 copy.16
  6.4 0.1 copy.18
  6.5 0.2 collective-permute-done
  6.8 3.5 %collective-permute-done.1 = f32[9,8,256]{2,1,0:T(8,128)S(1)} collective-permute-done((f32[9,8,256]{2,1,0:T(8,128)S(1)}, f32[9,8,256]{2,1,0:T(8,128)S(1)}, u32[]{:S(2)}, u32[]{:S(2)}) %collective-permute-start.1) | collective-permute-done | bytes 73760 | tf_op jit(solution)/shard_map/ppermute | solution.py:22
  10.2 0.1 fusion
  10.3 0.1 copy.10
  10.4 0.1 copy.14
  10.5 0.1 maximum_bitcast_fusion
  10.6 0.1 copy.11
  10.7 0.1 maximum_bitcast_fusion.1
  10.8 0.1 copy.15
  10.9 1.9 %collective-permute-start.3 = (f32[80,128]{1,0:T(8,128)S(1)}, f32[80,128]{1,0:T(8,128)S(1)}, u32[]{:S(2)}, u32[]{:S(2)}) collective-permute-start(f32[80,128]{1,0:T(8,128)S(1)} %get-tuple-element.14), channel_id=1, source_target_pairs={{2,4},{4,2},{3,5},{5,3},{10,12},{12,10},{11,13},{13,11},{18,20},{2... | collective-permute-start | bytes 122888 | tf_op jit(solution)/shard_map/ppermute | solution.py:22
  12.8 0.1 collective-permute-start.2
  12.9 0.7 %pad_maximum_fusion.rows_ref = f32[9,16,256]{2,1,0:T(8,128)} fusion(f32[9,8,256]{2,1,0:T(8,128)S(1)} %get-tuple-element.9, f32[9,8,256]{2,1,0:T(8,128)S(1)} %get-tuple-element.8), kind=kLoop, calls=%fused_computation.2 | loop fusion | flops 36864 | bytes 294912 | tf_op jit(solution)/shard_map/concatenate | solution.py:33
  13.6 2.6 %collective-permute-done.3 = f32[80,128]{1,0:T(8,128)S(1)} collective-permute-done((f32[80,128]{1,0:T(8,128)S(1)}, f32[80,128]{1,0:T(8,128)S(1)}, u32[]{:S(2)}, u32[]{:S(2)}) %collective-permute-start.3) | collective-permute-done | bytes 40992 | tf_op jit(solution)/shard_map/ppermute | solution.py:22
  16.2 0.0 collective-permute-done.2
  16.2 0.6 %broadcast_select_fusion.2 = (f32[80,128]{1,0:T(8,128)}, f32[80,128]{1,0:T(8,128)}) fusion(f32[80,128]{1,0:T(8,128)S(1)} %collective-permute-done.3, f32[80,128]{1,0:T(8,128)S(1)} %collective-permute-done.2, pred[]{:T(512)S(6)} %eq.10), kind=kLoop, calls=%fused_computation.17 | loop fusion | flops 20480 | bytes 163841 | tf_op jit(solution)/shard_map/jit(_where)/select_n | solution.py:23
  16.8 7.9 %shard_map.59 = (f32[8,64,256]{2,1,0:T(8,128)}, f32[8,32,128]{2,1,0:T(8,128)}) custom-call(s32[8]{0:T(128)} %seeds_ref.1, f32[8,8]{1,0:T(8,128)} %levels_ref.1, f32[8,64,256]{2,1,0:T(8,128)} %src_ref.1, s32[64,256]{1,0:T(8,128)} %cls_ref.1, f32[9,16,256]{2,1,0:T(8,128)} %pad_maximum_fusion.rows_ref, f32[80,128]{1,0:T(8,128)} %get-tuple-element.13.high_ref, ...), custom_call_target="tpu_custom_call" | custom-call | tf_op jit(solution)/shard_map/pallas_call | solution.py:220
  (5 shorter events, 0.1 us)
Async XLA Ops:
  0.6 5.4 %copy-start = (f32[8,64,256]{2,1,0:T(8,128)S(1)}, f32[8,64,256]{2,1,0:T(8,128)}, u32[]{:S(2)}) copy-start(f32[8,64,256]{2,1,0:T(8,128)} %src_ref.1) | copy-start | bytes 1572868
  2.3 3.6 %copy-start.1 = (s32[64,256]{1,0:T(8,128)S(1)}, s32[64,256]{1,0:T(8,128)}, u32[]{:S(2)}) copy-start(s32[64,256]{1,0:T(8,128)} %cls_ref.1) | copy-start | bytes 196612
  2.3 4.4 %collective-permute-start = (f32[9,8,256]{2,1,0:T(8,128)S(1)}, f32[9,8,256]{2,1,0:T(8,128)S(1)}, u32[]{:S(2)}, u32[]{:S(2)}) collective-permute-start(f32[9,8,256]{2,1,0:T(8,128)S(1)} %get-tuple-element.10), channel_id=1, source_target_pairs={{0,8},{8,0},{16,24},{24,16},{1,9},{9,1},{17,25},{25,17},{2,10},{10... | collective-permute-start | bytes 221192 | tf_op jit(solution)/shard_map/ppermute | solution.py:21
  4.0 6.2 %collective-permute-start.1 = (f32[9,8,256]{2,1,0:T(8,128)S(1)}, f32[9,8,256]{2,1,0:T(8,128)S(1)}, u32[]{:S(2)}, u32[]{:S(2)}) collective-permute-start(f32[9,8,256]{2,1,0:T(8,128)S(1)} %get-tuple-element.11), channel_id=1, source_target_pairs={{8,16},{16,8},{9,17},{17,9},{10,18},{18,10},{11,19},{19,11},{12,20... | collective-permute-start | bytes 221192 | tf_op jit(solution)/shard_map/ppermute | solution.py:22
  10.9 5.3 %collective-permute-start.3 = (f32[80,128]{1,0:T(8,128)S(1)}, f32[80,128]{1,0:T(8,128)S(1)}, u32[]{:S(2)}, u32[]{:S(2)}) collective-permute-start(f32[80,128]{1,0:T(8,128)S(1)} %get-tuple-element.14), channel_id=1, source_target_pairs={{2,4},{4,2},{3,5},{5,3},{10,12},{12,10},{11,13},{13,11},{18,20},{2... | collective-permute-start | bytes 122888 | tf_op jit(solution)/shard_map/ppermute | solution.py:22
  12.8 3.4 %collective-permute-start.2 = (f32[80,128]{1,0:T(8,128)S(1)}, f32[80,128]{1,0:T(8,128)S(1)}, u32[]{:S(2)}, u32[]{:S(2)}) collective-permute-start(f32[80,128]{1,0:T(8,128)S(1)} %get-tuple-element.15), channel_id=1, source_target_pairs={{0,2},{2,0},{4,6},{6,4},{1,3},{3,1},{5,7},{7,5},{8,10},{10,8},{12,... | collective-permute-start | bytes 122888 | tf_op jit(solution)/shard_map/ppermute | solution.py:21

commit v23 on v18

--- a/solution.py
+++ b/solution.py
@@ -18,8 +18,8 @@
     even = lax.axis_index(axis) % 2 == 0
     inner = [(k, k ^ 1) for k in range(n) if k ^ 1 < n]
     outer = [(k, k + 1) for k in range(1, n - 1, 2)] + [(k + 1, k) for k in range(1, n - 1, 2)]
+    two = lax.ppermute(jnp.where(even, first, last), axis, outer)
     one = lax.ppermute(jnp.where(even, last, first), axis, inner)
-    two = lax.ppermute(jnp.where(even, first, last), axis, outer)
     return jnp.where(even, two, one), jnp.where(even, one, two)
 
 

time: 24.9 us -> 24.9 us (level)
  no operation moved by 1% of the time
where the time goes in v23:
time: 24.9 us; the launch traced here: 24.6 us
  Pallas kernels  7.78 us (31%)
  waiting for transfers between devices  6.34 us (25%)
  starting transfers between devices  5.54 us (22%)
  other arithmetic  2.4 us (10%)
  local copies, waits for them, and re-layouts  1.81 us (7%)
  between operations  0.74 us (3%)
    pallas_call x1, Pallas kernels, shards(): pl.pallas_call(smooth_kernel, grid=(count // PER_STEP,), in_specs=[smem,...  7.78 us
    ppermute x2, waiting for transfers between devices, swap_exchange(): two = lax.ppermute(jnp.where(even, first, last), axis, outer)  6.09 us
    ppermute x2, starting transfers between devices, swap_exchange(): two = lax.ppermute(jnp.where(even, first, last), axis, outer)  3.83 us
    ppermute x2, starting transfers between devices, swap_exchange(): one = lax.ppermute(jnp.where(even, last, first), axis, inner)  1.71 us
    slice x1, local copies, waits for them, and re-layouts, halo_pieces(): source[:, -width:, :]  0.88 us
    broadcast_in_dim x3, other arithmetic, halo_pieces(): (b + 1).astype(a.dtype)[None]  0.79 us
    concatenate x2, other arithmetic, halo_pieces(): rows_halo = jnp.concatenate([high, low], axis=1)  0.76 us
    select_n x2, other arithmetic, swap_exchange(): return (jnp.where(even, two, one), jnp.where(even, one, two))  0.65 us
  transfers between devices with their start and end apart: 4, of which 3 were waited for; matrix products, arithmetic and copies ran while one was open for 5% of the time, Pallas kernels for 0%

profile of v23, /device:TPU:18, one launch (start us, length us, event | category | flops | bytes accessed | tf_op | source)
XLA Modules:
  0.0 24.6 jit_solution(8024386269941510507)
XLA Ops:
  0.6 0.0 copy-start
  0.7 0.8 %convert_bitcast_fusion.1 = (f32[1,8,256]{2,1,0:T(8,128)S(1)}, f32[1,8,256]{2,1,0:T(8,128)S(1)}) fusion(s32[64,256]{1,0:T(8,128)} %cls_ref.1), kind=kLoop, calls=%fused_computation.20 | loop fusion | flops 8192 | bytes 32768 | tf_op jit(solution)/shard_map/broadcast_in_dim | solution.py:27
  1.4 0.9 %fusion.5 = (f32[8,8,256]{2,1,0:T(8,128)S(1)}, f32[8,8,256]{2,1,0:T(8,128)S(1)}) fusion(f32[8,64,256]{2,1,0:T(8,128)} %src_ref.1), kind=kLoop, calls=%fused_computation.24 | loop fusion | bytes 262144 | tf_op jit(solution)/shard_map/slice | solution.py:29
  2.3 0.0 copy-start.1
  2.3 1.6 %collective-permute-start = (f32[9,8,256]{2,1,0:T(8,128)S(1)}, f32[9,8,256]{2,1,0:T(8,128)S(1)}, u32[]{:S(2)}, u32[]{:S(2)}) collective-permute-start(f32[9,8,256]{2,1,0:T(8,128)S(1)} %get-tuple-element.10), channel_id=1, source_target_pairs={{0,8},{8,0},{16,24},{24,16},{1,9},{9,1},{17,25},{25,17},{2,10},{10... | collective-permute-start | bytes 221192 | tf_op jit(solution)/shard_map/ppermute | solution.py:22
  4.0 1.9 %collective-permute-start.1 = (f32[9,8,256]{2,1,0:T(8,128)S(1)}, f32[9,8,256]{2,1,0:T(8,128)S(1)}, u32[]{:S(2)}, u32[]{:S(2)}) collective-permute-start(f32[9,8,256]{2,1,0:T(8,128)S(1)} %get-tuple-element.11), channel_id=1, source_target_pairs={{8,16},{16,8},{9,17},{17,9},{10,18},{18,10},{11,19},{19,11},{12,20... | collective-permute-start | bytes 221192 | tf_op jit(solution)/shard_map/ppermute | solution.py:21
  5.9 0.0 copy-done.1
  5.9 0.1 fusion.6
  6.0 0.0 copy-done
  6.0 0.1 fusion.4
  6.1 0.1 copy.17
  6.2 0.1 copy.19
  6.3 0.1 copy.16
  6.4 0.1 copy.18
  6.5 0.2 %collective-permute-done = f32[9,8,256]{2,1,0:T(8,128)S(1)} collective-permute-done((f32[9,8,256]{2,1,0:T(8,128)S(1)}, f32[9,8,256]{2,1,0:T(8,128)S(1)}, u32[]{:S(2)}, u32[]{:S(2)}) %collective-permute-start) | collective-permute-done | bytes 73760 | tf_op jit(solution)/shard_map/ppermute | solution.py:22
  6.8 3.5 %collective-permute-done.1 = f32[9,8,256]{2,1,0:T(8,128)S(1)} collective-permute-done((f32[9,8,256]{2,1,0:T(8,128)S(1)}, f32[9,8,256]{2,1,0:T(8,128)S(1)}, u32[]{:S(2)}, u32[]{:S(2)}) %collective-permute-start.1) | collective-permute-done | bytes 73760 | tf_op jit(solution)/shard_map/ppermute | solution.py:21
  10.2 0.1 fusion
  10.3 0.1 copy.10
  10.4 0.1 copy.14
  10.5 0.1 maximum_bitcast_fusion
  10.6 0.1 copy.11
  10.7 0.1 maximum_bitcast_fusion.1
  10.8 0.1 copy.15
  10.9 1.9 %collective-permute-start.3 = (f32[80,128]{1,0:T(8,128)S(1)}, f32[80,128]{1,0:T(8,128)S(1)}, u32[]{:S(2)}, u32[]{:S(2)}) collective-permute-start(f32[80,128]{1,0:T(8,128)S(1)} %get-tuple-element.14), channel_id=1, source_target_pairs={{2,4},{4,2},{3,5},{5,3},{10,12},{12,10},{11,13},{13,11},{18,20},{2... | collective-permute-start | bytes 122888 | tf_op jit(solution)/shard_map/ppermute | solution.py:21
  12.8 0.1 collective-permute-start.2
  12.9 0.7 %pad_maximum_fusion.rows_ref = f32[9,16,256]{2,1,0:T(8,128)} fusion(f32[9,8,256]{2,1,0:T(8,128)S(1)} %get-tuple-element.9, f32[9,8,256]{2,1,0:T(8,128)S(1)} %get-tuple-element.8), kind=kLoop, calls=%fused_computation.2 | loop fusion | flops 36864 | bytes 294912 | tf_op jit(solution)/shard_map/concatenate | solution.py:33
  13.6 2.6 %collective-permute-done.3 = f32[80,128]{1,0:T(8,128)S(1)} collective-permute-done((f32[80,128]{1,0:T(8,128)S(1)}, f32[80,128]{1,0:T(8,128)S(1)}, u32[]{:S(2)}, u32[]{:S(2)}) %collective-permute-start.3) | collective-permute-done | bytes 40992 | tf_op jit(solution)/shard_map/ppermute | solution.py:21
  16.2 0.0 collective-permute-done.2
  16.2 0.6 %broadcast_select_fusion.2 = (f32[80,128]{1,0:T(8,128)}, f32[80,128]{1,0:T(8,128)}) fusion(f32[80,128]{1,0:T(8,128)S(1)} %collective-permute-done.3, f32[80,128]{1,0:T(8,128)S(1)} %collective-permute-done.2, pred[]{:T(512)S(6)} %eq.10), kind=kLoop, calls=%fused_computation.17 | loop fusion | flops 20480 | bytes 163841 | tf_op jit(solution)/shard_map/jit(_where)/select_n | solution.py:23
  16.8 7.8 %shard_map.59 = (f32[8,64,256]{2,1,0:T(8,128)}, f32[8,32,128]{2,1,0:T(8,128)}) custom-call(s32[8]{0:T(128)} %seeds_ref.1, f32[8,8]{1,0:T(8,128)} %levels_ref.1, f32[8,64,256]{2,1,0:T(8,128)} %src_ref.1, s32[64,256]{1,0:T(8,128)} %cls_ref.1, f32[9,16,256]{2,1,0:T(8,128)} %pad_maximum_fusion.rows_ref, f32[80,128]{1,0:T(8,128)} %get-tuple-element.13.high_ref, ...), custom_call_target="tpu_custom_call" | custom-call | tf_op jit(solution)/shard_map/pallas_call | solution.py:201
  (5 shorter events, 0.1 us)
Async XLA Ops:
  0.6 5.4 %copy-start = (f32[8,64,256]{2,1,0:T(8,128)S(1)}, f32[8,64,256]{2,1,0:T(8,128)}, u32[]{:S(2)}) copy-start(f32[8,64,256]{2,1,0:T(8,128)} %src_ref.1) | copy-start | bytes 1572868
  2.3 3.6 %copy-start.1 = (s32[64,256]{1,0:T(8,128)S(1)}, s32[64,256]{1,0:T(8,128)}, u32[]{:S(2)}) copy-start(s32[64,256]{1,0:T(8,128)} %cls_ref.1) | copy-start | bytes 196612
  2.3 4.4 %collective-permute-start = (f32[9,8,256]{2,1,0:T(8,128)S(1)}, f32[9,8,256]{2,1,0:T(8,128)S(1)}, u32[]{:S(2)}, u32[]{:S(2)}) collective-permute-start(f32[9,8,256]{2,1,0:T(8,128)S(1)} %get-tuple-element.10), channel_id=1, source_target_pairs={{0,8},{8,0},{16,24},{24,16},{1,9},{9,1},{17,25},{25,17},{2,10},{10... | collective-permute-start | bytes 221192 | tf_op jit(solution)/shard_map/ppermute | solution.py:22
  4.0 6.2 %collective-permute-start.1 = (f32[9,8,256]{2,1,0:T(8,128)S(1)}, f32[9,8,256]{2,1,0:T(8,128)S(1)}, u32[]{:S(2)}, u32[]{:S(2)}) collective-permute-start(f32[9,8,256]{2,1,0:T(8,128)S(1)} %get-tuple-element.11), channel_id=1, source_target_pairs={{8,16},{16,8},{9,17},{17,9},{10,18},{18,10},{11,19},{19,11},{12,20... | collective-permute-start | bytes 221192 | tf_op jit(solution)/shard_map/ppermute | solution.py:21
  10.9 5.3 %collective-permute-start.3 = (f32[80,128]{1,0:T(8,128)S(1)}, f32[80,128]{1,0:T(8,128)S(1)}, u32[]{:S(2)}, u32[]{:S(2)}) collective-permute-start(f32[80,128]{1,0:T(8,128)S(1)} %get-tuple-element.14), channel_id=1, source_target_pairs={{2,4},{4,2},{3,5},{5,3},{10,12},{12,10},{11,13},{13,11},{18,20},{2... | collective-permute-start | bytes 122888 | tf_op jit(solution)/shard_map/ppermute | solution.py:21
  12.8 3.4 %collective-permute-start.2 = (f32[80,128]{1,0:T(8,128)S(1)}, f32[80,128]{1,0:T(8,128)S(1)}, u32[]{:S(2)}, u32[]{:S(2)}) collective-permute-start(f32[80,128]{1,0:T(8,128)S(1)} %get-tuple-element.15), channel_id=1, source_target_pairs={{0,2},{2,0},{4,6},{6,4},{1,3},{3,1},{5,7},{7,5},{8,10},{10,8},{12,... | collective-permute-start | bytes 122888 | tf_op jit(solution)/shard_map/ppermute | solution.py:22
